TPU v7x, 32 devices: a whole 2x2x4 slice. The times are simulated.
32 devices in a mesh: group: 16 (over z, y, core), shard: 2 (over x).
Axes of the slice: x: 2, y: 2, z: 4, core: 2. Of those that a mesh axis runs over, the one named last changes fastest.
Arguments:
- tokens: bfloat16 [32768, 768], P(('group', 'shard')), may hold values from -6 to 6
- doc_lengths: int32 [32, 5], P(('group', 'shard')), may hold values from 1 to 512, 1024 in all within a row
- first_gain: bfloat16 [768], P(('group', 'shard')), may hold values from 0.099609375 to 1.8984375
- first_shift: bfloat16 [768], P(('group', 'shard')), may hold values from -3 to 3
- qkv_weight: bfloat16 [768, 2304], P(('group', 'shard')), may hold values from -0.21875 to 0.21875
- query_bias: bfloat16 [768], P(('group', 'shard')), may hold values from -3 to 3
- value_bias: bfloat16 [768], P(('group', 'shard')), may hold values from -3 to 3
- inner_gain: bfloat16 [768], P(('group', 'shard')), may hold values from 0.099609375 to 1.8984375
- inner_shift: bfloat16 [768], P(('group', 'shard')), may hold values from -3 to 3
- proj_weight: bfloat16 [768, 768], P(('group', 'shard')), may hold values from -0.21875 to 0.21875
- proj_bias: bfloat16 [768], P(('group', 'shard')), may hold values from -3 to 3
- second_gain: bfloat16 [768], P(('group', 'shard')), may hold values from 0.099609375 to 1.8984375
- second_shift: bfloat16 [768], P(('group', 'shard')), may hold values from -3 to 3
- expand_weight: bfloat16 [768, 3072], P(('group', 'shard')), may hold values from -0.21875 to 0.21875
- expand_bias: bfloat16 [3072], P(('group', 'shard')), may hold values from -3 to 3
- hidden_gain: bfloat16 [3072], P(('group', 'shard')), may hold values from 0.099609375 to 1.8984375
- hidden_shift: bfloat16 [3072], P(('group', 'shard')), may hold values from -3 to 3
- shrink_weight: bfloat16 [3072, 768], P(('group', 'shard')), may hold values from -0.109375 to 0.109375
- shrink_bias: bfloat16 [768], P(('group', 'shard')), may hold values from -3 to 3
- out_cotangent: bfloat16 [32768, 768], P(('group', 'shard')), may hold values from -6 to 6
Outputs:
- block_output: bfloat16 [32768, 768], P(('group', 'shard'))
- input_grad: bfloat16 [32768, 768], P(('group', 'shard'))
- first_gain_grad: float32 [768], P('shard')
- first_shift_grad: float32 [768], P('shard')
- qkv_weight_grad: float32 [768, 2304], P('shard')
- query_bias_grad: float32 [768], P('shard')
- value_bias_grad: float32 [768], P('shard')
- inner_gain_grad: float32 [768], P('shard')
- inner_shift_grad: float32 [768], P('shard')
- proj_weight_grad: float32 [768, 768], P('shard')
- proj_bias_grad: float32 [768], P('shard')
- second_gain_grad: float32 [768], P('shard')
- second_shift_grad: float32 [768], P('shard')
- expand_weight_grad: float32 [768, 3072], P('shard')
- expand_bias_grad: float32 [3072], P('shard')
- hidden_gain_grad: float32 [3072], P('shard')
- hidden_shift_grad: float32 [3072], P('shard')
- shrink_weight_grad: float32 [3072, 768], P('shard')
- shrink_bias_grad: float32 [768], P('shard')
Inputs may be any that keep to these rules, and one draw needn't show every extreme that they name: `doc_lengths`: the last entry of each row is the padding at the row's end; one entry of every row is exactly 512; each row sums to 1024.
All inputs are finite; a program needn't handle non-finite values.
Results may differ from a plain program's by a relative error of at most 0.02.
Values may be sent and summed in bfloat16 or wider, within the bound.
No kernel may reach another device: no remote copies, remote signals or barrier semaphores. Data moves between devices by JAX's collectives and lax.ppermute only.
A program may use at most 320 MiB of HBM per device.

v0:
```python
import functools
import math

import jax
import jax.numpy as jnp
from jax import lax
from jax.sharding import PartitionSpec as P

HEADS = 12
HEAD = 64
NSEG = 5


EPSILON = 1e-05
MASKED = -1000000000.0


def norm_apply(values, gain, shift):
    average = jnp.mean(values, axis=-1, keepdims=True)
    centered = values - average
    inv_scale = lax.rsqrt(jnp.mean(centered * centered, axis=-1, keepdims=True) + EPSILON)
    unit = centered * inv_scale
    return (unit * gain + shift, unit, inv_scale)


def norm_back(unit, inv_scale, gain, grad):
    scaled = grad * gain
    back = inv_scale * (
        scaled
        - jnp.mean(scaled, axis=-1, keepdims=True)
        - unit * jnp.mean(scaled * unit, axis=-1, keepdims=True)
    )
    return (back, jnp.sum(grad * unit, axis=0), jnp.sum(grad, axis=0))


def gelu_exact(values):
    return jax.nn.gelu(values, approximate=False)


def segment_ids(lengths_row, length):
    ends = jnp.cumsum(lengths_row)
    places = jnp.arange(length, dtype=jnp.int32)
    return jnp.sum((places[:, None] >= ends[None, :]).astype(jnp.int32), axis=1)


def split_heads(qkv_row):
    length = qkv_row.shape[0]
    width = qkv_row.shape[1] // 3
    queries = qkv_row[:, :width].reshape(length, HEADS, HEAD)
    key_heads = qkv_row[:, width : 2 * width].reshape(length, HEADS, HEAD)
    value_heads = qkv_row[:, 2 * width :].reshape(length, HEADS, HEAD)
    return (queries, key_heads, value_heads)


def masked_scores(query_part, key_heads, segment, valid, offset):
    query_count = query_part.shape[0]
    scores = jnp.einsum(
        "qhd,khd->hqk", query_part, key_heads, preferred_element_type=jnp.float32
    ) * (1.0 / math.sqrt(HEAD))
    places = jnp.arange(segment.shape[0], dtype=jnp.int32)
    query_places = places[offset : offset + query_count]
    query_segment = segment[offset : offset + query_count]
    allowed = (
        (query_segment[:, None] == segment[None, :])
        & (query_places[:, None] >= places[None, :])
        & valid[None, :]
    )
    return jnp.where(allowed[None], scores, MASKED)


def row_forward(pieces):
    qkv_row, segment = pieces
    length = qkv_row.shape[0]
    queries, key_heads, value_heads = split_heads(qkv_row)
    valid = segment < NSEG - 1
    block_rows = min(512, length)
    attended_parts = []
    totals = []
    for offset in range(0, length, block_rows):
        scores = masked_scores(
            queries[offset : offset + block_rows], key_heads, segment, valid, offset
        )
        keep_rows = valid[offset : offset + block_rows].astype(jnp.float32)[None, :, None]
        peak = jnp.max(scores, axis=-1, keepdims=True)
        expd = jnp.exp(scores - peak)
        total = jnp.sum(expd, axis=-1, keepdims=True)
        probs = (expd / total * keep_rows).astype(jnp.bfloat16)
        attended_parts.append(
            jnp.einsum(
                "hqk,khd->qhd", probs, value_heads, preferred_element_type=jnp.float32
            ).reshape(block_rows, HEADS * HEAD)
        )
        totals.append((peak + jnp.log(total))[:, :, 0])
    return (jnp.concatenate(attended_parts, axis=0), jnp.concatenate(totals, axis=1))


def row_backward(pieces):
    qkv_row, segment, log_total, grad_rows = pieces
    length = qkv_row.shape[0]
    queries, key_heads, value_heads = split_heads(qkv_row)
    valid = segment < NSEG - 1
    grad_heads = grad_rows.reshape(length, HEADS, HEAD)
    block_rows = min(512, length)
    scale_factor = 1.0 / math.sqrt(HEAD)
    query_grads = []
    key_grad = jnp.zeros((length, HEADS, HEAD), jnp.float32)
    value_grad = jnp.zeros((length, HEADS, HEAD), jnp.float32)
    for offset in range(0, length, block_rows):
        query_part = queries[offset : offset + block_rows]
        scores = masked_scores(query_part, key_heads, segment, valid, offset)
        keep_rows = valid[offset : offset + block_rows].astype(jnp.float32)[None, :, None]
        probs = jnp.exp(scores - log_total[:, offset : offset + block_rows, None]) * keep_rows
        grad_block = grad_heads[offset : offset + block_rows]
        grad_probs = jnp.einsum(
            "qhd,khd->hqk", grad_block, value_heads, preferred_element_type=jnp.float32
        )
        inner_sum = jnp.sum(probs * grad_probs, axis=-1, keepdims=True)
        grad_scores = (probs * (grad_probs - inner_sum)).astype(jnp.bfloat16)
        query_grads.append(
            jnp.einsum("hqk,khd->qhd", grad_scores, key_heads, preferred_element_type=jnp.float32)
            * scale_factor
        )
        key_grad = (
            key_grad
            + jnp.einsum(
                "hqk,qhd->khd", grad_scores, query_part, preferred_element_type=jnp.float32
            )
            * scale_factor
        )
        value_grad = value_grad + jnp.einsum(
            "hqk,qhd->khd",
            probs.astype(jnp.bfloat16),
            grad_block,
            preferred_element_type=jnp.float32,
        )
    query_grad = jnp.concatenate(query_grads, axis=0)
    return jnp.concatenate(
        [
            query_grad.reshape(length, -1),
            key_grad.reshape(length, -1),
            value_grad.reshape(length, -1),
        ],
        axis=1,
    )


def per_device(
    tokens,
    doc_lengths,
    first_gain,
    first_shift,
    qkv_weight,
    query_bias,
    value_bias,
    inner_gain,
    inner_shift,
    proj_weight,
    proj_bias,
    second_gain,
    second_shift,
    expand_weight,
    expand_bias,
    hidden_gain,
    hidden_shift,
    shrink_weight,
    shrink_bias,
    out_cotangent,
):
    (
        gain_one,
        shift_one,
        qkv_full,
        qbias_full,
        vbias_full,
        gain_inner,
        shift_inner,
        proj_full,
        pbias_full,
    ) = (
        lax.all_gather(first_gain, ("group", "shard"), axis=0, tiled=True),
        lax.all_gather(first_shift, ("group", "shard"), axis=0, tiled=True),
        lax.all_gather(qkv_weight, ("group", "shard"), axis=0, tiled=True),
        lax.all_gather(query_bias, ("group", "shard"), axis=0, tiled=True),
        lax.all_gather(value_bias, ("group", "shard"), axis=0, tiled=True),
        lax.all_gather(inner_gain, ("group", "shard"), axis=0, tiled=True),
        lax.all_gather(inner_shift, ("group", "shard"), axis=0, tiled=True),
        lax.all_gather(proj_weight, ("group", "shard"), axis=0, tiled=True),
        lax.all_gather(proj_bias, ("group", "shard"), axis=0, tiled=True),
    )
    model_width = qkv_full.shape[0]
    row_count = doc_lengths.shape[0]
    length = tokens.shape[0] // row_count
    inputs = tokens.astype(jnp.float32)
    normed, unit_one, inv_one = norm_apply(
        inputs, gain_one.astype(jnp.float32), shift_one.astype(jnp.float32)
    )
    normed_low = normed.astype(jnp.bfloat16)
    bias_cat = jnp.concatenate([qbias_full, jnp.zeros_like(qbias_full), vbias_full]).astype(
        jnp.float32
    )
    qkv_low = (jnp.dot(normed_low, qkv_full, preferred_element_type=jnp.float32) + bias_cat).astype(
        jnp.bfloat16
    )
    segments = jax.vmap(functools.partial(segment_ids, length=length))(doc_lengths)
    qkv_rows = qkv_low.reshape(row_count, length, 3 * model_width)
    attended, log_totals = lax.map(row_forward, (qkv_rows, segments))
    attended = attended.reshape(-1, model_width)
    inner, unit_two, inv_two = norm_apply(
        attended, gain_inner.astype(jnp.float32), shift_inner.astype(jnp.float32)
    )
    inner_low = inner.astype(jnp.bfloat16)
    middle = (
        inputs
        + jnp.dot(inner_low, proj_full, preferred_element_type=jnp.float32)
        + pbias_full.astype(jnp.float32)
    )
    (
        gain_three,
        shift_three,
        expand_full,
        ebias_full,
        gain_four,
        shift_four,
        shrink_full,
        sbias_full,
    ) = (
        lax.all_gather(second_gain, ("group", "shard"), axis=0, tiled=True),
        lax.all_gather(second_shift, ("group", "shard"), axis=0, tiled=True),
        lax.all_gather(expand_weight, ("group", "shard"), axis=0, tiled=True),
        lax.all_gather(expand_bias, ("group", "shard"), axis=0, tiled=True),
        lax.all_gather(hidden_gain, ("group", "shard"), axis=0, tiled=True),
        lax.all_gather(hidden_shift, ("group", "shard"), axis=0, tiled=True),
        lax.all_gather(shrink_weight, ("group", "shard"), axis=0, tiled=True),
        lax.all_gather(shrink_bias, ("group", "shard"), axis=0, tiled=True),
    )
    second, unit_three, inv_three = norm_apply(
        middle, gain_three.astype(jnp.float32), shift_three.astype(jnp.float32)
    )
    second_low = second.astype(jnp.bfloat16)
    pre_act = jnp.dot(
        second_low, expand_full, preferred_element_type=jnp.float32
    ) + ebias_full.astype(jnp.float32)
    activ, gelu_pull = jax.vjp(gelu_exact, pre_act)
    hidden, unit_four, inv_four = norm_apply(
        activ, gain_four.astype(jnp.float32), shift_four.astype(jnp.float32)
    )
    hidden_low = hidden.astype(jnp.bfloat16)
    output = (
        middle
        + jnp.dot(hidden_low, shrink_full, preferred_element_type=jnp.float32)
        + sbias_full.astype(jnp.float32)
    )
    block_output = output.astype(jnp.bfloat16)
    back_gain_three, back_expand, back_gain_four, back_shrink = (
        lax.all_gather(second_gain, ("group", "shard"), axis=0, tiled=True),
        lax.all_gather(expand_weight, ("group", "shard"), axis=0, tiled=True),
        lax.all_gather(hidden_gain, ("group", "shard"), axis=0, tiled=True),
        lax.all_gather(shrink_weight, ("group", "shard"), axis=0, tiled=True),
    )
    grad_out = out_cotangent.astype(jnp.float32)
    shrink_weight_grad = jnp.einsum(
        "tf,td->fd", hidden_low, out_cotangent, preferred_element_type=jnp.float32
    )
    shrink_bias_grad = jnp.sum(grad_out, axis=0)
    grad_hidden = jnp.einsum(
        "td,fd->tf", out_cotangent, back_shrink, preferred_element_type=jnp.float32
    )
    grad_activ, hidden_gain_grad, hidden_shift_grad = norm_back(
        unit_four, inv_four, back_gain_four.astype(jnp.float32), grad_hidden
    )
    grad_pre = gelu_pull(grad_activ)[0].astype(jnp.bfloat16)
    expand_bias_grad = jnp.sum(grad_pre.astype(jnp.float32), axis=0)
    expand_weight_grad = jnp.einsum(
        "td,tf->df", second_low, grad_pre, preferred_element_type=jnp.float32
    )
    grad_second = jnp.einsum("tf,df->td", grad_pre, back_expand, preferred_element_type=jnp.float32)
    grad_mid_part, second_gain_grad, second_shift_grad = norm_back(
        unit_three, inv_three, back_gain_three.astype(jnp.float32), grad_second
    )
    grad_middle = grad_out + grad_mid_part
    ffn_parts = (
        lax.psum_scatter(
            second_gain_grad.astype(jnp.bfloat16), "shard", scatter_dimension=0, tiled=True
        ).astype(jnp.float32),
        lax.psum_scatter(
            second_shift_grad.astype(jnp.bfloat16), "shard", scatter_dimension=0, tiled=True
        ).astype(jnp.float32),
        lax.psum_scatter(
            expand_weight_grad.astype(jnp.bfloat16), "shard", scatter_dimension=0, tiled=True
        ).astype(jnp.float32),
        lax.psum_scatter(
            expand_bias_grad.astype(jnp.bfloat16), "shard", scatter_dimension=0, tiled=True
        ).astype(jnp.float32),
        lax.psum_scatter(
            hidden_gain_grad.astype(jnp.bfloat16), "shard", scatter_dimension=0, tiled=True
        ).astype(jnp.float32),
        lax.psum_scatter(
            hidden_shift_grad.astype(jnp.bfloat16), "shard", scatter_dimension=0, tiled=True
        ).astype(jnp.float32),
        lax.psum_scatter(
            shrink_weight_grad.astype(jnp.bfloat16), "shard", scatter_dimension=0, tiled=True
        ).astype(jnp.float32),
        lax.psum_scatter(
            shrink_bias_grad.astype(jnp.bfloat16), "shard", scatter_dimension=0, tiled=True
        ).astype(jnp.float32),
    )
    (
        part_gain_three,
        part_shift_three,
        part_expand,
        part_ebias,
        part_gain_four,
        part_shift_four,
        part_shrink,
        part_sbias,
    ) = ffn_parts
    ffn_totals = (
        lax.psum(part_gain_three.astype(jnp.bfloat16), "group").astype(jnp.float32),
        lax.psum(part_shift_three.astype(jnp.bfloat16), "group").astype(jnp.float32),
        lax.psum(part_expand.astype(jnp.bfloat16), "group").astype(jnp.float32),
        lax.psum(part_ebias.astype(jnp.bfloat16), "group").astype(jnp.float32),
        lax.psum(part_gain_four.astype(jnp.bfloat16), "group").astype(jnp.float32),
        lax.psum(part_shift_four.astype(jnp.bfloat16), "group").astype(jnp.float32),
        lax.psum(part_shrink.astype(jnp.bfloat16), "group").astype(jnp.float32),
        lax.psum(part_sbias.astype(jnp.bfloat16), "group").astype(jnp.float32),
    )
    back_gain_one, back_qkv, back_gain_inner, back_proj = (
        lax.all_gather(first_gain, ("group", "shard"), axis=0, tiled=True),
        lax.all_gather(qkv_weight, ("group", "shard"), axis=0, tiled=True),
        lax.all_gather(inner_gain, ("group", "shard"), axis=0, tiled=True),
        lax.all_gather(proj_weight, ("group", "shard"), axis=0, tiled=True),
    )
    grad_branch = grad_middle.astype(jnp.bfloat16)
    proj_bias_grad = jnp.sum(grad_branch.astype(jnp.float32), axis=0)
    proj_weight_grad = jnp.einsum(
        "td,te->de", inner_low, grad_branch, preferred_element_type=jnp.float32
    )
    grad_inner = jnp.einsum("te,de->td", grad_branch, back_proj, preferred_element_type=jnp.float32)
    grad_attended, inner_gain_grad, inner_shift_grad = norm_back(
        unit_two, inv_two, back_gain_inner.astype(jnp.float32), grad_inner
    )
    grad_att_low = grad_attended.astype(jnp.bfloat16).reshape(row_count, length, model_width)
    grad_qkv = (
        lax.map(row_backward, (qkv_rows, segments, log_totals, grad_att_low))
        .reshape(-1, 3 * model_width)
        .astype(jnp.bfloat16)
    )
    grad_qkv_wide = grad_qkv.astype(jnp.float32)
    query_bias_grad = jnp.sum(grad_qkv_wide[:, :model_width], axis=0)
    value_bias_grad = jnp.sum(grad_qkv_wide[:, 2 * model_width :], axis=0)
    qkv_weight_grad = jnp.einsum(
        "td,te->de", normed_low, grad_qkv, preferred_element_type=jnp.float32
    )
    grad_normed = jnp.einsum("te,de->td", grad_qkv, back_qkv, preferred_element_type=jnp.float32)
    grad_in_part, first_gain_grad, first_shift_grad = norm_back(
        unit_one, inv_one, back_gain_one.astype(jnp.float32), grad_normed
    )
    input_grad = (grad_middle + grad_in_part).astype(jnp.bfloat16)
    attn_parts = (
        lax.psum_scatter(
            first_gain_grad.astype(jnp.bfloat16), "shard", scatter_dimension=0, tiled=True
        ).astype(jnp.float32),
        lax.psum_scatter(
            first_shift_grad.astype(jnp.bfloat16), "shard", scatter_dimension=0, tiled=True
        ).astype(jnp.float32),
        lax.psum_scatter(
            qkv_weight_grad.astype(jnp.bfloat16), "shard", scatter_dimension=0, tiled=True
        ).astype(jnp.float32),
        lax.psum_scatter(
            query_bias_grad.astype(jnp.bfloat16), "shard", scatter_dimension=0, tiled=True
        ).astype(jnp.float32),
        lax.psum_scatter(
            value_bias_grad.astype(jnp.bfloat16), "shard", scatter_dimension=0, tiled=True
        ).astype(jnp.float32),
        lax.psum_scatter(
            inner_gain_grad.astype(jnp.bfloat16), "shard", scatter_dimension=0, tiled=True
        ).astype(jnp.float32),
        lax.psum_scatter(
            inner_shift_grad.astype(jnp.bfloat16), "shard", scatter_dimension=0, tiled=True
        ).astype(jnp.float32),
        lax.psum_scatter(
            proj_weight_grad.astype(jnp.bfloat16), "shard", scatter_dimension=0, tiled=True
        ).astype(jnp.float32),
        lax.psum_scatter(
            proj_bias_grad.astype(jnp.bfloat16), "shard", scatter_dimension=0, tiled=True
        ).astype(jnp.float32),
    )
    (
        part_gain_one,
        part_shift_one,
        part_qkv,
        part_qbias,
        part_vbias,
        part_gain_inner,
        part_shift_inner,
        part_proj,
        part_pbias,
    ) = attn_parts
    attn_totals = (
        lax.psum(part_gain_one.astype(jnp.bfloat16), "group").astype(jnp.float32),
        lax.psum(part_shift_one.astype(jnp.bfloat16), "group").astype(jnp.float32),
        lax.psum(part_qkv.astype(jnp.bfloat16), "group").astype(jnp.float32),
        lax.psum(part_qbias.astype(jnp.bfloat16), "group").astype(jnp.float32),
        lax.psum(part_vbias.astype(jnp.bfloat16), "group").astype(jnp.float32),
        lax.psum(part_gain_inner.astype(jnp.bfloat16), "group").astype(jnp.float32),
        lax.psum(part_shift_inner.astype(jnp.bfloat16), "group").astype(jnp.float32),
        lax.psum(part_proj.astype(jnp.bfloat16), "group").astype(jnp.float32),
        lax.psum(part_pbias.astype(jnp.bfloat16), "group").astype(jnp.float32),
    )
    all_totals = tuple(attn_totals) + tuple(ffn_totals)
    return (block_output, input_grad) + tuple(all_totals)


def solution(mesh):
    in_specs = (
        P(("group", "shard"), None),
        P(("group", "shard"), None),
        P(("group", "shard")),
        P(("group", "shard")),
        P(("group", "shard"), None),
        P(("group", "shard")),
        P(("group", "shard")),
        P(("group", "shard")),
        P(("group", "shard")),
        P(("group", "shard"), None),
        P(("group", "shard")),
        P(("group", "shard")),
        P(("group", "shard")),
        P(("group", "shard"), None),
        P(("group", "shard")),
        P(("group", "shard")),
        P(("group", "shard")),
        P(("group", "shard"), None),
        P(("group", "shard")),
        P(("group", "shard"), None),
    )
    out_specs = (
        P(("group", "shard"), None),
        P(("group", "shard"), None),
        P("shard"),
        P("shard"),
        P("shard", None),
        P("shard"),
        P("shard"),
        P("shard"),
        P("shard"),
        P("shard", None),
        P("shard"),
        P("shard"),
        P("shard"),
        P("shard", None),
        P("shard"),
        P("shard"),
        P("shard"),
        P("shard", None),
        P("shard"),
    )
    return jax.shard_map(
        per_device, mesh=mesh, in_specs=in_specs, out_specs=out_specs, check_vma=False
    )
```

profile of v0, /device:TPU:0, one launch (start us, length us, event | category | flops | bytes accessed | tf_op | source)
XLA Modules:
  0.0 814.0 jit_solution(16269880656947947035)
XLA Ops:
  22.0 43.5 %all-reduce.26 = (bf16[768]{0:T(1024)(128)(2,1)S(1)}, bf16[768]{0:T(1024)(128)(2,1)S(1)}, bf16[768]{0:T(1024)(128)(2,1)S(1)}, bf16[768]{0:T(1024)(128)(2,1)S(1)}...) all-reduce(bf16[768]{0:T(1024)(128)(2,1)S(1)} %dynamic-update-slice, ...), channel_id=1, replica_groups=mesh['group'=16,'shard'=2] {'group','shard'}, use_global_device_ids=true, to_apply=%add.6 | all-reduce | flops 16896 | bytes 67584
  76.7 6.4 add_convert_fusion.2
  88.0 2.9 copy.88
  95.7 12.0 %fusion.3 = (f32[12,512]{1,0:T(8,128)S(1)}, f32[12,512,1024]{2,1,0:T(8,128)}) fusion(pred[512,1024]{1,0:T(8,128)(4,1)} %get-tuple-element.202, bf16[512,12,64]{0,2,1:T(8,128)(2,1)} %bitcast.89, bf16[1024,12,64]{0,2,1:T(8,128)(2,1)S(1)} %bitcast.66), kind=kOutput, calls=%fused_computation.16 | convolution fusion | flops 824174592 | bytes 28073984 | tf_op jit(solution)/shard_map/while/body/eval_jaxpr/qhd,khd->hqk/dot_general | solution.py:57
  107.8 11.9 %fusion.1 = f32[12,512]{1,0:T(8,128)S(1)} fusion(f32[12,512,1024]{2,1,0:T(8,128)} %get-tuple-element.208, f32[12,512]{1,0:T(8,128)S(1)} %get-tuple-element.207, pred[512,1024]{1,0:T(8,128)(4,1)S(1)} %copy-done.20), kind=kLoop, calls=%fused_computation.13 | loop fusion | flops 25159680 | bytes 25739264 | tf_op jit(solution)/shard_map/while/body/eval_jaxpr/reduce_sum | solution.py:86
  120.3 13.3 %fusion.2 = (f32[12,512]{1,0:T(8,128)S(1)}, f32[12,512,1024]{2,1,0:T(8,128)}) fusion(pred[512,1024]{1,0:T(8,128)(4,1)S(1)} %copy-done.18, bf16[512,12,64]{0,2,1:T(8,128)(2,1)} %bitcast.91, bf16[1024,12,64]{0,2,1:T(8,128)(2,1)S(1)} %bitcast.67), kind=kOutput, calls=%fused_computation.15 | convolution fusion | flops 824174592 | bytes 28073984 | tf_op jit(solution)/shard_map/while/body/eval_jaxpr/qhd,khd->hqk/dot_general | solution.py:57
  133.6 12.8 %fusion = f32[12,512]{1,0:T(8,128)S(1)} fusion(f32[12,512,1024]{2,1,0:T(8,128)} %get-tuple-element.210, f32[12,512]{1,0:T(8,128)S(1)} %get-tuple-element.209, pred[512,1024]{1,0:T(8,128)(4,1)S(1)} %copy-done.18), kind=kLoop, calls=%fused_computation.12 | loop fusion | flops 25159680 | bytes 25739264 | tf_op jit(solution)/shard_map/while/body/eval_jaxpr/reduce_sum | solution.py:86
  147.1 9.7 %fusion.15 = f32[12,64,512]{2,1,0:T(8,128)} fusion(bf16[1024,12,64]{0,2,1:T(8,128)(2,1)S(1)} %bitcast.70, f32[12,512,1024]{2,1,0:T(8,128)S(1)} %bitcast.63, f32[512]{0:T(512)S(1)} %get-tuple-element.206, f32[12,512]{1,0:T(8,128)S(1)} %fusion.1, f32[12,512]{1,0:T(8,128)S(1)} %get-tuple-element.207, pred[512,1024]{1,0:T(8,128)(4,1)S(1)} %copy-done.21), kind=kOutput, calls=%fused_computation.41 | convolution fusion | flops 843055104 | bytes 28887040 | tf_op jit(solution)/shard_map/while/body/eval_jaxpr/hqk,khd->qhd/dot_general | solution.py:89
  156.9 14.3 %fusion.14 = f32[12,64,512]{2,1,0:T(8,128)S(1)} fusion(bf16[1024,12,64]{0,2,1:T(8,128)(2,1)S(1)} %bitcast.71, f32[12,512,1024]{2,1,0:T(8,128)} %get-tuple-element.210, f32[512]{0:T(512)S(1)} %get-tuple-element.205, f32[12,512]{1,0:T(8,128)S(1)} %fusion, f32[12,512]{1,0:T(8,128)S(1)} %get-tuple-element.209, pred[512,1024]{1,0:T(8,128)(4,1)S(1)} %copy-done.18), kind=kOutput, calls=%fused_computation.40 | convolution fusion | flops 843055104 | bytes 28887040 | tf_op jit(solution)/shard_map/while/body/eval_jaxpr/hqk,khd->qhd/dot_general | solution.py:89
  173.2 3.6 fusion.61
  178.8 16.6 %all-gather.9.cloned.1.call-done = bf16[768,3072]{1,0:T(8,128)(2,1)} async-done(((bf16[24,3072]{1,0:T(8,128)(2,1)}), bf16[768,3072]{1,0:T(8,128)(2,1)}) %all-gather.9.cloned.1.call-update) | async-done | bytes 4718608 | tf_op jit(solution)/shard_map/all_gather | solution.py:229
  195.4 38.7 %fusion.55 = (f32[1024]{0:T(1024)S(1)}, f32[1024,3072]{1,0:T(8,128)S(1)}, f32[1024,3072]{1,0:T(8,128)}, f32[1024,3072]{1,0:T(8,128)}) fusion(f32[3072]{0:T(1024)S(1)} %copy-done.39, bf16[768,3072]{1,0:T(8,128)(2,1)} %all-gather.9.cloned.1.call-done, f32[1024,768]{0,1:T(8,128)} %copy-done.5, f32[768]{0:T(1024)S(1)} %copy-done.58, f32[768]{0:T(1024)S(1)} %copy-done.45, ...), kind=kOutput, calls=%fused_computation.139 | convolution fusion | flops 5043387392 | bytes 45643776 | tf_op jit(solution)/shard_map/dot_general | solution.py:240
  235.5 3.4 copy-done.1
  238.9 21.1 %all-gather.11.cloned.1.call-done = bf16[3072,768]{1,0:T(8,128)(2,1)} async-done(((bf16[96,768]{1,0:T(8,128)(2,1)}), bf16[3072,768]{1,0:T(8,128)(2,1)}) %all-gather.11.cloned.1.call-update) | async-done | bytes 4718608 | tf_op jit(solution)/shard_map/all_gather | solution.py:233
  260.0 16.2 %multiply_reduce_fusion.2 = (bf16[3072]{0:T(1024)(128)(2,1)}, f32[1024]{0:T(1024)S(1)}, f32[1024]{0:T(1024)S(1)}, bf16[3072]{0:T(1024)(128)(2,1)}, bf16[1024,3072]{1,0:T(8,128)(2,1)}, /*index=5*/f32[1024,3072]{1,0:T(8,128)}) fusion(f32[1024,3072]{1,0:T(8,128)} %copy-done.1, f32[1024]{0:T(1024)S(1)} %add_rsqrt_fusion, ...), kind=kOutput, calls=%fused_computation.18 | convolution fusion | flops 4869578752 | bytes 37801984 | tf_op jit(solution)/shard_map/td,fd->tf/dot_general | solution.py:265
  276.2 18.8 %fusion.54 = (bf16[3072]{0:T(1024)(128)(2,1)}, bf16[1024,3072]{1,0:T(8,128)(2,1)S(1)}) fusion(f32[1024,3072]{1,0:T(8,128)} %get-tuple-element.193, f32[1024]{0:T(1024)S(1)} %broadcast_multiply_fusion, f32[1024,3072]{1,0:T(8,128)} %copy-done.1, f32[1024]{0:T(1024)S(1)} %broadcast_multiply_fusion.2, f32[1024]{0:T(1024)S(1)} %broadcast_multiply_fusion.1, ...), kind=kLoop, calls=%fused_computation.138 | loop fusion | flops 72348672 | bytes 56670208 | tf_op jit(solution)/shard_map/reduce_sum | solution.py:272
  294.9 11.9 %fusion.63 = (bf16[768]{0:T(1024)(128)(2,1)}, f32[1024,768]{1,0:T(8,128)}) fusion(bf16[1024,3072]{1,0:T(8,128)(2,1)S(1)} %get-tuple-element.188, bf16[768,3072]{1,0:T(8,128)(2,1)} %all-gather.9.cloned.1.call-done), kind=kOutput, calls=%fused_computation.146 | convolution fusion | flops 4832623616 | bytes 14157312 | tf_op jit(solution)/shard_map/tf,df->td/dot_general | solution.py:276
  306.9 3.9 copy.93
  310.8 3.6 multiply_reduce_fusion.6
  318.1 2.7 convolution_convert_fusion.3
  320.7 5.0 multiply_reduce_fusion.7
  327.6 13.9 %fusion.5 = f32[12,64,1024]{2,1,0:T(8,128)} fusion(bf16[512,12,64]{0,2,1:T(8,128)(2,1)S(1)} %bitcast.98, f32[12,512,1024]{2,1,0:T(8,128)} %get-tuple-element.208, f32[12,512]{1,0:T(8,128)S(1)} %copy-done.35, f32[512]{0:T(512)S(1)} %copy-done.50, pred[512,1024]{1,0:T(8,128)(4,1)S(1)} %copy-done.22), kind=kOutput, calls=%fused_computation.19 | convolution fusion | flops 836763648 | bytes 29648896 | tf_op jit(solution)/shard_map/while/body/eval_jaxpr/hqk,qhd->khd/dot_general | solution.py:130
  341.6 18.5 %multiply_reduce_fusion = (f32[12,512]{1,0:T(8,128)S(1)}, f32[12,512,1024]{2,1,0:T(8,128)}) fusion(f32[512]{0:T(512)S(1)} %copy-done.50, f32[12,512]{1,0:T(8,128)S(1)} %copy-done.35, f32[12,512,1024]{2,1,0:T(8,128)} %get-tuple-element.208, pred[512,1024]{1,0:T(8,128)(4,1)S(1)} %copy-done.23, bf16[512,12,64]{0,2,1:T(8,128)(2,1)} %bitcast.99, ...), kind=kOutput, calls=%fused_computation.1 | convolution fusion | flops 843048960 | bytes 53266432 | tf_op jit(solution)/shard_map/while/body/eval_jaxpr/qhd,khd->hqk/dot_general | solution.py:114
  360.1 20.9 %multiply_reduce_fusion.1 = (f32[12,512]{1,0:T(8,128)S(1)}, f32[12,512,1024]{2,1,0:T(8,128)}) fusion(f32[512]{0:T(512)S(1)} %copy-done.48, f32[12,512]{1,0:T(8,128)S(1)} %copy-done.36, f32[12,512,1024]{2,1,0:T(8,128)} %get-tuple-element.210, pred[512,1024]{1,0:T(8,128)(4,1)S(1)} %copy-done.19, bf16[512,12,64]{0,2,1:T(8,128)(2,1)S(1)} %bitcast.96, ...), kind=kOutput, calls=%fused_computation.4 | convolution fusion | flops 843048960 | bytes 53266432 | tf_op jit(solution)/shard_map/while/body/eval_jaxpr/qhd,khd->hqk/dot_general | solution.py:114
  381.0 14.5 %add_convert_fusion.3 = bf16[12,64,1024]{2,1,0:T(8,128)(2,1)} fusion(f32[12,64,1024]{2,1,0:T(8,128)} %fusion.5, bf16[512,12,64]{0,2,1:T(8,128)(2,1)S(1)} %bitcast.97, f32[12,512,1024]{2,1,0:T(8,128)} %get-tuple-element.210, f32[12,512]{1,0:T(8,128)S(1)} %copy-done.36, f32[512]{0:T(512)S(1)} %copy-done.48, pred[512,1024]{1,0:T(8,128)(4,1)S(1)} %copy-done.19), kind=kOutput, calls=%fused_computation.74 | convolution fusion | flops 838336512 | bytes 31221760 | tf_op jit(solution)/shard_map/while/body/eval_jaxpr/hqk,qhd->khd/dot_general | solution.py:130
  395.5 42.2 %multiply_convert_fusion = (bf16[12,512,1024]{2,1,0:T(8,128)(2,1)}, bf16[12,512,1024]{2,1,0:T(8,128)(2,1)}) fusion(f32[12,512,1024]{2,1,0:T(8,128)} %get-tuple-element.219, f32[12,512]{1,0:T(8,128)S(1)} %get-tuple-element.218, f32[512]{0:T(512)S(1)} %copy-done.51, f32[12,512]{1,0:T(8,128)S(1)} %copy-done.35, f32[12,512,1024]{2,1,0:T(8,128)} %get-tuple-element.208, ...), kind=kLoop, calls=%fused_computation | loop fusion | flops 88080384 | bytes 126980096 | tf_op jit(solution)/shard_map/while/body/eval_jaxpr/convert_element_type | solution.py:118
  437.8 10.0 %fusion.39 = bf16[512,12,64]{0,2,1:T(8,128)(2,1)} fusion(bf16[1024,12,64]{0,2,1:T(8,128)(2,1)} %bitcast.68, bf16[12,512,1024]{2,1,0:T(8,128)(2,1)} %get-tuple-element.224), kind=kOutput, calls=%fused_computation.101 | convolution fusion | flops 806092800 | bytes 14942208 | tf_op jit(solution)/shard_map/while/body/eval_jaxpr/hqk,khd->qhd/dot_general | solution.py:120
  447.8 6.2 fusion.38
  455.7 4.0 fusion.64
  462.7 6.1 convolution_convert_fusion.2
  468.9 9.7 %convolution_convert_fusion.1 = bf16[768,3072]{1,0:T(8,128)(2,1)} fusion(bf16[1024,3072]{1,0:T(8,128)(2,1)} %copy-done.30, f32[1024,768]{0,1:T(8,128)} %copy-done.5, f32[768]{0:T(1024)S(1)} %copy-done.59, f32[768]{0:T(1024)S(1)} %copy-done.45, f32[1024]{0:T(1024)S(1)} %add_rsqrt_fusion.1, f32[1024]{0:T(1024)S(1)} %broadcast_multiply_fusion.9), kind=kOutput, calls=%fused_computation.47 | convolution fusion | flops 4838129664 | bytes 14170112 | tf_op jit(solution)/shard_map/td,tf->df/dot_general | solution.py:273
  478.7 9.1 %convolution_convert_fusion = bf16[3072,768]{1,0:T(8,128)(2,1)} fusion(bf16[1024,3072]{1,0:T(8,128)(2,1)} %get-tuple-element.194, bf16[1024,768]{1,0:T(8,128)(2,1)} %param.39), kind=kOutput, calls=%fused_computation.46 | convolution fusion | flops 4834197504 | bytes 12582912 | tf_op jit(solution)/shard_map/tf,td->fd/dot_general | solution.py:261
  492.1 23.0 %reduce-scatter.5.cloned.1.call-done = bf16[384,2304]{1,0:T(8,128)(2,1)} async-done(((bf16[768,2304]{1,0:T(8,128)(2,1)}), bf16[384,2304]{1,0:T(8,128)(2,1)}) %reduce-scatter.5.cloned.1.call-update) | async-done | bytes 1769488 | tf_op jit(solution)/shard_map/reduce_scatter | solution.py:366
  515.2 63.0 %reduce-scatter.9.cloned.1.call-done = bf16[384,3072]{1,0:T(8,128)(2,1)} async-done(((bf16[768,3072]{1,0:T(8,128)(2,1)}), bf16[384,3072]{1,0:T(8,128)(2,1)}) %reduce-scatter.9.cloned.1.call-update) | async-done | bytes 2359312 | tf_op jit(solution)/shard_map/reduce_scatter | solution.py:288
  578.1 63.0 %reduce-scatter.11.cloned.1.call-done = bf16[1536,768]{1,0:T(8,128)(2,1)} async-done(((bf16[3072,768]{1,0:T(8,128)(2,1)}), bf16[1536,768]{1,0:T(8,128)(2,1)}) %reduce-scatter.11.cloned.1.call-update) | async-done | bytes 2359312 | tf_op jit(solution)/shard_map/reduce_scatter | solution.py:300
  641.1 10.0 %add_convert_fusion.4 = bf16[1024,768]{0,1:T(8,128)(2,1)} fusion(f32[1024,768]{0,1:T(8,128)} %copy-done.5, bf16[1024,3072]{1,0:T(8,128)(2,1)} %get-tuple-element.194, bf16[3072,768]{1,0:T(8,128)(2,1)} %all-gather.11.cloned.1.call-done, f32[768]{0:T(1024)S(1)} %convert_element_type.285), kind=kOutput, calls=%fused_computation.80 | convolution fusion | flops 4834197504 | bytes 15731712 | tf_op jit(solution)/shard_map/dot_general | solution.py:250
  651.1 2.6 copy.97
  653.7 8.5 %fusion.62 = (bf16[768]{0:T(1024)(128)(2,1)S(1)}, f32[1024,768]{1,0:T(8,128)}) fusion(bf16[768,2304]{1,0:T(8,128)(2,1)} %all-gather.5.cloned.1.call-done, bf16[1024,768]{0,1:T(8,128)(2,1)} %bitcast.100, bf16[1024,768]{0,1:T(8,128)(2,1)S(1)} %bitcast.87, bf16[1024,768]{0,1:T(8,128)(2,1)} %bitcast.94), kind=kOutput, calls=%fused_computation.145 | convolution fusion | flops 3638820096 | bytes 11404800 | tf_op jit(solution)/shard_map/te,de->td/dot_general | solution.py:354
  662.3 3.6 copy.94
  665.8 3.2 fusion.29
  669.0 4.1 fusion.28
  673.1 2.6 copy.98
  675.7 2.8 fusion.51
  679.3 7.5 all-reduce.29
  687.8 60.9 %all-reduce.27 = (bf16[384]{0:T(512)(128)(2,1)S(1)}, bf16[384]{0:T(512)(128)(2,1)S(1)}, bf16[384]{0:T(512)(128)(2,1)S(1)}, bf16[384]{0:T(512)(128)(2,1)S(1)}, bf...) all-reduce(bf16[384]{0:T(512)(128)(2,1)S(1)} %dynamic-slice.4, ...), channel_id=1, replica_groups=mesh['group'=16,'shard'=2] {'group'}, use_global_device_ids=true, to_apply=%region_26.27 | all-reduce | flops 8448 | bytes 33792 | tf_op jit(solution)/shard_map/psum | solution.py:400
  756.3 39.8 %all-reduce.32.cloned.1.call-done = (bf16[384,2304]{1,0:T(8,128)(2,1)}, bf16[384,768]{1,0:T(8,128)(2,1)}, bf16[384,3072]{1,0:T(8,128)(2,1)}, bf16[1536,768]{1,0:T(8,128)(2,1)}) async-done(((bf16[384,2304]{1,0:T(8,128)(2,1)}, bf16[384,768]{1,0:T(8,128)(2,1)}, bf16[384,3072]{1,0:T(8,128)(2,1)}, bf16[1536,768]{1,0:T(8,128)(2,1)}), (bf16[384,2304]{1,0:T(8,128)(2,1)}, bf16[384,768]{1,0:T(8,128)(2,1)}, ...) | async-done | bytes 7077904 | tf_op jit(solution)/shard_map/psum | solution.py:402
  798.4 3.5 convert_element_type.301
  801.9 2.8 convert_element_type.319
  (294 shorter events, 69.5 us)
Async XLA Ops:
  7.2 65.6 %copy-start.26 = (bf16[1024,768]{1,0:T(8,128)(2,1)S(1)}, bf16[1024,768]{1,0:T(8,128)(2,1)}, u32[]{:S(2)}) copy-start(bf16[1024,768]{1,0:T(8,128)(2,1)} %param.39) | copy-start | bytes 4718596
  7.2 69.5 %all-gather.5.cloned.1.call-start = ((), (), s32[]{:S(2)}) async-start(), calls=%async_computation.4 | async-start | bytes 3649536 | tf_op jit(solution)/shard_map/all_gather | solution.py:182
  7.9 164.4 %all-gather.7.cloned.1.call-start = ((), (), s32[]{:S(2)}) async-start(), calls=%async_computation.5 | async-start | bytes 1216512 | tf_op jit(solution)/shard_map/all_gather | solution.py:187
  8.7 186.7 %all-gather.9.cloned.1.call-start = ((), (), s32[]{:S(2)}) async-start(), calls=%async_computation.6 | async-start | bytes 4866048 | tf_op jit(solution)/shard_map/all_gather | solution.py:229
  9.4 250.6 %all-gather.11.cloned.1.call-start = ((), (), s32[]{:S(2)}) async-start(), calls=%async_computation.7 | async-start | bytes 4866048 | tf_op jit(solution)/shard_map/all_gather | solution.py:233
  10.0 482.1 %reduce-scatter.7.cloned.1.call-start = ((), (), s32[]{:S(2)}) async-start(), calls=%async_computation.9 | async-start | bytes 1769472 | tf_op jit(solution)/shard_map/reduce_scatter | solution.py:381
  11.1 136.0 %copy-start.49 = (f32[512]{0:T(512)}, f32[512]{0:T(512)S(1)}, u32[]{:S(2)}) copy-start(f32[512]{0:T(512)S(1)} %get-tuple-element.206) | copy-start | bytes 6148
  11.1 145.8 %copy-start.47 = (f32[512]{0:T(512)}, f32[512]{0:T(512)S(1)}, u32[]{:S(2)}) copy-start(f32[512]{0:T(512)S(1)} %get-tuple-element.205) | copy-start | bytes 6148
  66.7 10.0 %copy-start.41 = (f32[768]{0:T(1024)}, f32[768]{0:T(1024)S(1)}, u32[]{:S(2)}) copy-start(f32[768]{0:T(1024)S(1)} %convert_element_type.264) | copy-start | bytes 9220
  67.9 8.8 %copy-start.60 = (f32[768]{0:T(1024)}, f32[768]{0:T(1024)S(1)}, u32[]{:S(2)}) copy-start(f32[768]{0:T(1024)S(1)} %convert_element_type.265) | copy-start | bytes 9220
  72.0 100.3 %copy-start.2 = (bf16[1024,768]{0,1:T(8,128)(2,1)}, bf16[1024,768]{0,1:T(8,128)(2,1)S(1)}, u32[]{:S(2)}) copy-start(bf16[1024,768]{0,1:T(8,128)(2,1)S(1)} %copy.86) | copy-start | bytes 4718596
  72.3 10.8 %copy-start.37 = (f32[1024]{0:T(1024)}, f32[1024]{0:T(1024)S(1)}, u32[]{:S(2)}) copy-start(f32[1024]{0:T(1024)S(1)} %broadcast_multiply_fusion.11) | copy-start | bytes 12292
  72.8 10.3 %copy-start.43 = (f32[1024]{0:T(1024)}, f32[1024]{0:T(1024)S(1)}, u32[]{:S(2)}) copy-start(f32[1024]{0:T(1024)S(1)} %add_rsqrt_fusion.3) | copy-start | bytes 12292
  87.9 32.3 %copy-start.4 = (bf16[1024,768]{0,1:T(8,128)(2,1)}, bf16[1024,768]{0,1:T(8,128)(2,1)S(1)}, u32[]{:S(2)}) copy-start(bf16[1024,768]{0,1:T(8,128)(2,1)S(1)} %copy.89) | copy-start | bytes 4718596
  95.7 12.0 %copy-start.20 = (pred[512,1024]{1,0:T(8,128)(4,1)S(1)}, pred[512,1024]{1,0:T(8,128)(4,1)}, u32[]{:S(2)}) copy-start(pred[512,1024]{1,0:T(8,128)(4,1)} %get-tuple-element.202) | copy-start | bytes 1572868
  107.8 12.5 %copy-start.18 = (pred[512,1024]{1,0:T(8,128)(4,1)S(1)}, pred[512,1024]{1,0:T(8,128)(4,1)}, u32[]{:S(2)}) copy-start(pred[512,1024]{1,0:T(8,128)(4,1)} %get-tuple-element.201) | copy-start | bytes 1572868
  120.3 26.8 %slice-start = ((s8[25165824]{0:T(1024)(128)(4,1)}), s8[4194304]{0:T(1024)(128)(4,1)S(1)}, s32[]{:S(2)}) async-start(s8[25165824]{0:T(1024)(128)(4,1)} %bitcast.62), calls=%async_computation.13 | async-start | bytes 8388608
  120.3 26.8 %slice-start.1 = ((s8[25165824]{0:T(1024)(128)(4,1)}), s8[4194304]{0:T(1024)(128)(4,1)S(1)}, s32[]{:S(2)}) async-start(s8[25165824]{0:T(1024)(128)(4,1)} %bitcast.62), calls=%async_computation.14 | async-start | bytes 8388608
  120.3 26.8 %slice-start.2 = ((s8[25165824]{0:T(1024)(128)(4,1)}), s8[4194304]{0:T(1024)(128)(4,1)S(1)}, s32[]{:S(2)}) async-start(s8[25165824]{0:T(1024)(128)(4,1)} %bitcast.62), calls=%async_computation.15 | async-start | bytes 8388608
  120.3 26.8 %slice-start.3 = ((s8[25165824]{0:T(1024)(128)(4,1)}), s8[4194304]{0:T(1024)(128)(4,1)S(1)}, s32[]{:S(2)}) async-start(s8[25165824]{0:T(1024)(128)(4,1)} %bitcast.62), calls=%async_computation.16 | async-start | bytes 8388608
  133.6 13.5 %slice-start.4 = ((s8[25165824]{0:T(1024)(128)(4,1)}), s8[4194304]{0:T(1024)(128)(4,1)S(1)}, s32[]{:S(2)}) async-start(s8[25165824]{0:T(1024)(128)(4,1)} %bitcast.62), calls=%async_computation.17 | async-start | bytes 8388608
  133.6 13.5 %slice-start.5 = ((s8[25165824]{0:T(1024)(128)(4,1)}), s8[4194304]{0:T(1024)(128)(4,1)S(1)}, s32[]{:S(2)}) async-start(s8[25165824]{0:T(1024)(128)(4,1)} %bitcast.62), calls=%async_computation.18 | async-start | bytes 8388608
  133.6 13.5 %copy-start.9 = (bf16[1024,768]{0,1:T(8,128)(2,1)S(1)}, bf16[1024,768]{0,1:T(8,128)(2,1)}, u32[]{:S(2)}) copy-start(bf16[1024,768]{0,1:T(8,128)(2,1)} %copy.87) | copy-start | bytes 4718596
  133.6 13.5 %copy-start.21 = (pred[512,1024]{1,0:T(8,128)(4,1)S(1)}, pred[512,1024]{1,0:T(8,128)(4,1)}, u32[]{:S(2)}) copy-start(pred[512,1024]{1,0:T(8,128)(4,1)} %get-tuple-element.202) | copy-start | bytes 1572868
  156.9 14.3 %copy-start.11 = (f32[12,64,512]{2,1,0:T(8,128)S(1)}, f32[12,64,512]{2,1,0:T(8,128)}, u32[]{:S(2)}) copy-start(f32[12,64,512]{2,1,0:T(8,128)} %fusion.15) | copy-start | bytes 4718596
  172.3 23.1 %copy-start.39 = (f32[3072]{0:T(1024)S(1)}, f32[3072]{0:T(1024)}, u32[]{:S(2)}) copy-start(f32[3072]{0:T(1024)} %convert_element_type.281) | copy-start | bytes 36868
  172.3 23.1 %copy-start.45 = (f32[768]{0:T(1024)S(1)}, f32[768]{0:T(1024)}, u32[]{:S(2)}) copy-start(f32[768]{0:T(1024)} %convert_element_type.278) | copy-start | bytes 9220
  172.3 23.1 %copy-start.58 = (f32[768]{0:T(1024)S(1)}, f32[768]{0:T(1024)}, u32[]{:S(2)}) copy-start(f32[768]{0:T(1024)} %convert_element_type.279) | copy-start | bytes 9220
  234.1 4.8 copy-start.1
  234.1 25.9 %copy-start.27 = (bf16[1024,768]{1,0:T(8,128)(2,1)S(1)}, bf16[1024,768]{1,0:T(8,128)(2,1)}, u32[]{:S(2)}) copy-start(bf16[1024,768]{1,0:T(8,128)(2,1)} %param.39) | copy-start | bytes 4718596
  234.1 25.9 %copy-start.40 = (f32[3072]{0:T(1024)S(1)}, f32[3072]{0:T(1024)}, u32[]{:S(2)}) copy-start(f32[3072]{0:T(1024)} %convert_element_type.282) | copy-start | bytes 36868
  234.1 25.9 %copy-start.53 = (f32[3072]{0:T(1024)S(1)}, f32[3072]{0:T(1024)}, u32[]{:S(2)}) copy-start(f32[3072]{0:T(1024)} %convert_element_type.283) | copy-start | bytes 36868
  294.9 11.9 %copy-start.30 = (bf16[1024,3072]{1,0:T(8,128)(2,1)}, bf16[1024,3072]{1,0:T(8,128)(2,1)S(1)}, u32[]{:S(2)}) copy-start(bf16[1024,3072]{1,0:T(8,128)(2,1)S(1)} %get-tuple-element.188) | copy-start | bytes 18874372
  327.6 13.9 %copy-start.10 = (bf16[1024,768]{0,1:T(8,128)(2,1)S(1)}, bf16[1024,768]{0,1:T(8,128)(2,1)}, u32[]{:S(2)}) copy-start(bf16[1024,768]{0,1:T(8,128)(2,1)} %copy.87) | copy-start | bytes 4718596
  327.6 13.9 %copy-start.23 = (pred[512,1024]{1,0:T(8,128)(4,1)S(1)}, pred[512,1024]{1,0:T(8,128)(4,1)}, u32[]{:S(2)}) copy-start(pred[512,1024]{1,0:T(8,128)(4,1)} %get-tuple-element.202) | copy-start | bytes 1572868
  341.5 18.6 %copy-start.19 = (pred[512,1024]{1,0:T(8,128)(4,1)S(1)}, pred[512,1024]{1,0:T(8,128)(4,1)}, u32[]{:S(2)}) copy-start(pred[512,1024]{1,0:T(8,128)(4,1)} %get-tuple-element.201) | copy-start | bytes 1572868
  341.5 18.6 %copy-start.36 = (f32[12,512]{1,0:T(8,128)S(1)}, f32[12,512]{1,0:T(8,128)}, u32[]{:S(2)}) copy-start(f32[12,512]{1,0:T(8,128)} %log_add_fusion.1) | copy-start | bytes 73732
  341.6 18.6 %copy-start.48 = (f32[512]{0:T(512)S(1)}, f32[512]{0:T(512)}, u32[]{:S(2)}) copy-start(f32[512]{0:T(512)} %copy-done.47) | copy-start | bytes 6148
  360.1 155.1 %reduce-scatter.5.cloned.1.call-start = ((), (), s32[]{:S(2)}) async-start(), calls=%async_computation.8 | async-start | bytes 5308416 | tf_op jit(solution)/shard_map/reduce_scatter | solution.py:366
  381.0 14.5 %copy-start.51 = (f32[512]{0:T(512)S(1)}, f32[512]{0:T(512)}, u32[]{:S(2)}) copy-start(f32[512]{0:T(512)} %copy-done.49) | copy-start | bytes 6148
  437.8 10.0 %copy-start = (bf16[12,512,1024]{2,1,0:T(8,128)(2,1)S(1)}, bf16[12,512,1024]{2,1,0:T(8,128)(2,1)}, u32[]{:S(2)}) copy-start(bf16[12,512,1024]{2,1,0:T(8,128)(2,1)} %get-tuple-element.225) | copy-start | bytes 37748740
  454.0 5.8 slice-start.6
  455.7 6.9 copy-start.28
  462.7 6.2 copy-start.59
  468.9 109.3 %reduce-scatter.9.cloned.1.call-start = ((), (), s32[]{:S(2)}) async-start(), calls=%async_computation.10 | async-start | bytes 7077888 | tf_op jit(solution)/shard_map/reduce_scatter | solution.py:288
  478.7 162.4 %reduce-scatter.11.cloned.1.call-start = ((), (), s32[]{:S(2)}) async-start(), calls=%async_computation.11 | async-start | bytes 7077888 | tf_op jit(solution)/shard_map/reduce_scatter | solution.py:300
  487.9 308.2 %all-reduce.32.cloned.1.call-start = ((), (), s32[]{:S(2)}) async-start(), calls=%async_computation.12 | async-start | bytes 14155776 | tf_op jit(solution)/shard_map/psum | solution.py:402
  796.1 5.8 copy-start.33
  (39 other events, 86.3 us)
Sparse Core Ops, SparseCore 0:
  10.9 63.2 all-gather.4
  77.1 52.7 all-gather.6
  132.9 62.4 all-gather.8
  198.2 61.7 all-gather.10
  360.2 20.1 reduce-scatter.6
  469.0 46.1 reduce-scatter.4
  518.0 60.0 reduce-scatter.8
  581.0 60.0 reduce-scatter.10
  645.1 150.9 all-reduce.31
where the time goes:
time: 818 us; the launch traced here: 814 us
  matrix products  268 us (33%)
  waiting for transfers between devices  229 us (28%)
  other arithmetic  137 us (17%)
  blocking collectives  112 us (14%)
  local copies, waits for them, and re-layouts  51.7 us (6%)
  between operations  16.3 us (2%)
    reduce_scatter x1, waiting for transfers between devices, per_device(): lax.psum_scatter(expand_weight_grad.astype(jnp.bfloat16), 'shard', scatte...  63 us
    reduce_scatter x1, waiting for transfers between devices, per_device(): lax.psum_scatter(shrink_weight_grad.astype(jnp.bfloat16), 'shard', scatte...  63 us
    psum x1, blocking collectives, per_device(): lax.psum(part_gain_one.astype(jnp.bfloat16), 'group').astype(jnp.float32)  60.9 us
    unnamed x2, blocking collectives  51 us
    convert_element_type x1, other arithmetic, row_backward(): grad_scores = (probs * (grad_probs - inner_sum)).astype(jnp.bfloat16)  42.2 us
    psum x1, waiting for transfers between devices, per_device(): lax.psum(part_qkv.astype(jnp.bfloat16), 'group').astype(jnp.float32)  39.8 us
    dot_general x2, matrix products, row_backward(): jnp.einsum('qhd,khd->hqk', grad_block, value_heads, preferred_element_typ...  39.3 us
    dot_general x1, matrix products, per_device(): jnp.dot(second_low, expand_full, preferred_element_type=jnp.float32)  38.7 us
  transfers between devices with their start and end apart: 9, of which 6 were waited for; matrix products, arithmetic and copies ran while one was open for 41% of the time, Pallas kernels for 0%

commit v1 on v0

v1 whole, which is shorter than its diff:
```python
import functools
import math

import jax
import jax.numpy as jnp
from jax import lax
from jax.sharding import PartitionSpec as P


HEADS = 12
HEAD = 64
NSEG = 5


EPSILON = 1e-05

MASKED = -1000000000.0


def norm_apply(values, gain, shift):
    average = jnp.mean(values, axis=-1, keepdims=True)
    centered = values - average
    inv_scale = lax.rsqrt(jnp.mean(centered * centered, axis=-1, keepdims=True) + EPSILON)
    unit = centered * inv_scale
    return (unit * gain + shift, unit, inv_scale)


def norm_back(unit, inv_scale, gain, grad):
    scaled = grad * gain
    back = inv_scale * (
        scaled
        - jnp.mean(scaled, axis=-1, keepdims=True)
        - unit * jnp.mean(scaled * unit, axis=-1, keepdims=True)
    )
    return (back, jnp.sum(grad * unit, axis=0), jnp.sum(grad, axis=0))


def gelu_exact(values):
    return jax.nn.gelu(values, approximate=False)


def segment_ids(lengths_row, length):
    ends = jnp.cumsum(lengths_row)
    places = jnp.arange(length, dtype=jnp.int32)
    return jnp.sum((places[:, None] >= ends[None, :]).astype(jnp.int32), axis=1)


def split_heads(qkv_row):
    length = qkv_row.shape[0]
    width = qkv_row.shape[1] // 3
    queries = qkv_row[:, :width].reshape(length, HEADS, HEAD)
    key_heads = qkv_row[:, width : 2 * width].reshape(length, HEADS, HEAD)
    value_heads = qkv_row[:, 2 * width :].reshape(length, HEADS, HEAD)
    return (queries, key_heads, value_heads)


def masked_scores(query_part, key_heads, segment, valid, offset):
    query_count = query_part.shape[0]
    scores = jnp.einsum(
        "qhd,khd->hqk", query_part, key_heads, preferred_element_type=jnp.float32
    ) * (1.0 / math.sqrt(HEAD))
    places = jnp.arange(segment.shape[0], dtype=jnp.int32)
    query_places = places[offset : offset + query_count]
    query_segment = segment[offset : offset + query_count]
    allowed = (
        (query_segment[:, None] == segment[None, :])
        & (query_places[:, None] >= places[None, :])
        & valid[None, :]
    )
    return jnp.where(allowed[None], scores, MASKED)


def row_forward(pieces):
    qkv_row, segment = pieces
    length = qkv_row.shape[0]
    queries, key_heads, value_heads = split_heads(qkv_row)
    valid = segment < NSEG - 1
    block_rows = min(512, length)
    attended_parts = []
    totals = []
    for offset in range(0, length, block_rows):
        scores = masked_scores(
            queries[offset : offset + block_rows], key_heads, segment, valid, offset
        )
        keep_rows = valid[offset : offset + block_rows].astype(jnp.float32)[None, :, None]
        peak = jnp.max(scores, axis=-1, keepdims=True)
        expd = jnp.exp(scores - peak)
        total = jnp.sum(expd, axis=-1, keepdims=True)
        probs = (expd / total * keep_rows).astype(jnp.bfloat16)
        attended_parts.append(
            jnp.einsum(
                "hqk,khd->qhd", probs, value_heads, preferred_element_type=jnp.float32
            ).reshape(block_rows, HEADS * HEAD)
        )
        totals.append((peak + jnp.log(total))[:, :, 0])
    return (jnp.concatenate(attended_parts, axis=0), jnp.concatenate(totals, axis=1))


def row_backward(pieces):
    qkv_row, segment, log_total, grad_rows = pieces
    length = qkv_row.shape[0]
    queries, key_heads, value_heads = split_heads(qkv_row)
    valid = segment < NSEG - 1
    grad_heads = grad_rows.reshape(length, HEADS, HEAD)
    block_rows = min(512, length)
    scale_factor = 1.0 / math.sqrt(HEAD)
    query_grads = []
    key_grad = jnp.zeros((length, HEADS, HEAD), jnp.float32)
    value_grad = jnp.zeros((length, HEADS, HEAD), jnp.float32)
    for offset in range(0, length, block_rows):
        query_part = queries[offset : offset + block_rows]
        scores = masked_scores(query_part, key_heads, segment, valid, offset)
        keep_rows = valid[offset : offset + block_rows].astype(jnp.float32)[None, :, None]
        probs = jnp.exp(scores - log_total[:, offset : offset + block_rows, None]) * keep_rows
        grad_block = grad_heads[offset : offset + block_rows]
        grad_probs = jnp.einsum(
            "qhd,khd->hqk", grad_block, value_heads, preferred_element_type=jnp.float32
        )
        inner_sum = jnp.sum(probs * grad_probs, axis=-1, keepdims=True)
        grad_scores = (probs * (grad_probs - inner_sum)).astype(jnp.bfloat16)
        query_grads.append(
            jnp.einsum("hqk,khd->qhd", grad_scores, key_heads, preferred_element_type=jnp.float32)
            * scale_factor
        )
        key_grad = (
            key_grad
            + jnp.einsum(
                "hqk,qhd->khd", grad_scores, query_part, preferred_element_type=jnp.float32
            )
            * scale_factor
        )
        value_grad = value_grad + jnp.einsum(
            "hqk,qhd->khd",
            probs.astype(jnp.bfloat16),
            grad_block,
            preferred_element_type=jnp.float32,
        )
    query_grad = jnp.concatenate(query_grads, axis=0)
    return jnp.concatenate(
        [
            query_grad.reshape(length, -1),
            key_grad.reshape(length, -1),
            value_grad.reshape(length, -1),
        ],
        axis=1,
    )


def pack_columns(parts, rows):
    cols = [p.reshape(rows, -1) for p in parts]
    width = sum(c.shape[1] for c in cols)
    pad = (-width) % 128
    if pad:
        cols.append(jnp.zeros((rows, pad), cols[0].dtype))
    return jnp.concatenate(cols, axis=1)


def unpack_columns(block, widths):
    out = []
    offset = 0
    for w in widths:
        out.append(block[:, offset : offset + w].reshape(-1))
        offset += w
    return out


def grad_rows_reduce(packed, group_size, shard_size):
    rows, cols = packed.shape
    n = rows // (group_size * shard_size)
    permuted = (
        packed.reshape(shard_size, group_size, n, cols)
        .transpose(1, 0, 2, 3)
        .reshape(rows, cols)
    )
    return lax.psum_scatter(
        permuted, ("group", "shard"), scatter_dimension=0, tiled=True
    )


def per_device(
    tokens,
    doc_lengths,
    first_gain,
    first_shift,
    qkv_weight,
    query_bias,
    value_bias,
    inner_gain,
    inner_shift,
    proj_weight,
    proj_bias,
    second_gain,
    second_shift,
    expand_weight,
    expand_bias,
    hidden_gain,
    hidden_shift,
    shrink_weight,
    shrink_bias,
    out_cotangent,
):
    group_size = lax.axis_size("group")
    shard_size = lax.axis_size("shard")
    n = qkv_weight.shape[0]
    model_width = n * group_size * shard_size
    wide_width = expand_weight.shape[1]
    ratio = wide_width // model_width
    qkv_width = qkv_weight.shape[1]

    small_parts = (
        first_gain,
        first_shift,
        query_bias,
        value_bias,
        inner_gain,
        inner_shift,
        proj_bias,
        second_gain,
        second_shift,
        shrink_bias,
        expand_bias,
        hidden_gain,
        hidden_shift,
    )
    small_widths = [p.shape[0] // n for p in small_parts]
    first_pack = jnp.concatenate([qkv_weight, pack_columns(small_parts, n)], axis=1)
    first_full = lax.all_gather(first_pack, ("group", "shard"), axis=0, tiled=True)
    qkv_full = first_full[:, :qkv_width]
    (
        gain_one,
        shift_one,
        qbias_full,
        vbias_full,
        gain_inner,
        shift_inner,
        pbias_full,
        gain_three,
        shift_three,
        sbias_full,
        ebias_full,
        gain_four,
        shift_four,
    ) = unpack_columns(first_full[:, qkv_width:], small_widths)
    second_pack = jnp.concatenate(
        [proj_weight, expand_weight, shrink_weight.reshape(n, ratio * model_width)], axis=1
    )
    second_full = lax.all_gather(second_pack, ("group", "shard"), axis=0, tiled=True)
    proj_full = second_full[:, :model_width]
    expand_full = second_full[:, model_width : model_width + wide_width]
    shrink_full = second_full[:, model_width + wide_width :].reshape(wide_width, model_width)

    row_count = doc_lengths.shape[0]
    length = tokens.shape[0] // row_count
    inputs = tokens.astype(jnp.float32)
    normed, unit_one, inv_one = norm_apply(
        inputs, gain_one.astype(jnp.float32), shift_one.astype(jnp.float32)
    )
    normed_low = normed.astype(jnp.bfloat16)
    bias_cat = jnp.concatenate([qbias_full, jnp.zeros_like(qbias_full), vbias_full]).astype(
        jnp.float32
    )
    qkv_low = (jnp.dot(normed_low, qkv_full, preferred_element_type=jnp.float32) + bias_cat).astype(
        jnp.bfloat16
    )
    segments = jax.vmap(functools.partial(segment_ids, length=length))(doc_lengths)
    qkv_rows = qkv_low.reshape(row_count, length, 3 * model_width)
    attended, log_totals = lax.map(row_forward, (qkv_rows, segments))
    attended = attended.reshape(-1, model_width)
    inner, unit_two, inv_two = norm_apply(
        attended, gain_inner.astype(jnp.float32), shift_inner.astype(jnp.float32)
    )
    inner_low = inner.astype(jnp.bfloat16)
    middle = (
        inputs
        + jnp.dot(inner_low, proj_full, preferred_element_type=jnp.float32)
        + pbias_full.astype(jnp.float32)
    )
    second, unit_three, inv_three = norm_apply(
        middle, gain_three.astype(jnp.float32), shift_three.astype(jnp.float32)
    )
    second_low = second.astype(jnp.bfloat16)
    pre_act = jnp.dot(
        second_low, expand_full, preferred_element_type=jnp.float32
    ) + ebias_full.astype(jnp.float32)
    activ, gelu_pull = jax.vjp(gelu_exact, pre_act)
    hidden, unit_four, inv_four = norm_apply(
        activ, gain_four.astype(jnp.float32), shift_four.astype(jnp.float32)
    )
    hidden_low = hidden.astype(jnp.bfloat16)
    output = (
        middle
        + jnp.dot(hidden_low, shrink_full, preferred_element_type=jnp.float32)
        + sbias_full.astype(jnp.float32)
    )
    block_output = output.astype(jnp.bfloat16)
    grad_out = out_cotangent.astype(jnp.float32)
    shrink_weight_grad = jnp.einsum(
        "tf,td->fd", hidden_low, out_cotangent, preferred_element_type=jnp.float32
    )
    shrink_bias_grad = jnp.sum(grad_out, axis=0)
    grad_hidden = jnp.einsum(
        "td,fd->tf", out_cotangent, shrink_full, preferred_element_type=jnp.float32
    )
    grad_activ, hidden_gain_grad, hidden_shift_grad = norm_back(
        unit_four, inv_four, gain_four.astype(jnp.float32), grad_hidden
    )
    grad_pre = gelu_pull(grad_activ)[0].astype(jnp.bfloat16)
    expand_bias_grad = jnp.sum(grad_pre.astype(jnp.float32), axis=0)
    expand_weight_grad = jnp.einsum(
        "td,tf->df", second_low, grad_pre, preferred_element_type=jnp.float32
    )
    grad_second = jnp.einsum("tf,df->td", grad_pre, expand_full, preferred_element_type=jnp.float32)
    grad_mid_part, second_gain_grad, second_shift_grad = norm_back(
        unit_three, inv_three, gain_three.astype(jnp.float32), grad_second
    )
    grad_middle = grad_out + grad_mid_part
    ffn_small = (
        second_gain_grad,
        second_shift_grad,
        shrink_bias_grad,
        expand_bias_grad,
        hidden_gain_grad,
        hidden_shift_grad,
    )
    ffn_small_widths = [p.shape[0] // model_width for p in ffn_small]
    ffn_pack = jnp.concatenate(
        [
            expand_weight_grad,
            shrink_weight_grad.reshape(model_width, ratio * model_width),
            pack_columns(ffn_small, model_width),
        ],
        axis=1,
    ).astype(jnp.bfloat16)
    ffn_part = grad_rows_reduce(ffn_pack, group_size, shard_size)

    grad_branch = grad_middle.astype(jnp.bfloat16)
    proj_bias_grad = jnp.sum(grad_branch.astype(jnp.float32), axis=0)
    proj_weight_grad = jnp.einsum(
        "td,te->de", inner_low, grad_branch, preferred_element_type=jnp.float32
    )
    grad_inner = jnp.einsum("te,de->td", grad_branch, proj_full, preferred_element_type=jnp.float32)
    grad_attended, inner_gain_grad, inner_shift_grad = norm_back(
        unit_two, inv_two, gain_inner.astype(jnp.float32), grad_inner
    )
    grad_att_low = grad_attended.astype(jnp.bfloat16).reshape(row_count, length, model_width)
    grad_qkv = (
        lax.map(row_backward, (qkv_rows, segments, log_totals, grad_att_low))
        .reshape(-1, 3 * model_width)
        .astype(jnp.bfloat16)
    )
    grad_qkv_wide = grad_qkv.astype(jnp.float32)
    query_bias_grad = jnp.sum(grad_qkv_wide[:, :model_width], axis=0)
    value_bias_grad = jnp.sum(grad_qkv_wide[:, 2 * model_width :], axis=0)
    qkv_weight_grad = jnp.einsum(
        "td,te->de", normed_low, grad_qkv, preferred_element_type=jnp.float32
    )
    grad_normed = jnp.einsum("te,de->td", grad_qkv, qkv_full, preferred_element_type=jnp.float32)
    grad_in_part, first_gain_grad, first_shift_grad = norm_back(
        unit_one, inv_one, gain_one.astype(jnp.float32), grad_normed
    )
    input_grad = (grad_middle + grad_in_part).astype(jnp.bfloat16)
    attn_small = (
        first_gain_grad,
        first_shift_grad,
        query_bias_grad,
        value_bias_grad,
        inner_gain_grad,
        inner_shift_grad,
        proj_bias_grad,
    )
    attn_pack = jnp.concatenate(
        [qkv_weight_grad, proj_weight_grad, pack_columns(attn_small, model_width)], axis=1
    ).astype(jnp.bfloat16)
    ffn_part, attn_pack = lax.optimization_barrier((ffn_part, attn_pack))
    attn_part = grad_rows_reduce(attn_pack, group_size, shard_size)
    both = lax.all_gather(
        jnp.concatenate([ffn_part, attn_part], axis=1), "group", axis=0, tiled=True
    ).astype(jnp.float32)
    ffn_cols = ffn_pack.shape[1]
    ffn_back = both[:, :ffn_cols]
    attn_back = both[:, ffn_cols:]
    half = both.shape[0]
    expand_out = ffn_back[:, :wide_width]
    shrink_out = ffn_back[:, wide_width : 2 * wide_width].reshape(half * ratio, model_width)
    (
        second_gain_out,
        second_shift_out,
        sbias_out,
        ebias_out,
        gain_four_out,
        shift_four_out,
    ) = unpack_columns(ffn_back[:, 2 * wide_width :], ffn_small_widths)
    qkv_out = attn_back[:, :qkv_width]
    proj_out = attn_back[:, qkv_width : qkv_width + model_width]
    (
        gain_one_out,
        shift_one_out,
        qbias_out,
        vbias_out,
        gain_inner_out,
        shift_inner_out,
        pbias_out,
    ) = unpack_columns(attn_back[:, qkv_width + model_width :], [1] * 7)
    return (
        block_output,
        input_grad,
        gain_one_out,
        shift_one_out,
        qkv_out,
        qbias_out,
        vbias_out,
        gain_inner_out,
        shift_inner_out,
        proj_out,
        pbias_out,
        second_gain_out,
        second_shift_out,
        expand_out,
        ebias_out,
        gain_four_out,
        shift_four_out,
        shrink_out,
        sbias_out,
    )


def solution(mesh):
    in_specs = (
        P(("group", "shard"), None),
        P(("group", "shard"), None),
        P(("group", "shard")),
        P(("group", "shard")),
        P(("group", "shard"), None),
        P(("group", "shard")),
        P(("group", "shard")),
        P(("group", "shard")),
        P(("group", "shard")),
        P(("group", "shard"), None),
        P(("group", "shard")),
        P(("group", "shard")),
        P(("group", "shard")),
        P(("group", "shard"), None),
        P(("group", "shard")),
        P(("group", "shard")),
        P(("group", "shard")),
        P(("group", "shard"), None),
        P(("group", "shard")),
        P(("group", "shard"), None),
    )
    out_specs = (
        P(("group", "shard"), None),
        P(("group", "shard"), None),
        P("shard"),
        P("shard"),
        P("shard", None),
        P("shard"),
        P("shard"),
        P("shard"),
        P("shard"),
        P("shard", None),
        P("shard"),
        P("shard"),
        P("shard"),
        P("shard", None),
        P("shard"),
        P("shard"),
        P("shard"),
        P("shard", None),
        P("shard"),
    )

    return jax.shard_map(
        per_device, mesh=mesh, in_specs=in_specs, out_specs=out_specs, check_vma=False
    )
```

time: 818 us -> 775 us (0.947)
  blocking collectives: 112 us -> 0 us
  local copies, waits for them, and re-layouts: 51.7 us -> 151 us
  waiting for transfers between devices: 229 us -> 202 us
  matrix products: 268 us -> 258 us
    reduce_scatter x4 -> x0, waiting for transfers between devices: 149 us -> none  [the longest x1 63 us: per_device(): lax.psum_scatter(expand_weight_grad.astype(jnp.bfloat16), 'shard', scatte...]
    unnamed x9 -> x6, waiting for transfers between devices: 2.66 us -> 99.5 us
    all_gather x4 -> x3, waiting for transfers between devices: 37.7 us -> 102 us  [the longest x1 51.4 us: per_device(): lax.all_gather(first_pack, ('group', 'shard'), axis=0, tiled=True)]
    psum x1 -> x0, blocking collectives: 60.9 us -> none  [per_device(): lax.psum(part_gain_one.astype(jnp.bfloat16), 'group').astype(jnp.float32)]
    unnamed x2 -> x0, blocking collectives: 51 us -> none
    concatenate x0 -> x10, local copies, waits for them, and re-layouts: none -> 42.7 us  [the longest x8 31.6 us: per_device(): jnp.concatenate([expand_weight_grad, shrink_weight_grad.reshape(model_wid...]
    psum x1 -> x0, waiting for transfers between devices: 39.8 us -> none  [per_device(): lax.psum(part_qkv.astype(jnp.bfloat16), 'group').astype(jnp.float32)]
    reshape x0 -> x26, local copies, waits for them, and re-layouts: none -> 32.3 us  [the longest x20 14.4 us: pack_columns(): cols = [p.reshape(rows, -1) for p in parts]]
  transfers between devices with their start and end apart: 9 -> 5, of which waited for: 6 -> 3; matrix products, arithmetic and copies ran while one was open for 41% -> 40% of each run, Pallas kernels for 0% -> 0%
where the time goes in v1:
time: 775 us; the launch traced here: 764 us
  matrix products  258 us (33%)
  waiting for transfers between devices  202 us (26%)
  local copies, waits for them, and re-layouts  151 us (19%)
  other arithmetic  137 us (18%)
  between operations  15.4 us (2%)
    unnamed x6, waiting for transfers between devices  99.5 us
    all_gather x1, waiting for transfers between devices, per_device(): lax.all_gather(first_pack, ('group', 'shard'), axis=0, tiled=True)  51.4 us
    all_gather x1, waiting for transfers between devices, per_device(): lax.all_gather(jnp.concatenate([ffn_part, attn_part], axis=1), 'group', a...  50.8 us
    convert_element_type x1, other arithmetic, row_backward(): grad_scores = (probs * (grad_probs - inner_sum)).astype(jnp.bfloat16)  43.7 us
    dot_general x2, matrix products, row_backward(): jnp.einsum('qhd,khd->hqk', grad_block, value_heads, preferred_element_typ...  40.1 us
    dot_general x1, matrix products, per_device(): jnp.dot(second_low, expand_full, preferred_element_type=jnp.float32)  39 us
    concatenate x8, local copies, waits for them, and re-layouts, per_device(): jnp.concatenate([expand_weight_grad, shrink_weight_grad.reshape(model_wid...  31.6 us
    dot_general x2, matrix products, row_backward(): jnp.einsum('hqk,qhd->khd', probs.astype(jnp.bfloat16), grad_block, prefer...  27.7 us
  transfers between devices with their start and end apart: 5, of which 3 were waited for; matrix products, arithmetic and copies ran while one was open for 40% of the time, Pallas kernels for 0%

profile of v1, /device:TPU:0, one launch (start us, length us, event | category | flops | bytes accessed | tf_op | source)
XLA Modules:
  0.0 763.7 jit_solution(9982105746341952846)
XLA Ops:
  31.0 51.4 %all-gather.4.cloned.1.call-done = bf16[768,2432]{1,0:T(8,128)(2,1)} async-done(((bf16[24,2432]{1,0:T(8,128)(2,1)}), bf16[768,2432]{1,0:T(8,128)(2,1)}) %all-gather.4.cloned.1.call-update) | async-done | bytes 3735568 | tf_op jit(solution)/shard_map/all_gather | solution.py:227
  87.8 4.0 convert_reduce_fusion.1
  91.8 6.5 add_convert_fusion.2
  103.3 3.2 fusion.68
  113.9 12.2 %fusion.3 = (f32[12,512]{1,0:T(8,128)S(1)}, f32[12,512,1024]{2,1,0:T(8,128)}) fusion(pred[512,1024]{1,0:T(8,128)(4,1)} %get-tuple-element.190, bf16[512,12,64]{0,2,1:T(8,128)(2,1)} %bitcast.115, bf16[1024,12,64]{0,2,1:T(8,128)(2,1)S(1)} %bitcast.88), kind=kOutput, calls=%fused_computation.16 | convolution fusion | flops 824174592 | bytes 28073984 | tf_op jit(solution)/shard_map/while/body/eval_jaxpr/qhd,khd->hqk/dot_general | solution.py:59
  126.1 12.0 %fusion.2 = (f32[12,512]{1,0:T(8,128)S(1)}, f32[12,512,1024]{2,1,0:T(8,128)}) fusion(pred[512,1024]{1,0:T(8,128)(4,1)S(1)} %copy-done.16, bf16[512,12,64]{0,2,1:T(8,128)(2,1)S(1)} %bitcast.118, bf16[1024,12,64]{0,2,1:T(8,128)(2,1)S(1)} %bitcast.89), kind=kOutput, calls=%fused_computation.15 | convolution fusion | flops 824174592 | bytes 28073984 | tf_op jit(solution)/shard_map/while/body/eval_jaxpr/qhd,khd->hqk/dot_general | solution.py:59
  138.0 13.6 %fusion.1 = f32[12,512]{1,0:T(8,128)S(1)} fusion(f32[12,512,1024]{2,1,0:T(8,128)} %get-tuple-element.196, f32[12,512]{1,0:T(8,128)S(1)} %get-tuple-element.195, pred[512,1024]{1,0:T(8,128)(4,1)S(1)} %copy-done.20), kind=kLoop, calls=%fused_computation.13 | loop fusion | flops 25159680 | bytes 25739264 | tf_op jit(solution)/shard_map/while/body/eval_jaxpr/reduce_sum | solution.py:88
  153.7 7.4 fusion
  161.1 14.6 %fusion.16 = f32[12,64,512]{2,1,0:T(8,128)S(1)} fusion(bf16[1024,12,64]{0,2,1:T(8,128)(2,1)S(1)} %bitcast.96, f32[12,512,1024]{2,1,0:T(8,128)} %get-tuple-element.196, f32[512]{0:T(512)S(1)} %get-tuple-element.194, f32[12,512]{1,0:T(8,128)S(1)} %fusion.1, f32[12,512]{1,0:T(8,128)S(1)} %get-tuple-element.195, pred[512,1024]{1,0:T(8,128)(4,1)} %get-tuple-element.190), kind=kOutput, calls=%fused_computation.43 | convolution fusion | flops 843055104 | bytes 28887040 | tf_op jit(solution)/shard_map/while/body/eval_jaxpr/hqk,khd->qhd/dot_general | solution.py:91
  175.7 10.8 %fusion.15 = f32[12,64,512]{2,1,0:T(8,128)} fusion(bf16[1024,12,64]{0,2,1:T(8,128)(2,1)S(1)} %bitcast.97, f32[12,512,1024]{2,1,0:T(8,128)S(1)} %copy-done, f32[512]{0:T(512)S(1)} %get-tuple-element.193, f32[12,512]{1,0:T(8,128)S(1)} %fusion, f32[12,512]{1,0:T(8,128)S(1)} %get-tuple-element.197, pred[512,1024]{1,0:T(8,128)(4,1)} %get-tuple-element.189), kind=kOutput, calls=%fused_computation.42 | convolution fusion | flops 843055104 | bytes 28887040 | tf_op jit(solution)/shard_map/while/body/eval_jaxpr/hqk,khd->qhd/dot_general | solution.py:91
  191.3 4.8 slice.310
  196.1 8.5 %reshape.663 = bf16[3072,768]{1,0:T(8,128)(2,1)} reshape(bf16[768,3072]{1,0:T(8,128)(2,1)} %slice.310) | data formatting | bytes 9437184 | tf_op jit(solution)/shard_map/reshape | solution.py:250
  204.7 3.6 fusion.72
  208.7 39.0 %fusion.64 = (f32[1024]{0:T(1024)S(1)}, f32[1024,3072]{1,0:T(8,128)S(1)}, f32[1024,3072]{1,0:T(8,128)}, f32[1024,3072]{1,0:T(8,128)}) fusion(f32[3072]{0:T(1024)S(1)} %copy-done.56, bf16[768,6912]{1,0:T(8,128)(2,1)} %all-gather.6.cloned.1.call-done, f32[1024,768]{0,1:T(8,128)S(1)} %get-tuple-element.200, f32[768]{0:T(1024)S(1)} %copy-done.82, ...), kind=kOutput, calls=%fused_computation.173 | convolution fusion | flops 5043387392 | bytes 45643776 | tf_op jit(solution)/shard_map/dot_general | solution.py:282
  249.1 3.3 copy-done.2
  252.5 12.3 %fusion.5 = (bf16[3072]{0:T(1024)(128)(2,1)S(1)}, f32[1024]{0:T(1024)S(1)}, f32[1024]{0:T(1024)S(1)}, bf16[1024,3072]{1,0:T(8,128)(2,1)}, f32[3072,1024]{0,1:T(8,128)}) fusion(f32[1024,3072]{1,0:T(8,128)S(1)} %get-tuple-element.172, f32[1024]{0:T(1024)S(1)} %add_rsqrt_fusion, f32[1024]{0:T(1024)S(1)} %broadcast_multiply_fusion.2, f32[3072]{0:T(1024)S(1)} %copy-done.55, ...), kind=kOutput, calls=%fused_computation.20 | convolution fusion | flops 4866436096 | bytes 37795840 | tf_op jit(solution)/shard_map/td,fd->tf/dot_general | solution.py:301
  264.7 5.2 reduce_sum.339
  269.9 20.5 %fusion.63 = (bf16[3072]{0:T(1024)(128)(2,1)S(1)}, bf16[1024,3072]{1,0:T(8,128)(2,1)}) fusion(f32[1024,3072]{1,0:T(8,128)} %get-tuple-element.173, f32[1024]{0:T(1024)S(1)} %broadcast_multiply_fusion, f32[1024,3072]{1,0:T(8,128)} %copy-done.2, f32[1024]{0:T(1024)S(1)} %broadcast_multiply_fusion.2, f32[1024]{0:T(1024)S(1)} %broadcast_multiply_fusion.1, ...), kind=kLoop, calls=%fused_computation.172 | loop fusion | flops 72348672 | bytes 56670208 | tf_op jit(solution)/shard_map/reduce_sum | solution.py:308
  293.8 10.1 %convolution_convert_fusion.1 = bf16[768,3072]{1,0:T(8,128)(2,1)} fusion(bf16[1024,3072]{1,0:T(8,128)(2,1)} %get-tuple-element.170, f32[1024,768]{0,1:T(8,128)S(1)} %copy-done.7, f32[768]{0:T(1024)S(1)} %copy-done.82, f32[768]{0:T(1024)S(1)} %copy-done.62, f32[1024]{0:T(1024)S(1)} %add_rsqrt_fusion.1, f32[1024]{0:T(1024)S(1)} %broadcast_multiply_fusion.9), kind=kOutput, calls=%fused_computation.49 | convolution fusion | flops 4838129664 | bytes 14170112 | tf_op jit(solution)/shard_map/td,tf->df/dot_general | solution.py:309
  303.8 9.1 %fusion.73 = (bf16[768]{0:T(1024)(128)(2,1)S(1)}, f32[1024,768]{1,0:T(8,128)}) fusion(bf16[1024,3072]{1,0:T(8,128)(2,1)S(1)} %copy-done.33, bf16[768,6912]{1,0:T(8,128)(2,1)} %all-gather.6.cloned.1.call-done), kind=kOutput, calls=%fused_computation.181 | convolution fusion | flops 4832623616 | bytes 14157312 | tf_op jit(solution)/shard_map/tf,df->td/dot_general | solution.py:312
  314.0 3.6 copy.162
  322.7 4.0 multiply_reduce_fusion.4
  328.9 9.8 %convolution_convert_fusion = bf16[3072,768]{1,0:T(8,128)(2,1)} fusion(bf16[1024,3072]{1,0:T(8,128)(2,1)} %get-tuple-element.174, bf16[1024,768]{1,0:T(8,128)(2,1)S(1)} %copy-done.28), kind=kOutput, calls=%fused_computation.48 | convolution fusion | flops 4834197504 | bytes 12582912 | tf_op jit(solution)/shard_map/tf,td->fd/dot_general | solution.py:297
  338.7 8.6 %concatenate.70 = bf16[2,16,24,3072]{3,2,1,0:T(8,128)(2,1)} reshape(bf16[3072,768]{1,0:T(8,128)(2,1)} %convolution_convert_fusion) | data formatting | bytes 9437184 | tf_op jit(solution)/shard_map/concatenate | solution.py:326
  347.4 17.4 %concatenate.77 = bf16[2,16,24,6272]{3,2,1,0:T(8,128)(2,1)} concatenate(bf16[2,16,24,3072]{3,2,1,0:T(8,128)(2,1)} %bitcast.122, bf16[2,16,24,3072]{3,2,1,0:T(8,128)(2,1)} %concatenate.70, bf16[2,16,24,1]{3,2,1,0:T(8,128)(2,1)S(1)} %concatenate.80, bf16[2,16,24,1]{3,2,1,0:T(8,128)(2,1)S(1)} %copy-done.47, bf16[2,16,24,1]{3,2,1,0:T(8,128)(2,1)S(1)} %copy-done.43, ...), dimensions={3} | concatenate | bytes 19267584 | tf_op jit(solution)/shard_map/concatenate | solution.py:326
  364.7 8.0 %copy.168 = bf16[16,2,24,6272]{3,2,1,0:T(8,128)(2,1)} copy(bf16[16,2,24,6272]{3,2,0,1:T(8,128)(2,1)} %bitcast.92) | data formatting | bytes 19267584 | tf_op jit(solution)/shard_map/transpose | solution.py:172
  374.2 21.0 %multiply_reduce_fusion.1 = (f32[12,512]{1,0:T(8,128)S(1)}, f32[12,512,1024]{2,1,0:T(8,128)}) fusion(f32[512]{0:T(512)S(1)} %copy-done.66, f32[12,512]{1,0:T(8,128)S(1)} %copy-done.49, f32[12,512,1024]{2,1,0:T(8,128)} %get-tuple-element.198, pred[512,1024]{1,0:T(8,128)(4,1)S(1)} %copy-done.18, bf16[512,12,64]{0,2,1:T(8,128)(2,1)S(1)} %bitcast.123, ...), kind=kOutput, calls=%fused_computation.4 | convolution fusion | flops 843048960 | bytes 53266432 | tf_op jit(solution)/shard_map/while/body/eval_jaxpr/qhd,khd->hqk/dot_general | solution.py:116
  395.2 19.1 %multiply_reduce_fusion = (f32[12,512]{1,0:T(8,128)S(1)}, f32[12,512,1024]{2,1,0:T(8,128)}) fusion(f32[512]{0:T(512)S(1)} %copy-done.68, f32[12,512]{1,0:T(8,128)S(1)} %copy-done.51, f32[12,512,1024]{2,1,0:T(8,128)} %get-tuple-element.196, pred[512,1024]{1,0:T(8,128)(4,1)S(1)} %copy-done.21, bf16[512,12,64]{0,2,1:T(8,128)(2,1)} %bitcast.125, ...), kind=kOutput, calls=%fused_computation.1 | convolution fusion | flops 843048960 | bytes 53266432 | tf_op jit(solution)/shard_map/while/body/eval_jaxpr/qhd,khd->hqk/dot_general | solution.py:116
  414.4 43.7 %multiply_convert_fusion = (bf16[12,512,1024]{2,1,0:T(8,128)(2,1)}, bf16[12,512,1024]{2,1,0:T(8,128)(2,1)}) fusion(f32[12,512,1024]{2,1,0:T(8,128)} %get-tuple-element.207, f32[12,512]{1,0:T(8,128)S(1)} %get-tuple-element.206, f32[512]{0:T(512)S(1)} %copy-done.68, f32[12,512]{1,0:T(8,128)S(1)} %copy-done.51, f32[12,512,1024]{2,1,0:T(8,128)} %get-tuple-element.196, ...), kind=kLoop, calls=%fused_computation | loop fusion | flops 88080384 | bytes 126980096 | tf_op jit(solution)/shard_map/while/body/eval_jaxpr/convert_element_type | solution.py:120
  459.3 10.6 %fusion.48 = bf16[512,12,64]{0,2,1:T(8,128)(2,1)} fusion(bf16[1024,12,64]{0,2,1:T(8,128)(2,1)} %bitcast.90, bf16[12,512,1024]{2,1,0:T(8,128)(2,1)} %get-tuple-element.212), kind=kOutput, calls=%fused_computation.110 | convolution fusion | flops 806092800 | bytes 14942208 | tf_op jit(solution)/shard_map/while/body/eval_jaxpr/hqk,khd->qhd/dot_general | solution.py:122
  469.9 6.2 fusion.47
  479.0 3.6 fusion.75
  485.3 14.0 %fusion.6 = f32[12,64,1024]{2,1,0:T(8,128)} fusion(bf16[512,12,64]{0,2,1:T(8,128)(2,1)S(1)} %bitcast.126, f32[12,512,1024]{2,1,0:T(8,128)} %get-tuple-element.196, f32[12,512]{1,0:T(8,128)S(1)} %copy-done.52, f32[512]{0:T(512)S(1)} %copy-done.68, pred[512,1024]{1,0:T(8,128)(4,1)S(1)} %copy-done.22), kind=kOutput, calls=%fused_computation.21 | convolution fusion | flops 836763648 | bytes 29648896 | tf_op jit(solution)/shard_map/while/body/eval_jaxpr/hqk,qhd->khd/dot_general | solution.py:132
  499.3 13.7 %add_convert_fusion.3 = bf16[12,64,1024]{2,1,0:T(8,128)(2,1)S(1)} fusion(f32[12,64,1024]{2,1,0:T(8,128)} %fusion.6, bf16[512,12,64]{0,2,1:T(8,128)(2,1)S(1)} %bitcast.124, f32[12,512,1024]{2,1,0:T(8,128)} %get-tuple-element.198, f32[12,512]{1,0:T(8,128)S(1)} %copy-done.50, f32[512]{0:T(512)S(1)} %copy-done.66, pred[512,1024]{1,0:T(8,128)(4,1)S(1)} %copy-done.19), kind=kOutput, calls=%fused_computation.80 | convolution fusion | flops 838336512 | bytes 31221760 | tf_op jit(solution)/shard_map/while/body/eval_jaxpr/hqk,qhd->khd/dot_general | solution.py:132
  513.1 5.5 fusion.74
  519.5 3.8 copy.163
  523.3 3.7 fusion.35
  534.8 5.9 convolution_convert_fusion.2
  540.7 9.4 %concatenate.78 = bf16[768,3200]{1,0:T(8,128)(2,1)} concatenate(bf16[768,2304]{1,0:T(8,128)(2,1)} %convolution_convert_fusion.2, bf16[768,768]{1,0:T(8,128)(2,1)} %convolution_convert_fusion.3, bf16[768,1]{1,0:T(8,128)(2,1)} %reshape.702, bf16[768,1]{1,0:T(8,128)(2,1)} %reshape.703, bf16[768,1]{1,0:T(8,128)(2,1)} %reshape.704, bf16[768,1]{1,0:T(8,128)(2,1)} %reshape.705, ...), dimensions={1} | concatenate | bytes 9830400 | tf_op jit(solution)/shard_map/concatenate | solution.py:371
  550.2 5.0 copy.178
  555.2 99.4 %reduce-scatter.9.cloned.1.call-done = bf16[24,3200]{1,0:T(8,128)(2,1)} async-done(((bf16[768,3200]{1,0:T(8,128)(2,1)}), bf16[24,3200]{1,0:T(8,128)(2,1)}) %reduce-scatter.9.cloned.1.call-update) | async-done | bytes 153616
  656.4 9.4 %add_convert_fusion.4 = bf16[1024,768]{0,1:T(8,128)(2,1)S(1)} fusion(f32[1024,768]{0,1:T(8,128)} %copy-done.6, bf16[1024,3072]{1,0:T(8,128)(2,1)} %get-tuple-element.174, bf16[3072,768]{1,0:T(8,128)(2,1)} %reshape.663, f32[768]{0:T(1024)S(1)} %copy-done.77), kind=kOutput, calls=%fused_computation.86 | convolution fusion | flops 4834197504 | bytes 15731712 | tf_op jit(solution)/shard_map/dot_general | solution.py:292
  667.4 3.9 fusion.34
  672.8 50.8 %all-gather.8.cloned.1.call-done = bf16[384,9472]{1,0:T(8,128)(2,1)} async-done(((bf16[24,9472]{1,0:T(8,128)(2,1)}), bf16[384,9472]{1,0:T(8,128)(2,1)}) %all-gather.8.cloned.1.call-update) | async-done | bytes 7274512 | tf_op jit(solution)/shard_map/all_gather | solution.py:376
  727.0 7.4 fusion.66
  734.4 6.2 reshape.689
  740.7 9.3 %convert_element_type.267 = f32[384,9472]{1,0:T(8,128)} convert(bf16[384,9472]{1,0:T(8,128)(2,1)} %all-gather.8.cloned.1.call-done) | non-fusion elementwise | flops 3637248 | bytes 21823488 | tf_op jit(solution)/shard_map/convert_element_type | solution.py:378
  750.0 3.6 slice_reduce_fusion.2
  (292 shorter events, 90.0 us)
Async XLA Ops:
  7.2 19.8 %copy-start.42 = (bf16[1024,768]{1,0:T(8,128)(2,1)S(1)}, bf16[1024,768]{1,0:T(8,128)(2,1)}, u32[]{:S(2)}) copy-start(bf16[1024,768]{1,0:T(8,128)(2,1)} %param.20) | copy-start | bytes 4718596
  7.2 75.2 %all-gather.4.cloned.1.call-start = ((), (), s32[]{:S(2)}) async-start(), calls=%async_computation.2 | async-start | bytes 3852288 | tf_op jit(solution)/shard_map/all_gather | solution.py:227
  18.8 8.9 %copy-start.84 = (s32[1,5]{1,0:T(1,128)S(1)}, s32[1,5]{1,0:T(1,128)}, u32[]{:S(2)}) copy-start(s32[1,5]{1,0:T(1,128)} %param.21) | copy-start | bytes 64
  18.8 172.5 %all-gather.6.cloned.1.call-start = ((), (), s32[]{:S(2)}) async-start(), calls=%async_computation.3 | async-start | bytes 10948608 | tf_op jit(solution)/shard_map/all_gather | solution.py:247
  21.6 528.6 %reduce-scatter.7.cloned.1.call-start = ((), (), s32[]{:S(2)}) async-start(), calls=%async_computation.5 | async-start | bytes 9934848
  27.7 176.9 %copy-start.3 = (bf16[1024,768]{0,1:T(8,128)(2,1)}, bf16[1024,768]{0,1:T(8,128)(2,1)S(1)}, u32[]{:S(2)}) copy-start(bf16[1024,768]{0,1:T(8,128)(2,1)S(1)} %copy.145) | copy-start | bytes 4718596
  28.3 132.8 %copy-start.67 = (f32[512]{0:T(512)}, f32[512]{0:T(512)S(1)}, u32[]{:S(2)}) copy-start(f32[512]{0:T(512)S(1)} %get-tuple-element.194) | copy-start | bytes 6148
  28.3 147.4 %copy-start.65 = (f32[512]{0:T(512)}, f32[512]{0:T(512)S(1)}, u32[]{:S(2)}) copy-start(f32[512]{0:T(512)S(1)} %get-tuple-element.193) | copy-start | bytes 6148
  28.4 70.0 %copy-start.53 = (f32[1024]{0:T(1024)}, f32[1024]{0:T(1024)S(1)}, u32[]{:S(2)}) copy-start(f32[1024]{0:T(1024)S(1)} %broadcast_multiply_fusion.11) | copy-start | bytes 12292
  28.8 69.5 %copy-start.63 = (f32[1024]{0:T(1024)}, f32[1024]{0:T(1024)S(1)}, u32[]{:S(2)}) copy-start(f32[1024]{0:T(1024)S(1)} %add_rsqrt_fusion.3) | copy-start | bytes 12292
  103.2 22.8 %copy-start.5 = (bf16[1024,768]{0,1:T(8,128)(2,1)}, bf16[1024,768]{0,1:T(8,128)(2,1)S(1)}, u32[]{:S(2)}) copy-start(bf16[1024,768]{0,1:T(8,128)(2,1)S(1)} %copy.158) | copy-start | bytes 4718596
  113.9 12.2 %copy-start.16 = (pred[512,1024]{1,0:T(8,128)(4,1)S(1)}, pred[512,1024]{1,0:T(8,128)(4,1)}, u32[]{:S(2)}) copy-start(pred[512,1024]{1,0:T(8,128)(4,1)} %get-tuple-element.189) | copy-start | bytes 1572868
  113.9 12.2 %copy-start.26 = (bf16[512,768]{0,1:T(8,128)(2,1)S(1)}, bf16[512,768]{0,1:T(8,128)(2,1)}, u32[]{:S(2)}) copy-start(bf16[512,768]{0,1:T(8,128)(2,1)} %copy.157) | copy-start | bytes 2359300
  126.1 12.0 %copy-start.20 = (pred[512,1024]{1,0:T(8,128)(4,1)S(1)}, pred[512,1024]{1,0:T(8,128)(4,1)}, u32[]{:S(2)}) copy-start(pred[512,1024]{1,0:T(8,128)(4,1)} %get-tuple-element.190) | copy-start | bytes 1572868
  138.0 15.6 %copy-start = (f32[12,512,1024]{2,1,0:T(8,128)S(1)}, f32[12,512,1024]{2,1,0:T(8,128)}, u32[]{:S(2)}) copy-start(f32[12,512,1024]{2,1,0:T(8,128)} %get-tuple-element.198) | copy-start | bytes 75497472
  138.0 15.7 %copy-start.17 = (pred[512,1024]{1,0:T(8,128)(4,1)S(1)}, pred[512,1024]{1,0:T(8,128)(4,1)}, u32[]{:S(2)}) copy-start(pred[512,1024]{1,0:T(8,128)(4,1)} %get-tuple-element.189) | copy-start | bytes 1572868
  153.7 7.4 copy-start.9
  175.7 28.9 %copy-start.11 = (f32[12,64,512]{2,1,0:T(8,128)}, f32[12,64,512]{2,1,0:T(8,128)S(1)}, u32[]{:S(2)}) copy-start(f32[12,64,512]{2,1,0:T(8,128)S(1)} %fusion.16) | copy-start | bytes 4718596
  188.2 16.4 %copy-start.57 = (f32[1024]{0:T(1024)}, f32[1024]{0:T(1024)S(1)}, u32[]{:S(2)}) copy-start(f32[1024]{0:T(1024)S(1)} %broadcast_multiply_fusion.10) | copy-start | bytes 12292
  190.0 14.6 %copy-start.72 = (f32[1024]{0:T(1024)}, f32[1024]{0:T(1024)S(1)}, u32[]{:S(2)}) copy-start(f32[1024]{0:T(1024)S(1)} %add_rsqrt_fusion.2) | copy-start | bytes 12292
  196.1 8.5 %copy-start.69 = (f32[768]{0:T(1024)S(1)}, f32[768]{0:T(1024)}, u32[]{:S(2)}) copy-start(f32[768]{0:T(1024)} %get-tuple-element.158) | copy-start | bytes 9220
  196.1 8.5 %copy-start.80 = (f32[768]{0:T(1024)S(1)}, f32[768]{0:T(1024)}, u32[]{:S(2)}) copy-start(f32[768]{0:T(1024)} %get-tuple-element.157) | copy-start | bytes 9220
  196.1 8.5 %copy-start.83 = (f32[768]{0:T(1024)S(1)}, f32[768]{0:T(1024)}, u32[]{:S(2)}) copy-start(f32[768]{0:T(1024)} %get-tuple-element.156) | copy-start | bytes 9220
  208.2 39.4 %copy-start.6 = (f32[1024,768]{0,1:T(8,128)}, f32[1024,768]{0,1:T(8,128)S(1)}, u32[]{:S(2)}) copy-start(f32[1024,768]{0,1:T(8,128)S(1)} %get-tuple-element.200) | copy-start | bytes 9437188
  269.9 23.8 %copy-start.7 = (f32[1024,768]{0,1:T(8,128)S(1)}, f32[1024,768]{0,1:T(8,128)}, u32[]{:S(2)}) copy-start(f32[1024,768]{0,1:T(8,128)} %copy-done.6) | copy-start | bytes 9437188
  293.8 10.1 %copy-start.33 = (bf16[1024,3072]{1,0:T(8,128)(2,1)S(1)}, bf16[1024,3072]{1,0:T(8,128)(2,1)}, u32[]{:S(2)}) copy-start(bf16[1024,3072]{1,0:T(8,128)(2,1)} %get-tuple-element.170) | copy-start | bytes 18874372
  328.6 44.2 %copy-start.35 = (bf16[512,768]{0,1:T(8,128)(2,1)}, bf16[512,768]{0,1:T(8,128)(2,1)S(1)}, u32[]{:S(2)}) copy-start(bf16[512,768]{0,1:T(8,128)(2,1)S(1)} %get-tuple-element.187) | copy-start | bytes 2359300
  338.7 8.6 %copy-start.43 = (bf16[2,16,24,1]{3,2,1,0:T(8,128)(2,1)S(1)}, bf16[2,16,24,1]{3,2,1,0:T(8,128)(2,1)}, u32[]{:S(2)}) copy-start(bf16[2,16,24,1]{3,2,1,0:T(8,128)(2,1)} %concatenate.82) | copy-start | bytes 4612
  338.7 8.6 %copy-start.44 = (bf16[2,16,24,4]{3,2,1,0:T(8,128)(2,1)S(1)}, bf16[2,16,24,4]{3,2,1,0:T(8,128)(2,1)}, u32[]{:S(2)}) copy-start(bf16[2,16,24,4]{3,2,1,0:T(8,128)(2,1)} %concatenate.74) | copy-start | bytes 18436
  338.7 8.6 %copy-start.45 = (bf16[2,16,24,4]{3,2,1,0:T(8,128)(2,1)S(1)}, bf16[2,16,24,4]{3,2,1,0:T(8,128)(2,1)}, u32[]{:S(2)}) copy-start(bf16[2,16,24,4]{3,2,1,0:T(8,128)(2,1)} %concatenate.76) | copy-start | bytes 18436
  338.7 8.6 %copy-start.46 = (bf16[2,16,24,4]{3,2,1,0:T(8,128)(2,1)S(1)}, bf16[2,16,24,4]{3,2,1,0:T(8,128)(2,1)}, u32[]{:S(2)}) copy-start(bf16[2,16,24,4]{3,2,1,0:T(8,128)(2,1)} %concatenate.75) | copy-start | bytes 18436
  338.7 8.6 %copy-start.47 = (bf16[2,16,24,1]{3,2,1,0:T(8,128)(2,1)S(1)}, bf16[2,16,24,1]{3,2,1,0:T(8,128)(2,1)}, u32[]{:S(2)}) copy-start(bf16[2,16,24,1]{3,2,1,0:T(8,128)(2,1)} %concatenate.81) | copy-start | bytes 4612
  372.7 281.9 %reduce-scatter.9.cloned.1.call-start = ((), (), s32[]{:S(2)}) async-start(), calls=%async_computation.6 | async-start | bytes 5068800
  374.2 21.0 %copy-start.21 = (pred[512,1024]{1,0:T(8,128)(4,1)S(1)}, pred[512,1024]{1,0:T(8,128)(4,1)}, u32[]{:S(2)}) copy-start(pred[512,1024]{1,0:T(8,128)(4,1)} %get-tuple-element.190) | copy-start | bytes 1572868
  374.2 21.0 %copy-start.51 = (f32[12,512]{1,0:T(8,128)S(1)}, f32[12,512]{1,0:T(8,128)}, u32[]{:S(2)}) copy-start(f32[12,512]{1,0:T(8,128)} %log_add_fusion) | copy-start | bytes 73732
  374.2 21.0 %copy-start.68 = (f32[512]{0:T(512)S(1)}, f32[512]{0:T(512)}, u32[]{:S(2)}) copy-start(f32[512]{0:T(512)} %copy-done.67) | copy-start | bytes 6148
  459.3 10.6 %copy-start.1 = (bf16[12,512,1024]{2,1,0:T(8,128)(2,1)S(1)}, bf16[12,512,1024]{2,1,0:T(8,128)(2,1)}, u32[]{:S(2)}) copy-start(bf16[12,512,1024]{2,1,0:T(8,128)(2,1)} %get-tuple-element.213) | copy-start | bytes 37748740
  485.2 14.1 %copy-start.19 = (pred[512,1024]{1,0:T(8,128)(4,1)S(1)}, pred[512,1024]{1,0:T(8,128)(4,1)}, u32[]{:S(2)}) copy-start(pred[512,1024]{1,0:T(8,128)(4,1)} %get-tuple-element.189) | copy-start | bytes 1572868
  485.2 14.1 %copy-start.36 = (bf16[512,768]{0,1:T(8,128)(2,1)S(1)}, bf16[512,768]{0,1:T(8,128)(2,1)}, u32[]{:S(2)}) copy-start(bf16[512,768]{0,1:T(8,128)(2,1)} %copy-done.35) | copy-start | bytes 2359300
  485.3 14.1 %copy-start.50 = (f32[12,512]{1,0:T(8,128)S(1)}, f32[12,512]{1,0:T(8,128)}, u32[]{:S(2)}) copy-start(f32[12,512]{1,0:T(8,128)} %log_add_fusion.1) | copy-start | bytes 73732
  499.3 13.7 %copy-start.29 = (bf16[1024,12,64]{0,2,1:T(8,128)(2,1)S(1)}, bf16[1024,12,64]{0,2,1:T(8,128)(2,1)}, u32[]{:S(2)}) copy-start(bf16[1024,12,64]{0,2,1:T(8,128)(2,1)} %pad_maximum_fusion.2) | copy-start | bytes 4718596
  499.3 13.7 %copy-start.38 = (bf16[768,2432]{1,0:T(8,128)(2,1)S(1)}, bf16[768,2432]{1,0:T(8,128)(2,1)}, u32[]{:S(2)}) copy-start(bf16[768,2432]{1,0:T(8,128)(2,1)} %all-gather.4.cloned.1.call-done) | copy-start | bytes 11206660
  555.1 99.5 %copy-start.48 = (bf16[24,6272]{1,0:T(8,128)(2,1)S(1)}, bf16[24,6272]{1,0:T(8,128)(2,1)}, u32[]{:S(2)}) copy-start(bf16[24,6272]{1,0:T(8,128)(2,1)} %reduce-scatter.7.cloned.1.call-done) | copy-start | bytes 903172
  555.1 101.2 %copy-start.77 = (f32[768]{0:T(1024)S(1)}, f32[768]{0:T(1024)}, u32[]{:S(2)}) copy-start(f32[768]{0:T(1024)} %get-tuple-element.153) | copy-start | bytes 9220
  555.1 168.4 %all-gather.8.cloned.1.call-start = ((), (), s32[]{:S(2)}) async-start(), calls=%async_computation.4 | async-start | bytes 7729152 | tf_op jit(solution)/shard_map/all_gather | solution.py:376
  656.4 11.0 %copy-start.75 = (f32[1024]{0:T(1024)S(1)}, f32[1024]{0:T(1024)}, u32[]{:S(2)}) copy-start(f32[1024]{0:T(1024)} %get-tuple-element.152) | copy-start | bytes 12292
  734.4 19.1 %slice-start.3 = ((s8[7274496]{0:T(1024)(128)(4,1)}), s8[3080192]{0:T(1024)(128)(4,1)S(1)}, s32[]{:S(2)}) async-start(s8[7274496]{0:T(1024)(128)(4,1)} %bitcast.86), calls=%async_computation.10 | async-start | bytes 6160384
  740.7 12.9 %slice-start.4 = ((s8[7274496]{0:T(1024)(128)(4,1)}), s8[4194304]{0:T(1024)(128)(4,1)S(1)}, s32[]{:S(2)}) async-start(s8[7274496]{0:T(1024)(128)(4,1)} %bitcast.86), calls=%async_computation.11 | async-start | bytes 8388608
  (47 other events, 160.3 us)
Sparse Core Ops, SparseCore 0:
  18.9 63.4 all-gather.3
  85.9 85.3 all-gather.5
  372.9 129.5 reduce-scatter.6
  555.3 99.3 reduce-scatter.8
  657.2 66.3 all-gather.7

commit v2 on v1

--- a/solution.py
+++ b/solution.py
@@ -13,6 +13,7 @@
 
 
 EPSILON = 1e-05
+
 
 MASKED = -1000000000.0
 
@@ -177,6 +178,44 @@
     )
 
 
+def hypercube_orders(group_size, shard_size):
+    gbits = [("group", b) for b in range(group_size.bit_length() - 1)]
+    sbits = [("shard", b) for b in range(shard_size.bit_length() - 1)]
+    first = gbits[:-1] + sbits + gbits[-1:]
+    second = list(first)
+    if len(gbits) >= 3:
+        second[1], second[2] = first[2], first[1]
+    return first, second
+
+
+def hypercube_reduce_scatter(x, order, group_size, shard_size):
+    total = group_size * shard_size
+    levels = total.bit_length() - 1
+    rows, cols = x.shape
+    n = rows // total
+    sbits = shard_size.bit_length() - 1
+
+    def k_bit(axis, b):
+        return b if axis == "shard" else sbits + b
+
+    axes = [levels - 1 - k_bit(axis, b) for axis, b in order]
+    cur = (
+        x.reshape([2] * levels + [n, cols])
+        .transpose(axes + [levels, levels + 1])
+        .reshape(rows, cols)
+    )
+    for axis, b in order:
+        size = group_size if axis == "group" else shard_size
+        half = cur.shape[0] // 2
+        mine = (lax.axis_index(axis) >> b) & 1
+        low, high = cur[:half], cur[half:]
+        keep = jnp.where(mine == 1, high, low)
+        send = jnp.where(mine == 1, low, high).astype(jnp.bfloat16)
+        got = lax.ppermute(send, axis, [(j, j ^ (1 << b)) for j in range(size)])
+        cur = keep + got.astype(jnp.float32)
+    return cur
+
+
 def per_device(
     tokens,
     doc_lengths,
@@ -241,13 +280,11 @@
         gain_four,
         shift_four,
     ) = unpack_columns(first_full[:, qkv_width:], small_widths)
-    second_pack = jnp.concatenate(
-        [proj_weight, expand_weight, shrink_weight.reshape(n, ratio * model_width)], axis=1
-    )
+    second_pack = jnp.concatenate([proj_weight, expand_weight], axis=1)
     second_full = lax.all_gather(second_pack, ("group", "shard"), axis=0, tiled=True)
     proj_full = second_full[:, :model_width]
-    expand_full = second_full[:, model_width : model_width + wide_width]
-    shrink_full = second_full[:, model_width + wide_width :].reshape(wide_width, model_width)
+    expand_full = second_full[:, model_width:]
+    shrink_full = lax.all_gather(shrink_weight, ("group", "shard"), axis=0, tiled=True)
 
     row_count = doc_lengths.shape[0]
     length = tokens.shape[0] // row_count
@@ -314,6 +351,21 @@
         unit_three, inv_three, gain_three.astype(jnp.float32), grad_second
     )
     grad_middle = grad_out + grad_mid_part
+    order_a, order_b = hypercube_orders(group_size, shard_size)
+    shrink_in = (
+        shrink_weight_grad.reshape(shard_size, group_size, -1, model_width)
+        .transpose(1, 0, 2, 3)
+        .reshape(wide_width, model_width)
+    )
+    grad_branch = grad_middle.astype(jnp.bfloat16)
+    proj_bias_grad = jnp.sum(grad_branch.astype(jnp.float32), axis=0)
+    proj_weight_grad = jnp.einsum(
+        "td,te->de", inner_low, grad_branch, preferred_element_type=jnp.float32
+    )
+    grad_inner = jnp.einsum("te,de->td", grad_branch, proj_full, preferred_element_type=jnp.float32)
+    grad_attended, inner_gain_grad, inner_shift_grad = norm_back(
+        unit_two, inv_two, gain_inner.astype(jnp.float32), grad_inner
+    )
     ffn_small = (
         second_gain_grad,
         second_shift_grad,
@@ -321,28 +373,25 @@
         expand_bias_grad,
         hidden_gain_grad,
         hidden_shift_grad,
+        inner_gain_grad,
+        inner_shift_grad,
+        proj_bias_grad,
     )
     ffn_small_widths = [p.shape[0] // model_width for p in ffn_small]
     ffn_pack = jnp.concatenate(
         [
             expand_weight_grad,
-            shrink_weight_grad.reshape(model_width, ratio * model_width),
+            proj_weight_grad,
             pack_columns(ffn_small, model_width),
         ],
         axis=1,
     ).astype(jnp.bfloat16)
+    grad_att_low = grad_attended.astype(jnp.bfloat16).reshape(row_count, length, model_width)
+    ffn_pack, shrink_in, grad_att_low = lax.optimization_barrier(
+        (ffn_pack, shrink_in, grad_att_low)
+    )
     ffn_part = grad_rows_reduce(ffn_pack, group_size, shard_size)
-
-    grad_branch = grad_middle.astype(jnp.bfloat16)
-    proj_bias_grad = jnp.sum(grad_branch.astype(jnp.float32), axis=0)
-    proj_weight_grad = jnp.einsum(
-        "td,te->de", inner_low, grad_branch, preferred_element_type=jnp.float32
-    )
-    grad_inner = jnp.einsum("te,de->td", grad_branch, proj_full, preferred_element_type=jnp.float32)
-    grad_attended, inner_gain_grad, inner_shift_grad = norm_back(
-        unit_two, inv_two, gain_inner.astype(jnp.float32), grad_inner
-    )
-    grad_att_low = grad_attended.astype(jnp.bfloat16).reshape(row_count, length, model_width)
+    shrink_part = hypercube_reduce_scatter(shrink_in, order_a, group_size, shard_size)
     grad_qkv = (
         lax.map(row_backward, (qkv_rows, segments, log_totals, grad_att_low))
         .reshape(-1, 3 * model_width)
@@ -364,24 +413,47 @@
         first_shift_grad,
         query_bias_grad,
         value_bias_grad,
-        inner_gain_grad,
-        inner_shift_grad,
-        proj_bias_grad,
     )
     attn_pack = jnp.concatenate(
-        [qkv_weight_grad, proj_weight_grad, pack_columns(attn_small, model_width)], axis=1
-    ).astype(jnp.bfloat16)
-    ffn_part, attn_pack = lax.optimization_barrier((ffn_part, attn_pack))
-    attn_part = grad_rows_reduce(attn_pack, group_size, shard_size)
+        [qkv_weight_grad, pack_columns(attn_small, model_width)], axis=1
+    )
+    attn_pack = (
+        attn_pack.reshape(shard_size, group_size, n, -1)
+        .transpose(1, 0, 2, 3)
+        .reshape(model_width, -1)
+    )
+    ffn_part, shrink_part, attn_pack = lax.optimization_barrier(
+        (ffn_part, shrink_part, attn_pack)
+    )
+    split = (attn_pack.shape[1] // 256) * 128
+    attn_left = hypercube_reduce_scatter(
+        attn_pack[:, :split], order_a, group_size, shard_size
+    )
+    attn_right = hypercube_reduce_scatter(
+        attn_pack[:, split:], order_b, group_size, shard_size
+    )
     both = lax.all_gather(
-        jnp.concatenate([ffn_part, attn_part], axis=1), "group", axis=0, tiled=True
+        jnp.concatenate(
+            [
+                ffn_part,
+                shrink_part.astype(jnp.bfloat16).reshape(n, ratio * model_width),
+                attn_left.astype(jnp.bfloat16),
+                attn_right.astype(jnp.bfloat16),
+            ],
+            axis=1,
+        ),
+        "group",
+        axis=0,
+        tiled=True,
     ).astype(jnp.float32)
     ffn_cols = ffn_pack.shape[1]
     ffn_back = both[:, :ffn_cols]
-    attn_back = both[:, ffn_cols:]
+    shrink_back = both[:, ffn_cols : ffn_cols + ratio * model_width]
+    attn_back = both[:, ffn_cols + ratio * model_width :]
     half = both.shape[0]
     expand_out = ffn_back[:, :wide_width]
-    shrink_out = ffn_back[:, wide_width : 2 * wide_width].reshape(half * ratio, model_width)
+    proj_out = ffn_back[:, wide_width : wide_width + model_width]
+    shrink_out = shrink_back.reshape(half * ratio, model_width)
     (
         second_gain_out,
         second_shift_out,
@@ -389,18 +461,17 @@
         ebias_out,
         gain_four_out,
         shift_four_out,
-    ) = unpack_columns(ffn_back[:, 2 * wide_width :], ffn_small_widths)
+        gain_inner_out,
+        shift_inner_out,
+        pbias_out,
+    ) = unpack_columns(ffn_back[:, wide_width + model_width :], ffn_small_widths)
     qkv_out = attn_back[:, :qkv_width]
-    proj_out = attn_back[:, qkv_width : qkv_width + model_width]
     (
         gain_one_out,
         shift_one_out,
         qbias_out,
         vbias_out,
-        gain_inner_out,
-        shift_inner_out,
-        pbias_out,
-    ) = unpack_columns(attn_back[:, qkv_width + model_width :], [1] * 7)
+    ) = unpack_columns(attn_back[:, qkv_width:], [1] * 4)
     return (
         block_output,
         input_grad,

time: 775 us -> 768 us (level)
  waiting for transfers between devices: 202 us -> 157 us
  other arithmetic: 137 us -> 157 us
  starting transfers between devices: 0.21 us -> 12.3 us
    unnamed x6 -> x5, waiting for transfers between devices: 99.5 us -> 0.75 us
    ppermute x0 -> x15, waiting for transfers between devices: none -> 56 us  [hypercube_reduce_scatter(): got = lax.ppermute(send, axis, [(j, j ^ 1 << b) for j in range(size)])]
    concatenate x9 -> x11, local copies, waits for them, and re-layouts: 41 us -> 28.7 us  [the longest x10 18.3 us: per_device(): jnp.concatenate([qkv_weight_grad, pack_columns(attn_small, model_width)],...]
    ppermute x0 -> x15, starting transfers between devices: none -> 12.1 us  [hypercube_reduce_scatter(): got = lax.ppermute(send, axis, [(j, j ^ 1 << b) for j in range(size)])]
    add x0 -> x13, other arithmetic: none -> 8.75 us  [hypercube_reduce_scatter(): cur = keep + got.astype(jnp.float32)]
    convert_element_type x2 -> x18, other arithmetic: 10.1 us -> 17.4 us  [the longest x1 9.31 us: per_device(): both = lax.all_gather(jnp.concatenate([ffn_part, shrink_part.astype(jnp.b...]
    unnamed x184 -> x158, local copies, waits for them, and re-layouts: 16.8 us -> 22.6 us
    reshape x20 -> x22, local copies, waits for them, and re-layouts: 14.4 us -> 18.2 us  [pack_columns(): cols = [p.reshape(rows, -1) for p in parts]]
  transfers between devices with their start and end apart: 5 -> 20, of which waited for: 3 -> 14; matrix products, arithmetic and copies ran while one was open for 40% -> 37% of each run, Pallas kernels for 0% -> 0%
where the time goes in v2:
time: 768 us; the launch traced here: 757 us
  matrix products  264 us (34%)
  waiting for transfers between devices  157 us (20%)
  other arithmetic  157 us (20%)
  local copies, waits for them, and re-layouts  151 us (20%)
  between operations  15.2 us (2%)
  starting transfers between devices  12.3 us (2%)
    ppermute x15, waiting for transfers between devices, hypercube_reduce_scatter(): got = lax.ppermute(send, axis, [(j, j ^ 1 << b) for j in range(size)])  56 us
    all_gather x1, waiting for transfers between devices, per_device(): lax.all_gather(first_pack, ('group', 'shard'), axis=0, tiled=True)  51.9 us
    all_gather x1, waiting for transfers between devices, per_device(): lax.all_gather(jnp.concatenate([ffn_part, shrink_part.astype(jnp.bfloat16...  48.3 us
    convert_element_type x1, other arithmetic, row_backward(): grad_scores = (probs * (grad_probs - inner_sum)).astype(jnp.bfloat16)  42.2 us
    dot_general x1, matrix products, per_device(): jnp.dot(second_low, expand_full, preferred_element_type=jnp.float32)  39.3 us
    dot_general x2, matrix products, row_backward(): jnp.einsum('qhd,khd->hqk', grad_block, value_heads, preferred_element_typ...  37.2 us
    dot_general x2, matrix products, row_backward(): jnp.einsum('hqk,qhd->khd', probs.astype(jnp.bfloat16), grad_block, prefer...  28.7 us
    reduce_sum x2, other arithmetic, row_forward(): total = jnp.sum(expd, axis=-1, keepdims=True)  25.3 us
  transfers between devices with their start and end apart: 20, of which 14 were waited for; matrix products, arithmetic and copies ran while one was open for 37% of the time, Pallas kernels for 0%

profile of v2, /device:TPU:0, one launch (start us, length us, event | category | flops | bytes accessed | tf_op | source)
XLA Modules:
  0.0 756.7 jit_solution(7884175611358899023)
XLA Ops:
  30.5 51.9 %all-gather.5.cloned.1.call-done = bf16[768,2432]{1,0:T(8,128)(2,1)} async-done(((bf16[24,2432]{1,0:T(8,128)(2,1)}), bf16[768,2432]{1,0:T(8,128)(2,1)}) %all-gather.5.cloned.1.call-update) | async-done | bytes 3735568 | tf_op jit(solution)/shard_map/all_gather | solution.py:266
  87.3 6.4 add_convert_fusion.2
  109.6 12.2 %fusion.3 = (f32[12,512]{1,0:T(8,128)S(1)}, f32[12,512,1024]{2,1,0:T(8,128)}) fusion(pred[512,1024]{1,0:T(8,128)(4,1)} %get-tuple-element.218, bf16[512,12,64]{0,2,1:T(8,128)(2,1)} %bitcast.122, bf16[1024,12,64]{0,2,1:T(8,128)(2,1)S(1)} %bitcast.103), kind=kOutput, calls=%fused_computation.16 | convolution fusion | flops 824174592 | bytes 28073984 | tf_op jit(solution)/shard_map/while/body/eval_jaxpr/qhd,khd->hqk/dot_general | solution.py:60
  121.7 12.9 %fusion.1 = f32[12,512]{1,0:T(8,128)S(1)} fusion(f32[12,512,1024]{2,1,0:T(8,128)} %get-tuple-element.224, f32[12,512]{1,0:T(8,128)S(1)} %get-tuple-element.223, pred[512,1024]{1,0:T(8,128)(4,1)} %get-tuple-element.218), kind=kLoop, calls=%fused_computation.13 | loop fusion | flops 25159680 | bytes 25739264 | tf_op jit(solution)/shard_map/while/body/eval_jaxpr/reduce_sum | solution.py:89
  138.5 11.1 %fusion.15 = f32[12,64,512]{2,1,0:T(8,128)} fusion(bf16[1024,12,64]{0,2,1:T(8,128)(2,1)S(1)} %bitcast.115, f32[12,512,1024]{2,1,0:T(8,128)S(1)} %copy-done.1, f32[512]{0:T(512)S(1)} %get-tuple-element.222, f32[12,512]{1,0:T(8,128)S(1)} %fusion.1, f32[12,512]{1,0:T(8,128)S(1)} %get-tuple-element.223, pred[512,1024]{1,0:T(8,128)(4,1)} %get-tuple-element.218), kind=kOutput, calls=%fused_computation.41 | convolution fusion | flops 843055104 | bytes 28887040 | tf_op jit(solution)/shard_map/while/body/eval_jaxpr/hqk,khd->qhd/dot_general | solution.py:92
  152.8 12.3 %fusion.2 = (f32[12,512]{1,0:T(8,128)S(1)}, f32[12,512,1024]{2,1,0:T(8,128)}) fusion(pred[512,1024]{1,0:T(8,128)(4,1)} %get-tuple-element.217, bf16[512,12,64]{0,2,1:T(8,128)(2,1)} %bitcast.125, bf16[1024,12,64]{0,2,1:T(8,128)(2,1)S(1)} %bitcast.104), kind=kOutput, calls=%fused_computation.15 | convolution fusion | flops 824174592 | bytes 28073984 | tf_op jit(solution)/shard_map/while/body/eval_jaxpr/qhd,khd->hqk/dot_general | solution.py:60
  165.0 12.3 %fusion = f32[12,512]{1,0:T(8,128)S(1)} fusion(f32[12,512,1024]{2,1,0:T(8,128)} %get-tuple-element.226, f32[12,512]{1,0:T(8,128)S(1)} %get-tuple-element.225, pred[512,1024]{1,0:T(8,128)(4,1)} %get-tuple-element.217), kind=kLoop, calls=%fused_computation.12 | loop fusion | flops 25159680 | bytes 25739264 | tf_op jit(solution)/shard_map/while/body/eval_jaxpr/reduce_sum | solution.py:89
  181.1 10.8 %fusion.14 = f32[12,64,512]{2,1,0:T(8,128)} fusion(bf16[1024,12,64]{0,2,1:T(8,128)(2,1)S(1)} %bitcast.116, f32[12,512,1024]{2,1,0:T(8,128)S(1)} %copy-done, f32[512]{0:T(512)S(1)} %get-tuple-element.221, f32[12,512]{1,0:T(8,128)S(1)} %fusion, f32[12,512]{1,0:T(8,128)S(1)} %get-tuple-element.225, pred[512,1024]{1,0:T(8,128)(4,1)} %get-tuple-element.217), kind=kOutput, calls=%fused_computation.40 | convolution fusion | flops 843055104 | bytes 28887040 | tf_op jit(solution)/shard_map/while/body/eval_jaxpr/hqk,khd->qhd/dot_general | solution.py:92
  198.9 3.7 fusion.72
  203.1 39.3 %fusion.64 = (f32[1024]{0:T(1024)S(1)}, f32[1024,3072]{1,0:T(8,128)S(1)}, f32[1024,3072]{1,0:T(8,128)}, f32[1024,3072]{1,0:T(8,128)}) fusion(f32[3072]{0:T(1024)S(1)} %reshape.732, bf16[768,3840]{1,0:T(8,128)(2,1)} %all-gather.7.cloned.1.call-done, f32[1024,768]{0,1:T(8,128)S(1)} %get-tuple-element.228, f32[768]{0:T(1024)S(1)} %copy-done.66, ...), kind=kOutput, calls=%fused_computation.204 | convolution fusion | flops 5043387392 | bytes 45643776 | tf_op jit(solution)/shard_map/dot_general | solution.py:319
  247.2 16.0 %multiply_reduce_fusion.2 = (bf16[3072]{0:T(1024)(128)(2,1)}, f32[1024]{0:T(1024)S(1)}, f32[1024]{0:T(1024)S(1)}, bf16[3072]{0:T(1024)(128)(2,1)}, bf16[1024,3072]{1,0:T(8,128)(2,1)}, /*index=5*/f32[1024,3072]{1,0:T(8,128)}) fusion(f32[1024,3072]{1,0:T(8,128)} %copy-done.3, f32[1024]{0:T(1024)S(1)} %add_rsqrt_fusion, ...), kind=kOutput, calls=%fused_computation.22 | convolution fusion | flops 4869578752 | bytes 37801984 | tf_op jit(solution)/shard_map/td,fd->tf/dot_general | solution.py:338
  263.2 20.5 %fusion.63 = (bf16[3072]{0:T(1024)(128)(2,1)S(1)}, bf16[1024,3072]{1,0:T(8,128)(2,1)}) fusion(f32[1024,3072]{1,0:T(8,128)} %get-tuple-element.201, f32[1024]{0:T(1024)S(1)} %broadcast_multiply_fusion, f32[1024,3072]{1,0:T(8,128)} %copy-done.3, f32[1024]{0:T(1024)S(1)} %broadcast_multiply_fusion.2, f32[1024]{0:T(1024)S(1)} %broadcast_multiply_fusion.1, ...), kind=kLoop, calls=%fused_computation.203 | loop fusion | flops 72348672 | bytes 56670208 | tf_op jit(solution)/shard_map/reduce_sum | solution.py:345
  287.1 9.9 %convolution_convert_fusion = bf16[768,3072]{1,0:T(8,128)(2,1)} fusion(bf16[1024,3072]{1,0:T(8,128)(2,1)} %get-tuple-element.198, f32[1024,768]{0,1:T(8,128)S(1)} %copy-done.9, f32[768]{0:T(1024)S(1)} %copy-done.66, f32[768]{0:T(1024)S(1)} %copy-done.49, f32[1024]{0:T(1024)S(1)} %add_rsqrt_fusion.1, f32[1024]{0:T(1024)S(1)} %broadcast_multiply_fusion.9), kind=kOutput, calls=%fused_computation.46 | convolution fusion | flops 4838129664 | bytes 14170112 | tf_op jit(solution)/shard_map/td,tf->df/dot_general | solution.py:346
  297.0 9.1 %fusion.73 = (bf16[768]{0:T(1024)(128)(2,1)S(1)}, f32[1024,768]{1,0:T(8,128)}) fusion(bf16[1024,3072]{1,0:T(8,128)(2,1)S(1)} %copy-done.29, bf16[768,3840]{1,0:T(8,128)(2,1)} %all-gather.7.cloned.1.call-done), kind=kOutput, calls=%fused_computation.212 | convolution fusion | flops 4832623616 | bytes 14157312 | tf_op jit(solution)/shard_map/tf,df->td/dot_general | solution.py:349
  307.0 3.7 copy.232
  318.0 4.1 multiply_reduce_fusion.6
  325.5 5.7 fusion.75
  331.2 4.6 copy.241
  337.9 10.3 %concatenate.60 = bf16[768,3968]{1,0:T(8,128)(2,1)} concatenate(bf16[768,3072]{1,0:T(8,128)(2,1)} %convolution_convert_fusion, bf16[768,768]{1,0:T(8,128)(2,1)S(1)} %convolution_convert_fusion.1, bf16[768,1]{1,0:T(8,128)(2,1)} %reshape.736, bf16[768,1]{1,0:T(8,128)(2,1)} %reshape.737, bf16[768,1]{1,0:T(8,128)(2,1)S(1)} %copy-done.37, bf16[768,4]{1,0:T(8,128)(2,1)S(1)} %reshape.692, ...), dimensions={1} | concatenate | bytes 12189696 | tf_op jit(solution)/shard_map/concatenate | solution.py:381
  351.6 13.9 %fusion.5 = f32[12,64,1024]{2,1,0:T(8,128)} fusion(bf16[512,12,64]{0,2,1:T(8,128)(2,1)} %bitcast.133, f32[12,512,1024]{2,1,0:T(8,128)} %get-tuple-element.224, f32[12,512]{1,0:T(8,128)S(1)} %copy-done.40, f32[512]{0:T(512)S(1)} %copy-done.55, pred[512,1024]{1,0:T(8,128)(4,1)S(1)} %copy-done.21), kind=kOutput, calls=%fused_computation.18 | convolution fusion | flops 836763648 | bytes 29648896 | tf_op jit(solution)/shard_map/while/body/eval_jaxpr/hqk,qhd->khd/dot_general | solution.py:133
  365.5 18.4 %multiply_reduce_fusion = (f32[12,512]{1,0:T(8,128)S(1)}, f32[12,512,1024]{2,1,0:T(8,128)}) fusion(f32[512]{0:T(512)S(1)} %copy-done.55, f32[12,512]{1,0:T(8,128)S(1)} %copy-done.40, f32[12,512,1024]{2,1,0:T(8,128)} %get-tuple-element.224, pred[512,1024]{1,0:T(8,128)(4,1)S(1)} %copy-done.21, bf16[512,12,64]{0,2,1:T(8,128)(2,1)} %bitcast.134, ...), kind=kOutput, calls=%fused_computation.1 | convolution fusion | flops 843048960 | bytes 53266432 | tf_op jit(solution)/shard_map/while/body/eval_jaxpr/qhd,khd->hqk/dot_general | solution.py:117
  385.1 18.8 %multiply_reduce_fusion.1 = (f32[12,512]{1,0:T(8,128)S(1)}, f32[12,512,1024]{2,1,0:T(8,128)}) fusion(f32[512]{0:T(512)S(1)} %copy-done.53, f32[12,512]{1,0:T(8,128)S(1)} %copy-done.39, f32[12,512,1024]{2,1,0:T(8,128)} %get-tuple-element.226, pred[512,1024]{1,0:T(8,128)(4,1)S(1)} %copy-done.19, bf16[512,12,64]{0,2,1:T(8,128)(2,1)} %bitcast.131, ...), kind=kOutput, calls=%fused_computation.4 | convolution fusion | flops 843048960 | bytes 53266432 | tf_op jit(solution)/shard_map/while/body/eval_jaxpr/qhd,khd->hqk/dot_general | solution.py:117
  403.8 42.2 %multiply_convert_fusion = (bf16[12,512,1024]{2,1,0:T(8,128)(2,1)}, bf16[12,512,1024]{2,1,0:T(8,128)(2,1)}) fusion(f32[12,512,1024]{2,1,0:T(8,128)} %get-tuple-element.237, f32[12,512]{1,0:T(8,128)S(1)} %get-tuple-element.236, f32[512]{0:T(512)S(1)} %copy-done.55, f32[12,512]{1,0:T(8,128)S(1)} %copy-done.40, f32[12,512,1024]{2,1,0:T(8,128)} %get-tuple-element.224, ...), kind=kLoop, calls=%fused_computation | loop fusion | flops 88080384 | bytes 126980096 | tf_op jit(solution)/shard_map/while/body/eval_jaxpr/convert_element_type | solution.py:121
  446.1 10.1 %fusion.46 = bf16[512,12,64]{0,2,1:T(8,128)(2,1)} fusion(bf16[1024,12,64]{0,2,1:T(8,128)(2,1)} %bitcast.105, bf16[12,512,1024]{2,1,0:T(8,128)(2,1)} %get-tuple-element.241), kind=kOutput, calls=%fused_computation.117 | convolution fusion | flops 806092800 | bytes 14942208 | tf_op jit(solution)/shard_map/while/body/eval_jaxpr/hqk,khd->qhd/dot_general | solution.py:123
  456.2 5.1 fusion.76
  461.2 5.6 copy.245
  467.0 4.3 select_convert_fusion
  472.9 11.0 %fusion.47 = bf16[512,12,64]{0,2,1:T(8,128)(2,1)} fusion(bf16[1024,12,64]{0,2,1:T(8,128)(2,1)} %bitcast.106, bf16[12,512,1024]{2,1,0:T(8,128)(2,1)} %get-tuple-element.240), kind=kOutput, calls=%fused_computation.118 | convolution fusion | flops 806092800 | bytes 14942208 | tf_op jit(solution)/shard_map/while/body/eval_jaxpr/hqk,khd->qhd/dot_general | solution.py:123
  483.9 5.7 multiply_convert_fusion.6
  489.6 4.8 slice_select_fusion
  497.4 14.8 %add_convert_fusion.3 = bf16[12,64,1024]{2,1,0:T(8,128)(2,1)} fusion(f32[12,64,1024]{2,1,0:T(8,128)S(1)} %copy-done.69, bf16[512,12,64]{0,2,1:T(8,128)(2,1)S(1)} %bitcast.132, f32[12,512,1024]{2,1,0:T(8,128)} %get-tuple-element.226, f32[12,512]{1,0:T(8,128)S(1)} %copy-done.39, f32[512]{0:T(512)S(1)} %copy-done.53, pred[512,1024]{1,0:T(8,128)(4,1)S(1)} %copy-done.20), kind=kOutput, calls=%fused_computation.77 | convolution fusion | flops 838336512 | bytes 31221760 | tf_op jit(solution)/shard_map/while/body/eval_jaxpr/hqk,qhd->khd/dot_general | solution.py:133
  519.6 5.5 fusion.74
  529.9 8.8 %fusion.59 = f32[768,2304]{1,0:T(8,128)} fusion(bf16[1024,768]{0,1:T(8,128)(2,1)S(1)} %copy-done.5, f32[768]{0:T(1024)S(1)} %copy-done.63, f32[768]{0:T(1024)S(1)} %copy-done.48, f32[1024]{0:T(1024)S(1)} %copy-done.51, f32[1024]{0:T(1024)S(1)} %copy-done.43, bf16[1024,768]{0,1:T(8,128)(2,1)} %bitcast.135, bf16[1024,768]{0,1:T(8,128)(2,1)S(1)} %bitcast.120, ...), kind=kOutput, calls=%fused_computation.201 | convolution fusion | flops 3642753024 | bytes 13383680 | tf_op jit(solution)/shard_map/td,te->de/dot_general | solution.py:403
  538.7 13.3 %collective-permute-done.1 = bf16[768,768]{1,0:T(8,128)(2,1)} collective-permute-done((bf16[768,768]{1,0:T(8,128)(2,1)}, bf16[768,768]{1,0:T(8,128)(2,1)}, u32[]{:S(2)}, u32[]{:S(2)}) %collective-permute-start.1) | collective-permute-done | bytes 1179680 | tf_op jit(solution)/shard_map/ppermute | solution.py:214
  555.5 4.8 fusion.62
  560.3 12.0 %collective-permute-done.2 = bf16[384,768]{1,0:T(8,128)(2,1)S(1)} collective-permute-done((bf16[384,768]{1,0:T(8,128)(2,1)S(1)}, bf16[384,768]{1,0:T(8,128)(2,1)S(1)}, u32[]{:S(2)}, u32[]{:S(2)}) %collective-permute-start.2) | collective-permute-done | bytes 589856 | tf_op jit(solution)/shard_map/ppermute | solution.py:214
  576.3 6.8 copy.249
  590.5 8.7 %concatenate.68 = f32[2,16,24,2432]{3,2,0,1:T(8,128)} concatenate(f32[2,16,24,2304]{3,2,0,1:T(8,128)} %copy.249, f32[2,16,24,1]{3,2,0,1:T(8,128)} %copy.250, f32[2,16,24,1]{3,2,0,1:T(8,128)} %copy.251, f32[2,16,24,1]{3,2,0,1:T(8,128)S(1)} %copy.252, f32[2,16,24,1]{3,2,0,1:T(8,128)S(1)} %copy.253, f32[2,16,24,124]{3,2,0,1:T(8,128)S(1)} %broadcast_in_dim.168), dimensions={3} | concatenate | bytes 14942208 | tf_op jit(solution)/shard_map/concatenate | solution.py:417
  602.2 4.3 slice.390
  615.3 10.0 %collective-permute-done.6 = bf16[192,1152]{1,0:T(8,128)(2,1)S(1)} collective-permute-done((bf16[192,1152]{1,0:T(8,128)(2,1)S(1)}, bf16[192,1152]{1,0:T(8,128)(2,1)S(1)}, u32[]{:S(2)}, u32[]{:S(2)}) %collective-permute-start.6) | collective-permute-done | bytes 442400 | tf_op jit(solution)/shard_map/ppermute | solution.py:214
  628.8 4.0 collective-permute-done.7
  652.0 9.1 %add_convert_fusion.4 = bf16[1024,768]{0,1:T(8,128)(2,1)S(1)} fusion(f32[1024,768]{0,1:T(8,128)} %copy-done.8, bf16[1024,3072]{1,0:T(8,128)(2,1)} %get-tuple-element.202, bf16[3072,768]{1,0:T(8,128)(2,1)} %all-gather.9.cloned.1.call-done, f32[768]{0:T(1024)S(1)} %copy-done.61), kind=kOutput, calls=%fused_computation.85 | convolution fusion | flops 4834197504 | bytes 15731712 | tf_op jit(solution)/shard_map/dot_general | solution.py:329
  662.7 3.9 fusion.32
  668.3 48.3 %all-gather.11.cloned.1.call-done = bf16[384,9472]{1,0:T(8,128)(2,1)} async-done(((bf16[24,9472]{1,0:T(8,128)(2,1)}), bf16[384,9472]{1,0:T(8,128)(2,1)}) %all-gather.11.cloned.1.call-update) | async-done | bytes 7274512 | tf_op jit(solution)/shard_map/all_gather | solution.py:435
  720.1 7.4 fusion.66
  727.5 6.2 reshape.723
  733.7 9.3 %convert_element_type.409 = f32[384,9472]{1,0:T(8,128)} convert(bf16[384,9472]{1,0:T(8,128)(2,1)} %all-gather.11.cloned.1.call-done) | non-fusion elementwise | flops 3637248 | bytes 21823488 | tf_op jit(solution)/shard_map/convert_element_type | solution.py:448
  743.0 3.8 slice_reduce_fusion.2
  (343 shorter events, 163.8 us)
Async XLA Ops:
  7.2 18.4 %copy-start.68 = (s32[1,5]{1,0:T(1,128)S(1)}, s32[1,5]{1,0:T(1,128)}, u32[]{:S(2)}) copy-start(s32[1,5]{1,0:T(1,128)} %param.21) | copy-start | bytes 64
  7.2 19.6 %copy-start.36 = (bf16[1024,768]{1,0:T(8,128)(2,1)S(1)}, bf16[1024,768]{1,0:T(8,128)(2,1)}, u32[]{:S(2)}) copy-start(bf16[1024,768]{1,0:T(8,128)(2,1)} %param.20) | copy-start | bytes 4718596
  7.2 75.2 %all-gather.5.cloned.1.call-start = ((), (), s32[]{:S(2)}) async-start(), calls=%async_computation.1 | async-start | bytes 3852288 | tf_op jit(solution)/shard_map/all_gather | solution.py:266
  18.8 180.0 %all-gather.7.cloned.1.call-start = ((), (), s32[]{:S(2)}) async-start(), calls=%async_computation.2 | async-start | bytes 6082560 | tf_op jit(solution)/shard_map/all_gather | solution.py:284
  20.5 226.7 %all-gather.9.cloned.1.call-start = ((), (), s32[]{:S(2)}) async-start(), calls=%async_computation.3 | async-start | bytes 4866048 | tf_op jit(solution)/shard_map/all_gather | solution.py:287
  21.2 578.7 %reduce-scatter.4.cloned.1.call-start = ((), (), s32[]{:S(2)}) async-start(), calls=%async_computation.5 | async-start | bytes 6285312
  25.9 109.4 %copy-start.54 = (f32[512]{0:T(512)}, f32[512]{0:T(512)S(1)}, u32[]{:S(2)}) copy-start(f32[512]{0:T(512)S(1)} %get-tuple-element.222) | copy-start | bytes 6148
  25.9 152.1 %copy-start.52 = (f32[512]{0:T(512)}, f32[512]{0:T(512)S(1)}, u32[]{:S(2)}) copy-start(f32[512]{0:T(512)S(1)} %get-tuple-element.221) | copy-start | bytes 6148
  27.5 171.3 %copy-start.4 = (bf16[1024,768]{0,1:T(8,128)(2,1)}, bf16[1024,768]{0,1:T(8,128)(2,1)S(1)}, u32[]{:S(2)}) copy-start(bf16[1024,768]{0,1:T(8,128)(2,1)S(1)} %copy.213) | copy-start | bytes 4718596
  27.8 65.9 %copy-start.42 = (f32[1024]{0:T(1024)}, f32[1024]{0:T(1024)S(1)}, u32[]{:S(2)}) copy-start(f32[1024]{0:T(1024)S(1)} %broadcast_multiply_fusion.11) | copy-start | bytes 12292
  28.3 65.4 %copy-start.50 = (f32[1024]{0:T(1024)}, f32[1024]{0:T(1024)S(1)}, u32[]{:S(2)}) copy-start(f32[1024]{0:T(1024)S(1)} %add_rsqrt_fusion.3) | copy-start | bytes 12292
  101.7 51.0 %copy-start.6 = (bf16[1024,768]{0,1:T(8,128)(2,1)}, bf16[1024,768]{0,1:T(8,128)(2,1)S(1)}, u32[]{:S(2)}) copy-start(bf16[1024,768]{0,1:T(8,128)(2,1)S(1)} %copy.226) | copy-start | bytes 4718596
  109.6 25.7 %copy-start.16 = (bf16[1024,768]{0,1:T(8,128)(2,1)S(1)}, bf16[1024,768]{0,1:T(8,128)(2,1)}, u32[]{:S(2)}) copy-start(bf16[1024,768]{0,1:T(8,128)(2,1)} %copy.224) | copy-start | bytes 4718596
  121.7 16.7 %copy-start.1 = (f32[12,512,1024]{2,1,0:T(8,128)S(1)}, f32[12,512,1024]{2,1,0:T(8,128)}, u32[]{:S(2)}) copy-start(f32[12,512,1024]{2,1,0:T(8,128)} %get-tuple-element.224) | copy-start | bytes 75497472
  152.8 25.2 %copy-start.17 = (bf16[1024,768]{0,1:T(8,128)(2,1)S(1)}, bf16[1024,768]{0,1:T(8,128)(2,1)}, u32[]{:S(2)}) copy-start(bf16[1024,768]{0,1:T(8,128)(2,1)} %copy.224) | copy-start | bytes 4718596
  165.0 16.0 %copy-start = (f32[12,512,1024]{2,1,0:T(8,128)S(1)}, f32[12,512,1024]{2,1,0:T(8,128)}, u32[]{:S(2)}) copy-start(f32[12,512,1024]{2,1,0:T(8,128)} %get-tuple-element.226) | copy-start | bytes 75497472
  181.1 13.9 %copy-start.12 = (f32[512,768]{1,0:T(8,128)S(1)}, f32[512,768]{1,0:T(8,128)}, u32[]{:S(2)}) copy-start(f32[512,768]{1,0:T(8,128)} %copy.229) | copy-start | bytes 4718596
  202.7 39.7 %copy-start.8 = (f32[1024,768]{0,1:T(8,128)}, f32[1024,768]{0,1:T(8,128)S(1)}, u32[]{:S(2)}) copy-start(f32[1024,768]{0,1:T(8,128)S(1)} %get-tuple-element.228) | copy-start | bytes 9437188
  263.2 23.9 %copy-start.9 = (f32[1024,768]{0,1:T(8,128)S(1)}, f32[1024,768]{0,1:T(8,128)}, u32[]{:S(2)}) copy-start(f32[1024,768]{0,1:T(8,128)} %copy-done.8) | copy-start | bytes 9437188
  351.6 13.9 %copy-start.18 = (bf16[1024,768]{0,1:T(8,128)(2,1)S(1)}, bf16[1024,768]{0,1:T(8,128)(2,1)}, u32[]{:S(2)}) copy-start(bf16[1024,768]{0,1:T(8,128)(2,1)} %copy.224) | copy-start | bytes 4718596
  365.4 19.6 %copy-start.19 = (pred[512,1024]{1,0:T(8,128)(4,1)S(1)}, pred[512,1024]{1,0:T(8,128)(4,1)}, u32[]{:S(2)}) copy-start(pred[512,1024]{1,0:T(8,128)(4,1)} %get-tuple-element.217) | copy-start | bytes 1572868
  365.4 19.6 %copy-start.39 = (f32[12,512]{1,0:T(8,128)S(1)}, f32[12,512]{1,0:T(8,128)}, u32[]{:S(2)}) copy-start(f32[12,512]{1,0:T(8,128)} %log_add_fusion.1) | copy-start | bytes 73732
  365.4 19.6 %copy-start.53 = (f32[512]{0:T(512)S(1)}, f32[512]{0:T(512)}, u32[]{:S(2)}) copy-start(f32[512]{0:T(512)} %copy-done.52) | copy-start | bytes 6148
  466.9 249.8 %all-gather.11.cloned.1.call-start = ((), (), s32[]{:S(2)}) async-start(), calls=%async_computation.4 | async-start | bytes 7729152 | tf_op jit(solution)/shard_map/all_gather | solution.py:435
  466.9 17.0 %slice-start = ((s8[12582912]{0:T(1024)(128)(4,1)}), s8[4194304]{0:T(1024)(128)(4,1)S(1)}, s32[]{:S(2)}) async-start(s8[12582912]{0:T(1024)(128)(4,1)} %bitcast.97), calls=%async_computation.6 | async-start | bytes 8388608
  472.9 39.4 %collective-permute-start = (bf16[1536,768]{1,0:T(8,128)(2,1)}, bf16[1536,768]{1,0:T(8,128)(2,1)}, u32[]{:S(2)}, u32[]{:S(2)}) collective-permute-start(bf16[1536,768]{1,0:T(8,128)(2,1)} %bitcast.42), channel_id=1, source_target_pairs={{0,2},{2,0},{4,6},{6,4},{8,10},{10,8},{12,14},{14,12},{16,18},{18,... | collective-permute-start | bytes 7077896 | tf_op jit(solution)/shard_map/ppermute | solution.py:214
  497.4 22.2 %copy-start.26 = (bf16[1024,12,64]{0,2,1:T(8,128)(2,1)}, bf16[1024,12,64]{0,2,1:T(8,128)(2,1)S(1)}, u32[]{:S(2)}) copy-start(bf16[1024,12,64]{0,2,1:T(8,128)(2,1)S(1)} %pad_maximum_fusion.2) | copy-start | bytes 4718596
  518.5 33.5 %collective-permute-start.1 = (bf16[768,768]{1,0:T(8,128)(2,1)}, bf16[768,768]{1,0:T(8,128)(2,1)}, u32[]{:S(2)}, u32[]{:S(2)}) collective-permute-start(bf16[768,768]{1,0:T(8,128)(2,1)} %select_convert_fusion.1), channel_id=1, source_target_pairs={{0,4},{2,6},{4,0},{6,2},{8,12},{10,14},{12,8},{14,10},{16,20},{18,... | collective-permute-start | bytes 3538952 | tf_op jit(solution)/shard_map/ppermute | solution.py:214
  538.7 16.8 %copy-start.27 = (bf16[1024,12,64]{0,2,1:T(8,128)(2,1)S(1)}, bf16[1024,12,64]{0,2,1:T(8,128)(2,1)}, u32[]{:S(2)}) copy-start(bf16[1024,12,64]{0,2,1:T(8,128)(2,1)} %copy-done.26) | copy-start | bytes 4718596
  538.7 16.8 %copy-start.35 = (bf16[12,64,1024]{2,1,0:T(8,128)(2,1)S(1)}, bf16[12,64,1024]{2,1,0:T(8,128)(2,1)}, u32[]{:S(2)}) copy-start(bf16[12,64,1024]{2,1,0:T(8,128)(2,1)} %add_convert_fusion.3) | copy-start | bytes 4718596
  555.3 17.0 %collective-permute-start.2 = (bf16[384,768]{1,0:T(8,128)(2,1)S(1)}, bf16[384,768]{1,0:T(8,128)(2,1)S(1)}, u32[]{:S(2)}, u32[]{:S(2)}) collective-permute-start(bf16[384,768]{1,0:T(8,128)(2,1)S(1)} %select_convert_fusion.4), channel_id=1, source_target_pairs={{0,8},{2,10},{4,12},{6,14},{8,0},{10,2},{12,4},{14,6},{16,24},{18,... | collective-permute-start | bytes 1769480 | tf_op jit(solution)/shard_map/ppermute | solution.py:214
  560.3 13.7 %copy-start.10 = (f32[1024,768]{0,1:T(8,128)S(1)}, f32[1024,768]{0,1:T(8,128)}, u32[]{:S(2)}) copy-start(f32[1024,768]{0,1:T(8,128)} %copy.244) | copy-start | bytes 9437188
  572.6 10.5 %collective-permute-start.3 = (bf16[192,768]{1,0:T(8,128)(2,1)S(1)}, bf16[192,768]{1,0:T(8,128)(2,1)}, u32[]{:S(2)}, u32[]{:S(2)}) collective-permute-start(bf16[192,768]{1,0:T(8,128)(2,1)S(1)} %select_convert_fusion.7), channel_id=1, source_target_pairs={{0,1},{1,0},{2,3},{3,2},{4,5},{5,4},{6,7},{7,6},{8,9},{9,8},{10,11... | collective-permute-start | bytes 884744 | tf_op jit(solution)/shard_map/ppermute | solution.py:214
  584.8 14.4 %collective-permute-start.4 = (bf16[96,768]{1,0:T(8,128)(2,1)}, bf16[96,768]{1,0:T(8,128)(2,1)S(1)}, u32[]{:S(2)}, u32[]{:S(2)}) collective-permute-start(bf16[96,768]{1,0:T(8,128)(2,1)} %select_convert_fusion.10), channel_id=1, source_target_pairs={{0,16},{2,18},{4,20},{6,22},{8,24},{10,26},{12,28},{14,30},{16,0},... | collective-permute-start | bytes 442376 | tf_op jit(solution)/shard_map/ppermute | solution.py:214
  610.2 2.5 collective-permute-start.5
  611.8 2.6 collective-permute-start.10
  613.0 12.3 %collective-permute-start.6 = (bf16[192,1152]{1,0:T(8,128)(2,1)S(1)}, bf16[192,1152]{1,0:T(8,128)(2,1)S(1)}, u32[]{:S(2)}, u32[]{:S(2)}) collective-permute-start(bf16[192,1152]{1,0:T(8,128)(2,1)S(1)} %select_convert_fusion.6), channel_id=1, source_target_pairs={{0,4},{2,6},{4,0},{6,2},{8,12},{10,14},{12,8},{14,10},{16,20},{18,... | collective-permute-start | bytes 1327112 | tf_op jit(solution)/shard_map/ppermute | solution.py:214
  614.7 13.9 %collective-permute-start.11 = (bf16[192,1280]{1,0:T(8,128)(2,1)S(1)}, bf16[192,1280]{1,0:T(8,128)(2,1)S(1)}, u32[]{:S(2)}, u32[]{:S(2)}) collective-permute-start(bf16[192,1280]{1,0:T(8,128)(2,1)S(1)} %select_convert_fusion.5), channel_id=1, source_target_pairs={{0,8},{2,10},{4,12},{6,14},{8,0},{10,2},{12,4},{14,6},{16,24},{18,... | collective-permute-start | bytes 1474568 | tf_op jit(solution)/shard_map/ppermute | solution.py:214
  625.4 25.7 %copy-start.41 = (bf16[24,3968]{1,0:T(8,128)(2,1)S(1)}, bf16[24,3968]{1,0:T(8,128)(2,1)}, u32[]{:S(2)}) copy-start(bf16[24,3968]{1,0:T(8,128)(2,1)} %reduce-scatter.4.cloned.1.call-done) | copy-start | bytes 571396
  625.4 7.3 collective-permute-start.7
  628.8 23.2 %copy-start.61 = (f32[768]{0:T(1024)S(1)}, f32[768]{0:T(1024)}, u32[]{:S(2)}) copy-start(f32[768]{0:T(1024)} %get-tuple-element.181) | copy-start | bytes 9220
  632.8 4.8 collective-permute-start.8
  633.5 6.7 collective-permute-start.12
  640.3 4.9 collective-permute-start.13
  641.9 6.3 collective-permute-start.9
  645.3 5.8 collective-permute-start.14
  727.5 19.4 %slice-start.3 = ((s8[7274496]{0:T(1024)(128)(4,1)}), s8[3080192]{0:T(1024)(128)(4,1)S(1)}, s32[]{:S(2)}) async-start(s8[7274496]{0:T(1024)(128)(4,1)} %bitcast.99), calls=%async_computation.9 | async-start | bytes 6160384
  733.7 13.1 %slice-start.4 = ((s8[7274496]{0:T(1024)(128)(4,1)}), s8[4194304]{0:T(1024)(128)(4,1)S(1)}, s32[]{:S(2)}) async-start(s8[7274496]{0:T(1024)(128)(4,1)} %bitcast.99), calls=%async_computation.10 | async-start | bytes 8388608
  (49 other events, 232.6 us)
Sparse Core Ops, SparseCore 0:
  18.9 63.4 all-gather.4
  85.9 66.2 all-gather.6
  155.1 62.1 all-gather.8
  467.0 112.6 reduce-scatter.3
  652.1 64.4 all-gather.10

commit v3 on v2

--- a/solution.py
+++ b/solution.py
@@ -1,9 +1,10 @@
 import functools
-import math
 
 import jax
 import jax.numpy as jnp
 from jax import lax
+from jax.experimental import pallas as pl
+from jax.experimental.pallas import tpu as pltpu
 from jax.sharding import PartitionSpec as P
 
 
@@ -16,6 +17,166 @@
 
 
 MASKED = -1000000000.0
+
+CHUNK = 128
+QBLOCK = 256
+
+
+def _scores(q, k_ref, segq, posq, segk_ref, c, scale):
+    kc = k_ref[0, pl.ds(c * CHUNK, CHUNK), :]
+    s = lax.dot_general(q, kc, (((1,), (1,)), ((), ())), preferred_element_type=jnp.float32) * scale
+    segk = segk_ref[:, pl.ds(c * CHUNK, CHUNK)]
+    posk = c * CHUNK + lax.broadcasted_iota(jnp.int32, (1, CHUNK), 1)
+    allowed = (segq == segk) & (posq >= posk) & (segk < NSEG - 1)
+    return jnp.where(allowed, s, MASKED)
+
+
+def _softmax_rows(q, k_ref, segq, posq, segk_ref, lo, hi, s_ref, scale):
+    tq = q.shape[0]
+
+    def first(c, m):
+        s = _scores(q, k_ref, segq, posq, segk_ref, c, scale)
+        s_ref[:, pl.ds(c * CHUNK, CHUNK)] = s
+        return jnp.maximum(m, jnp.max(s, axis=1, keepdims=True))
+
+    m = lax.fori_loop(lo, hi, first, jnp.full((tq, 1), -jnp.inf, jnp.float32))
+
+    def second(c, l):
+        e = jnp.exp(s_ref[:, pl.ds(c * CHUNK, CHUNK)] - m)
+        s_ref[:, pl.ds(c * CHUNK, CHUNK)] = e
+        return l + jnp.sum(e, axis=1, keepdims=True)
+
+    return lax.fori_loop(lo, hi, second, jnp.zeros((tq, 1), jnp.float32))
+
+
+def _fwd_kernel(lo_ref, q_ref, k_ref, v_ref, segq_ref, segk_ref, o_ref, s_ref):
+    i = pl.program_id(1)
+    tq = q_ref.shape[1]
+    q = q_ref[0]
+    segq = segq_ref[...]
+    posq = i * tq + lax.broadcasted_iota(jnp.int32, (tq, 1), 0)
+    keep = (segq < NSEG - 1).astype(jnp.float32)
+    lo = lo_ref[i]
+    hi = (i + 1) * (tq // CHUNK)
+    total = _softmax_rows(q, k_ref, segq, posq, segk_ref, lo, hi, s_ref, 0.125)
+
+    def third(c, acc):
+        p = (s_ref[:, pl.ds(c * CHUNK, CHUNK)] / total * keep).astype(jnp.bfloat16)
+        vc = v_ref[0, pl.ds(c * CHUNK, CHUNK), :]
+        return acc + jnp.dot(p, vc, preferred_element_type=jnp.float32)
+
+    o_ref[0] = lax.fori_loop(lo, hi, third, jnp.zeros((tq, q.shape[1]), jnp.float32))
+
+
+def _bwd_kernel(lo_ref, q_ref, k_ref, v_ref, do_ref, segq_ref, segk_ref, dq_ref, dk_ref, dv_ref, s_ref, dp_ref):
+    i = pl.program_id(1)
+    tq = q_ref.shape[1]
+
+    @pl.when(i == 0)
+    def _():
+        dk_ref[...] = jnp.zeros_like(dk_ref)
+        dv_ref[...] = jnp.zeros_like(dv_ref)
+
+    q = q_ref[0]
+    do = do_ref[0]
+    segq = segq_ref[...]
+    posq = i * tq + lax.broadcasted_iota(jnp.int32, (tq, 1), 0)
+    keep = (segq < NSEG - 1).astype(jnp.float32)
+    lo = lo_ref[i]
+    hi = (i + 1) * (tq // CHUNK)
+    total = _softmax_rows(q, k_ref, segq, posq, segk_ref, lo, hi, s_ref, 0.125)
+
+    def third(c, inner):
+        p = s_ref[:, pl.ds(c * CHUNK, CHUNK)] / total * keep
+        vc = v_ref[0, pl.ds(c * CHUNK, CHUNK), :]
+        dp = lax.dot_general(do, vc, (((1,), (1,)), ((), ())), preferred_element_type=jnp.float32)
+        s_ref[:, pl.ds(c * CHUNK, CHUNK)] = p
+        dp_ref[:, pl.ds(c * CHUNK, CHUNK)] = dp
+        return inner + jnp.sum(p * dp, axis=1, keepdims=True)
+
+    inner = lax.fori_loop(lo, hi, third, jnp.zeros((tq, 1), jnp.float32))
+
+    def fourth(c, dq):
+        p = s_ref[:, pl.ds(c * CHUNK, CHUNK)]
+        ds = (p * (dp_ref[:, pl.ds(c * CHUNK, CHUNK)] - inner)).astype(jnp.bfloat16)
+        kc = k_ref[0, pl.ds(c * CHUNK, CHUNK), :]
+        rows = pl.ds(c * CHUNK, CHUNK)
+        dk_ref[0, rows, :] += lax.dot_general(ds, q, (((0,), (0,)), ((), ())), preferred_element_type=jnp.float32) * 0.125
+        dv_ref[0, rows, :] += lax.dot_general(p.astype(jnp.bfloat16), do, (((0,), (0,)), ((), ())), preferred_element_type=jnp.float32)
+        return dq + jnp.dot(ds, kc, preferred_element_type=jnp.float32)
+
+    dq = lax.fori_loop(lo, hi, fourth, jnp.zeros((tq, q.shape[1]), jnp.float32))
+    dq_ref[0] = dq * 0.125
+
+
+def _specs(length, head, tq):
+    qspec = pl.BlockSpec((1, tq, head), lambda h, i, lo: (h, i, 0))
+    kspec = pl.BlockSpec((1, length, head), lambda h, i, lo: (h, 0, 0))
+    segq = pl.BlockSpec((tq, 1), lambda h, i, lo: (i, 0))
+    segk = pl.BlockSpec((1, length), lambda h, i, lo: (0, 0))
+    return qspec, kspec, segq, segk
+
+
+def attention_forward(q, k, v, seg, lo):
+    heads, length, head = q.shape
+    tq = min(QBLOCK, length)
+    qspec, kspec, segq, segk = _specs(length, head, tq)
+    return pl.pallas_call(
+        _fwd_kernel,
+        out_shape=jax.ShapeDtypeStruct((heads, length, head), jnp.float32),
+        grid_spec=pltpu.PrefetchScalarGridSpec(
+            num_scalar_prefetch=1,
+            grid=(heads, length // tq),
+            in_specs=[qspec, kspec, kspec, segq, segk],
+            out_specs=qspec,
+            scratch_shapes=[pltpu.VMEM((tq, length), jnp.float32)],
+        ),
+        compiler_params=pltpu.CompilerParams(dimension_semantics=("arbitrary", "arbitrary")),
+        cost_estimate=pl.CostEstimate(
+            flops=2 * heads * length * length * head,
+            transcendentals=heads * length * length // 2,
+            bytes_accessed=4 * heads * length * head * 2,
+        ),
+    )(lo, q, k, v, seg[:, None], seg[None, :])
+
+
+def attention_backward(q, k, v, do, seg, lo):
+    heads, length, head = q.shape
+    tq = min(QBLOCK, length)
+    qspec, kspec, segq, segk = _specs(length, head, tq)
+    out = jax.ShapeDtypeStruct((heads, length, head), jnp.float32)
+    return pl.pallas_call(
+        _bwd_kernel,
+        out_shape=(out, out, out),
+        grid_spec=pltpu.PrefetchScalarGridSpec(
+            num_scalar_prefetch=1,
+            grid=(heads, length // tq),
+            in_specs=[qspec, kspec, kspec, qspec, segq, segk],
+            out_specs=(qspec, kspec, kspec),
+            scratch_shapes=[pltpu.VMEM((tq, length), jnp.float32), pltpu.VMEM((tq, length), jnp.float32)],
+        ),
+        compiler_params=pltpu.CompilerParams(dimension_semantics=("arbitrary", "arbitrary")),
+        cost_estimate=pl.CostEstimate(
+            flops=5 * heads * length * length * head,
+            transcendentals=heads * length * length // 2,
+            bytes_accessed=8 * heads * length * head * 2,
+        ),
+    )(lo, q, k, v, do, seg[:, None], seg[None, :])
+
+
+def block_starts(seg, lengths, tq):
+    ends = jnp.cumsum(lengths)
+    starts = jnp.concatenate([jnp.zeros((1,), ends.dtype), ends[:-1]])
+    first_seg = seg[::tq]
+    return (starts[first_seg] // CHUNK).astype(jnp.int32)
+
+
+def heads_major(block):
+    return block.reshape(block.shape[0], HEADS, HEAD).transpose(1, 0, 2)
+
+
+def tokens_major(block):
+    return block.transpose(1, 0, 2).reshape(block.shape[1], HEADS * HEAD)
 
 
 def norm_apply(values, gain, shift):
@@ -44,107 +205,6 @@
     ends = jnp.cumsum(lengths_row)
     places = jnp.arange(length, dtype=jnp.int32)
     return jnp.sum((places[:, None] >= ends[None, :]).astype(jnp.int32), axis=1)
-
-
-def split_heads(qkv_row):
-    length = qkv_row.shape[0]
-    width = qkv_row.shape[1] // 3
-    queries = qkv_row[:, :width].reshape(length, HEADS, HEAD)
-    key_heads = qkv_row[:, width : 2 * width].reshape(length, HEADS, HEAD)
-    value_heads = qkv_row[:, 2 * width :].reshape(length, HEADS, HEAD)
-    return (queries, key_heads, value_heads)
-
-
-def masked_scores(query_part, key_heads, segment, valid, offset):
-    query_count = query_part.shape[0]
-    scores = jnp.einsum(
-        "qhd,khd->hqk", query_part, key_heads, preferred_element_type=jnp.float32
-    ) * (1.0 / math.sqrt(HEAD))
-    places = jnp.arange(segment.shape[0], dtype=jnp.int32)
-    query_places = places[offset : offset + query_count]
-    query_segment = segment[offset : offset + query_count]
-    allowed = (
-        (query_segment[:, None] == segment[None, :])
-        & (query_places[:, None] >= places[None, :])
-        & valid[None, :]
-    )
-    return jnp.where(allowed[None], scores, MASKED)
-
-
-def row_forward(pieces):
-    qkv_row, segment = pieces
-    length = qkv_row.shape[0]
-    queries, key_heads, value_heads = split_heads(qkv_row)
-    valid = segment < NSEG - 1
-    block_rows = min(512, length)
-    attended_parts = []
-    totals = []
-    for offset in range(0, length, block_rows):
-        scores = masked_scores(
-            queries[offset : offset + block_rows], key_heads, segment, valid, offset
-        )
-        keep_rows = valid[offset : offset + block_rows].astype(jnp.float32)[None, :, None]
-        peak = jnp.max(scores, axis=-1, keepdims=True)
-        expd = jnp.exp(scores - peak)
-        total = jnp.sum(expd, axis=-1, keepdims=True)
-        probs = (expd / total * keep_rows).astype(jnp.bfloat16)
-        attended_parts.append(
-            jnp.einsum(
-                "hqk,khd->qhd", probs, value_heads, preferred_element_type=jnp.float32
-            ).reshape(block_rows, HEADS * HEAD)
-        )
-        totals.append((peak + jnp.log(total))[:, :, 0])
-    return (jnp.concatenate(attended_parts, axis=0), jnp.concatenate(totals, axis=1))
-
-
-def row_backward(pieces):
-    qkv_row, segment, log_total, grad_rows = pieces
-    length = qkv_row.shape[0]
-    queries, key_heads, value_heads = split_heads(qkv_row)
-    valid = segment < NSEG - 1
-    grad_heads = grad_rows.reshape(length, HEADS, HEAD)
-    block_rows = min(512, length)
-    scale_factor = 1.0 / math.sqrt(HEAD)
-    query_grads = []
-    key_grad = jnp.zeros((length, HEADS, HEAD), jnp.float32)
-    value_grad = jnp.zeros((length, HEADS, HEAD), jnp.float32)
-    for offset in range(0, length, block_rows):
-        query_part = queries[offset : offset + block_rows]
-        scores = masked_scores(query_part, key_heads, segment, valid, offset)
-        keep_rows = valid[offset : offset + block_rows].astype(jnp.float32)[None, :, None]
-        probs = jnp.exp(scores - log_total[:, offset : offset + block_rows, None]) * keep_rows
-        grad_block = grad_heads[offset : offset + block_rows]
-        grad_probs = jnp.einsum(
-            "qhd,khd->hqk", grad_block, value_heads, preferred_element_type=jnp.float32
-        )
-        inner_sum = jnp.sum(probs * grad_probs, axis=-1, keepdims=True)
-        grad_scores = (probs * (grad_probs - inner_sum)).astype(jnp.bfloat16)
-        query_grads.append(
-            jnp.einsum("hqk,khd->qhd", grad_scores, key_heads, preferred_element_type=jnp.float32)
-            * scale_factor
-        )
-        key_grad = (
-            key_grad
-            + jnp.einsum(
-                "hqk,qhd->khd", grad_scores, query_part, preferred_element_type=jnp.float32
-            )
-            * scale_factor
-        )
-        value_grad = value_grad + jnp.einsum(
-            "hqk,qhd->khd",
-            probs.astype(jnp.bfloat16),
-            grad_block,
-            preferred_element_type=jnp.float32,
-        )
-    query_grad = jnp.concatenate(query_grads, axis=0)
-    return jnp.concatenate(
-        [
-            query_grad.reshape(length, -1),
-            key_grad.reshape(length, -1),
-            value_grad.reshape(length, -1),
-        ],
-        axis=1,
-    )
 
 
 def pack_columns(parts, rows):
@@ -299,10 +359,23 @@
     qkv_low = (jnp.dot(normed_low, qkv_full, preferred_element_type=jnp.float32) + bias_cat).astype(
         jnp.bfloat16
     )
-    segments = jax.vmap(functools.partial(segment_ids, length=length))(doc_lengths)
-    qkv_rows = qkv_low.reshape(row_count, length, 3 * model_width)
-    attended, log_totals = lax.map(row_forward, (qkv_rows, segments))
-    attended = attended.reshape(-1, model_width)
+    segments = jax.vmap(functools.partial(segment_ids, length=length))(doc_lengths).astype(
+        jnp.int32
+    )
+    tq = min(QBLOCK, length)
+    row_heads = []
+    row_starts = []
+    attended_rows = []
+    for r in range(row_count):
+        piece = qkv_low[r * length : (r + 1) * length]
+        heads = tuple(
+            heads_major(piece[:, j * model_width : (j + 1) * model_width]) for j in range(3)
+        )
+        lo = block_starts(segments[r], doc_lengths[r], tq)
+        row_heads.append(heads)
+        row_starts.append(lo)
+        attended_rows.append(tokens_major(attention_forward(*heads, segments[r], lo)))
+    attended = jnp.concatenate(attended_rows, axis=0)
     inner, unit_two, inv_two = norm_apply(
         attended, gain_inner.astype(jnp.float32), shift_inner.astype(jnp.float32)
     )
@@ -386,17 +459,22 @@
         ],
         axis=1,
     ).astype(jnp.bfloat16)
-    grad_att_low = grad_attended.astype(jnp.bfloat16).reshape(row_count, length, model_width)
+    grad_att_low = grad_attended.astype(jnp.bfloat16)
     ffn_pack, shrink_in, grad_att_low = lax.optimization_barrier(
         (ffn_pack, shrink_in, grad_att_low)
     )
     ffn_part = grad_rows_reduce(ffn_pack, group_size, shard_size)
     shrink_part = hypercube_reduce_scatter(shrink_in, order_a, group_size, shard_size)
-    grad_qkv = (
-        lax.map(row_backward, (qkv_rows, segments, log_totals, grad_att_low))
-        .reshape(-1, 3 * model_width)
-        .astype(jnp.bfloat16)
-    )
+    grad_rows = []
+    for r in range(row_count):
+        parts = attention_backward(
+            *row_heads[r],
+            heads_major(grad_att_low[r * length : (r + 1) * length]),
+            segments[r],
+            row_starts[r],
+        )
+        grad_rows.append(jnp.concatenate([tokens_major(p) for p in parts], axis=1))
+    grad_qkv = jnp.concatenate(grad_rows, axis=0).astype(jnp.bfloat16)
     grad_qkv_wide = grad_qkv.astype(jnp.float32)
     query_bias_grad = jnp.sum(grad_qkv_wide[:, :model_width], axis=0)
     value_bias_grad = jnp.sum(grad_qkv_wide[:, 2 * model_width :], axis=0)

time: 768 us -> 876 us (1.14)
  Pallas kernels: 0 us -> 245 us
  matrix products: 264 us -> 115 us
  starting transfers between devices: 12.3 us -> 87.8 us
  other arithmetic: 157 us -> 101 us
  waiting for transfers between devices: 157 us -> 135 us
  local copies, waits for them, and re-layouts: 151 us -> 167 us
    pallas_call x0 -> x2, Pallas kernels: none -> 245 us  [the longest x1 148 us: attention_backward(): pl.pallas_call(_bwd_kernel, out_shape=(out, out, out), grid_spec=pltpu.Pr...]
    dot_general x12 -> x0, matrix products: 144 us -> none  [the longest x2 37.2 us: row_backward(): jnp.einsum('qhd,khd->hqk', grad_block, value_heads, preferred_element_typ...]
    ppermute x15, starting transfers between devices: 12.1 us -> 87.6 us  [hypercube_reduce_scatter(): got = lax.ppermute(send, axis, [(j, j ^ 1 << b) for j in range(size)])]
    convert_element_type x2 -> x1, other arithmetic: 42.2 us -> 1.95 us  [per_device(): grad_att_low = grad_attended.astype(jnp.bfloat16)]
    reduce_sum x2 -> x0, other arithmetic: 25.3 us -> none  [row_forward(): total = jnp.sum(expd, axis=-1, keepdims=True)]
    ppermute x15, waiting for transfers between devices: 56 us -> 33.3 us  [hypercube_reduce_scatter(): got = lax.ppermute(send, axis, [(j, j ^ 1 << b) for j in range(size)])]
    transpose x0 -> x4, local copies, waits for them, and re-layouts: none -> 13.4 us  [tokens_major(): return block.transpose(1, 0, 2).reshape(block.shape[1], HEADS * HEAD)]
    reshape x2 -> x5, local copies, waits for them, and re-layouts: 6.24 us -> 18.8 us  [the longest x4 15 us: heads_major(): return block.reshape(block.shape[0], HEADS, HEAD).transpose(1, 0, 2)]
  transfers between devices with their start and end apart: 20 -> 20, of which waited for: 14 -> 12; matrix products, arithmetic and copies ran while one was open for 37% -> 26% of each run, Pallas kernels for 0% -> 28%
where the time goes in v3:
time: 876 us; the launch traced here: 867 us
  Pallas kernels  245 us (28%)
  local copies, waits for them, and re-layouts  167 us (19%)
  waiting for transfers between devices  135 us (15%)
  matrix products  115 us (13%)
  other arithmetic  101 us (12%)
  starting transfers between devices  87.8 us (10%)
  between operations  15 us (2%)
    pallas_call x1, Pallas kernels, attention_backward(): pl.pallas_call(_bwd_kernel, out_shape=(out, out, out), grid_spec=pltpu.Pr...  148 us
    pallas_call x1, Pallas kernels, attention_forward(): pl.pallas_call(_fwd_kernel, out_shape=jax.ShapeDtypeStruct((heads, length...  96.3 us
    ppermute x15, starting transfers between devices, hypercube_reduce_scatter(): got = lax.ppermute(send, axis, [(j, j ^ 1 << b) for j in range(size)])  87.6 us
    all_gather x1, waiting for transfers between devices, per_device(): lax.all_gather(first_pack, ('group', 'shard'), axis=0, tiled=True)  52 us
    all_gather x1, waiting for transfers between devices, per_device(): lax.all_gather(jnp.concatenate([ffn_part, shrink_part.astype(jnp.bfloat16...  49.4 us
    dot_general x1, matrix products, per_device(): jnp.dot(second_low, expand_full, preferred_element_type=jnp.float32)  38.8 us
    ppermute x15, waiting for transfers between devices, hypercube_reduce_scatter(): got = lax.ppermute(send, axis, [(j, j ^ 1 << b) for j in range(size)])  33.3 us
    reduce_sum x1, other arithmetic, per_device(): expand_bias_grad = jnp.sum(grad_pre.astype(jnp.float32), axis=0)  18.3 us
  transfers between devices with their start and end apart: 20, of which 12 were waited for; matrix products, arithmetic and copies ran while one was open for 26% of the time, Pallas kernels for 28%

profile of v3, /device:TPU:0, one launch (start us, length us, event | category | flops | bytes accessed | tf_op | source)
XLA Modules:
  0.0 866.6 jit_solution(15277791637522567641)
XLA Ops:
  30.4 52.0 %all-gather.5.cloned.1.call-done = bf16[768,2432]{1,0:T(8,128)(2,1)} async-done(((bf16[24,2432]{1,0:T(8,128)(2,1)}), bf16[768,2432]{1,0:T(8,128)(2,1)}) %all-gather.5.cloned.1.call-update) | async-done | bytes 3735568 | tf_op jit(solution)/shard_map/all_gather | solution.py:326
  83.9 4.2 convert_reduce_fusion.1
  88.1 6.4 add_convert_fusion.2
  99.4 4.1 copy.228
  106.0 4.1 copy.230
  112.7 4.1 copy.232
  116.8 96.3 %shard_map.339 = f32[12,1024,64]{2,1,0:T(8,128)} custom-call(s32[4]{0:T(128)} %and_select_fusion.lo_ref, bf16[12,1024,64]{2,1,0:T(8,128)(2,1)} %bitcast.86, bf16[12,1024,64]{2,1,0:T(8,128)(2,1)} %bitcast.88, bf16[12,1024,64]{2,1,0:T(8,128)(2,1)} %bitcast.90, s32[1024,1]{1,0:T(8,128)} %copy.233.segq_ref, s32[1,1024]{1,0:T(1,128)} %bitcast.109), custom_call_target="tpu_custom_call" | custom-call | flops 1610612736 | bytes 6291456 | tf_op jit(solution)/shard_map/pallas_call | solution.py:124
  213.2 6.2 copy.234
  219.4 3.8 copy.235
  226.4 3.7 multiply_reduce_fusion.4
  237.1 4.2 fusion.45
  242.1 38.8 %fusion.40 = (f32[1024]{0:T(1024)S(1)}, f32[1024,3072]{1,0:T(8,128)S(1)}, f32[1024,3072]{1,0:T(8,128)}, f32[1024,3072]{1,0:T(8,128)}) fusion(f32[3072]{0:T(1024)S(1)} %reshape.560, bf16[768,3840]{1,0:T(8,128)(2,1)} %all-gather.7.cloned.1.call-done, f32[1024,768]{0,1:T(8,128)S(1)} %get-tuple-element.188, f32[768]{0:T(1024)S(1)} %copy-done.45, ...), kind=kOutput, calls=%fused_computation.169 | convolution fusion | flops 5043387392 | bytes 45643776 | tf_op jit(solution)/shard_map/dot_general | solution.py:392
  285.5 15.4 %multiply_reduce_fusion = (bf16[3072]{0:T(1024)(128)(2,1)S(1)}, f32[1024]{0:T(1024)S(1)}, f32[1024]{0:T(1024)S(1)}, bf16[3072]{0:T(1024)(128)(2,1)S(1)}, bf16[1024,3072]{1,0:T(8,128)(2,1)}, /*index=5*/f32[1024,3072]{1,0:T(8,128)}) fusion(f32[1024,3072]{1,0:T(8,128)} %copy-done, f32[1024]{0:T(1024)S(1)} %add_rsqrt_fusion, ...), kind=kOutput, calls=%fused_computation.3 | convolution fusion | flops 4869578752 | bytes 37801984 | tf_op jit(solution)/shard_map/td,fd->tf/dot_general | solution.py:411
  301.0 18.3 %fusion.39 = (bf16[3072]{0:T(1024)(128)(2,1)S(1)}, bf16[1024,3072]{1,0:T(8,128)(2,1)S(1)}) fusion(f32[1024,3072]{1,0:T(8,128)} %get-tuple-element.174, f32[1024]{0:T(1024)S(1)} %get-tuple-element.196, f32[1024,3072]{1,0:T(8,128)} %copy-done, f32[1024]{0:T(1024)S(1)} %broadcast_multiply_fusion.2, f32[1024]{0:T(1024)S(1)} %get-tuple-element.197, ...), kind=kLoop, calls=%fused_computation.168 | loop fusion | flops 72348672 | bytes 56670208 | tf_op jit(solution)/shard_map/reduce_sum | solution.py:418
  319.3 7.2 convolution_convert_fusion
  326.5 6.8 fusion.46
  333.3 3.6 copy.238
  349.4 4.7 multiply_reduce_fusion.5
  356.7 7.5 fusion.48
  364.3 4.7 copy.247
  370.9 10.5 %concatenate.51 = bf16[768,3968]{1,0:T(8,128)(2,1)} concatenate(bf16[768,3072]{1,0:T(8,128)(2,1)} %convolution_convert_fusion, bf16[768,768]{1,0:T(8,128)(2,1)} %convolution_convert_fusion.1, bf16[768,1]{1,0:T(8,128)(2,1)S(1)} %reshape.573, bf16[768,1]{1,0:T(8,128)(2,1)} %reshape.574, bf16[768,1]{1,0:T(8,128)(2,1)S(1)} %copy-done.23, bf16[768,4]{1,0:T(8,128)(2,1)} %reshape.520, ...), dimensions={1} | concatenate | bytes 12189696 | tf_op jit(solution)/shard_map/concatenate | solution.py:454
  381.4 4.2 select_convert_fusion
  387.2 7.5 collective-permute-start
  398.2 5.7 copy.255
  404.0 148.4 %shard_map.340 = (f32[12,1024,64]{2,1,0:T(8,128)}, f32[12,1024,64]{2,1,0:T(8,128)}, f32[12,1024,64]{2,1,0:T(8,128)}) custom-call(s32[4]{0:T(128)} %and_select_fusion.lo_ref, bf16[12,1024,64]{2,1,0:T(8,128)(2,1)} %bitcast.87, bf16[12,1024,64]{2,1,0:T(8,128)(2,1)} %bitcast.89, bf16[12,1024,64]{2,1,0:T(8,128)(2,1)} %bitcast.91, ...), custom_call_target="tpu_custom_call" | custom-call | flops 4026531840 | bytes 12582912 | tf_op jit(solution)/shard_map/pallas_call | solution.py:148
  569.6 4.4 slice_select_fusion
  581.8 5.7 fusion.47
  587.5 3.8 copy.254
  591.4 6.0 fusion.35
  597.4 3.7 copy.259
  604.5 49.7 %collective-permute-start.2 = (bf16[384,768]{1,0:T(8,128)(2,1)S(1)}, bf16[384,768]{1,0:T(8,128)(2,1)S(1)}, u32[]{:S(2)}, u32[]{:S(2)}) collective-permute-start(bf16[384,768]{1,0:T(8,128)(2,1)S(1)} %select_convert_fusion.4), channel_id=1, source_target_pairs={{0,8},{2,10},{4,12},{6,14},{8,0},{10,2},{12,4},{14,6},{16,24},{18,... | collective-permute-start | bytes 1769480 | tf_op jit(solution)/shard_map/ppermute | solution.py:274
  654.2 4.3 fusion.38
  658.5 3.6 collective-permute-done.2
  677.0 8.7 %concatenate.58 = f32[2,16,24,2432]{3,2,0,1:T(8,128)} concatenate(f32[2,16,24,2304]{3,2,0,1:T(8,128)} %copy.259, f32[2,16,24,1]{3,2,0,1:T(8,128)S(1)} %copy-done.21, f32[2,16,24,1]{3,2,0,1:T(8,128)S(1)} %copy-done.22, f32[2,16,24,1]{3,2,0,1:T(8,128)S(1)} %copy.262, f32[2,16,24,1]{3,2,0,1:T(8,128)} %copy.263, f32[2,16,24,124]{3,2,0,1:T(8,128)} %broadcast_in_dim.14), dimensions={3} | concatenate | bytes 14942208 | tf_op jit(solution)/shard_map/concatenate | solution.py:495
  692.4 18.9 %collective-permute-start.5 = (bf16[384,1152]{1,0:T(8,128)(2,1)}, bf16[384,1152]{1,0:T(8,128)(2,1)}, u32[]{:S(2)}, u32[]{:S(2)}) collective-permute-start(bf16[384,1152]{1,0:T(8,128)(2,1)} %bitcast.49), channel_id=1, source_target_pairs={{0,2},{2,0},{4,6},{6,4},{8,10},{10,8},{12,14},{14,12},{16,18},{18,... | collective-permute-start | bytes 2654216 | tf_op jit(solution)/shard_map/ppermute | solution.py:274
  721.9 8.5 collective-permute-done.6
  734.3 3.9 collective-permute-done.7
  743.3 4.1 collective-permute-done.12
  748.2 4.2 collective-permute-done.13
  753.0 4.7 collective-permute-done.14
  758.5 9.3 %add_convert_fusion.3 = bf16[1024,768]{0,1:T(8,128)(2,1)S(1)} fusion(f32[1024,768]{0,1:T(8,128)} %copy-done.4, bf16[1024,3072]{1,0:T(8,128)(2,1)} %get-tuple-element.175, bf16[3072,768]{1,0:T(8,128)(2,1)} %all-gather.9.cloned.1.call-done, f32[768]{0:T(1024)S(1)} %copy-done.41), kind=kOutput, calls=%fused_computation.65 | convolution fusion | flops 4834197504 | bytes 15731712 | tf_op jit(solution)/shard_map/dot_general | solution.py:402
  769.5 3.9 fusion.22
  774.9 49.4 %all-gather.11.cloned.1.call-done = bf16[384,9472]{1,0:T(8,128)(2,1)} async-done(((bf16[24,9472]{1,0:T(8,128)(2,1)}), bf16[384,9472]{1,0:T(8,128)(2,1)}) %all-gather.11.cloned.1.call-update) | async-done | bytes 7274512 | tf_op jit(solution)/shard_map/all_gather | solution.py:513
  824.3 9.2 %convert_element_type.365 = f32[384,9472]{1,0:T(8,128)} convert(bf16[384,9472]{1,0:T(8,128)(2,1)} %all-gather.11.cloned.1.call-done) | non-fusion elementwise | flops 3637248 | bytes 21823488 | tf_op jit(solution)/shard_map/convert_element_type | solution.py:526
  833.5 3.8 slice_reduce_fusion.2
  840.7 7.4 fusion.42
  848.1 6.1 reshape.551
  854.2 3.5 slice.389
  (275 shorter events, 152.5 us)
Async XLA Ops:
  7.2 16.7 %copy-start.11 = (bf16[1024,768]{1,0:T(8,128)(2,1)S(1)}, bf16[1024,768]{1,0:T(8,128)(2,1)}, u32[]{:S(2)}) copy-start(bf16[1024,768]{1,0:T(8,128)(2,1)} %param.39) | copy-start | bytes 4718596
  7.2 16.9 %copy-start.46 = (s32[1,5]{1,0:T(1,128)S(1)}, s32[1,5]{1,0:T(1,128)}, u32[]{:S(2)}) copy-start(s32[1,5]{1,0:T(1,128)} %param.21) | copy-start | bytes 64
  7.2 75.2 %all-gather.5.cloned.1.call-start = ((), (), s32[]{:S(2)}) async-start(), calls=%async_computation.1 | async-start | bytes 3852288 | tf_op jit(solution)/shard_map/all_gather | solution.py:326
  18.8 218.3 %all-gather.7.cloned.1.call-start = ((), (), s32[]{:S(2)}) async-start(), calls=%async_computation.2 | async-start | bytes 6082560 | tf_op jit(solution)/shard_map/all_gather | solution.py:344
  20.5 265.0 %all-gather.9.cloned.1.call-start = ((), (), s32[]{:S(2)}) async-start(), calls=%async_computation.3 | async-start | bytes 4866048 | tf_op jit(solution)/shard_map/all_gather | solution.py:347
  21.2 665.2 %reduce-scatter.4.cloned.1.call-start = ((), (), s32[]{:S(2)}) async-start(), calls=%async_computation.5 | async-start | bytes 6285312
  27.7 209.4 %copy-start.1 = (bf16[1024,768]{0,1:T(8,128)(2,1)}, bf16[1024,768]{0,1:T(8,128)(2,1)S(1)}, u32[]{:S(2)}) copy-start(bf16[1024,768]{0,1:T(8,128)(2,1)S(1)} %copy.216) | copy-start | bytes 4718596
  28.0 66.5 %copy-start.26 = (f32[1024]{0:T(1024)}, f32[1024]{0:T(1024)S(1)}, u32[]{:S(2)}) copy-start(f32[1024]{0:T(1024)S(1)} %broadcast_multiply_fusion.11) | copy-start | bytes 12292
  28.4 66.0 %copy-start.34 = (f32[1024]{0:T(1024)}, f32[1024]{0:T(1024)S(1)}, u32[]{:S(2)}) copy-start(f32[1024]{0:T(1024)S(1)} %add_rsqrt_fusion.3) | copy-start | bytes 12292
  88.1 6.4 copy-start.31
  88.1 6.4 copy-start.42
  226.4 10.7 %copy-start.29 = (f32[1024]{0:T(1024)}, f32[1024]{0:T(1024)S(1)}, u32[]{:S(2)}) copy-start(f32[1024]{0:T(1024)S(1)} %broadcast_multiply_fusion.10) | copy-start | bytes 12292
  241.3 39.6 %copy-start.4 = (f32[1024,768]{0,1:T(8,128)}, f32[1024,768]{0,1:T(8,128)S(1)}, u32[]{:S(2)}) copy-start(f32[1024,768]{0,1:T(8,128)S(1)} %get-tuple-element.188) | copy-start | bytes 9437188
  280.9 4.6 copy-start
  280.9 4.6 copy-start.28
  280.9 4.6 copy-start.40
  285.5 41.0 %slice-start = ((s8[5898240]{0:T(1024)(128)(4,1)}), s8[1703936]{0:T(1024)(128)(4,1)S(1)}, s32[]{:S(2)}) async-start(s8[5898240]{0:T(1024)(128)(4,1)} %bitcast.122), calls=%async_computation.6 | async-start | bytes 3407872
  301.0 18.4 %copy-start.5 = (f32[1024,768]{0,1:T(8,128)S(1)}, f32[1024,768]{0,1:T(8,128)}, u32[]{:S(2)}) copy-start(f32[1024,768]{0,1:T(8,128)} %copy-done.4) | copy-start | bytes 9437188
  301.0 25.5 %slice-start.1 = ((s8[5898240]{0:T(1024)(128)(4,1)}), s8[4194304]{0:T(1024)(128)(4,1)S(1)}, s32[]{:S(2)}) async-start(s8[5898240]{0:T(1024)(128)(4,1)} %bitcast.122), calls=%async_computation.7 | async-start | bytes 8388608
  342.1 7.4 copy-start.9
  349.4 7.3 copy-start.12
  385.6 9.1 %copy-start.13 = (bf16[1024,768]{1,0:T(8,128)(2,1)S(1)}, bf16[1024,768]{1,0:T(8,128)(2,1)}, u32[]{:S(2)}) copy-start(bf16[1024,768]{1,0:T(8,128)(2,1)} %multiply_convert_fusion) | copy-start | bytes 4718596
  387.2 187.2 %collective-permute-start = (bf16[1536,768]{1,0:T(8,128)(2,1)}, bf16[1536,768]{1,0:T(8,128)(2,1)}, u32[]{:S(2)}, u32[]{:S(2)}) collective-permute-start(bf16[1536,768]{1,0:T(8,128)(2,1)} %bitcast.41), channel_id=1, source_target_pairs={{0,2},{2,0},{4,6},{6,4},{8,10},{10,8},{12,14},{14,12},{16,18},{18,... | collective-permute-start | bytes 7077896 | tf_op jit(solution)/shard_map/ppermute | solution.py:274
  403.9 420.4 %all-gather.11.cloned.1.call-start = ((), (), s32[]{:S(2)}) async-start(), calls=%async_computation.4 | async-start | bytes 7729152 | tf_op jit(solution)/shard_map/all_gather | solution.py:513
  574.4 6.3 copy-start.17
  574.4 6.3 copy-start.20
  580.7 20.4 %collective-permute-start.1 = (bf16[768,768]{1,0:T(8,128)(2,1)}, bf16[768,768]{1,0:T(8,128)(2,1)}, u32[]{:S(2)}, u32[]{:S(2)}) collective-permute-start(bf16[768,768]{1,0:T(8,128)(2,1)} %select_convert_fusion.1), channel_id=1, source_target_pairs={{0,4},{2,6},{4,0},{6,2},{8,12},{10,14},{12,8},{14,10},{16,20},{18,... | collective-permute-start | bytes 3538952 | tf_op jit(solution)/shard_map/ppermute | solution.py:274
  601.1 53.1 %copy-start.16 = (bf16[1024,12,64]{0,2,1:T(8,128)(2,1)S(1)}, bf16[1024,12,64]{0,2,1:T(8,128)(2,1)}, u32[]{:S(2)}) copy-start(bf16[1024,12,64]{0,2,1:T(8,128)(2,1)} %copy.252) | copy-start | bytes 4718596
  601.1 53.1 %copy-start.18 = (bf16[1024,12,64]{0,2,1:T(8,128)(2,1)S(1)}, bf16[1024,12,64]{0,2,1:T(8,128)(2,1)}, u32[]{:S(2)}) copy-start(bf16[1024,12,64]{0,2,1:T(8,128)(2,1)} %copy.251) | copy-start | bytes 4718596
  604.5 57.6 %collective-permute-start.2 = (bf16[384,768]{1,0:T(8,128)(2,1)S(1)}, bf16[384,768]{1,0:T(8,128)(2,1)S(1)}, u32[]{:S(2)}, u32[]{:S(2)}) collective-permute-start(bf16[384,768]{1,0:T(8,128)(2,1)S(1)} %select_convert_fusion.4), channel_id=1, source_target_pairs={{0,8},{2,10},{4,12},{6,14},{8,0},{10,2},{12,4},{14,6},{16,24},{18,... | collective-permute-start | bytes 1769480 | tf_op jit(solution)/shard_map/ppermute | solution.py:274
  658.5 6.2 copy-start.6
  662.3 7.2 collective-permute-start.3
  671.2 5.8 copy-start.21
  671.2 5.8 copy-start.22
  671.2 14.5 %collective-permute-start.4 = (bf16[96,768]{1,0:T(8,128)(2,1)}, bf16[96,768]{1,0:T(8,128)(2,1)S(1)}, u32[]{:S(2)}, u32[]{:S(2)}) collective-permute-start(bf16[96,768]{1,0:T(8,128)(2,1)} %select_convert_fusion.10), channel_id=1, source_target_pairs={{0,16},{2,18},{4,20},{6,22},{8,24},{10,26},{12,28},{14,30},{16,0},... | collective-permute-start | bytes 442376 | tf_op jit(solution)/shard_map/ppermute | solution.py:274
  692.4 23.5 %collective-permute-start.5 = (bf16[384,1152]{1,0:T(8,128)(2,1)}, bf16[384,1152]{1,0:T(8,128)(2,1)}, u32[]{:S(2)}, u32[]{:S(2)}) collective-permute-start(bf16[384,1152]{1,0:T(8,128)(2,1)} %bitcast.49), channel_id=1, source_target_pairs={{0,2},{2,0},{4,6},{6,4},{8,10},{10,8},{12,14},{14,12},{16,18},{18,... | collective-permute-start | bytes 2654216 | tf_op jit(solution)/shard_map/ppermute | solution.py:274
  712.7 5.9 collective-permute-start.10
  717.8 12.6 %collective-permute-start.6 = (bf16[192,1152]{1,0:T(8,128)(2,1)S(1)}, bf16[192,1152]{1,0:T(8,128)(2,1)S(1)}, u32[]{:S(2)}, u32[]{:S(2)}) collective-permute-start(bf16[192,1152]{1,0:T(8,128)(2,1)S(1)} %select_convert_fusion.6), channel_id=1, source_target_pairs={{0,4},{2,6},{4,0},{6,2},{8,12},{10,14},{12,8},{14,10},{16,20},{18,... | collective-permute-start | bytes 1327112 | tf_op jit(solution)/shard_map/ppermute | solution.py:274
  720.1 14.0 %collective-permute-start.11 = (bf16[192,1280]{1,0:T(8,128)(2,1)S(1)}, bf16[192,1280]{1,0:T(8,128)(2,1)S(1)}, u32[]{:S(2)}, u32[]{:S(2)}) collective-permute-start(bf16[192,1280]{1,0:T(8,128)(2,1)S(1)} %select_convert_fusion.5), channel_id=1, source_target_pairs={{0,8},{2,10},{4,12},{6,14},{8,0},{10,2},{12,4},{14,6},{16,24},{18,... | collective-permute-start | bytes 1474568 | tf_op jit(solution)/shard_map/ppermute | solution.py:274
  730.6 7.7 collective-permute-start.7
  738.3 19.3 %copy-start.24 = (bf16[24,3072]{1,0:T(8,128)(2,1)S(1)}, bf16[24,3072]{1,0:T(8,128)(2,1)}, u32[]{:S(2)}) copy-start(bf16[24,3072]{1,0:T(8,128)(2,1)} %reshape.536) | copy-start | bytes 442372
  738.4 19.3 %copy-start.25 = (bf16[24,3968]{1,0:T(8,128)(2,1)S(1)}, bf16[24,3968]{1,0:T(8,128)(2,1)}, u32[]{:S(2)}) copy-start(bf16[24,3968]{1,0:T(8,128)(2,1)} %reduce-scatter.4.cloned.1.call-done) | copy-start | bytes 571396
  738.4 4.8 collective-permute-start.8
  740.3 18.3 %copy-start.41 = (f32[768]{0:T(1024)S(1)}, f32[768]{0:T(1024)}, u32[]{:S(2)}) copy-start(f32[768]{0:T(1024)} %get-tuple-element.154) | copy-start | bytes 9220
  740.3 7.1 collective-permute-start.12
  747.5 4.9 collective-permute-start.13
  747.8 5.1 collective-permute-start.9
  752.5 5.2 collective-permute-start.14
  (21 other events, 53.8 us)
Sparse Core Ops, SparseCore 0:
  18.9 63.4 all-gather.4
  85.3 66.3 all-gather.6
  154.7 62.6 all-gather.8
  404.0 128.8 reduce-scatter.3
  758.6 65.6 all-gather.10

commit v4 on v3

--- a/solution.py
+++ b/solution.py
@@ -19,116 +19,119 @@
 MASKED = -1000000000.0
 
 CHUNK = 128
-QBLOCK = 256
-
-
-def _scores(q, k_ref, segq, posq, segk_ref, c, scale):
-    kc = k_ref[0, pl.ds(c * CHUNK, CHUNK), :]
-    s = lax.dot_general(q, kc, (((1,), (1,)), ((), ())), preferred_element_type=jnp.float32) * scale
-    segk = segk_ref[:, pl.ds(c * CHUNK, CHUNK)]
-    posk = c * CHUNK + lax.broadcasted_iota(jnp.int32, (1, CHUNK), 1)
-    allowed = (segq == segk) & (posq >= posk) & (segk < NSEG - 1)
-    return jnp.where(allowed, s, MASKED)
-
-
-def _softmax_rows(q, k_ref, segq, posq, segk_ref, lo, hi, s_ref, scale):
+QBLOCK = 512
+
+
+def _row_setup(segq_ref, i, tq):
+    segq = segq_ref[...]
+    own = jnp.broadcast_to(jnp.where(segq < NSEG - 1, segq, -1), (tq, CHUNK))
+    rel = (i * tq + lax.broadcasted_iota(jnp.int32, (tq, CHUNK), 0)) - lax.broadcasted_iota(
+        jnp.int32, (tq, CHUNK), 1
+    )
+    keep = (segq < NSEG - 1).astype(jnp.float32)
+    return own, rel, keep
+
+
+def _softmax_rows(q, kt_ref, own, rel, segk_ref, lo, hi, s_ref):
     tq = q.shape[0]
 
-    def first(c, m):
-        s = _scores(q, k_ref, segq, posq, segk_ref, c, scale)
+    def first(c, top):
+        kc = kt_ref[0, :, pl.ds(c * CHUNK, CHUNK)]
+        s = jnp.dot(q, kc, preferred_element_type=jnp.float32)
+        allowed = (own == segk_ref[:, pl.ds(c * CHUNK, CHUNK)]) & (rel >= c * CHUNK)
+        s = jnp.where(allowed, s, MASKED)
         s_ref[:, pl.ds(c * CHUNK, CHUNK)] = s
-        return jnp.maximum(m, jnp.max(s, axis=1, keepdims=True))
-
-    m = lax.fori_loop(lo, hi, first, jnp.full((tq, 1), -jnp.inf, jnp.float32))
-
-    def second(c, l):
-        e = jnp.exp(s_ref[:, pl.ds(c * CHUNK, CHUNK)] - m)
+        return jnp.maximum(top, s)
+
+    top = lax.fori_loop(lo, hi, first, jnp.full((tq, CHUNK), MASKED, jnp.float32))
+    peak = jnp.broadcast_to(jnp.max(top, axis=1, keepdims=True), (tq, CHUNK))
+
+    def second(c, acc):
+        e = jnp.exp(s_ref[:, pl.ds(c * CHUNK, CHUNK)] - peak)
         s_ref[:, pl.ds(c * CHUNK, CHUNK)] = e
-        return l + jnp.sum(e, axis=1, keepdims=True)
-
-    return lax.fori_loop(lo, hi, second, jnp.zeros((tq, 1), jnp.float32))
-
-
-def _fwd_kernel(lo_ref, q_ref, k_ref, v_ref, segq_ref, segk_ref, o_ref, s_ref):
+        return acc + e
+
+    acc = lax.fori_loop(lo, hi, second, jnp.zeros((tq, CHUNK), jnp.float32))
+    return jnp.sum(acc, axis=1, keepdims=True)
+
+
+def _fwd_kernel(lo_ref, q_ref, kt_ref, v_ref, segq_ref, segk_ref, o_ref, s_ref):
     i = pl.program_id(1)
     tq = q_ref.shape[1]
-    q = q_ref[0]
-    segq = segq_ref[...]
-    posq = i * tq + lax.broadcasted_iota(jnp.int32, (tq, 1), 0)
-    keep = (segq < NSEG - 1).astype(jnp.float32)
+    q = q_ref[0] * jnp.asarray(0.125, q_ref.dtype)
+    own, rel, keep = _row_setup(segq_ref, i, tq)
     lo = lo_ref[i]
     hi = (i + 1) * (tq // CHUNK)
-    total = _softmax_rows(q, k_ref, segq, posq, segk_ref, lo, hi, s_ref, 0.125)
+    total = _softmax_rows(q, kt_ref, own, rel, segk_ref, lo, hi, s_ref)
+    scale = jnp.broadcast_to(keep / total, (tq, CHUNK))
 
     def third(c, acc):
-        p = (s_ref[:, pl.ds(c * CHUNK, CHUNK)] / total * keep).astype(jnp.bfloat16)
+        p = (s_ref[:, pl.ds(c * CHUNK, CHUNK)] * scale).astype(jnp.bfloat16)
         vc = v_ref[0, pl.ds(c * CHUNK, CHUNK), :]
         return acc + jnp.dot(p, vc, preferred_element_type=jnp.float32)
 
     o_ref[0] = lax.fori_loop(lo, hi, third, jnp.zeros((tq, q.shape[1]), jnp.float32))
 
 
-def _bwd_kernel(lo_ref, q_ref, k_ref, v_ref, do_ref, segq_ref, segk_ref, dq_ref, dk_ref, dv_ref, s_ref, dp_ref):
+def _bwd_kernel(lo_ref, q_ref, qt_ref, k_ref, kt_ref, vt_ref, do_ref, dot_ref, segq_ref, segk_ref,
+                dq_ref, dkt_ref, dvt_ref, s_ref, dp_ref):
     i = pl.program_id(1)
     tq = q_ref.shape[1]
 
     @pl.when(i == 0)
     def _():
-        dk_ref[...] = jnp.zeros_like(dk_ref)
-        dv_ref[...] = jnp.zeros_like(dv_ref)
-
-    q = q_ref[0]
+        dkt_ref[...] = jnp.zeros_like(dkt_ref)
+        dvt_ref[...] = jnp.zeros_like(dvt_ref)
+
+    eighth = jnp.asarray(0.125, q_ref.dtype)
+    qs = q_ref[0] * eighth
+    qts = qt_ref[0] * eighth
     do = do_ref[0]
-    segq = segq_ref[...]
-    posq = i * tq + lax.broadcasted_iota(jnp.int32, (tq, 1), 0)
-    keep = (segq < NSEG - 1).astype(jnp.float32)
+    dot_ = dot_ref[0]
+    own, rel, keep = _row_setup(segq_ref, i, tq)
     lo = lo_ref[i]
     hi = (i + 1) * (tq // CHUNK)
-    total = _softmax_rows(q, k_ref, segq, posq, segk_ref, lo, hi, s_ref, 0.125)
-
-    def third(c, inner):
-        p = s_ref[:, pl.ds(c * CHUNK, CHUNK)] / total * keep
-        vc = v_ref[0, pl.ds(c * CHUNK, CHUNK), :]
-        dp = lax.dot_general(do, vc, (((1,), (1,)), ((), ())), preferred_element_type=jnp.float32)
+    total = _softmax_rows(qs, kt_ref, own, rel, segk_ref, lo, hi, s_ref)
+    scale = jnp.broadcast_to(keep / total, (tq, CHUNK))
+
+    def third(c, acc):
+        p = s_ref[:, pl.ds(c * CHUNK, CHUNK)] * scale
+        dp = jnp.dot(do, vt_ref[0, :, pl.ds(c * CHUNK, CHUNK)], preferred_element_type=jnp.float32)
         s_ref[:, pl.ds(c * CHUNK, CHUNK)] = p
         dp_ref[:, pl.ds(c * CHUNK, CHUNK)] = dp
-        return inner + jnp.sum(p * dp, axis=1, keepdims=True)
-
-    inner = lax.fori_loop(lo, hi, third, jnp.zeros((tq, 1), jnp.float32))
+        return acc + p * dp
+
+    acc = lax.fori_loop(lo, hi, third, jnp.zeros((tq, CHUNK), jnp.float32))
+    inner = jnp.broadcast_to(jnp.sum(acc, axis=1, keepdims=True), (tq, CHUNK))
 
     def fourth(c, dq):
-        p = s_ref[:, pl.ds(c * CHUNK, CHUNK)]
-        ds = (p * (dp_ref[:, pl.ds(c * CHUNK, CHUNK)] - inner)).astype(jnp.bfloat16)
-        kc = k_ref[0, pl.ds(c * CHUNK, CHUNK), :]
-        rows = pl.ds(c * CHUNK, CHUNK)
-        dk_ref[0, rows, :] += lax.dot_general(ds, q, (((0,), (0,)), ((), ())), preferred_element_type=jnp.float32) * 0.125
-        dv_ref[0, rows, :] += lax.dot_general(p.astype(jnp.bfloat16), do, (((0,), (0,)), ((), ())), preferred_element_type=jnp.float32)
-        return dq + jnp.dot(ds, kc, preferred_element_type=jnp.float32)
-
-    dq = lax.fori_loop(lo, hi, fourth, jnp.zeros((tq, q.shape[1]), jnp.float32))
+        cols = pl.ds(c * CHUNK, CHUNK)
+        p = s_ref[:, cols]
+        ds = (p * (dp_ref[:, cols] - inner)).astype(jnp.bfloat16)
+        dkt_ref[0, :, cols] += jnp.dot(qts, ds, preferred_element_type=jnp.float32)
+        dvt_ref[0, :, cols] += jnp.dot(dot_, p.astype(jnp.bfloat16), preferred_element_type=jnp.float32)
+        return dq + jnp.dot(ds, k_ref[0, cols, :], preferred_element_type=jnp.float32)
+
+    dq = lax.fori_loop(lo, hi, fourth, jnp.zeros((tq, q_ref.shape[2]), jnp.float32))
     dq_ref[0] = dq * 0.125
-
-
-def _specs(length, head, tq):
-    qspec = pl.BlockSpec((1, tq, head), lambda h, i, lo: (h, i, 0))
-    kspec = pl.BlockSpec((1, length, head), lambda h, i, lo: (h, 0, 0))
-    segq = pl.BlockSpec((tq, 1), lambda h, i, lo: (i, 0))
-    segk = pl.BlockSpec((1, length), lambda h, i, lo: (0, 0))
-    return qspec, kspec, segq, segk
 
 
 def attention_forward(q, k, v, seg, lo):
     heads, length, head = q.shape
     tq = min(QBLOCK, length)
-    qspec, kspec, segq, segk = _specs(length, head, tq)
+    rows = pl.BlockSpec((1, tq, head), lambda h, i, lo: (h, i, 0))
+    whole = pl.BlockSpec((1, length, head), lambda h, i, lo: (h, 0, 0))
+    wide = pl.BlockSpec((1, head, length), lambda h, i, lo: (h, 0, 0))
+    segq = pl.BlockSpec((tq, 1), lambda h, i, lo: (i, 0))
+    segk = pl.BlockSpec((1, length), lambda h, i, lo: (0, 0))
     return pl.pallas_call(
         _fwd_kernel,
         out_shape=jax.ShapeDtypeStruct((heads, length, head), jnp.float32),
         grid_spec=pltpu.PrefetchScalarGridSpec(
             num_scalar_prefetch=1,
             grid=(heads, length // tq),
-            in_specs=[qspec, kspec, kspec, segq, segk],
-            out_specs=qspec,
+            in_specs=[rows, wide, whole, segq, segk],
+            out_specs=rows,
             scratch_shapes=[pltpu.VMEM((tq, length), jnp.float32)],
         ),
         compiler_params=pltpu.CompilerParams(dimension_semantics=("arbitrary", "arbitrary")),
@@ -137,22 +140,30 @@
             transcendentals=heads * length * length // 2,
             bytes_accessed=4 * heads * length * head * 2,
         ),
-    )(lo, q, k, v, seg[:, None], seg[None, :])
+    )(lo, q, k.transpose(0, 2, 1), v, seg[:, None], seg[None, :])
 
 
 def attention_backward(q, k, v, do, seg, lo):
     heads, length, head = q.shape
     tq = min(QBLOCK, length)
-    qspec, kspec, segq, segk = _specs(length, head, tq)
-    out = jax.ShapeDtypeStruct((heads, length, head), jnp.float32)
-    return pl.pallas_call(
+    rows = pl.BlockSpec((1, tq, head), lambda h, i, lo: (h, i, 0))
+    rows_t = pl.BlockSpec((1, head, tq), lambda h, i, lo: (h, 0, i))
+    whole = pl.BlockSpec((1, length, head), lambda h, i, lo: (h, 0, 0))
+    wide = pl.BlockSpec((1, head, length), lambda h, i, lo: (h, 0, 0))
+    segq = pl.BlockSpec((tq, 1), lambda h, i, lo: (i, 0))
+    segk = pl.BlockSpec((1, length), lambda h, i, lo: (0, 0))
+    dq, dkt, dvt = pl.pallas_call(
         _bwd_kernel,
-        out_shape=(out, out, out),
+        out_shape=(
+            jax.ShapeDtypeStruct((heads, length, head), jnp.float32),
+            jax.ShapeDtypeStruct((heads, head, length), jnp.float32),
+            jax.ShapeDtypeStruct((heads, head, length), jnp.float32),
+        ),
         grid_spec=pltpu.PrefetchScalarGridSpec(
             num_scalar_prefetch=1,
             grid=(heads, length // tq),
-            in_specs=[qspec, kspec, kspec, qspec, segq, segk],
-            out_specs=(qspec, kspec, kspec),
+            in_specs=[rows, rows_t, whole, wide, wide, rows, rows_t, segq, segk],
+            out_specs=(rows, wide, wide),
             scratch_shapes=[pltpu.VMEM((tq, length), jnp.float32), pltpu.VMEM((tq, length), jnp.float32)],
         ),
         compiler_params=pltpu.CompilerParams(dimension_semantics=("arbitrary", "arbitrary")),
@@ -161,7 +172,8 @@
             transcendentals=heads * length * length // 2,
             bytes_accessed=8 * heads * length * head * 2,
         ),
-    )(lo, q, k, v, do, seg[:, None], seg[None, :])
+    )(lo, q, q.transpose(0, 2, 1), k, k.transpose(0, 2, 1), v.transpose(0, 2, 1), do, do.transpose(0, 2, 1), seg[:, None], seg[None, :])
+    return dq, dkt.transpose(0, 2, 1), dvt.transpose(0, 2, 1)
 
 
 def block_starts(seg, lengths, tq):

time: 876 us -> 765 us (0.87)
  Pallas kernels: 245 us -> 166 us
  local copies, waits for them, and re-layouts: 167 us -> 151 us
  starting transfers between devices: 87.8 us -> 78 us
    pallas_call x1, Pallas kernels: 148 us -> 101 us  [attention_backward(): pl.pallas_call(_bwd_kernel, out_shape=(jax.ShapeDtypeStruct((heads, lengt...]
    pallas_call x1, Pallas kernels: 96.3 us -> 65.5 us  [attention_forward(): pl.pallas_call(_fwd_kernel, out_shape=jax.ShapeDtypeStruct((heads, length...]
    reshape x4 -> x0, local copies, waits for them, and re-layouts: 15 us -> none  [heads_major(): return block.reshape(block.shape[0], HEADS, HEAD).transpose(1, 0, 2)]
    transpose x0 -> x4, local copies, waits for them, and re-layouts: none -> 11.1 us  [heads_major(): return block.reshape(block.shape[0], HEADS, HEAD).transpose(1, 0, 2)]
    ppermute x15, starting transfers between devices: 87.6 us -> 77.8 us  [hypercube_reduce_scatter(): got = lax.ppermute(send, axis, [(j, j ^ 1 << b) for j in range(size)])]
    transpose x3 -> x1, other arithmetic: 10 us -> 0.49 us  [tokens_major(): return block.transpose(1, 0, 2).reshape(block.shape[1], HEADS * HEAD)]
  transfers between devices with their start and end apart: 20 -> 20, of which waited for: 12 -> 13; matrix products, arithmetic and copies ran while one was open for 26% -> 26% of each run, Pallas kernels for 28% -> 22%
where the time goes in v4:
time: 765 us; the launch traced here: 756 us
  Pallas kernels  166 us (22%)
  local copies, waits for them, and re-layouts  151 us (20%)
  waiting for transfers between devices  135 us (18%)
  matrix products  116 us (15%)
  other arithmetic  95.2 us (12%)
  starting transfers between devices  78 us (10%)
  between operations  15.1 us (2%)
    pallas_call x1, Pallas kernels, attention_backward(): pl.pallas_call(_bwd_kernel, out_shape=(jax.ShapeDtypeStruct((heads, lengt...  101 us
    ppermute x15, starting transfers between devices, hypercube_reduce_scatter(): got = lax.ppermute(send, axis, [(j, j ^ 1 << b) for j in range(size)])  77.8 us
    pallas_call x1, Pallas kernels, attention_forward(): pl.pallas_call(_fwd_kernel, out_shape=jax.ShapeDtypeStruct((heads, length...  65.5 us
    all_gather x1, waiting for transfers between devices, per_device(): lax.all_gather(first_pack, ('group', 'shard'), axis=0, tiled=True)  52.9 us
    all_gather x1, waiting for transfers between devices, per_device(): lax.all_gather(jnp.concatenate([ffn_part, shrink_part.astype(jnp.bfloat16...  49 us
    dot_general x1, matrix products, per_device(): jnp.dot(second_low, expand_full, preferred_element_type=jnp.float32)  39.5 us
    ppermute x15, waiting for transfers between devices, hypercube_reduce_scatter(): got = lax.ppermute(send, axis, [(j, j ^ 1 << b) for j in range(size)])  32 us
    reduce_sum x1, other arithmetic, per_device(): expand_bias_grad = jnp.sum(grad_pre.astype(jnp.float32), axis=0)  18.3 us
  transfers between devices with their start and end apart: 20, of which 13 were waited for; matrix products, arithmetic and copies ran while one was open for 26% of the time, Pallas kernels for 22%

profile of v4, /device:TPU:0, one launch (start us, length us, event | category | flops | bytes accessed | tf_op | source)
XLA Modules:
  0.0 756.3 jit_solution(15407774426411652991)
XLA Ops:
  29.6 52.9 %all-gather.5.cloned.1.call-done = bf16[768,2432]{1,0:T(8,128)(2,1)} async-done(((bf16[24,2432]{1,0:T(8,128)(2,1)}), bf16[768,2432]{1,0:T(8,128)(2,1)}) %all-gather.5.cloned.1.call-update) | async-done | bytes 3735568 | tf_op jit(solution)/shard_map/all_gather | solution.py:338
  84.0 4.2 convert_reduce_fusion.1
  88.2 6.4 add_convert_fusion.2
  108.5 65.5 %shard_map.339 = f32[12,1024,64]{2,1,0:T(8,128)} custom-call(s32[2]{0:T(128)} %and_select_fusion.lo_ref, bf16[12,1024,64]{2,1,0:T(8,128)(2,1)} %copy.236.q_ref, bf16[12,64,1024]{2,1,0:T(8,128)(2,1)} %bitcast.91, bf16[12,1024,64]{2,1,0:T(8,128)(2,1)} %copy.237.v_ref, s32[1024,1]{1,0:T(8,128)} %copy.238.segq_ref, s32[1,1024]{1,0:T(1,128)} %bitcast.121), custom_call_target="tpu_custom_call" | custom-call | flops 1610612736 | bytes 6291456 | tf_op jit(solution)/shard_map/pallas_call | solution.py:127
  174.0 6.1 copy.239
  180.1 3.7 copy.240
  183.8 3.3 reduce_sum.276
  187.1 3.8 multiply_reduce_fusion.4
  193.2 4.2 fusion.45
  197.8 39.5 %fusion.40 = (f32[1024]{0:T(1024)S(1)}, f32[1024,3072]{1,0:T(8,128)S(1)}, f32[1024,3072]{1,0:T(8,128)}, f32[1024,3072]{1,0:T(8,128)}) fusion(f32[3072]{0:T(1024)S(1)} %reshape.560, bf16[768,3840]{1,0:T(8,128)(2,1)} %all-gather.7.cloned.1.call-done, f32[1024,768]{0,1:T(8,128)S(1)} %get-tuple-element.188, f32[768]{0:T(1024)S(1)} %get-tuple-element.155, ...), kind=kOutput, calls=%fused_computation.167 | convolution fusion | flops 5043387392 | bytes 45643776 | tf_op jit(solution)/shard_map/dot_general | solution.py:404
  238.7 3.3 copy-done
  242.1 15.4 %multiply_reduce_fusion = (bf16[3072]{0:T(1024)(128)(2,1)S(1)}, f32[1024]{0:T(1024)S(1)}, f32[1024]{0:T(1024)S(1)}, bf16[3072]{0:T(1024)(128)(2,1)S(1)}, bf16[1024,3072]{1,0:T(8,128)(2,1)}, /*index=5*/f32[1024,3072]{1,0:T(8,128)}) fusion(f32[1024,3072]{1,0:T(8,128)} %copy-done, f32[1024]{0:T(1024)S(1)} %add_rsqrt_fusion, ...), kind=kOutput, calls=%fused_computation.3 | convolution fusion | flops 4869578752 | bytes 37801984 | tf_op jit(solution)/shard_map/td,fd->tf/dot_general | solution.py:423
  257.5 18.3 %fusion.39 = (bf16[3072]{0:T(1024)(128)(2,1)S(1)}, bf16[1024,3072]{1,0:T(8,128)(2,1)S(1)}) fusion(f32[1024,3072]{1,0:T(8,128)} %get-tuple-element.174, f32[1024]{0:T(1024)S(1)} %get-tuple-element.196, f32[1024,3072]{1,0:T(8,128)} %copy-done, f32[1024]{0:T(1024)S(1)} %broadcast_multiply_fusion.2, f32[1024]{0:T(1024)S(1)} %get-tuple-element.197, ...), kind=kLoop, calls=%fused_computation.166 | loop fusion | flops 72348672 | bytes 56670208 | tf_op jit(solution)/shard_map/reduce_sum | solution.py:430
  275.8 7.1 convolution_convert_fusion
  283.0 6.8 fusion.46
  289.8 3.6 copy.243
  305.9 4.7 multiply_reduce_fusion.5
  313.2 7.7 %fusion.48 = f32[3072,768]{1,0:T(8,128)S(1)} fusion(bf16[1024,3072]{1,0:T(8,128)(2,1)} %get-tuple-element.175, bf16[1024,768]{1,0:T(8,128)(2,1)S(1)} %copy-done.18), kind=kOutput, calls=%fused_computation.174 | convolution fusion | flops 4831838208 | bytes 17301504 | tf_op jit(solution)/shard_map/tf,td->fd/dot_general | solution.py:419
  320.9 4.7 copy.252
  327.6 10.5 %concatenate.51 = bf16[768,3968]{1,0:T(8,128)(2,1)} concatenate(bf16[768,3072]{1,0:T(8,128)(2,1)} %convolution_convert_fusion, bf16[768,768]{1,0:T(8,128)(2,1)} %convolution_convert_fusion.1, bf16[768,1]{1,0:T(8,128)(2,1)S(1)} %reshape.573, bf16[768,1]{1,0:T(8,128)(2,1)} %reshape.574, bf16[768,1]{1,0:T(8,128)(2,1)S(1)} %copy-done.31, bf16[768,4]{1,0:T(8,128)(2,1)} %reshape.520, ...), dimensions={1} | concatenate | bytes 12189696 | tf_op jit(solution)/shard_map/concatenate | solution.py:466
  338.1 4.3 select_convert_fusion
  344.0 5.7 collective-permute-start
  360.4 100.6 %shard_map.340 = (f32[12,1024,64]{2,1,0:T(8,128)}, f32[12,64,1024]{2,1,0:T(8,128)}, f32[12,64,1024]{2,1,0:T(8,128)}) custom-call(s32[2]{0:T(128)} %and_select_fusion.lo_ref, bf16[12,1024,64]{2,1,0:T(8,128)(2,1)} %copy.236.q_ref, bf16[12,64,1024]{2,1,0:T(8,128)(2,1)} %bitcast.103, bf16[12,1024,64]{2,1,0:T(8,128)(2,1)} %copy.255.k_ref, ...), custom_call_target="tpu_custom_call" | custom-call | flops 4026531840 | bytes 12582912 | tf_op jit(solution)/shard_map/pallas_call | solution.py:155
  461.1 3.4 convert.83
  470.0 4.4 slice_select_fusion
  482.6 5.7 fusion.47
  488.3 3.8 copy.259
  492.2 6.0 fusion.35
  498.2 3.7 copy.264
  502.0 3.2 convert_add_fusion.1
  505.3 25.1 %collective-permute-start.2 = (bf16[384,768]{1,0:T(8,128)(2,1)S(1)}, bf16[384,768]{1,0:T(8,128)(2,1)S(1)}, u32[]{:S(2)}, u32[]{:S(2)}) collective-permute-start(bf16[384,768]{1,0:T(8,128)(2,1)S(1)} %select_convert_fusion.4), channel_id=1, source_target_pairs={{0,8},{2,10},{4,12},{6,14},{8,0},{10,2},{12,4},{14,6},{16,24},{18,... | collective-permute-start | bytes 1769480 | tf_op jit(solution)/shard_map/ppermute | solution.py:286
  530.4 4.3 fusion.38
  534.7 3.6 collective-permute-done.2
  538.5 32.7 %collective-permute-start.3 = (bf16[192,768]{1,0:T(8,128)(2,1)S(1)}, bf16[192,768]{1,0:T(8,128)(2,1)}, u32[]{:S(2)}, u32[]{:S(2)}) collective-permute-start(bf16[192,768]{1,0:T(8,128)(2,1)S(1)} %select_convert_fusion.7), channel_id=1, source_target_pairs={{0,1},{1,0},{2,3},{3,2},{4,5},{5,4},{6,7},{7,6},{8,9},{9,8},{10,11... | collective-permute-start | bytes 884744 | tf_op jit(solution)/shard_map/ppermute | solution.py:286
  585.0 8.7 %concatenate.58 = f32[2,16,24,2432]{3,2,0,1:T(8,128)} concatenate(f32[2,16,24,2304]{3,2,0,1:T(8,128)} %copy.264, f32[2,16,24,1]{3,2,0,1:T(8,128)S(1)} %copy-done.29, f32[2,16,24,1]{3,2,0,1:T(8,128)S(1)} %copy-done.30, f32[2,16,24,1]{3,2,0,1:T(8,128)S(1)} %copy.267, f32[2,16,24,1]{3,2,0,1:T(8,128)} %copy.268, f32[2,16,24,124]{3,2,0,1:T(8,128)} %broadcast_in_dim.14), dimensions={3} | concatenate | bytes 14942208 | tf_op jit(solution)/shard_map/concatenate | solution.py:507
  612.5 7.1 collective-permute-done.6
  624.7 3.6 collective-permute-done.7
  633.3 4.1 collective-permute-done.12
  638.3 4.1 collective-permute-done.13
  643.1 4.6 collective-permute-done.14
  648.6 9.3 %add_convert_fusion.3 = bf16[1024,768]{0,1:T(8,128)(2,1)S(1)} fusion(f32[1024,768]{0,1:T(8,128)} %copy-done.4, bf16[1024,3072]{1,0:T(8,128)(2,1)} %get-tuple-element.175, bf16[3072,768]{1,0:T(8,128)(2,1)} %all-gather.9.cloned.1.call-done, f32[768]{0:T(1024)S(1)} %copy-done.48), kind=kOutput, calls=%fused_computation.63 | convolution fusion | flops 4834197504 | bytes 15731712 | tf_op jit(solution)/shard_map/dot_general | solution.py:414
  659.5 3.9 fusion.22
  665.0 49.0 %all-gather.11.cloned.1.call-done = bf16[384,9472]{1,0:T(8,128)(2,1)} async-done(((bf16[24,9472]{1,0:T(8,128)(2,1)}), bf16[384,9472]{1,0:T(8,128)(2,1)}) %all-gather.11.cloned.1.call-update) | async-done | bytes 7274512 | tf_op jit(solution)/shard_map/all_gather | solution.py:525
  714.0 9.2 %convert_element_type.365 = f32[384,9472]{1,0:T(8,128)} convert(bf16[384,9472]{1,0:T(8,128)(2,1)} %all-gather.11.cloned.1.call-done) | non-fusion elementwise | flops 3637248 | bytes 21823488 | tf_op jit(solution)/shard_map/convert_element_type | solution.py:538
  723.1 3.8 slice_reduce_fusion.2
  730.4 7.4 fusion.42
  737.8 6.1 reshape.551
  743.9 3.5 slice.389
  (292 shorter events, 138.5 us)
Async XLA Ops:
  7.2 16.9 %copy-start.16 = (bf16[1024,768]{1,0:T(8,128)(2,1)S(1)}, bf16[1024,768]{1,0:T(8,128)(2,1)}, u32[]{:S(2)}) copy-start(bf16[1024,768]{1,0:T(8,128)(2,1)} %param.39) | copy-start | bytes 4718596
  7.2 17.1 %copy-start.53 = (s32[1,5]{1,0:T(1,128)S(1)}, s32[1,5]{1,0:T(1,128)}, u32[]{:S(2)}) copy-start(s32[1,5]{1,0:T(1,128)} %param.21) | copy-start | bytes 64
  7.2 75.3 %all-gather.5.cloned.1.call-start = ((), (), s32[]{:S(2)}) async-start(), calls=%async_computation.1 | async-start | bytes 3852288 | tf_op jit(solution)/shard_map/all_gather | solution.py:338
  17.1 9.0 %copy-start.28 = (bf16[1024,768]{1,0:T(8,128)(2,1)S(1)}, bf16[1024,768]{1,0:T(8,128)(2,1)}, u32[]{:S(2)}) copy-start(bf16[1024,768]{1,0:T(8,128)(2,1)} %param.20) | copy-start | bytes 4718596
  18.9 174.2 %all-gather.7.cloned.1.call-start = ((), (), s32[]{:S(2)}) async-start(), calls=%async_computation.2 | async-start | bytes 6082560 | tf_op jit(solution)/shard_map/all_gather | solution.py:356
  20.6 221.4 %all-gather.9.cloned.1.call-start = ((), (), s32[]{:S(2)}) async-start(), calls=%async_computation.3 | async-start | bytes 4866048 | tf_op jit(solution)/shard_map/all_gather | solution.py:359
  21.4 573.1 %reduce-scatter.4.cloned.1.call-start = ((), (), s32[]{:S(2)}) async-start(), calls=%async_computation.5 | async-start | bytes 6285312
  26.9 166.2 %copy-start.1 = (bf16[1024,768]{0,1:T(8,128)(2,1)}, bf16[1024,768]{0,1:T(8,128)(2,1)S(1)}, u32[]{:S(2)}) copy-start(bf16[1024,768]{0,1:T(8,128)(2,1)S(1)} %copy.222) | copy-start | bytes 4718596
  27.2 67.4 %copy-start.34 = (f32[1024]{0:T(1024)}, f32[1024]{0:T(1024)S(1)}, u32[]{:S(2)}) copy-start(f32[1024]{0:T(1024)S(1)} %broadcast_multiply_fusion.11) | copy-start | bytes 12292
  27.7 66.9 %copy-start.41 = (f32[1024]{0:T(1024)}, f32[1024]{0:T(1024)S(1)}, u32[]{:S(2)}) copy-start(f32[1024]{0:T(1024)S(1)} %add_rsqrt_fusion.3) | copy-start | bytes 12292
  88.2 105.0 %copy-start.43 = (f32[768]{0:T(1024)}, f32[768]{0:T(1024)S(1)}, u32[]{:S(2)}) copy-start(f32[768]{0:T(1024)S(1)} %get-tuple-element.159) | copy-start | bytes 9220
  88.2 105.0 %copy-start.51 = (f32[768]{0:T(1024)}, f32[768]{0:T(1024)S(1)}, u32[]{:S(2)}) copy-start(f32[768]{0:T(1024)S(1)} %get-tuple-element.158) | copy-start | bytes 9220
  105.7 68.3 %copy-start.10 = (bf16[1024,768]{0,1:T(8,128)(2,1)}, bf16[1024,768]{0,1:T(8,128)(2,1)S(1)}, u32[]{:S(2)}) copy-start(bf16[1024,768]{0,1:T(8,128)(2,1)S(1)} %copy.235) | copy-start | bytes 4718596
  190.9 6.5 copy-start.45
  197.4 39.9 %copy-start.4 = (f32[1024,768]{0,1:T(8,128)}, f32[1024,768]{0,1:T(8,128)S(1)}, u32[]{:S(2)}) copy-start(f32[1024,768]{0,1:T(8,128)S(1)} %get-tuple-element.188) | copy-start | bytes 9437188
  242.1 40.9 %slice-start.2 = ((s8[5898240]{0:T(1024)(128)(4,1)}), s8[1703936]{0:T(1024)(128)(4,1)S(1)}, s32[]{:S(2)}) async-start(s8[5898240]{0:T(1024)(128)(4,1)} %bitcast.134), calls=%async_computation.8 | async-start | bytes 3407872
  257.5 18.4 %copy-start.5 = (f32[1024,768]{0,1:T(8,128)S(1)}, f32[1024,768]{0,1:T(8,128)}, u32[]{:S(2)}) copy-start(f32[1024,768]{0,1:T(8,128)} %copy-done.4) | copy-start | bytes 9437188
  257.5 25.5 %slice-start.3 = ((s8[5898240]{0:T(1024)(128)(4,1)}), s8[4194304]{0:T(1024)(128)(4,1)S(1)}, s32[]{:S(2)}) async-start(s8[5898240]{0:T(1024)(128)(4,1)} %bitcast.134), calls=%async_computation.9 | async-start | bytes 8388608
  298.5 7.4 copy-start.13
  305.9 7.3 copy-start.18
  338.1 11.7 %slice-start = ((s8[6094848]{0:T(1024)(128)(4,1)}), s8[4194304]{0:T(1024)(128)(4,1)S(1)}, s32[]{:S(2)}) async-start(s8[6094848]{0:T(1024)(128)(4,1)} %bitcast.97), calls=%async_computation.6 | async-start | bytes 8388608
  338.1 11.7 %slice-start.1 = ((s8[6094848]{0:T(1024)(128)(4,1)}), s8[1900544]{0:T(1024)(128)(4,1)S(1)}, s32[]{:S(2)}) async-start(s8[6094848]{0:T(1024)(128)(4,1)} %bitcast.97), calls=%async_computation.7 | async-start | bytes 3801088
  344.0 130.9 %collective-permute-start = (bf16[1536,768]{1,0:T(8,128)(2,1)}, bf16[1536,768]{1,0:T(8,128)(2,1)}, u32[]{:S(2)}, u32[]{:S(2)}) collective-permute-start(bf16[1536,768]{1,0:T(8,128)(2,1)} %bitcast.47), channel_id=1, source_target_pairs={{0,2},{2,0},{4,6},{6,4},{8,10},{10,8},{12,14},{14,12},{16,18},{18,... | collective-permute-start | bytes 7077896 | tf_op jit(solution)/shard_map/ppermute | solution.py:286
  352.8 361.2 %all-gather.11.cloned.1.call-start = ((), (), s32[]{:S(2)}) async-start(), calls=%async_computation.4 | async-start | bytes 7729152 | tf_op jit(solution)/shard_map/all_gather | solution.py:525
  474.9 7.7 %copy-start.23 = (bf16[1024,12,64]{0,2,1:T(8,128)(2,1)S(1)}, bf16[1024,12,64]{0,2,1:T(8,128)(2,1)}, u32[]{:S(2)}) copy-start(bf16[1024,12,64]{0,2,1:T(8,128)(2,1)} %copy.258) | copy-start | bytes 4718596
  474.9 7.7 %copy-start.27 = (bf16[768,2432]{1,0:T(8,128)(2,1)S(1)}, bf16[768,2432]{1,0:T(8,128)(2,1)}, u32[]{:S(2)}) copy-start(bf16[768,2432]{1,0:T(8,128)(2,1)} %all-gather.5.cloned.1.call-done) | copy-start | bytes 11206660
  481.2 20.8 %collective-permute-start.1 = (bf16[768,768]{1,0:T(8,128)(2,1)}, bf16[768,768]{1,0:T(8,128)(2,1)}, u32[]{:S(2)}, u32[]{:S(2)}) collective-permute-start(bf16[768,768]{1,0:T(8,128)(2,1)} %select_convert_fusion.1), channel_id=1, source_target_pairs={{0,4},{2,6},{4,0},{6,2},{8,12},{10,14},{12,8},{14,10},{16,20},{18,... | collective-permute-start | bytes 3538952 | tf_op jit(solution)/shard_map/ppermute | solution.py:286
  501.9 28.6 %copy-start.22 = (bf16[12,64,1024]{2,1,0:T(8,128)(2,1)S(1)}, bf16[12,64,1024]{2,1,0:T(8,128)(2,1)}, u32[]{:S(2)}) copy-start(bf16[12,64,1024]{2,1,0:T(8,128)(2,1)} %convert.82) | copy-start | bytes 4718596
  501.9 28.6 %copy-start.24 = (bf16[1024,12,64]{0,2,1:T(8,128)(2,1)S(1)}, bf16[1024,12,64]{0,2,1:T(8,128)(2,1)}, u32[]{:S(2)}) copy-start(bf16[1024,12,64]{0,2,1:T(8,128)(2,1)} %copy.258) | copy-start | bytes 4718596
  505.3 33.0 %collective-permute-start.2 = (bf16[384,768]{1,0:T(8,128)(2,1)S(1)}, bf16[384,768]{1,0:T(8,128)(2,1)S(1)}, u32[]{:S(2)}, u32[]{:S(2)}) collective-permute-start(bf16[384,768]{1,0:T(8,128)(2,1)S(1)} %select_convert_fusion.4), channel_id=1, source_target_pairs={{0,8},{2,10},{4,12},{6,14},{8,0},{10,2},{12,4},{14,6},{16,24},{18,... | collective-permute-start | bytes 1769480 | tf_op jit(solution)/shard_map/ppermute | solution.py:286
  534.7 36.5 %copy-start.6 = (f32[1024,768]{0,1:T(8,128)S(1)}, f32[1024,768]{0,1:T(8,128)}, u32[]{:S(2)}) copy-start(f32[1024,768]{0,1:T(8,128)} %copy.259) | copy-start | bytes 9437188
  538.5 37.5 %collective-permute-start.3 = (bf16[192,768]{1,0:T(8,128)(2,1)S(1)}, bf16[192,768]{1,0:T(8,128)(2,1)}, u32[]{:S(2)}, u32[]{:S(2)}) collective-permute-start(bf16[192,768]{1,0:T(8,128)(2,1)S(1)} %select_convert_fusion.7), channel_id=1, source_target_pairs={{0,1},{1,0},{2,3},{3,2},{4,5},{5,4},{6,7},{7,6},{8,9},{9,8},{10,11... | collective-permute-start | bytes 884744 | tf_op jit(solution)/shard_map/ppermute | solution.py:286
  577.8 7.2 copy-start.29
  577.8 7.2 copy-start.30
  577.8 15.9 %collective-permute-start.4 = (bf16[96,768]{1,0:T(8,128)(2,1)}, bf16[96,768]{1,0:T(8,128)(2,1)S(1)}, u32[]{:S(2)}, u32[]{:S(2)}) collective-permute-start(bf16[96,768]{1,0:T(8,128)(2,1)} %select_convert_fusion.10), channel_id=1, source_target_pairs={{0,16},{2,18},{4,20},{6,22},{8,24},{10,26},{12,28},{14,30},{16,0},... | collective-permute-start | bytes 442376 | tf_op jit(solution)/shard_map/ppermute | solution.py:286
  600.4 5.1 collective-permute-start.5
  601.8 6.6 collective-permute-start.10
  607.4 12.1 %collective-permute-start.6 = (bf16[192,1152]{1,0:T(8,128)(2,1)S(1)}, bf16[192,1152]{1,0:T(8,128)(2,1)S(1)}, u32[]{:S(2)}, u32[]{:S(2)}) collective-permute-start(bf16[192,1152]{1,0:T(8,128)(2,1)S(1)} %select_convert_fusion.6), channel_id=1, source_target_pairs={{0,4},{2,6},{4,0},{6,2},{8,12},{10,14},{12,8},{14,10},{16,20},{18,... | collective-permute-start | bytes 1327112 | tf_op jit(solution)/shard_map/ppermute | solution.py:286
  610.0 14.6 %collective-permute-start.11 = (bf16[192,1280]{1,0:T(8,128)(2,1)S(1)}, bf16[192,1280]{1,0:T(8,128)(2,1)S(1)}, u32[]{:S(2)}, u32[]{:S(2)}) collective-permute-start(bf16[192,1280]{1,0:T(8,128)(2,1)S(1)} %select_convert_fusion.5), channel_id=1, source_target_pairs={{0,8},{2,10},{4,12},{6,14},{8,0},{10,2},{12,4},{14,6},{16,24},{18,... | collective-permute-start | bytes 1474568 | tf_op jit(solution)/shard_map/ppermute | solution.py:286
  619.7 8.6 %collective-permute-start.7 = (bf16[96,1152]{1,0:T(8,128)(2,1)S(1)}, bf16[96,1152]{1,0:T(8,128)(2,1)S(1)}, u32[]{:S(2)}, u32[]{:S(2)}) collective-permute-start(bf16[96,1152]{1,0:T(8,128)(2,1)S(1)} %select_convert_fusion.9), channel_id=1, source_target_pairs={{0,8},{2,10},{4,12},{6,14},{8,0},{10,2},{12,4},{14,6},{16,24},{18,... | collective-permute-start | bytes 663560 | tf_op jit(solution)/shard_map/ppermute | solution.py:286
  628.4 19.3 %copy-start.32 = (bf16[24,3072]{1,0:T(8,128)(2,1)S(1)}, bf16[24,3072]{1,0:T(8,128)(2,1)}, u32[]{:S(2)}) copy-start(bf16[24,3072]{1,0:T(8,128)(2,1)} %reshape.536) | copy-start | bytes 442372
  628.4 19.3 %copy-start.33 = (bf16[24,3968]{1,0:T(8,128)(2,1)S(1)}, bf16[24,3968]{1,0:T(8,128)(2,1)}, u32[]{:S(2)}) copy-start(bf16[24,3968]{1,0:T(8,128)(2,1)} %reduce-scatter.4.cloned.1.call-done) | copy-start | bytes 571396
  628.5 4.8 collective-permute-start.8
  630.6 18.0 %copy-start.48 = (f32[768]{0:T(1024)S(1)}, f32[768]{0:T(1024)}, u32[]{:S(2)}) copy-start(f32[768]{0:T(1024)} %get-tuple-element.154) | copy-start | bytes 9220
  630.6 6.8 collective-permute-start.12
  637.5 4.9 collective-permute-start.13
  637.9 5.2 collective-permute-start.9
  642.5 5.2 collective-permute-start.14
  (30 other events, 104.0 us)
Sparse Core Ops, SparseCore 0:
  19.1 63.4 all-gather.4
  86.0 66.3 all-gather.6
  155.4 62.2 all-gather.8
  352.9 123.9 reduce-scatter.3
  648.7 65.2 all-gather.10

commit v5 on v4

--- a/solution.py
+++ b/solution.py
@@ -20,6 +20,7 @@
 
 CHUNK = 128
 QBLOCK = 512
+HEAD_GROUP = 2
 
 
 def _row_setup(segq_ref, i, tq):
@@ -260,7 +261,7 @@
     return first, second
 
 
-def hypercube_reduce_scatter(x, order, group_size, shard_size):
+def hypercube_reduce_scatter(x, order, group_size, shard_size, ties=()):
     total = group_size * shard_size
     levels = total.bit_length() - 1
     rows, cols = x.shape
@@ -276,7 +277,7 @@
         .transpose(axes + [levels, levels + 1])
         .reshape(rows, cols)
     )
-    for axis, b in order:
+    for step, (axis, b) in enumerate(order):
         size = group_size if axis == "group" else shard_size
         half = cur.shape[0] // 2
         mine = (lax.axis_index(axis) >> b) & 1
@@ -285,7 +286,10 @@
         send = jnp.where(mine == 1, low, high).astype(jnp.bfloat16)
         got = lax.ppermute(send, axis, [(j, j ^ (1 << b)) for j in range(size)])
         cur = keep + got.astype(jnp.float32)
-    return cur
+        if step < len(ties):
+            cur, tied = lax.optimization_barrier((cur, ties[step]))
+            ties = ties[:step] + (tied,) + ties[step + 1 :]
+    return cur, ties
 
 
 def per_device(
@@ -476,15 +480,27 @@
         (ffn_pack, shrink_in, grad_att_low)
     )
     ffn_part = grad_rows_reduce(ffn_pack, group_size, shard_size)
-    shrink_part = hypercube_reduce_scatter(shrink_in, order_a, group_size, shard_size)
+    grad_att_low = grad_att_low.astype(jnp.bfloat16)
+    group_inputs = []
+    for r in range(row_count):
+        grad_heads = heads_major(grad_att_low[r * length : (r + 1) * length])
+        for h in range(0, HEADS, HEAD_GROUP):
+            group_inputs.append(
+                tuple(x[h : h + HEAD_GROUP] for x in row_heads[r])
+                + (grad_heads[h : h + HEAD_GROUP],)
+            )
+    shrink_part, tied = hypercube_reduce_scatter(
+        shrink_in, order_a, group_size, shard_size, tuple(group_inputs[1:])
+    )
+    group_inputs = group_inputs[:1] + list(tied)
     grad_rows = []
+    per_row = HEADS // HEAD_GROUP
     for r in range(row_count):
-        parts = attention_backward(
-            *row_heads[r],
-            heads_major(grad_att_low[r * length : (r + 1) * length]),
-            segments[r],
-            row_starts[r],
-        )
+        pieces = [
+            attention_backward(*group_inputs[r * per_row + j], segments[r], row_starts[r])
+            for j in range(per_row)
+        ]
+        parts = [jnp.concatenate([p[j] for p in pieces], axis=0) for j in range(3)]
         grad_rows.append(jnp.concatenate([tokens_major(p) for p in parts], axis=1))
     grad_qkv = jnp.concatenate(grad_rows, axis=0).astype(jnp.bfloat16)
     grad_qkv_wide = grad_qkv.astype(jnp.float32)
@@ -516,31 +532,29 @@
         (ffn_part, shrink_part, attn_pack)
     )
     split = (attn_pack.shape[1] // 256) * 128
-    attn_left = hypercube_reduce_scatter(
-        attn_pack[:, :split], order_a, group_size, shard_size
-    )
-    attn_right = hypercube_reduce_scatter(
-        attn_pack[:, split:], order_b, group_size, shard_size
-    )
-    both = lax.all_gather(
+    attn_left, _ = hypercube_reduce_scatter(attn_pack[:, :split], order_a, group_size, shard_size)
+    attn_right, _ = hypercube_reduce_scatter(attn_pack[:, split:], order_b, group_size, shard_size)
+    ffn_both = lax.all_gather(
         jnp.concatenate(
-            [
-                ffn_part,
-                shrink_part.astype(jnp.bfloat16).reshape(n, ratio * model_width),
-                attn_left.astype(jnp.bfloat16),
-                attn_right.astype(jnp.bfloat16),
-            ],
+            [ffn_part, shrink_part.astype(jnp.bfloat16).reshape(n, ratio * model_width)],
             axis=1,
         ),
         "group",
         axis=0,
         tiled=True,
     ).astype(jnp.float32)
+    attn_back = lax.all_gather(
+        jnp.concatenate(
+            [attn_left.astype(jnp.bfloat16), attn_right.astype(jnp.bfloat16)], axis=1
+        ),
+        "group",
+        axis=0,
+        tiled=True,
+    ).astype(jnp.float32)
     ffn_cols = ffn_pack.shape[1]
-    ffn_back = both[:, :ffn_cols]
-    shrink_back = both[:, ffn_cols : ffn_cols + ratio * model_width]
-    attn_back = both[:, ffn_cols + ratio * model_width :]
-    half = both.shape[0]
+    ffn_back = ffn_both[:, :ffn_cols]
+    shrink_back = ffn_both[:, ffn_cols:]
+    half = ffn_both.shape[0]
     expand_out = ffn_back[:, :wide_width]
     proj_out = ffn_back[:, wide_width : wide_width + model_width]
     shrink_out = shrink_back.reshape(half * ratio, model_width)

time: 765 us -> 840 us (1.098)
  local copies, waits for them, and re-layouts: 151 us -> 173 us
  other arithmetic: 95.2 us -> 111 us
  Pallas kernels: 166 us -> 181 us
  waiting for transfers between devices: 135 us -> 147 us
    unnamed x2 -> x17, other arithmetic: 0.01 us -> 26.1 us
    all_gather x0 -> x1, waiting for transfers between devices: none -> 24.1 us  [per_device(): lax.all_gather(jnp.concatenate([attn_left.astype(jnp.bfloat16), attn_righ...]
    optimization_barrier x0 -> x15, local copies, waits for them, and re-layouts: none -> 20.9 us  [hypercube_reduce_scatter(): cur, tied = lax.optimization_barrier((cur, ties[step]))]
    ppermute x15, waiting for transfers between devices: 32 us -> 15.9 us  [hypercube_reduce_scatter(): got = lax.ppermute(send, axis, [(j, j ^ 1 << b) for j in range(size)])]
    pallas_call x1 -> x6, Pallas kernels: 101 us -> 115 us  [attention_backward(): pl.pallas_call(_bwd_kernel, out_shape=(jax.ShapeDtypeStruct((heads, lengt...]
    slice x1 -> x7, local copies, waits for them, and re-layouts: 7.4 us -> 17 us  [the longest x1 7.4 us: per_device(): shrink_back = ffn_both[:, ffn_cols:]]
  transfers between devices with their start and end apart: 20 -> 21, of which waited for: 13 -> 10; matrix products, arithmetic and copies ran while one was open for 26% -> 30% of each run, Pallas kernels for 22% -> 22%
where the time goes in v5:
time: 840 us; the launch traced here: 830 us
  Pallas kernels  181 us (22%)
  local copies, waits for them, and re-layouts  173 us (21%)
  waiting for transfers between devices  147 us (18%)
  matrix products  118 us (14%)
  other arithmetic  111 us (13%)
  starting transfers between devices  85.1 us (10%)
  between operations  15.5 us (2%)
    pallas_call x6, Pallas kernels, attention_backward(): pl.pallas_call(_bwd_kernel, out_shape=(jax.ShapeDtypeStruct((heads, lengt...  115 us
    ppermute x15, starting transfers between devices, hypercube_reduce_scatter(): got = lax.ppermute(send, axis, [(j, j ^ 1 << b) for j in range(size)])  84.9 us
    pallas_call x1, Pallas kernels, attention_forward(): pl.pallas_call(_fwd_kernel, out_shape=jax.ShapeDtypeStruct((heads, length...  65.4 us
    all_gather x1, waiting for transfers between devices, per_device(): lax.all_gather(jnp.concatenate([ffn_part, shrink_part.astype(jnp.bfloat16...  53.2 us
    all_gather x1, waiting for transfers between devices, per_device(): lax.all_gather(first_pack, ('group', 'shard'), axis=0, tiled=True)  53 us
    dot_general x1, matrix products, per_device(): jnp.dot(second_low, expand_full, preferred_element_type=jnp.float32)  39.5 us
    unnamed x17, other arithmetic  26.1 us
    all_gather x1, waiting for transfers between devices, per_device(): lax.all_gather(jnp.concatenate([attn_left.astype(jnp.bfloat16), attn_righ...  24.1 us
  transfers between devices with their start and end apart: 21, of which 10 were waited for; matrix products, arithmetic and copies ran while one was open for 30% of the time, Pallas kernels for 22%

profile of v5, /device:TPU:0, one launch (start us, length us, event | category | flops | bytes accessed | tf_op | source)
XLA Modules:
  0.0 830.0 jit_solution(16452417130694513004)
XLA Ops:
  29.5 53.0 %all-gather.6.cloned.1.call-done = bf16[768,2432]{1,0:T(8,128)(2,1)} async-done(((bf16[24,2432]{1,0:T(8,128)(2,1)}), bf16[768,2432]{1,0:T(8,128)(2,1)}) %all-gather.6.cloned.1.call-update) | async-done | bytes 3735568 | tf_op jit(solution)/shard_map/all_gather | solution.py:342
  84.0 4.2 convert_reduce_fusion.1
  88.2 6.4 add_convert_fusion.2
  108.5 65.4 %shard_map.339 = f32[12,1024,64]{2,1,0:T(8,128)} custom-call(s32[2]{0:T(128)} %and_select_fusion.lo_ref, bf16[12,1024,64]{2,1,0:T(8,128)(2,1)} %copy.311.q_ref, bf16[12,64,1024]{2,1,0:T(8,128)(2,1)} %bitcast.144, bf16[12,1024,64]{2,1,0:T(8,128)(2,1)} %copy.312.v_ref, s32[1024,1]{1,0:T(8,128)} %copy.313.segq_ref, s32[1,1024]{1,0:T(1,128)} %bitcast.187), custom_call_target="tpu_custom_call" | custom-call | flops 1610612736 | bytes 6291456 | tf_op jit(solution)/shard_map/pallas_call | solution.py:128
  173.9 6.1 copy.314
  180.0 3.7 copy.315
  187.0 3.8 multiply_reduce_fusion.4
  193.1 4.2 fusion.49
  197.7 39.5 %fusion.40 = (f32[1024]{0:T(1024)S(1)}, f32[1024,3072]{1,0:T(8,128)S(1)}, f32[1024,3072]{1,0:T(8,128)}, f32[1024,3072]{1,0:T(8,128)}) fusion(f32[3072]{0:T(1024)S(1)} %reshape.560, bf16[768,3840]{1,0:T(8,128)(2,1)} %all-gather.8.cloned.1.call-done, f32[1024,768]{0,1:T(8,128)S(1)} %get-tuple-element.295, f32[768]{0:T(1024)S(1)} %get-tuple-element.235, ...), kind=kOutput, calls=%fused_computation.189 | convolution fusion | flops 5043387392 | bytes 45643776 | tf_op jit(solution)/shard_map/dot_general | solution.py:408
  242.0 15.4 %multiply_reduce_fusion = (bf16[3072]{0:T(1024)(128)(2,1)S(1)}, f32[1024]{0:T(1024)S(1)}, f32[1024]{0:T(1024)S(1)}, bf16[3072]{0:T(1024)(128)(2,1)S(1)}, bf16[1024,3072]{1,0:T(8,128)(2,1)}, /*index=5*/f32[1024,3072]{1,0:T(8,128)}) fusion(f32[1024,3072]{1,0:T(8,128)} %copy-done, f32[1024]{0:T(1024)S(1)} %add_rsqrt_fusion, ...), kind=kOutput, calls=%fused_computation.3 | convolution fusion | flops 4869578752 | bytes 37801984 | tf_op jit(solution)/shard_map/td,fd->tf/dot_general | solution.py:427
  257.4 18.3 %fusion.39 = (bf16[3072]{0:T(1024)(128)(2,1)S(1)}, bf16[1024,3072]{1,0:T(8,128)(2,1)S(1)}) fusion(f32[1024,3072]{1,0:T(8,128)} %get-tuple-element.254, f32[1024]{0:T(1024)S(1)} %get-tuple-element.303, f32[1024,3072]{1,0:T(8,128)} %copy-done, f32[1024]{0:T(1024)S(1)} %broadcast_multiply_fusion.2, f32[1024]{0:T(1024)S(1)} %get-tuple-element.304, ...), kind=kLoop, calls=%fused_computation.188 | loop fusion | flops 72348672 | bytes 56670208 | tf_op jit(solution)/shard_map/reduce_sum | solution.py:434
  275.7 7.1 convolution_convert_fusion
  282.9 6.8 fusion.50
  289.7 3.6 copy.318
  305.9 4.7 multiply_reduce_fusion.5
  313.2 7.5 fusion.52
  320.7 4.7 copy.327
  327.4 10.5 %concatenate.66 = bf16[768,3968]{1,0:T(8,128)(2,1)} concatenate(bf16[768,3072]{1,0:T(8,128)(2,1)} %convolution_convert_fusion, bf16[768,768]{1,0:T(8,128)(2,1)} %convolution_convert_fusion.1, bf16[768,1]{1,0:T(8,128)(2,1)S(1)} %reshape.573, bf16[768,1]{1,0:T(8,128)(2,1)} %reshape.574, bf16[768,1]{1,0:T(8,128)(2,1)S(1)} %copy-done.34, bf16[768,4]{1,0:T(8,128)(2,1)} %reshape.520, ...), dimensions={1} | concatenate | bytes 12189696 | tf_op jit(solution)/shard_map/concatenate | solution.py:470
  337.8 4.2 select_convert_fusion
  343.6 5.8 collective-permute-start
  360.7 4.4 slice_select_fusion
  367.6 19.1 %shard_map.340 = (f32[2,1024,64]{2,1,0:T(8,128)}, f32[2,64,1024]{2,1,0:T(8,128)}, f32[2,64,1024]{2,1,0:T(8,128)}) custom-call(s32[2]{0:T(128)} %and_select_fusion.lo_ref, bf16[2,1024,64]{2,1,0:T(8,128)(2,1)} %copy.329.q_ref, bf16[2,64,1024]{2,1,0:T(8,128)(2,1)} %get-tuple-element.288.qt_ref, bf16[2,1024,64]{2,1,0:T(8,128)(2,1)} %copy.330.k_ref, ...), custom_call_target="tpu_custom_call" | custom-call | flops 671088640 | bytes 2097152 | tf_op jit(solution)/shard_map/pallas_call | solution.py:156
  388.7 3.7 bitcast_add_fusion
  408.2 19.5 %shard_map.341 = (f32[2,1024,64]{2,1,0:T(8,128)}, f32[2,64,1024]{2,1,0:T(8,128)}, f32[2,64,1024]{2,1,0:T(8,128)}) custom-call(s32[2]{0:T(128)} %and_select_fusion.lo_ref, bf16[2,1024,64]{2,1,0:T(8,128)(2,1)} %copy.335.q_ref, bf16[2,64,1024]{2,1,0:T(8,128)(2,1)} %bitcast.171, bf16[2,1024,64]{2,1,0:T(8,128)(2,1)} %copy.336.k_ref, ...), custom_call_target="tpu_custom_call" | custom-call | flops 671088640 | bytes 2097152 | tf_op jit(solution)/shard_map/pallas_call | solution.py:156
  434.4 3.4 convert_add_fusion.1
  440.9 17.8 %collective-permute-start.2 = (bf16[384,768]{1,0:T(8,128)(2,1)S(1)}, bf16[384,768]{1,0:T(8,128)(2,1)}, u32[]{:S(2)}, u32[]{:S(2)}) collective-permute-start(bf16[384,768]{1,0:T(8,128)(2,1)S(1)} %select_convert_fusion.4), channel_id=1, source_target_pairs={{0,8},{2,10},{4,12},{6,14},{8,0},{10,2},{12,4},{14,6},{16,24},{18,... | collective-permute-start | bytes 1769480 | tf_op jit(solution)/shard_map/ppermute | solution.py:287
  458.7 19.1 %shard_map.342 = (f32[2,1024,64]{2,1,0:T(8,128)}, f32[2,64,1024]{2,1,0:T(8,128)}, f32[2,64,1024]{2,1,0:T(8,128)}) custom-call(s32[2]{0:T(128)} %and_select_fusion.lo_ref, bf16[2,1024,64]{2,1,0:T(8,128)(2,1)} %copy.339.q_ref, bf16[2,64,1024]{2,1,0:T(8,128)(2,1)} %bitcast.169, bf16[2,1024,64]{2,1,0:T(8,128)(2,1)} %copy.340.k_ref, ...), custom_call_target="tpu_custom_call" | custom-call | flops 671088640 | bytes 2097152 | tf_op jit(solution)/shard_map/pallas_call | solution.py:156
  490.7 16.4 %collective-permute-start.3 = (bf16[192,768]{1,0:T(8,128)(2,1)S(1)}, bf16[192,768]{1,0:T(8,128)(2,1)S(1)}, u32[]{:S(2)}, u32[]{:S(2)}) collective-permute-start(bf16[192,768]{1,0:T(8,128)(2,1)S(1)} %select_convert_fusion.7), channel_id=1, source_target_pairs={{0,1},{1,0},{2,3},{3,2},{4,5},{5,4},{6,7},{7,6},{8,9},{9,8},{10,11... | collective-permute-start | bytes 884744 | tf_op jit(solution)/shard_map/ppermute | solution.py:287
  507.1 19.1 %shard_map.343 = (f32[2,1024,64]{2,1,0:T(8,128)}, f32[2,64,1024]{2,1,0:T(8,128)}, f32[2,64,1024]{2,1,0:T(8,128)}) custom-call(s32[2]{0:T(128)} %and_select_fusion.lo_ref, bf16[2,1024,64]{2,1,0:T(8,128)(2,1)} %copy.343.q_ref, bf16[2,64,1024]{2,1,0:T(8,128)(2,1)} %bitcast.167, bf16[2,1024,64]{2,1,0:T(8,128)(2,1)} %copy.344.k_ref, ...), custom_call_target="tpu_custom_call" | custom-call | flops 671088640 | bytes 2097152 | tf_op jit(solution)/shard_map/pallas_call | solution.py:156
  535.2 19.2 %shard_map.344 = (f32[2,1024,64]{2,1,0:T(8,128)}, f32[2,64,1024]{2,1,0:T(8,128)}, f32[2,64,1024]{2,1,0:T(8,128)}) custom-call(s32[2]{0:T(128)} %and_select_fusion.lo_ref, bf16[2,1024,64]{2,1,0:T(8,128)(2,1)} %copy.347.q_ref, bf16[2,64,1024]{2,1,0:T(8,128)(2,1)} %bitcast.165, bf16[2,1024,64]{2,1,0:T(8,128)(2,1)} %copy.348.k_ref, ...), custom_call_target="tpu_custom_call" | custom-call | flops 671088640 | bytes 2097152 | tf_op jit(solution)/shard_map/pallas_call | solution.py:156
  563.9 19.1 %shard_map.345 = (f32[2,1024,64]{2,1,0:T(8,128)}, f32[2,64,1024]{2,1,0:T(8,128)}, f32[2,64,1024]{2,1,0:T(8,128)}) custom-call(s32[2]{0:T(128)} %and_select_fusion.lo_ref, bf16[2,1024,64]{2,1,0:T(8,128)(2,1)} %copy.351.q_ref, bf16[2,64,1024]{2,1,0:T(8,128)(2,1)} %bitcast.163, bf16[2,1024,64]{2,1,0:T(8,128)(2,1)} %copy.352.k_ref, ...), custom_call_target="tpu_custom_call" | custom-call | flops 671088640 | bytes 2097152 | tf_op jit(solution)/shard_map/pallas_call | solution.py:156
  591.8 8.6 %fusion.51 = (f32[768]{0:T(1024)}, f32[1024,768]{1,0:T(8,128)}) fusion(bf16[768,2432]{1,0:T(8,128)(2,1)} %all-gather.6.cloned.1.call-done, bf16[1024,768]{0,1:T(8,128)(2,1)S(1)} %bitcast.173, bf16[1024,768]{0,1:T(8,128)(2,1)} %bitcast.176, bf16[1024,768]{0,1:T(8,128)(2,1)S(1)} %bitcast.153), kind=kOutput, calls=%fused_computation.199 | convolution fusion | flops 3638820096 | bytes 11406336 | tf_op jit(solution)/shard_map/te,de->td/dot_general | solution.py:512
  600.4 3.7 copy.356
  604.1 6.0 fusion.35
  610.1 3.7 copy.359
  624.0 8.7 %concatenate.76 = f32[2,16,24,2432]{3,2,0,1:T(8,128)} concatenate(f32[2,16,24,2304]{3,2,0,1:T(8,128)} %copy.359, f32[2,16,24,1]{3,2,0,1:T(8,128)S(1)} %copy.360, f32[2,16,24,1]{3,2,0,1:T(8,128)S(1)} %copy-done.33, f32[2,16,24,1]{3,2,0,1:T(8,128)S(1)} %copy.362, f32[2,16,24,1]{3,2,0,1:T(8,128)S(1)} %copy.363, f32[2,16,24,124]{3,2,0,1:T(8,128)S(1)} %broadcast_in_dim.14), dimensions={3} | concatenate | bytes 14942208 | tf_op jit(solution)/shard_map/concatenate | solution.py:523
  640.6 4.1 collective-permute-start.6
  645.0 10.8 %collective-permute-start.11 = (bf16[192,1280]{1,0:T(8,128)(2,1)S(1)}, bf16[192,1280]{1,0:T(8,128)(2,1)S(1)}, u32[]{:S(2)}, u32[]{:S(2)}) collective-permute-start(bf16[192,1280]{1,0:T(8,128)(2,1)S(1)} %select_convert_fusion.5), channel_id=1, source_target_pairs={{0,8},{2,10},{4,12},{6,14},{8,0},{10,2},{12,4},{14,6},{16,24},{18,... | collective-permute-start | bytes 1474568 | tf_op jit(solution)/shard_map/ppermute | solution.py:287
  655.9 10.9 %collective-permute-start.7 = (bf16[96,1152]{1,0:T(8,128)(2,1)S(1)}, bf16[96,1152]{1,0:T(8,128)(2,1)S(1)}, u32[]{:S(2)}, u32[]{:S(2)}) collective-permute-start(bf16[96,1152]{1,0:T(8,128)(2,1)S(1)} %select_convert_fusion.9), channel_id=1, source_target_pairs={{0,8},{2,10},{4,12},{6,14},{8,0},{10,2},{12,4},{14,6},{16,24},{18,... | collective-permute-start | bytes 663560 | tf_op jit(solution)/shard_map/ppermute | solution.py:287
  667.8 4.2 collective-permute-done.7
  672.2 9.7 %collective-permute-start.8 = (bf16[48,1152]{1,0:T(8,128)(2,1)S(1)}, bf16[48,1152]{1,0:T(8,128)(2,1)S(1)}, u32[]{:S(2)}, u32[]{:S(2)}) collective-permute-start(bf16[48,1152]{1,0:T(8,128)(2,1)S(1)} %select_convert_fusion.12), channel_id=1, source_target_pairs={{0,1},{1,0},{2,3},{3,2},{4,5},{5,4},{6,7},{7,6},{8,9},{9,8},{10,11... | collective-permute-start | bytes 331784 | tf_op jit(solution)/shard_map/ppermute | solution.py:287
  684.6 4.2 collective-permute-done.12
  700.9 9.1 %add_convert_fusion.3 = bf16[1024,768]{0,1:T(8,128)(2,1)S(1)} fusion(f32[1024,768]{0,1:T(8,128)} %copy-done.4, bf16[1024,3072]{1,0:T(8,128)(2,1)} %get-tuple-element.255, bf16[3072,768]{1,0:T(8,128)(2,1)} %all-gather.10.cloned.1.call-done, f32[768]{0:T(1024)S(1)} %copy-done.52), kind=kOutput, calls=%fused_computation.62 | convolution fusion | flops 4834197504 | bytes 15731712 | tf_op jit(solution)/shard_map/dot_general | solution.py:418
  711.6 3.9 fusion.22
  717.0 24.1 %all-gather.12.cloned.1.call-done = bf16[384,2432]{1,0:T(8,128)(2,1)} async-done(((bf16[24,2432]{1,0:T(8,128)(2,1)}), bf16[384,2432]{1,0:T(8,128)(2,1)}) %all-gather.12.cloned.1.call-update) | async-done | bytes 1867792 | tf_op jit(solution)/shard_map/all_gather | solution.py:546
  746.2 53.2 %all-gather.14.cloned.1.call-done = bf16[384,7040]{1,0:T(8,128)(2,1)} async-done(((bf16[24,7040]{1,0:T(8,128)(2,1)}), bf16[384,7040]{1,0:T(8,128)(2,1)}) %all-gather.14.cloned.1.call-update) | async-done | bytes 5406736 | tf_op jit(solution)/shard_map/all_gather | solution.py:537
  807.3 7.4 fusion.42
  814.7 6.1 reshape.551
  (345 shorter events, 200.8 us)
Async XLA Ops:
  7.2 16.8 %copy-start.16 = (bf16[1024,768]{1,0:T(8,128)(2,1)S(1)}, bf16[1024,768]{1,0:T(8,128)(2,1)}, u32[]{:S(2)}) copy-start(bf16[1024,768]{1,0:T(8,128)(2,1)} %param.39) | copy-start | bytes 4718596
  7.2 17.1 %copy-start.57 = (s32[1,5]{1,0:T(1,128)S(1)}, s32[1,5]{1,0:T(1,128)}, u32[]{:S(2)}) copy-start(s32[1,5]{1,0:T(1,128)} %param.21) | copy-start | bytes 64
  7.2 75.3 %all-gather.6.cloned.1.call-start = ((), (), s32[]{:S(2)}) async-start(), calls=%async_computation.1 | async-start | bytes 3852288 | tf_op jit(solution)/shard_map/all_gather | solution.py:342
  17.1 9.0 %copy-start.32 = (bf16[1024,768]{1,0:T(8,128)(2,1)S(1)}, bf16[1024,768]{1,0:T(8,128)(2,1)}, u32[]{:S(2)}) copy-start(bf16[1024,768]{1,0:T(8,128)(2,1)} %param.20) | copy-start | bytes 4718596
  18.9 174.1 %all-gather.8.cloned.1.call-start = ((), (), s32[]{:S(2)}) async-start(), calls=%async_computation.2 | async-start | bytes 6082560 | tf_op jit(solution)/shard_map/all_gather | solution.py:360
  20.6 221.4 %all-gather.10.cloned.1.call-start = ((), (), s32[]{:S(2)}) async-start(), calls=%async_computation.3 | async-start | bytes 4866048 | tf_op jit(solution)/shard_map/all_gather | solution.py:363
  21.4 611.4 %reduce-scatter.4.cloned.1.call-start = ((), (), s32[]{:S(2)}) async-start(), calls=%async_computation.6 | async-start | bytes 6285312
  26.9 166.2 %copy-start.1 = (bf16[1024,768]{0,1:T(8,128)(2,1)}, bf16[1024,768]{0,1:T(8,128)(2,1)S(1)}, u32[]{:S(2)}) copy-start(bf16[1024,768]{0,1:T(8,128)(2,1)S(1)} %copy.297) | copy-start | bytes 4718596
  27.1 67.4 %copy-start.39 = (f32[1024]{0:T(1024)}, f32[1024]{0:T(1024)S(1)}, u32[]{:S(2)}) copy-start(f32[1024]{0:T(1024)S(1)} %broadcast_multiply_fusion.11) | copy-start | bytes 12292
  27.6 67.0 %copy-start.45 = (f32[1024]{0:T(1024)}, f32[1024]{0:T(1024)S(1)}, u32[]{:S(2)}) copy-start(f32[1024]{0:T(1024)S(1)} %add_rsqrt_fusion.3) | copy-start | bytes 12292
  88.2 104.9 %copy-start.47 = (f32[768]{0:T(1024)}, f32[768]{0:T(1024)S(1)}, u32[]{:S(2)}) copy-start(f32[768]{0:T(1024)S(1)} %get-tuple-element.239) | copy-start | bytes 9220
  88.2 104.9 %copy-start.55 = (f32[768]{0:T(1024)}, f32[768]{0:T(1024)S(1)}, u32[]{:S(2)}) copy-start(f32[768]{0:T(1024)S(1)} %get-tuple-element.238) | copy-start | bytes 9220
  105.7 68.2 %copy-start.10 = (bf16[1024,768]{0,1:T(8,128)(2,1)}, bf16[1024,768]{0,1:T(8,128)(2,1)S(1)}, u32[]{:S(2)}) copy-start(bf16[1024,768]{0,1:T(8,128)(2,1)S(1)} %copy.310) | copy-start | bytes 4718596
  197.3 39.9 %copy-start.4 = (f32[1024,768]{0,1:T(8,128)}, f32[1024,768]{0,1:T(8,128)S(1)}, u32[]{:S(2)}) copy-start(f32[1024,768]{0,1:T(8,128)S(1)} %get-tuple-element.295) | copy-start | bytes 9437188
  242.0 40.9 %slice-start.2 = ((s8[5898240]{0:T(1024)(128)(4,1)}), s8[1703936]{0:T(1024)(128)(4,1)S(1)}, s32[]{:S(2)}) async-start(s8[5898240]{0:T(1024)(128)(4,1)} %bitcast.205), calls=%async_computation.9 | async-start | bytes 3407872
  257.4 18.4 %copy-start.5 = (f32[1024,768]{0,1:T(8,128)S(1)}, f32[1024,768]{0,1:T(8,128)}, u32[]{:S(2)}) copy-start(f32[1024,768]{0,1:T(8,128)} %copy-done.4) | copy-start | bytes 9437188
  257.4 25.5 %slice-start.3 = ((s8[5898240]{0:T(1024)(128)(4,1)}), s8[4194304]{0:T(1024)(128)(4,1)S(1)}, s32[]{:S(2)}) async-start(s8[5898240]{0:T(1024)(128)(4,1)} %bitcast.205), calls=%async_computation.10 | async-start | bytes 8388608
  298.5 7.4 copy-start.14
  305.9 7.3 copy-start.18
  343.6 9.5 %copy-start.9 = (bf16[1024,768]{0,1:T(8,128)(2,1)S(1)}, bf16[1024,768]{0,1:T(8,128)(2,1)}, u32[]{:S(2)}) copy-start(bf16[1024,768]{0,1:T(8,128)(2,1)} %copy.309) | copy-start | bytes 4718596
  343.6 9.5 %copy-start.11 = (bf16[1024,768]{0,1:T(8,128)(2,1)S(1)}, bf16[1024,768]{0,1:T(8,128)(2,1)}, u32[]{:S(2)}) copy-start(bf16[1024,768]{0,1:T(8,128)(2,1)} %copy-done.10) | copy-start | bytes 4718596
  343.6 45.1 %collective-permute-start = (bf16[1536,768]{1,0:T(8,128)(2,1)}, bf16[1536,768]{1,0:T(8,128)(2,1)}, u32[]{:S(2)}, u32[]{:S(2)}) collective-permute-start(bf16[1536,768]{1,0:T(8,128)(2,1)} %bitcast.39), channel_id=1, source_target_pairs={{0,2},{2,0},{4,6},{6,4},{8,10},{10,8},{12,14},{14,12},{16,18},{18,... | collective-permute-start | bytes 7077896 | tf_op jit(solution)/shard_map/ppermute | solution.py:287
  354.8 84.0 %copy-start.23 = (bf16[2,1024,64]{1,2,0:T(8,128)(2,1)}, bf16[2,1024,64]{1,2,0:T(8,128)(2,1)S(1)}, u32[]{:S(2)}) copy-start(bf16[2,1024,64]{1,2,0:T(8,128)(2,1)S(1)} %get-tuple-element.78) | copy-start | bytes 786436
  386.8 11.2 %slice-start = ((s8[6094848]{0:T(1024)(128)(4,1)}), s8[4194304]{0:T(1024)(128)(4,1)S(1)}, s32[]{:S(2)}) async-start(s8[6094848]{0:T(1024)(128)(4,1)} %bitcast.139), calls=%async_computation.7 | async-start | bytes 8388608
  388.7 9.3 %slice-start.1 = ((s8[6094848]{0:T(1024)(128)(4,1)}), s8[1900544]{0:T(1024)(128)(4,1)S(1)}, s32[]{:S(2)}) async-start(s8[6094848]{0:T(1024)(128)(4,1)} %bitcast.139), calls=%async_computation.8 | async-start | bytes 3801088
  395.8 38.6 %collective-permute-start.1 = (bf16[768,768]{1,0:T(8,128)(2,1)}, bf16[768,768]{1,0:T(8,128)(2,1)}, u32[]{:S(2)}, u32[]{:S(2)}) collective-permute-start(bf16[768,768]{1,0:T(8,128)(2,1)} %select_convert_fusion.1), channel_id=1, source_target_pairs={{0,4},{2,6},{4,0},{6,2},{8,12},{10,14},{12,8},{14,10},{16,20},{18,... | collective-permute-start | bytes 3538952 | tf_op jit(solution)/shard_map/ppermute | solution.py:287
  401.0 340.1 %all-gather.12.cloned.1.call-start = ((), (), s32[]{:S(2)}) async-start(), calls=%async_computation.4 | async-start | bytes 1984512 | tf_op jit(solution)/shard_map/all_gather | solution.py:546
  440.9 42.6 %collective-permute-start.2 = (bf16[384,768]{1,0:T(8,128)(2,1)S(1)}, bf16[384,768]{1,0:T(8,128)(2,1)}, u32[]{:S(2)}, u32[]{:S(2)}) collective-permute-start(bf16[384,768]{1,0:T(8,128)(2,1)S(1)} %select_convert_fusion.4), channel_id=1, source_target_pairs={{0,8},{2,10},{4,12},{6,14},{8,0},{10,2},{12,4},{14,6},{16,24},{18,... | collective-permute-start | bytes 1769480 | tf_op jit(solution)/shard_map/ppermute | solution.py:287
  490.7 41.2 %collective-permute-start.3 = (bf16[192,768]{1,0:T(8,128)(2,1)S(1)}, bf16[192,768]{1,0:T(8,128)(2,1)S(1)}, u32[]{:S(2)}, u32[]{:S(2)}) collective-permute-start(bf16[192,768]{1,0:T(8,128)(2,1)S(1)} %select_convert_fusion.7), channel_id=1, source_target_pairs={{0,1},{1,0},{2,3},{3,2},{4,5},{5,4},{6,7},{7,6},{8,9},{9,8},{10,11... | collective-permute-start | bytes 884744 | tf_op jit(solution)/shard_map/ppermute | solution.py:287
  535.1 25.1 %collective-permute-start.4 = (bf16[96,768]{1,0:T(8,128)(2,1)S(1)}, bf16[96,768]{1,0:T(8,128)(2,1)S(1)}, u32[]{:S(2)}, u32[]{:S(2)}) collective-permute-start(bf16[96,768]{1,0:T(8,128)(2,1)S(1)} %select_convert_fusion.10), channel_id=1, source_target_pairs={{0,16},{2,18},{4,20},{6,22},{8,24},{10,26},{12,28},{14,30},{16,0},... | collective-permute-start | bytes 442376 | tf_op jit(solution)/shard_map/ppermute | solution.py:287
  535.2 25.7 %copy-start.24 = (bf16[2,1024,64]{1,2,0:T(8,128)(2,1)S(1)}, bf16[2,1024,64]{1,2,0:T(8,128)(2,1)}, u32[]{:S(2)}) copy-start(bf16[2,1024,64]{1,2,0:T(8,128)(2,1)} %get-tuple-element.95) | copy-start | bytes 786436
  554.4 7.4 copy-start.21
  554.4 8.5 %copy-start.25 = (bf16[2,1024,64]{1,2,0:T(8,128)(2,1)S(1)}, bf16[2,1024,64]{1,2,0:T(8,128)(2,1)}, u32[]{:S(2)}) copy-start(bf16[2,1024,64]{1,2,0:T(8,128)(2,1)} %get-tuple-element.98) | copy-start | bytes 786436
  589.6 10.8 %copy-start.31 = (bf16[12,1024,64]{1,2,0:T(8,128)(2,1)}, bf16[12,1024,64]{1,2,0:T(8,128)(2,1)S(1)}, u32[]{:S(2)}) copy-start(bf16[12,1024,64]{1,2,0:T(8,128)(2,1)S(1)} %bitcast_dynamic-update-slice_fusion) | copy-start | bytes 4718596
  637.8 2.5 collective-permute-start.5
  638.4 6.3 collective-permute-start.10
  640.6 15.2 %collective-permute-start.6 = (bf16[192,1152]{1,0:T(8,128)(2,1)S(1)}, bf16[192,1152]{1,0:T(8,128)(2,1)S(1)}, u32[]{:S(2)}, u32[]{:S(2)}) collective-permute-start(bf16[192,1152]{1,0:T(8,128)(2,1)S(1)} %select_convert_fusion.6), channel_id=1, source_target_pairs={{0,4},{2,6},{4,0},{6,2},{8,12},{10,14},{12,8},{14,10},{16,20},{18,... | collective-permute-start | bytes 1327112 | tf_op jit(solution)/shard_map/ppermute | solution.py:287
  645.0 22.7 %collective-permute-start.11 = (bf16[192,1280]{1,0:T(8,128)(2,1)S(1)}, bf16[192,1280]{1,0:T(8,128)(2,1)S(1)}, u32[]{:S(2)}, u32[]{:S(2)}) collective-permute-start(bf16[192,1280]{1,0:T(8,128)(2,1)S(1)} %select_convert_fusion.5), channel_id=1, source_target_pairs={{0,8},{2,10},{4,12},{6,14},{8,0},{10,2},{12,4},{14,6},{16,24},{18,... | collective-permute-start | bytes 1474568 | tf_op jit(solution)/shard_map/ppermute | solution.py:287
  655.9 16.1 %collective-permute-start.7 = (bf16[96,1152]{1,0:T(8,128)(2,1)S(1)}, bf16[96,1152]{1,0:T(8,128)(2,1)S(1)}, u32[]{:S(2)}, u32[]{:S(2)}) collective-permute-start(bf16[96,1152]{1,0:T(8,128)(2,1)S(1)} %select_convert_fusion.9), channel_id=1, source_target_pairs={{0,8},{2,10},{4,12},{6,14},{8,0},{10,2},{12,4},{14,6},{16,24},{18,... | collective-permute-start | bytes 663560 | tf_op jit(solution)/shard_map/ppermute | solution.py:287
  672.1 27.8 %copy-start.35 = (bf16[96,768]{1,0:T(8,128)(2,1)S(1)}, bf16[96,768]{1,0:T(8,128)(2,1)}, u32[]{:S(2)}) copy-start(bf16[96,768]{1,0:T(8,128)(2,1)} %convert_add_fusion.8) | copy-start | bytes 442372
  672.2 27.9 %copy-start.38 = (bf16[24,3968]{1,0:T(8,128)(2,1)S(1)}, bf16[24,3968]{1,0:T(8,128)(2,1)}, u32[]{:S(2)}) copy-start(bf16[24,3968]{1,0:T(8,128)(2,1)} %reduce-scatter.4.cloned.1.call-done) | copy-start | bytes 571396
  672.2 12.4 %collective-permute-start.8 = (bf16[48,1152]{1,0:T(8,128)(2,1)S(1)}, bf16[48,1152]{1,0:T(8,128)(2,1)S(1)}, u32[]{:S(2)}, u32[]{:S(2)}) collective-permute-start(bf16[48,1152]{1,0:T(8,128)(2,1)S(1)} %select_convert_fusion.12), channel_id=1, source_target_pairs={{0,1},{1,0},{2,3},{3,2},{4,5},{5,4},{6,7},{7,6},{8,9},{9,8},{10,11... | collective-permute-start | bytes 331784 | tf_op jit(solution)/shard_map/ppermute | solution.py:287
  681.9 18.9 %copy-start.52 = (f32[768]{0:T(1024)S(1)}, f32[768]{0:T(1024)}, u32[]{:S(2)}) copy-start(f32[768]{0:T(1024)} %get-tuple-element.234) | copy-start | bytes 9220
  681.9 6.9 collective-permute-start.12
  689.0 4.9 collective-permute-start.13
  689.4 7.4 collective-permute-start.9
  694.0 5.2 collective-permute-start.14
  699.9 99.5 %all-gather.14.cloned.1.call-start = ((), (), s32[]{:S(2)}) async-start(), calls=%async_computation.5 | async-start | bytes 5744640 | tf_op jit(solution)/shard_map/all_gather | solution.py:537
  (35 other events, 133.2 us)
Sparse Core Ops, SparseCore 0:
  19.1 63.4 all-gather.5
  86.0 66.3 all-gather.7
  155.4 62.3 all-gather.9
  401.1 136.3 reduce-scatter.3
  700.0 41.0 all-gather.11
  743.7 55.6 all-gather.13

commit v6 on v4

--- a/solution.py
+++ b/solution.py
@@ -437,11 +437,6 @@
     )
     grad_middle = grad_out + grad_mid_part
     order_a, order_b = hypercube_orders(group_size, shard_size)
-    shrink_in = (
-        shrink_weight_grad.reshape(shard_size, group_size, -1, model_width)
-        .transpose(1, 0, 2, 3)
-        .reshape(wide_width, model_width)
-    )
     grad_branch = grad_middle.astype(jnp.bfloat16)
     proj_bias_grad = jnp.sum(grad_branch.astype(jnp.float32), axis=0)
     proj_weight_grad = jnp.einsum(
@@ -466,17 +461,15 @@
     ffn_pack = jnp.concatenate(
         [
             expand_weight_grad,
+            shrink_weight_grad.reshape(model_width, ratio * model_width),
             proj_weight_grad,
             pack_columns(ffn_small, model_width),
         ],
         axis=1,
     ).astype(jnp.bfloat16)
     grad_att_low = grad_attended.astype(jnp.bfloat16)
-    ffn_pack, shrink_in, grad_att_low = lax.optimization_barrier(
-        (ffn_pack, shrink_in, grad_att_low)
-    )
+    ffn_pack, grad_att_low = lax.optimization_barrier((ffn_pack, grad_att_low))
     ffn_part = grad_rows_reduce(ffn_pack, group_size, shard_size)
-    shrink_part = hypercube_reduce_scatter(shrink_in, order_a, group_size, shard_size)
     grad_rows = []
     for r in range(row_count):
         parts = attention_backward(
@@ -512,9 +505,7 @@
         .transpose(1, 0, 2, 3)
         .reshape(model_width, -1)
     )
-    ffn_part, shrink_part, attn_pack = lax.optimization_barrier(
-        (ffn_part, shrink_part, attn_pack)
-    )
+    ffn_part, attn_pack = lax.optimization_barrier((ffn_part, attn_pack))
     split = (attn_pack.shape[1] // 256) * 128
     attn_left = hypercube_reduce_scatter(
         attn_pack[:, :split], order_a, group_size, shard_size
@@ -526,7 +517,6 @@
         jnp.concatenate(
             [
                 ffn_part,
-                shrink_part.astype(jnp.bfloat16).reshape(n, ratio * model_width),
                 attn_left.astype(jnp.bfloat16),
                 attn_right.astype(jnp.bfloat16),
             ],
@@ -538,12 +528,11 @@
     ).astype(jnp.float32)
     ffn_cols = ffn_pack.shape[1]
     ffn_back = both[:, :ffn_cols]
-    shrink_back = both[:, ffn_cols : ffn_cols + ratio * model_width]
-    attn_back = both[:, ffn_cols + ratio * model_width :]
+    attn_back = both[:, ffn_cols:]
     half = both.shape[0]
     expand_out = ffn_back[:, :wide_width]
-    proj_out = ffn_back[:, wide_width : wide_width + model_width]
-    shrink_out = shrink_back.reshape(half * ratio, model_width)
+    shrink_out = ffn_back[:, wide_width : 2 * wide_width].reshape(half * ratio, model_width)
+    proj_out = ffn_back[:, 2 * wide_width : 2 * wide_width + model_width]
     (
         second_gain_out,
         second_shift_out,
@@ -554,7 +543,7 @@
         gain_inner_out,
         shift_inner_out,
         pbias_out,
-    ) = unpack_columns(ffn_back[:, wide_width + model_width :], ffn_small_widths)
+    ) = unpack_columns(ffn_back[:, 2 * wide_width + model_width :], ffn_small_widths)
     qkv_out = attn_back[:, :qkv_width]
     (
         gain_one_out,

time: 765 us -> 747 us (0.976)
  other arithmetic: 95.2 us -> 71.4 us
  waiting for transfers between devices: 135 us -> 124 us
  local copies, waits for them, and re-layouts: 151 us -> 161 us
    ppermute x15 -> x10, waiting for transfers between devices: 32 us -> 19.6 us  [hypercube_reduce_scatter(): got = lax.ppermute(send, axis, [(j, j ^ 1 << b) for j in range(size)])]
    add x13 -> x8, other arithmetic: 11.9 us -> 0.83 us  [hypercube_reduce_scatter(): cur = keep + got.astype(jnp.float32)]
    unnamed x120 -> x96, local copies, waits for them, and re-layouts: 15.5 us -> 12.4 us
    ppermute x15 -> x10, starting transfers between devices: 77.8 us -> 79.4 us  [hypercube_reduce_scatter(): got = lax.ppermute(send, axis, [(j, j ^ 1 << b) for j in range(size)])]
  transfers between devices with their start and end apart: 20 -> 15, of which waited for: 13 -> 11; matrix products, arithmetic and copies ran while one was open for 26% -> 24% of each run, Pallas kernels for 22% -> 23%
where the time goes in v6:
time: 747 us; the launch traced here: 738 us
  Pallas kernels  166 us (22%)
  local copies, waits for them, and re-layouts  161 us (22%)
  waiting for transfers between devices  124 us (17%)
  matrix products  121 us (16%)
  starting transfers between devices  79.6 us (11%)
  other arithmetic  71.4 us (10%)
  between operations  15 us (2%)
    pallas_call x1, Pallas kernels, attention_backward(): pl.pallas_call(_bwd_kernel, out_shape=(jax.ShapeDtypeStruct((heads, lengt...  101 us
    ppermute x10, starting transfers between devices, hypercube_reduce_scatter(): got = lax.ppermute(send, axis, [(j, j ^ 1 << b) for j in range(size)])  79.4 us
    pallas_call x1, Pallas kernels, attention_forward(): pl.pallas_call(_fwd_kernel, out_shape=jax.ShapeDtypeStruct((heads, length...  65.5 us
    all_gather x1, waiting for transfers between devices, per_device(): lax.all_gather(first_pack, ('group', 'shard'), axis=0, tiled=True)  53 us
    all_gather x1, waiting for transfers between devices, per_device(): lax.all_gather(jnp.concatenate([ffn_part, attn_left.astype(jnp.bfloat16),...  49.4 us
    dot_general x1, matrix products, per_device(): jnp.dot(second_low, expand_full, preferred_element_type=jnp.float32)  39 us
    ppermute x10, waiting for transfers between devices, hypercube_reduce_scatter(): got = lax.ppermute(send, axis, [(j, j ^ 1 << b) for j in range(size)])  19.6 us
    reduce_sum x1, other arithmetic, per_device(): expand_bias_grad = jnp.sum(grad_pre.astype(jnp.float32), axis=0)  18.3 us
  transfers between devices with their start and end apart: 15, of which 11 were waited for; matrix products, arithmetic and copies ran while one was open for 24% of the time, Pallas kernels for 23%

profile of v6, /device:TPU:0, one launch (start us, length us, event | category | flops | bytes accessed | tf_op | source)
XLA Modules:
  0.0 738.1 jit_solution(14195341793600384193)
XLA Ops:
  29.5 53.0 %all-gather.5.cloned.1.call-done = bf16[768,2432]{1,0:T(8,128)(2,1)} async-done(((bf16[24,2432]{1,0:T(8,128)(2,1)}), bf16[768,2432]{1,0:T(8,128)(2,1)}) %all-gather.5.cloned.1.call-update) | async-done | bytes 3735568 | tf_op jit(solution)/shard_map/all_gather | solution.py:338
  84.0 4.2 convert_reduce_fusion.1
  88.2 6.4 add_convert_fusion.2
  108.6 65.5 %shard_map.339 = f32[12,1024,64]{2,1,0:T(8,128)} custom-call(s32[2]{0:T(128)} %and_select_fusion.lo_ref, bf16[12,1024,64]{2,1,0:T(8,128)(2,1)} %copy.229.q_ref, bf16[12,64,1024]{2,1,0:T(8,128)(2,1)} %bitcast.81, bf16[12,1024,64]{2,1,0:T(8,128)(2,1)} %copy.230.v_ref, s32[1024,1]{1,0:T(8,128)} %copy.231.segq_ref, s32[1,1024]{1,0:T(1,128)} %bitcast.108), custom_call_target="tpu_custom_call" | custom-call | flops 1610612736 | bytes 6291456 | tf_op jit(solution)/shard_map/pallas_call | solution.py:127
  174.1 6.1 copy.232
  180.2 4.0 copy.233
  184.2 3.3 reduce_sum.276
  187.5 3.8 multiply_reduce_fusion.4
  193.6 4.2 fusion.45
  198.2 39.0 %fusion.40 = (f32[1024]{0:T(1024)S(1)}, f32[1024,3072]{1,0:T(8,128)S(1)}, f32[1024,3072]{1,0:T(8,128)}, f32[1024,3072]{1,0:T(8,128)}) fusion(f32[3072]{0:T(1024)S(1)} %reshape.541, bf16[768,3840]{1,0:T(8,128)(2,1)} %all-gather.7.cloned.1.call-done, f32[1024,768]{0,1:T(8,128)S(1)} %get-tuple-element.184, f32[768]{0:T(1024)S(1)} %get-tuple-element.151, ...), kind=kOutput, calls=%fused_computation.157 | convolution fusion | flops 5043387392 | bytes 45643776 | tf_op jit(solution)/shard_map/dot_general | solution.py:404
  238.7 3.3 copy-done
  242.0 15.4 %multiply_reduce_fusion = (bf16[3072]{0:T(1024)(128)(2,1)S(1)}, f32[1024]{0:T(1024)S(1)}, f32[1024]{0:T(1024)S(1)}, bf16[3072]{0:T(1024)(128)(2,1)S(1)}, bf16[1024,3072]{1,0:T(8,128)(2,1)}, /*index=5*/f32[1024,3072]{1,0:T(8,128)}) fusion(f32[1024,3072]{1,0:T(8,128)} %copy-done, f32[1024]{0:T(1024)S(1)} %add_rsqrt_fusion, ...), kind=kOutput, calls=%fused_computation.3 | convolution fusion | flops 4869578752 | bytes 37801984 | tf_op jit(solution)/shard_map/td,fd->tf/dot_general | solution.py:423
  257.4 18.3 %fusion.39 = (bf16[3072]{0:T(1024)(128)(2,1)S(1)}, bf16[1024,3072]{1,0:T(8,128)(2,1)S(1)}) fusion(f32[1024,3072]{1,0:T(8,128)} %get-tuple-element.170, f32[1024]{0:T(1024)S(1)} %get-tuple-element.192, f32[1024,3072]{1,0:T(8,128)} %copy-done, f32[1024]{0:T(1024)S(1)} %broadcast_multiply_fusion.2, f32[1024]{0:T(1024)S(1)} %get-tuple-element.193, ...), kind=kLoop, calls=%fused_computation.156 | loop fusion | flops 72348672 | bytes 56670208 | tf_op jit(solution)/shard_map/reduce_sum | solution.py:430
  275.8 7.2 convolution_convert_fusion.1
  283.0 6.8 fusion.46
  289.8 3.5 copy.236
  293.3 3.0 multiply_reduce_fusion.7
  296.3 9.7 %convolution_convert_fusion = bf16[3072,768]{1,0:T(8,128)(2,1)} fusion(bf16[1024,3072]{1,0:T(8,128)(2,1)} %get-tuple-element.171, bf16[1024,768]{1,0:T(8,128)(2,1)S(1)} %copy-done.16), kind=kOutput, calls=%fused_computation.26 | convolution fusion | flops 4834197504 | bytes 12582912 | tf_op jit(solution)/shard_map/tf,td->fd/dot_general | solution.py:419
  306.0 8.5 %reshape.501 = bf16[768,3072]{1,0:T(8,128)(2,1)} reshape(bf16[3072,768]{1,0:T(8,128)(2,1)} %convolution_convert_fusion) | data formatting | bytes 9437184 | tf_op jit(solution)/shard_map/reshape | solution.py:464
  314.5 3.8 convert_reduce_fusion.9
  318.3 3.0 convolution_convert_fusion.2
  325.7 4.9 multiply_reduce_fusion.5
  335.1 18.0 %concatenate.51 = bf16[768,7040]{1,0:T(8,128)(2,1)} concatenate(bf16[768,3072]{1,0:T(8,128)(2,1)} %convolution_convert_fusion.1, bf16[768,3072]{1,0:T(8,128)(2,1)} %reshape.501, bf16[768,768]{1,0:T(8,128)(2,1)} %convolution_convert_fusion.2, bf16[768,1]{1,0:T(8,128)(2,1)S(1)} %reshape.554, bf16[768,1]{1,0:T(8,128)(2,1)} %reshape.555, bf16[768,1]{1,0:T(8,128)(2,1)S(1)} %copy-done.22, ...), dimensions={1} | concatenate | bytes 21626880 | tf_op jit(solution)/shard_map/concatenate | solution.py:461
  353.1 10.1 %copy.252 = bf16[16,2,24,7040]{3,2,1,0:T(8,128)(2,1)} copy(bf16[16,2,24,7040]{3,2,0,1:T(8,128)(2,1)} %bitcast.78) | data formatting | bytes 21626880 | tf_op jit(solution)/shard_map/transpose | solution.py:245
  368.0 2.8 copy.248.do_ref
  370.9 100.6 %shard_map.340 = (f32[12,1024,64]{2,1,0:T(8,128)}, f32[12,64,1024]{2,1,0:T(8,128)}, f32[12,64,1024]{2,1,0:T(8,128)}) custom-call(s32[2]{0:T(128)} %and_select_fusion.lo_ref, bf16[12,1024,64]{2,1,0:T(8,128)(2,1)} %copy.229.q_ref, bf16[12,64,1024]{2,1,0:T(8,128)(2,1)} %bitcast.89, bf16[12,1024,64]{2,1,0:T(8,128)(2,1)} %copy.247.k_ref, ...), custom_call_target="tpu_custom_call" | custom-call | flops 4026531840 | bytes 12582912 | tf_op jit(solution)/shard_map/pallas_call | solution.py:155
  471.5 3.7 convert.88
  480.6 9.6 %fusion.47 = (f32[768]{0:T(1024)}, f32[1024,768]{1,0:T(8,128)}) fusion(bf16[768,2432]{1,0:T(8,128)(2,1)} %all-gather.5.cloned.1.call-done, bf16[1024,768]{0,1:T(8,128)(2,1)} %bitcast.96, bf16[1024,768]{0,1:T(8,128)(2,1)} %bitcast.99, bf16[1024,768]{0,1:T(8,128)(2,1)} %bitcast.102), kind=kOutput, calls=%fused_computation.163 | convolution fusion | flops 3638820096 | bytes 11406336 | tf_op jit(solution)/shard_map/te,de->td/dot_general | solution.py:489
  490.2 3.8 copy.251
  494.1 6.0 fusion.35
  500.1 3.6 copy.254
  513.9 8.5 %concatenate.58 = f32[2,16,24,2432]{3,2,0,1:T(8,128)} concatenate(f32[2,16,24,2304]{3,2,0,1:T(8,128)} %copy.254, f32[2,16,24,1]{3,2,0,1:T(8,128)S(1)} %copy.255, f32[2,16,24,1]{3,2,0,1:T(8,128)S(1)} %copy-done.21, f32[2,16,24,1]{3,2,0,1:T(8,128)S(1)} %copy.257, f32[2,16,24,1]{3,2,0,1:T(8,128)S(1)} %copy.258, f32[2,16,24,124]{3,2,0,1:T(8,128)S(1)} %broadcast_in_dim.14), dimensions={3} | concatenate | bytes 14942208 | tf_op jit(solution)/shard_map/concatenate | solution.py:500
  528.4 14.4 %collective-permute-start = (bf16[384,1152]{1,0:T(8,128)(2,1)S(1)}, bf16[384,1152]{1,0:T(8,128)(2,1)S(1)}, u32[]{:S(2)}, u32[]{:S(2)}) collective-permute-start(bf16[384,1152]{1,0:T(8,128)(2,1)S(1)} %bitcast.106), channel_id=1, source_target_pairs={{0,2},{2,0},{4,6},{6,4},{8,10},{10,8},{12,14},{14,12},{16,18},{18,... | collective-permute-start | bytes 2654216 | tf_op jit(solution)/shard_map/ppermute | solution.py:286
  546.8 32.0 %collective-permute-start.6 = (bf16[192,1280]{1,0:T(8,128)(2,1)S(1)}, bf16[192,1280]{1,0:T(8,128)(2,1)S(1)}, u32[]{:S(2)}, u32[]{:S(2)}) collective-permute-start(bf16[192,1280]{1,0:T(8,128)(2,1)S(1)} %select_convert_fusion.2), channel_id=1, source_target_pairs={{0,8},{2,10},{4,12},{6,14},{8,0},{10,2},{12,4},{14,6},{16,24},{18,... | collective-permute-start | bytes 1474568 | tf_op jit(solution)/shard_map/ppermute | solution.py:286
  579.0 10.4 %collective-permute-start.2 = (bf16[96,1152]{1,0:T(8,128)(2,1)S(1)}, bf16[96,1152]{1,0:T(8,128)(2,1)S(1)}, u32[]{:S(2)}, u32[]{:S(2)}) collective-permute-start(bf16[96,1152]{1,0:T(8,128)(2,1)S(1)} %select_convert_fusion.5), channel_id=1, source_target_pairs={{0,8},{2,10},{4,12},{6,14},{8,0},{10,2},{12,4},{14,6},{16,24},{18,... | collective-permute-start | bytes 663560 | tf_op jit(solution)/shard_map/ppermute | solution.py:286
  590.7 4.4 collective-permute-done.2
  595.2 16.4 %collective-permute-start.3 = (bf16[48,1152]{1,0:T(8,128)(2,1)S(1)}, bf16[48,1152]{1,0:T(8,128)(2,1)S(1)}, u32[]{:S(2)}, u32[]{:S(2)}) collective-permute-start(bf16[48,1152]{1,0:T(8,128)(2,1)S(1)} %select_convert_fusion.7), channel_id=1, source_target_pairs={{0,1},{1,0},{2,3},{3,2},{4,5},{5,4},{6,7},{7,6},{8,9},{9,8},{10,11... | collective-permute-start | bytes 331784 | tf_op jit(solution)/shard_map/ppermute | solution.py:286
  614.4 4.1 collective-permute-done.7
  620.4 3.2 collective-permute-done.8
  625.6 3.9 collective-permute-done.9
  630.3 9.3 %add_convert_fusion.3 = bf16[1024,768]{0,1:T(8,128)(2,1)S(1)} fusion(f32[1024,768]{0,1:T(8,128)} %copy-done.3, bf16[1024,3072]{1,0:T(8,128)(2,1)} %get-tuple-element.171, bf16[3072,768]{1,0:T(8,128)(2,1)} %all-gather.9.cloned.1.call-done, f32[768]{0:T(1024)S(1)} %copy-done.38), kind=kOutput, calls=%fused_computation.61 | convolution fusion | flops 4834197504 | bytes 15731712 | tf_op jit(solution)/shard_map/dot_general | solution.py:414
  641.2 3.9 fusion.22
  646.7 49.4 %all-gather.11.cloned.1.call-done = bf16[384,9472]{1,0:T(8,128)(2,1)} async-done(((bf16[24,9472]{1,0:T(8,128)(2,1)}), bf16[384,9472]{1,0:T(8,128)(2,1)}) %all-gather.11.cloned.1.call-update) | async-done | bytes 7274512 | tf_op jit(solution)/shard_map/all_gather | solution.py:516
  696.1 9.2 %convert_element_type.317 = f32[384,9472]{1,0:T(8,128)} convert(bf16[384,9472]{1,0:T(8,128)(2,1)} %all-gather.11.cloned.1.call-done) | non-fusion elementwise | flops 3637248 | bytes 21823488 | tf_op jit(solution)/shard_map/convert_element_type | solution.py:528
  705.2 3.5 slice_reduce_fusion.2
  712.2 7.4 %fusion.42 = (f32[384,3072]{1,0:T(8,128)}, f32[384,3072]{1,0:T(8,128)}) fusion(bf16[384,9472]{1,0:T(8,128)(2,1)} %all-gather.11.cloned.1.call-done), kind=kLoop, calls=%fused_computation.158 | loop fusion | bytes 18874368 | tf_op jit(solution)/shard_map/slice | solution.py:534
  719.6 6.1 reshape.532
  725.7 3.5 slice.338
  (243 shorter events, 98.6 us)
Async XLA Ops:
  7.2 16.8 %copy-start.14 = (bf16[1024,768]{1,0:T(8,128)(2,1)S(1)}, bf16[1024,768]{1,0:T(8,128)(2,1)}, u32[]{:S(2)}) copy-start(bf16[1024,768]{1,0:T(8,128)(2,1)} %param.39) | copy-start | bytes 4718596
  7.2 17.1 %copy-start.43 = (s32[1,5]{1,0:T(1,128)S(1)}, s32[1,5]{1,0:T(1,128)}, u32[]{:S(2)}) copy-start(s32[1,5]{1,0:T(1,128)} %param.21) | copy-start | bytes 64
  7.2 75.3 %all-gather.5.cloned.1.call-start = ((), (), s32[]{:S(2)}) async-start(), calls=%async_computation.1 | async-start | bytes 3852288 | tf_op jit(solution)/shard_map/all_gather | solution.py:338
  17.1 9.0 %copy-start.20 = (bf16[1024,768]{1,0:T(8,128)(2,1)S(1)}, bf16[1024,768]{1,0:T(8,128)(2,1)}, u32[]{:S(2)}) copy-start(bf16[1024,768]{1,0:T(8,128)(2,1)} %param.20) | copy-start | bytes 4718596
  18.9 174.7 %all-gather.7.cloned.1.call-start = ((), (), s32[]{:S(2)}) async-start(), calls=%async_computation.2 | async-start | bytes 6082560 | tf_op jit(solution)/shard_map/all_gather | solution.py:356
  20.6 221.4 %all-gather.9.cloned.1.call-start = ((), (), s32[]{:S(2)}) async-start(), calls=%async_computation.3 | async-start | bytes 4866048 | tf_op jit(solution)/shard_map/all_gather | solution.py:359
  21.4 501.9 %reduce-scatter.4.cloned.1.call-start = ((), (), s32[]{:S(2)}) async-start(), calls=%async_computation.5 | async-start | bytes 11151360
  26.9 166.8 %copy-start.1 = (bf16[1024,768]{0,1:T(8,128)(2,1)}, bf16[1024,768]{0,1:T(8,128)(2,1)S(1)}, u32[]{:S(2)}) copy-start(bf16[1024,768]{0,1:T(8,128)(2,1)S(1)} %copy.215) | copy-start | bytes 4718596
  27.1 67.5 %copy-start.24 = (f32[1024]{0:T(1024)}, f32[1024]{0:T(1024)S(1)}, u32[]{:S(2)}) copy-start(f32[1024]{0:T(1024)S(1)} %broadcast_multiply_fusion.11) | copy-start | bytes 12292
  27.6 67.0 %copy-start.31 = (f32[1024]{0:T(1024)}, f32[1024]{0:T(1024)S(1)}, u32[]{:S(2)}) copy-start(f32[1024]{0:T(1024)S(1)} %add_rsqrt_fusion.3) | copy-start | bytes 12292
  88.2 6.4 copy-start.29
  88.2 6.4 copy-start.39
  88.2 105.4 %copy-start.33 = (f32[768]{0:T(1024)}, f32[768]{0:T(1024)S(1)}, u32[]{:S(2)}) copy-start(f32[768]{0:T(1024)S(1)} %get-tuple-element.155) | copy-start | bytes 9220
  88.2 105.4 %copy-start.41 = (f32[768]{0:T(1024)}, f32[768]{0:T(1024)S(1)}, u32[]{:S(2)}) copy-start(f32[768]{0:T(1024)S(1)} %get-tuple-element.154) | copy-start | bytes 9220
  98.6 5.5 copy-start.7
  105.8 68.3 %copy-start.8 = (bf16[1024,768]{0,1:T(8,128)(2,1)}, bf16[1024,768]{0,1:T(8,128)(2,1)S(1)}, u32[]{:S(2)}) copy-start(bf16[1024,768]{0,1:T(8,128)(2,1)S(1)} %copy.228) | copy-start | bytes 4718596
  187.5 6.1 copy-start.27
  191.3 6.5 copy-start.35
  197.8 39.4 %copy-start.3 = (f32[1024,768]{0,1:T(8,128)}, f32[1024,768]{0,1:T(8,128)S(1)}, u32[]{:S(2)}) copy-start(f32[1024,768]{0,1:T(8,128)S(1)} %get-tuple-element.184) | copy-start | bytes 9437188
  237.3 4.7 copy-start
  237.3 4.7 copy-start.15
  242.0 40.9 %slice-start = ((s8[5898240]{0:T(1024)(128)(4,1)}), s8[1703936]{0:T(1024)(128)(4,1)S(1)}, s32[]{:S(2)}) async-start(s8[5898240]{0:T(1024)(128)(4,1)} %bitcast.121), calls=%async_computation.6 | async-start | bytes 3407872
  257.4 18.4 %copy-start.4 = (f32[1024,768]{0,1:T(8,128)S(1)}, f32[1024,768]{0,1:T(8,128)}, u32[]{:S(2)}) copy-start(f32[1024,768]{0,1:T(8,128)} %copy-done.3) | copy-start | bytes 9437188
  257.4 25.6 %slice-start.1 = ((s8[5898240]{0:T(1024)(128)(4,1)}), s8[4194304]{0:T(1024)(128)(4,1)S(1)}, s32[]{:S(2)}) async-start(s8[5898240]{0:T(1024)(128)(4,1)} %bitcast.121), calls=%async_computation.7 | async-start | bytes 8388608
  314.4 3.9 copy-start.36
  314.4 3.9 copy-start.42
  318.3 7.4 copy-start.11
  363.2 4.1 copy-start.17
  363.2 332.9 %all-gather.11.cloned.1.call-start = ((), (), s32[]{:S(2)}) async-start(), calls=%async_computation.4 | async-start | bytes 7729152 | tf_op jit(solution)/shard_map/all_gather | solution.py:516
  471.5 6.1 copy-start.13
  490.1 3.9 copy-start.2
  490.1 3.9 copy-start.18
  490.1 3.9 copy-start.25
  490.2 3.9 copy-start.30
  490.2 3.9 copy-start.32
  490.2 3.9 copy-start.40
  528.4 16.5 %collective-permute-start = (bf16[384,1152]{1,0:T(8,128)(2,1)S(1)}, bf16[384,1152]{1,0:T(8,128)(2,1)S(1)}, u32[]{:S(2)}, u32[]{:S(2)}) collective-permute-start(bf16[384,1152]{1,0:T(8,128)(2,1)S(1)} %bitcast.106), channel_id=1, source_target_pairs={{0,2},{2,0},{4,6},{6,4},{8,10},{10,8},{12,14},{14,12},{16,18},{18,... | collective-permute-start | bytes 2654216 | tf_op jit(solution)/shard_map/ppermute | solution.py:286
  543.2 3.4 collective-permute-start.5
  545.1 33.8 %collective-permute-start.1 = (bf16[192,1152]{1,0:T(8,128)(2,1)S(1)}, bf16[192,1152]{1,0:T(8,128)(2,1)S(1)}, u32[]{:S(2)}, u32[]{:S(2)}) collective-permute-start(bf16[192,1152]{1,0:T(8,128)(2,1)S(1)} %select_convert_fusion.3), channel_id=1, source_target_pairs={{0,4},{2,6},{4,0},{6,2},{8,12},{10,14},{12,8},{14,10},{16,20},{18,... | collective-permute-start | bytes 1327112 | tf_op jit(solution)/shard_map/ppermute | solution.py:286
  546.8 43.7 %collective-permute-start.6 = (bf16[192,1280]{1,0:T(8,128)(2,1)S(1)}, bf16[192,1280]{1,0:T(8,128)(2,1)S(1)}, u32[]{:S(2)}, u32[]{:S(2)}) collective-permute-start(bf16[192,1280]{1,0:T(8,128)(2,1)S(1)} %select_convert_fusion.2), channel_id=1, source_target_pairs={{0,8},{2,10},{4,12},{6,14},{8,0},{10,2},{12,4},{14,6},{16,24},{18,... | collective-permute-start | bytes 1474568 | tf_op jit(solution)/shard_map/ppermute | solution.py:286
  579.0 16.1 %collective-permute-start.2 = (bf16[96,1152]{1,0:T(8,128)(2,1)S(1)}, bf16[96,1152]{1,0:T(8,128)(2,1)S(1)}, u32[]{:S(2)}, u32[]{:S(2)}) collective-permute-start(bf16[96,1152]{1,0:T(8,128)(2,1)S(1)} %select_convert_fusion.5), channel_id=1, source_target_pairs={{0,8},{2,10},{4,12},{6,14},{8,0},{10,2},{12,4},{14,6},{16,24},{18,... | collective-permute-start | bytes 663560 | tf_op jit(solution)/shard_map/ppermute | solution.py:286
  595.2 34.3 %copy-start.23 = (bf16[24,7040]{1,0:T(8,128)(2,1)S(1)}, bf16[24,7040]{1,0:T(8,128)(2,1)}, u32[]{:S(2)}) copy-start(bf16[24,7040]{1,0:T(8,128)(2,1)} %reduce-scatter.4.cloned.1.call-done) | copy-start | bytes 1013764
  595.2 19.1 %collective-permute-start.3 = (bf16[48,1152]{1,0:T(8,128)(2,1)S(1)}, bf16[48,1152]{1,0:T(8,128)(2,1)S(1)}, u32[]{:S(2)}, u32[]{:S(2)}) collective-permute-start(bf16[48,1152]{1,0:T(8,128)(2,1)S(1)} %select_convert_fusion.7), channel_id=1, source_target_pairs={{0,1},{1,0},{2,3},{3,2},{4,5},{5,4},{6,7},{7,6},{8,9},{9,8},{10,11... | collective-permute-start | bytes 331784 | tf_op jit(solution)/shard_map/ppermute | solution.py:286
  611.6 18.6 %copy-start.38 = (f32[768]{0:T(1024)S(1)}, f32[768]{0:T(1024)}, u32[]{:S(2)}) copy-start(f32[768]{0:T(1024)} %get-tuple-element.150) | copy-start | bytes 9220
  611.7 6.8 collective-permute-start.7
  618.6 4.9 collective-permute-start.8
  618.9 6.6 collective-permute-start.4
  623.6 5.8 collective-permute-start.9
  (13 other events, 36.8 us)
Sparse Core Ops, SparseCore 0:
  19.1 63.4 all-gather.4
  86.0 66.4 all-gather.6
  155.5 62.3 all-gather.8
  363.3 159.9 reduce-scatter.3
  630.4 65.6 all-gather.10

commit v7 on v6

--- a/solution.py
+++ b/solution.py
@@ -237,16 +237,17 @@
     return out
 
 
-def grad_rows_reduce(packed, group_size, shard_size):
-    rows, cols = packed.shape
-    n = rows // (group_size * shard_size)
-    permuted = (
-        packed.reshape(shard_size, group_size, n, cols)
-        .transpose(1, 0, 2, 3)
-        .reshape(rows, cols)
-    )
+def destination_order(x, group_size, shard_size, axis):
+    shape = x.shape
+    lead, size, rest = shape[:axis], shape[axis], shape[axis + 1 :]
+    blocks = x.reshape(lead + (shard_size, group_size, size // (group_size * shard_size)) + rest)
+    moved = jnp.swapaxes(blocks, len(lead), len(lead) + 1)
+    return moved.reshape(shape)
+
+
+def grad_rows_reduce(packed):
     return lax.psum_scatter(
-        permuted, ("group", "shard"), scatter_dimension=0, tiled=True
+        packed, ("group", "shard"), scatter_dimension=0, tiled=True
     )
 
 
@@ -417,7 +418,10 @@
     block_output = output.astype(jnp.bfloat16)
     grad_out = out_cotangent.astype(jnp.float32)
     shrink_weight_grad = jnp.einsum(
-        "tf,td->fd", hidden_low, out_cotangent, preferred_element_type=jnp.float32
+        "tf,td->fd",
+        destination_order(hidden_low, group_size, shard_size, 1),
+        out_cotangent,
+        preferred_element_type=jnp.float32,
     )
     shrink_bias_grad = jnp.sum(grad_out, axis=0)
     grad_hidden = jnp.einsum(
@@ -429,7 +433,10 @@
     grad_pre = gelu_pull(grad_activ)[0].astype(jnp.bfloat16)
     expand_bias_grad = jnp.sum(grad_pre.astype(jnp.float32), axis=0)
     expand_weight_grad = jnp.einsum(
-        "td,tf->df", second_low, grad_pre, preferred_element_type=jnp.float32
+        "td,tf->df",
+        destination_order(second_low, group_size, shard_size, 1),
+        grad_pre,
+        preferred_element_type=jnp.float32,
     )
     grad_second = jnp.einsum("tf,df->td", grad_pre, expand_full, preferred_element_type=jnp.float32)
     grad_mid_part, second_gain_grad, second_shift_grad = norm_back(
@@ -440,7 +447,10 @@
     grad_branch = grad_middle.astype(jnp.bfloat16)
     proj_bias_grad = jnp.sum(grad_branch.astype(jnp.float32), axis=0)
     proj_weight_grad = jnp.einsum(
-        "td,te->de", inner_low, grad_branch, preferred_element_type=jnp.float32
+        "td,te->de",
+        destination_order(inner_low, group_size, shard_size, 1),
+        grad_branch,
+        preferred_element_type=jnp.float32,
     )
     grad_inner = jnp.einsum("te,de->td", grad_branch, proj_full, preferred_element_type=jnp.float32)
     grad_attended, inner_gain_grad, inner_shift_grad = norm_back(
@@ -463,13 +473,13 @@
             expand_weight_grad,
             shrink_weight_grad.reshape(model_width, ratio * model_width),
             proj_weight_grad,
-            pack_columns(ffn_small, model_width),
+            destination_order(pack_columns(ffn_small, model_width), group_size, shard_size, 0),
         ],
         axis=1,
     ).astype(jnp.bfloat16)
     grad_att_low = grad_attended.astype(jnp.bfloat16)
     ffn_pack, grad_att_low = lax.optimization_barrier((ffn_pack, grad_att_low))
-    ffn_part = grad_rows_reduce(ffn_pack, group_size, shard_size)
+    ffn_part = grad_rows_reduce(ffn_pack)
     grad_rows = []
     for r in range(row_count):
         parts = attention_backward(
@@ -484,7 +494,10 @@
     query_bias_grad = jnp.sum(grad_qkv_wide[:, :model_width], axis=0)
     value_bias_grad = jnp.sum(grad_qkv_wide[:, 2 * model_width :], axis=0)
     qkv_weight_grad = jnp.einsum(
-        "td,te->de", normed_low, grad_qkv, preferred_element_type=jnp.float32
+        "td,te->de",
+        destination_order(normed_low, group_size, shard_size, 1),
+        grad_qkv,
+        preferred_element_type=jnp.float32,
     )
     grad_normed = jnp.einsum("te,de->td", grad_qkv, qkv_full, preferred_element_type=jnp.float32)
     grad_in_part, first_gain_grad, first_shift_grad = norm_back(
@@ -498,12 +511,11 @@
         value_bias_grad,
     )
     attn_pack = jnp.concatenate(
-        [qkv_weight_grad, pack_columns(attn_small, model_width)], axis=1
-    )
-    attn_pack = (
-        attn_pack.reshape(shard_size, group_size, n, -1)
-        .transpose(1, 0, 2, 3)
-        .reshape(model_width, -1)
+        [
+            qkv_weight_grad,
+            destination_order(pack_columns(attn_small, model_width), group_size, shard_size, 0),
+        ],
+        axis=1,
     )
     ffn_part, attn_pack = lax.optimization_barrier((ffn_part, attn_pack))
     split = (attn_pack.shape[1] // 256) * 128

time: 747 us -> 760 us (1.017)
  other arithmetic: 71.4 us -> 92 us
    concatenate x0 -> x2, other arithmetic: none -> 12.4 us  [the longest x1 8.9 us: per_device(): jnp.concatenate([expand_weight_grad, shrink_weight_grad.reshape(model_wid...]
    convert_element_type x0 -> x3, local copies, waits for them, and re-layouts: none -> 8.8 us  [the longest x1 8.63 us: per_device(): hidden_low = hidden.astype(jnp.bfloat16)]
    reshape x22 -> x13, local copies, waits for them, and re-layouts: 17.5 us -> 9.89 us  [pack_columns(): cols = [p.reshape(rows, -1) for p in parts]]
    concatenate x11 -> x28, local copies, waits for them, and re-layouts: 35.6 us -> 29.8 us  [pack_columns(): return jnp.concatenate(cols, axis=1)]
    unnamed x96 -> x136, local copies, waits for them, and re-layouts: 12.4 us -> 15.7 us
  transfers between devices with their start and end apart: 15 -> 15, of which waited for: 11 -> 10; matrix products, arithmetic and copies ran while one was open for 24% -> 23% of each run, Pallas kernels for 23% -> 22%
where the time goes in v7:
time: 760 us; the launch traced here: 750 us
  Pallas kernels  166 us (22%)
  local copies, waits for them, and re-layouts  158 us (21%)
  waiting for transfers between devices  123 us (16%)
  matrix products  116 us (15%)
  other arithmetic  92 us (12%)
  starting transfers between devices  79.9 us (11%)
  between operations  15.1 us (2%)
    pallas_call x1, Pallas kernels, attention_backward(): pl.pallas_call(_bwd_kernel, out_shape=(jax.ShapeDtypeStruct((heads, lengt...  101 us
    ppermute x10, starting transfers between devices, hypercube_reduce_scatter(): got = lax.ppermute(send, axis, [(j, j ^ 1 << b) for j in range(size)])  79.7 us
    pallas_call x1, Pallas kernels, attention_forward(): pl.pallas_call(_fwd_kernel, out_shape=jax.ShapeDtypeStruct((heads, length...  65.5 us
    all_gather x1, waiting for transfers between devices, per_device(): lax.all_gather(first_pack, ('group', 'shard'), axis=0, tiled=True)  52.8 us
    all_gather x1, waiting for transfers between devices, per_device(): lax.all_gather(jnp.concatenate([ffn_part, attn_left.astype(jnp.bfloat16),...  49 us
    dot_general x1, matrix products, per_device(): jnp.dot(second_low, expand_full, preferred_element_type=jnp.float32)  34.2 us
    concatenate x28, local copies, waits for them, and re-layouts, pack_columns(): return jnp.concatenate(cols, axis=1)  29.8 us
    ppermute x10, waiting for transfers between devices, hypercube_reduce_scatter(): got = lax.ppermute(send, axis, [(j, j ^ 1 << b) for j in range(size)])  20.4 us
  transfers between devices with their start and end apart: 15, of which 10 were waited for; matrix products, arithmetic and copies ran while one was open for 23% of the time, Pallas kernels for 22%

profile of v7, /device:TPU:0, one launch (start us, length us, event | category | flops | bytes accessed | tf_op | source)
XLA Modules:
  0.0 750.1 jit_solution(10623135829453245240)
XLA Ops:
  29.6 52.8 %all-gather.5.cloned.1.call-done = bf16[768,2432]{1,0:T(8,128)(2,1)} async-done(((bf16[24,2432]{1,0:T(8,128)(2,1)}), bf16[768,2432]{1,0:T(8,128)(2,1)}) %all-gather.5.cloned.1.call-update) | async-done | bytes 3735568 | tf_op jit(solution)/shard_map/all_gather | solution.py:339
  82.5 4.2 convert_reduce_fusion.1
  87.6 4.2 add_convert_fusion.2
  105.9 65.5 %shard_map.339 = f32[12,1024,64]{2,1,0:T(8,128)} custom-call(s32[2]{0:T(128)} %and_select_fusion.lo_ref, bf16[12,1024,64]{2,1,0:T(8,128)(2,1)} %copy.196.q_ref, bf16[12,64,1024]{2,1,0:T(8,128)(2,1)} %bitcast.99, bf16[12,1024,64]{2,1,0:T(8,128)(2,1)} %copy.197.v_ref, s32[1024,1]{1,0:T(8,128)} %copy.198.segq_ref, s32[1,1024]{1,0:T(1,128)} %bitcast.132), custom_call_target="tpu_custom_call" | custom-call | flops 1610612736 | bytes 6291456 | tf_op jit(solution)/shard_map/pallas_call | solution.py:127
  171.3 6.1 copy.199
  177.5 3.8 copy.200
  181.3 3.3 reduce_sum.276
  184.6 3.7 multiply_reduce_fusion.4
  195.7 4.1 fusion.48
  203.6 34.2 %fusion.43 = (f32[1024]{0:T(1024)S(1)}, f32[1024,3072]{1,0:T(8,128)S(1)}, f32[1024,3072]{1,0:T(8,128)}, f32[1024,3072]{1,0:T(8,128)}) fusion(f32[3072]{0:T(1024)S(1)} %reshape.589, bf16[1024,768]{0,1:T(8,128)(2,1)S(1)} %add_convert_fusion.5, bf16[768,3840]{1,0:T(8,128)(2,1)S(1)} %copy-done.63), kind=kOutput, calls=%fused_computation.165 | convolution fusion | flops 5039455232 | bytes 44056576 | tf_op jit(solution)/shard_map/dot_general | solution.py:405
  239.3 3.4 copy-done.4
  242.7 16.4 %multiply_reduce_fusion = (bf16[3072]{0:T(1024)(128)(2,1)}, f32[1024]{0:T(1024)S(1)}, f32[1024]{0:T(1024)S(1)}, bf16[3072]{0:T(1024)(128)(2,1)}, bf16[1024,3072]{1,0:T(8,128)(2,1)}, /*index=5*/f32[1024,3072]{1,0:T(8,128)}) fusion(f32[1024,3072]{1,0:T(8,128)} %copy-done.4, f32[1024]{0:T(1024)S(1)} %add_rsqrt_fusion, f32[1024]{0:T(1024)S(1)} %broadcast_multiply_fusion.2, ...), kind=kOutput, calls=%fused_computation.3 | convolution fusion | flops 4869578752 | bytes 37801984 | tf_op jit(solution)/shard_map/td,fd->tf/dot_general | solution.py:427
  259.1 18.9 %fusion.42 = (bf16[3072]{0:T(1024)(128)(2,1)}, bf16[1024,3072]{1,0:T(8,128)(2,1)S(1)}) fusion(f32[1024,3072]{1,0:T(8,128)} %get-tuple-element.151, f32[1024]{0:T(1024)S(1)} %get-tuple-element.173, f32[1024,3072]{1,0:T(8,128)} %copy-done.4, f32[1024]{0:T(1024)S(1)} %broadcast_multiply_fusion.2, f32[1024]{0:T(1024)S(1)} %get-tuple-element.174, ...), kind=kLoop, calls=%fused_computation.164 | loop fusion | flops 72348672 | bytes 56670208 | tf_op jit(solution)/shard_map/reduce_sum | solution.py:434
  278.0 6.7 fusion.49
  284.8 3.8 copy.203
  288.7 2.9 multiply_reduce_fusion.7
  305.0 4.4 convert_reduce_fusion.9
  309.5 6.4 multiply_reduce_fusion.5
  319.0 3.3 convolution_convert_fusion.2
  322.4 8.6 %copy.205 = bf16[1024,3072]{0,1:T(8,128)(2,1)} copy(bf16[1024,3072]{1,0:T(8,128)(2,1)} %get-tuple-element.152) | data formatting | bytes 12582912 | tf_op jit(solution)/shard_map/convert_element_type | solution.py:412
  331.0 3.6 copy.206
  334.6 6.7 convolution_convert_fusion
  341.3 8.6 %reshape.555 = bf16[768,3072]{1,0:T(8,128)(2,1)} reshape(bf16[3072,768]{1,0:T(8,128)(2,1)} %convolution_convert_fusion) | data formatting | bytes 9437184 | tf_op jit(solution)/shard_map/reshape | solution.py:474
  350.1 9.8 %convolution_convert_fusion.1 = bf16[768,3072]{1,0:T(8,128)(2,1)} fusion(bf16[1024,768]{0,1:T(8,128)(2,1)S(1)} %bitcast.126, bf16[1024,3072]{1,0:T(8,128)(2,1)} %copy-done.21), kind=kOutput, calls=%fused_computation.29 | convolution fusion | flops 4834197504 | bytes 12582912 | tf_op jit(solution)/shard_map/td,tf->df/dot_general | solution.py:435
  363.0 8.9 %pad_maximum_fusion = bf16[768,7040]{1,0:T(8,128)(2,1)} fusion(bf16[768,128]{1,0:T(8,128)(2,1)S(1)} %bitcast.130, bf16[768,768]{1,0:T(8,128)(2,1)S(1)} %convolution_convert_fusion.2, bf16[768,3072]{1,0:T(8,128)(2,1)} %reshape.555, bf16[768,3072]{1,0:T(8,128)(2,1)} %convolution_convert_fusion.1), kind=kLoop, calls=%fused_computation.24 | loop fusion | flops 43253760 | bytes 21626880 | tf_op jit(solution)/shard_map/concatenate | solution.py:471
  381.9 100.6 %shard_map.340 = (f32[12,1024,64]{2,1,0:T(8,128)}, f32[12,64,1024]{2,1,0:T(8,128)}, f32[12,64,1024]{2,1,0:T(8,128)}) custom-call(s32[2]{0:T(128)} %and_select_fusion.lo_ref, bf16[12,1024,64]{2,1,0:T(8,128)(2,1)} %copy.196.q_ref, bf16[12,64,1024]{2,1,0:T(8,128)(2,1)} %bitcast.107, bf16[12,1024,64]{2,1,0:T(8,128)(2,1)} %copy.222.k_ref, ...), custom_call_target="tpu_custom_call" | custom-call | flops 4026531840 | bytes 12582912 | tf_op jit(solution)/shard_map/pallas_call | solution.py:155
  482.5 3.4 convert.93
  491.5 9.0 %fusion.50 = (f32[768]{0:T(1024)S(1)}, f32[1024,768]{1,0:T(8,128)}) fusion(bf16[768,2432]{1,0:T(8,128)(2,1)} %all-gather.5.cloned.1.call-done, bf16[1024,768]{0,1:T(8,128)(2,1)} %bitcast.114, bf16[1024,768]{0,1:T(8,128)(2,1)} %bitcast.117, bf16[1024,768]{0,1:T(8,128)(2,1)} %bitcast.120), kind=kOutput, calls=%fused_computation.171 | convolution fusion | flops 3638820096 | bytes 11406336 | tf_op jit(solution)/shard_map/te,de->td/dot_general | solution.py:502
  500.5 3.7 copy.226
  504.2 3.7 fusion.23
  524.7 6.3 fusion.41
  531.1 3.5 pad_maximum_fusion.1
  539.7 15.7 %collective-permute-start = (bf16[384,1152]{1,0:T(8,128)(2,1)S(1)}, bf16[384,1152]{1,0:T(8,128)(2,1)S(1)}, u32[]{:S(2)}, u32[]{:S(2)}) collective-permute-start(bf16[384,1152]{1,0:T(8,128)(2,1)S(1)} %bitcast.129), channel_id=1, source_target_pairs={{0,2},{2,0},{4,6},{6,4},{8,10},{10,8},{12,14},{14,12},{16,18},{18,... | collective-permute-start | bytes 2654216 | tf_op jit(solution)/shard_map/ppermute | solution.py:287
  559.9 31.4 %collective-permute-start.6 = (bf16[192,1280]{1,0:T(8,128)(2,1)S(1)}, bf16[192,1280]{1,0:T(8,128)(2,1)S(1)}, u32[]{:S(2)}, u32[]{:S(2)}) collective-permute-start(bf16[192,1280]{1,0:T(8,128)(2,1)S(1)} %select_convert_fusion.2), channel_id=1, source_target_pairs={{0,8},{2,10},{4,12},{6,14},{8,0},{10,2},{12,4},{14,6},{16,24},{18,... | collective-permute-start | bytes 1474568 | tf_op jit(solution)/shard_map/ppermute | solution.py:287
  591.4 10.4 %collective-permute-start.2 = (bf16[96,1152]{1,0:T(8,128)(2,1)S(1)}, bf16[96,1152]{1,0:T(8,128)(2,1)S(1)}, u32[]{:S(2)}, u32[]{:S(2)}) collective-permute-start(bf16[96,1152]{1,0:T(8,128)(2,1)S(1)} %select_convert_fusion.5), channel_id=1, source_target_pairs={{0,8},{2,10},{4,12},{6,14},{8,0},{10,2},{12,4},{14,6},{16,24},{18,... | collective-permute-start | bytes 663560 | tf_op jit(solution)/shard_map/ppermute | solution.py:287
  603.1 4.3 collective-permute-done.2
  607.6 16.5 %collective-permute-start.3 = (bf16[48,1152]{1,0:T(8,128)(2,1)S(1)}, bf16[48,1152]{1,0:T(8,128)(2,1)S(1)}, u32[]{:S(2)}, u32[]{:S(2)}) collective-permute-start(bf16[48,1152]{1,0:T(8,128)(2,1)S(1)} %select_convert_fusion.7), channel_id=1, source_target_pairs={{0,1},{1,0},{2,3},{3,2},{4,5},{5,4},{6,7},{7,6},{8,9},{9,8},{10,11... | collective-permute-start | bytes 331784 | tf_op jit(solution)/shard_map/ppermute | solution.py:287
  626.8 4.1 collective-permute-done.7
  632.4 3.6 collective-permute-done.8
  638.0 3.8 collective-permute-done.9
  642.8 9.1 %add_convert_fusion.4 = bf16[1024,768]{0,1:T(8,128)(2,1)S(1)} fusion(f32[1024,768]{0,1:T(8,128)} %copy-done.2, bf16[1024,3072]{1,0:T(8,128)(2,1)} %get-tuple-element.152, bf16[3072,768]{1,0:T(8,128)(2,1)} %all-gather.9.cloned.1.call-done, f32[768]{0:T(1024)S(1)} %copy-done.62), kind=kOutput, calls=%fused_computation.64 | convolution fusion | flops 4834197504 | bytes 15731712 | tf_op jit(solution)/shard_map/dot_general | solution.py:415
  653.5 3.9 fusion.22
  659.1 49.0 %all-gather.11.cloned.1.call-done = bf16[384,9472]{1,0:T(8,128)(2,1)} async-done(((bf16[24,9472]{1,0:T(8,128)(2,1)}), bf16[384,9472]{1,0:T(8,128)(2,1)}) %all-gather.11.cloned.1.call-update) | async-done | bytes 7274512 | tf_op jit(solution)/shard_map/all_gather | solution.py:528
  708.1 9.2 %convert_element_type.337 = f32[384,9472]{1,0:T(8,128)} convert(bf16[384,9472]{1,0:T(8,128)(2,1)} %all-gather.11.cloned.1.call-done) | non-fusion elementwise | flops 3637248 | bytes 21823488 | tf_op jit(solution)/shard_map/convert_element_type | solution.py:540
  717.3 3.5 slice_reduce_fusion.2
  724.2 7.4 fusion.45
  731.6 6.1 reshape.580
  737.7 3.5 slice.338
  (301 shorter events, 128.8 us)
Async XLA Ops:
  7.2 16.7 %copy-start.13 = (bf16[1024,768]{1,0:T(8,128)(2,1)S(1)}, bf16[1024,768]{1,0:T(8,128)(2,1)}, u32[]{:S(2)}) copy-start(bf16[1024,768]{1,0:T(8,128)(2,1)} %param.39) | copy-start | bytes 4718596
  7.2 17.0 %copy-start.65 = (s32[1,5]{1,0:T(1,128)S(1)}, s32[1,5]{1,0:T(1,128)}, u32[]{:S(2)}) copy-start(s32[1,5]{1,0:T(1,128)} %param.21) | copy-start | bytes 64
  7.2 18.8 %copy-start.25 = (bf16[1024,768]{1,0:T(8,128)(2,1)S(1)}, bf16[1024,768]{1,0:T(8,128)(2,1)}, u32[]{:S(2)}) copy-start(bf16[1024,768]{1,0:T(8,128)(2,1)} %param.20) | copy-start | bytes 4718596
  7.2 75.2 %all-gather.5.cloned.1.call-start = ((), (), s32[]{:S(2)}) async-start(), calls=%async_computation.1 | async-start | bytes 3852288 | tf_op jit(solution)/shard_map/all_gather | solution.py:339
  18.9 176.8 %all-gather.7.cloned.1.call-start = ((), (), s32[]{:S(2)}) async-start(), calls=%async_computation.2 | async-start | bytes 6082560 | tf_op jit(solution)/shard_map/all_gather | solution.py:357
  20.5 222.1 %all-gather.9.cloned.1.call-start = ((), (), s32[]{:S(2)}) async-start(), calls=%async_computation.3 | async-start | bytes 4866048 | tf_op jit(solution)/shard_map/all_gather | solution.py:360
  21.3 513.3 %reduce-scatter.4.cloned.1.call-start = ((), (), s32[]{:S(2)}) async-start(), calls=%async_computation.5 | async-start | bytes 11151360
  26.8 168.9 %copy-start = (bf16[1024,768]{0,1:T(8,128)(2,1)}, bf16[1024,768]{0,1:T(8,128)(2,1)S(1)}, u32[]{:S(2)}) copy-start(bf16[1024,768]{0,1:T(8,128)(2,1)S(1)} %copy.182) | copy-start | bytes 4718596
  27.1 60.2 %copy-start.36 = (f32[1024]{0:T(1024)}, f32[1024]{0:T(1024)S(1)}, u32[]{:S(2)}) copy-start(f32[1024]{0:T(1024)S(1)} %broadcast_multiply_fusion.11) | copy-start | bytes 12292
  27.6 64.3 %copy-start.46 = (f32[1024]{0:T(1024)}, f32[1024]{0:T(1024)S(1)}, u32[]{:S(2)}) copy-start(f32[1024]{0:T(1024)S(1)} %add_rsqrt_fusion.3) | copy-start | bytes 12292
  82.5 4.8 copy-start.24
  86.7 109.0 %copy-start.52 = (f32[768]{0:T(1024)}, f32[768]{0:T(1024)S(1)}, u32[]{:S(2)}) copy-start(f32[768]{0:T(1024)S(1)} %get-tuple-element.136) | copy-start | bytes 9220
  86.7 113.6 %copy-start.44 = (f32[768]{0:T(1024)}, f32[768]{0:T(1024)S(1)}, u32[]{:S(2)}) copy-start(f32[768]{0:T(1024)S(1)} %get-tuple-element.133) | copy-start | bytes 9220
  95.9 5.5 copy-start.6
  103.1 68.3 %copy-start.7 = (bf16[1024,768]{0,1:T(8,128)(2,1)}, bf16[1024,768]{0,1:T(8,128)(2,1)S(1)}, u32[]{:S(2)}) copy-start(bf16[1024,768]{0,1:T(8,128)(2,1)S(1)} %copy.195) | copy-start | bytes 4718596
  184.6 11.1 %copy-start.40 = (f32[1024]{0:T(1024)}, f32[1024]{0:T(1024)S(1)}, u32[]{:S(2)}) copy-start(f32[1024]{0:T(1024)S(1)} %broadcast_multiply_fusion.10) | copy-start | bytes 12292
  188.3 7.3 copy-start.55
  200.2 37.7 %copy-start.48 = (f32[1024]{0:T(1024)}, f32[1024]{0:T(1024)S(1)}, u32[]{:S(2)}) copy-start(f32[1024]{0:T(1024)S(1)} %add_rsqrt_fusion.1) | copy-start | bytes 12292
  203.6 34.2 %copy-start.19 = (bf16[1024,768]{0,1:T(8,128)(2,1)}, bf16[1024,768]{0,1:T(8,128)(2,1)S(1)}, u32[]{:S(2)}) copy-start(bf16[1024,768]{0,1:T(8,128)(2,1)S(1)} %add_convert_fusion.5) | copy-start | bytes 4718596
  237.9 4.8 copy-start.4
  259.1 18.9 %copy-start.64 = (bf16[768,3840]{1,0:T(8,128)(2,1)S(1)}, bf16[768,3840]{1,0:T(8,128)(2,1)}, u32[]{:S(2)}) copy-start(bf16[768,3840]{1,0:T(8,128)(2,1)} %all-gather.7.cloned.1.call-done) | copy-start | bytes 17694724
  278.0 6.7 copy-start.21
  309.4 6.4 copy-start.11
  309.4 8.6 %copy-start.61 = (bf16[768]{0:T(1024)(128)(2,1)S(1)}, bf16[768]{0:T(1024)(128)(2,1)}, u32[]{:S(2)}) copy-start(bf16[768]{0:T(1024)(128)(2,1)} %get-tuple-element.145) | copy-start | bytes 4612
  309.5 9.6 %copy-start.26 = (bf16[1024,16,2,24]{0,3,2,1:T(8,128)(2,1)S(1)}, bf16[1024,16,2,24]{0,3,2,1:T(8,128)(2,1)}, u32[]{:S(2)}) copy-start(bf16[1024,16,2,24]{0,3,2,1:T(8,128)(2,1)} %copy.208) | copy-start | bytes 4718596
  341.3 8.6 %copy-start.20 = (bf16[1024,768]{0,1:T(8,128)(2,1)S(1)}, bf16[1024,768]{0,1:T(8,128)(2,1)}, u32[]{:S(2)}) copy-start(bf16[1024,768]{0,1:T(8,128)(2,1)} %copy-done.19) | copy-start | bytes 4718596
  350.1 9.8 %copy-start.10 = (f32[1024,768]{1,0:T(8,128)S(1)}, f32[1024,768]{1,0:T(8,128)}, u32[]{:S(2)}) copy-start(f32[1024,768]{1,0:T(8,128)} %copy.200) | copy-start | bytes 9437188
  350.1 9.8 %copy-start.22 = (f32[1024,768]{1,0:T(8,128)S(1)}, f32[1024,768]{1,0:T(8,128)}, u32[]{:S(2)}) copy-start(f32[1024,768]{1,0:T(8,128)} %get-tuple-element.170) | copy-start | bytes 9437188
  350.1 9.8 %copy-start.54 = (f32[768]{0:T(1024)S(1)}, f32[768]{0:T(1024)}, u32[]{:S(2)}) copy-start(f32[768]{0:T(1024)} %copy-done.52) | copy-start | bytes 9220
  350.1 9.8 %copy-start.57 = (f32[1024]{0:T(1024)S(1)}, f32[1024]{0:T(1024)}, u32[]{:S(2)}) copy-start(f32[1024]{0:T(1024)} %copy-done.55) | copy-start | bytes 12292
  371.9 336.2 %all-gather.11.cloned.1.call-start = ((), (), s32[]{:S(2)}) async-start(), calls=%async_computation.4 | async-start | bytes 7729152 | tf_op jit(solution)/shard_map/all_gather | solution.py:528
  482.5 6.1 copy-start.12
  504.2 7.8 %copy-start.18 = (bf16[12,64,1024]{2,1,0:T(8,128)(2,1)S(1)}, bf16[12,64,1024]{2,1,0:T(8,128)(2,1)}, u32[]{:S(2)}) copy-start(bf16[12,64,1024]{2,1,0:T(8,128)(2,1)} %convert.93) | copy-start | bytes 4718596
  524.7 6.3 copy-start.27
  539.7 17.7 %collective-permute-start = (bf16[384,1152]{1,0:T(8,128)(2,1)S(1)}, bf16[384,1152]{1,0:T(8,128)(2,1)S(1)}, u32[]{:S(2)}, u32[]{:S(2)}) collective-permute-start(bf16[384,1152]{1,0:T(8,128)(2,1)S(1)} %bitcast.129), channel_id=1, source_target_pairs={{0,2},{2,0},{4,6},{6,4},{8,10},{10,8},{12,14},{14,12},{16,18},{18,... | collective-permute-start | bytes 2654216 | tf_op jit(solution)/shard_map/ppermute | solution.py:287
  555.8 3.8 collective-permute-start.5
  557.7 33.5 %collective-permute-start.1 = (bf16[192,1152]{1,0:T(8,128)(2,1)S(1)}, bf16[192,1152]{1,0:T(8,128)(2,1)S(1)}, u32[]{:S(2)}, u32[]{:S(2)}) collective-permute-start(bf16[192,1152]{1,0:T(8,128)(2,1)S(1)} %select_convert_fusion.3), channel_id=1, source_target_pairs={{0,4},{2,6},{4,0},{6,2},{8,12},{10,14},{12,8},{14,10},{16,20},{18,... | collective-permute-start | bytes 1327112 | tf_op jit(solution)/shard_map/ppermute | solution.py:287
  559.9 43.1 %collective-permute-start.6 = (bf16[192,1280]{1,0:T(8,128)(2,1)S(1)}, bf16[192,1280]{1,0:T(8,128)(2,1)S(1)}, u32[]{:S(2)}, u32[]{:S(2)}) collective-permute-start(bf16[192,1280]{1,0:T(8,128)(2,1)S(1)} %select_convert_fusion.2), channel_id=1, source_target_pairs={{0,8},{2,10},{4,12},{6,14},{8,0},{10,2},{12,4},{14,6},{16,24},{18,... | collective-permute-start | bytes 1474568 | tf_op jit(solution)/shard_map/ppermute | solution.py:287
  591.4 16.1 %collective-permute-start.2 = (bf16[96,1152]{1,0:T(8,128)(2,1)S(1)}, bf16[96,1152]{1,0:T(8,128)(2,1)S(1)}, u32[]{:S(2)}, u32[]{:S(2)}) collective-permute-start(bf16[96,1152]{1,0:T(8,128)(2,1)S(1)} %select_convert_fusion.5), channel_id=1, source_target_pairs={{0,8},{2,10},{4,12},{6,14},{8,0},{10,2},{12,4},{14,6},{16,24},{18,... | collective-permute-start | bytes 663560 | tf_op jit(solution)/shard_map/ppermute | solution.py:287
  603.1 38.8 %copy-start.35 = (bf16[24,7040]{1,0:T(8,128)(2,1)S(1)}, bf16[24,7040]{1,0:T(8,128)(2,1)}, u32[]{:S(2)}) copy-start(bf16[24,7040]{1,0:T(8,128)(2,1)} %reduce-scatter.4.cloned.1.call-done) | copy-start | bytes 1013764
  607.5 35.2 %copy-start.62 = (f32[768]{0:T(1024)S(1)}, f32[768]{0:T(1024)}, u32[]{:S(2)}) copy-start(f32[768]{0:T(1024)} %get-tuple-element.131) | copy-start | bytes 9220
  607.6 19.2 %collective-permute-start.3 = (bf16[48,1152]{1,0:T(8,128)(2,1)S(1)}, bf16[48,1152]{1,0:T(8,128)(2,1)S(1)}, u32[]{:S(2)}, u32[]{:S(2)}) collective-permute-start(bf16[48,1152]{1,0:T(8,128)(2,1)S(1)} %select_convert_fusion.7), channel_id=1, source_target_pairs={{0,1},{1,0},{2,3},{3,2},{4,5},{5,4},{6,7},{7,6},{8,9},{9,8},{10,11... | collective-permute-start | bytes 331784 | tf_op jit(solution)/shard_map/ppermute | solution.py:287
  624.1 6.8 collective-permute-start.7
  631.0 4.9 collective-permute-start.8
  631.4 6.6 collective-permute-start.4
  636.0 5.8 collective-permute-start.9
  642.7 10.7 %copy-start.59 = (f32[1024]{0:T(1024)S(1)}, f32[1024]{0:T(1024)}, u32[]{:S(2)}) copy-start(f32[1024]{0:T(1024)} %get-tuple-element.130) | copy-start | bytes 12292
  642.7 10.7 %copy-start.58 = (f32[1024]{0:T(1024)S(1)}, f32[1024]{0:T(1024)}, u32[]{:S(2)}) copy-start(f32[1024]{0:T(1024)} %get-tuple-element.141) | copy-start | bytes 12292
  (33 other events, 108.7 us)
Sparse Core Ops, SparseCore 0:
  19.0 63.4 all-gather.4
  85.9 66.3 all-gather.6
  155.3 62.4 all-gather.8
  372.0 159.6 reduce-scatter.3
  642.8 65.2 all-gather.10

commit v8 on v6

--- a/solution.py
+++ b/solution.py
@@ -525,14 +525,18 @@
         "group",
         axis=0,
         tiled=True,
-    ).astype(jnp.float32)
+    )
     ffn_cols = ffn_pack.shape[1]
     ffn_back = both[:, :ffn_cols]
     attn_back = both[:, ffn_cols:]
     half = both.shape[0]
-    expand_out = ffn_back[:, :wide_width]
-    shrink_out = ffn_back[:, wide_width : 2 * wide_width].reshape(half * ratio, model_width)
-    proj_out = ffn_back[:, 2 * wide_width : 2 * wide_width + model_width]
+    expand_out = ffn_back[:, :wide_width].astype(jnp.float32)
+    shrink_out = (
+        ffn_back[:, wide_width : 2 * wide_width]
+        .reshape(half * ratio, model_width)
+        .astype(jnp.float32)
+    )
+    proj_out = ffn_back[:, 2 * wide_width : 2 * wide_width + model_width].astype(jnp.float32)
     (
         second_gain_out,
         second_shift_out,
@@ -543,14 +547,16 @@
         gain_inner_out,
         shift_inner_out,
         pbias_out,
-    ) = unpack_columns(ffn_back[:, 2 * wide_width + model_width :], ffn_small_widths)
-    qkv_out = attn_back[:, :qkv_width]
+    ) = unpack_columns(
+        ffn_back[:, 2 * wide_width + model_width :].astype(jnp.float32), ffn_small_widths
+    )
+    qkv_out = attn_back[:, :qkv_width].astype(jnp.float32)
     (
         gain_one_out,
         shift_one_out,
         qbias_out,
         vbias_out,
-    ) = unpack_columns(attn_back[:, qkv_width:], [1] * 4)
+    ) = unpack_columns(attn_back[:, qkv_width:].astype(jnp.float32), [1] * 4)
     return (
         block_output,
         input_grad,

time: 747 us -> 737 us (0.987)
  local copies, waits for them, and re-layouts: 161 us -> 146 us
    slice x3 -> x0, local copies, waits for them, and re-layouts: 13.1 us -> none  [the longest x1 7.4 us: per_device(): ffn_back[:, wide_width:2 * wide_width].reshape(half * ratio, model_width)]
where the time goes in v8:
time: 737 us; the launch traced here: 728 us
  Pallas kernels  166 us (23%)
  local copies, waits for them, and re-layouts  146 us (20%)
  waiting for transfers between devices  124 us (17%)
  matrix products  121 us (16%)
  starting transfers between devices  79.6 us (11%)
  other arithmetic  76.3 us (10%)
  between operations  15 us (2%)
    pallas_call x1, Pallas kernels, attention_backward(): pl.pallas_call(_bwd_kernel, out_shape=(jax.ShapeDtypeStruct((heads, lengt...  101 us
    ppermute x10, starting transfers between devices, hypercube_reduce_scatter(): got = lax.ppermute(send, axis, [(j, j ^ 1 << b) for j in range(size)])  79.4 us
    pallas_call x1, Pallas kernels, attention_forward(): pl.pallas_call(_fwd_kernel, out_shape=jax.ShapeDtypeStruct((heads, length...  65.5 us
    all_gather x1, waiting for transfers between devices, per_device(): lax.all_gather(first_pack, ('group', 'shard'), axis=0, tiled=True)  53 us
    all_gather x1, waiting for transfers between devices, per_device(): lax.all_gather(jnp.concatenate([ffn_part, attn_left.astype(jnp.bfloat16),...  49.4 us
    dot_general x1, matrix products, per_device(): jnp.dot(second_low, expand_full, preferred_element_type=jnp.float32)  39 us
    ppermute x10, waiting for transfers between devices, hypercube_reduce_scatter(): got = lax.ppermute(send, axis, [(j, j ^ 1 << b) for j in range(size)])  19.6 us
    reduce_sum x1, other arithmetic, per_device(): expand_bias_grad = jnp.sum(grad_pre.astype(jnp.float32), axis=0)  18.3 us
  transfers between devices with their start and end apart: 15, of which 11 were waited for; matrix products, arithmetic and copies ran while one was open for 24% of the time, Pallas kernels for 23%

profile of v8, /device:TPU:0, one launch (start us, length us, event | category | flops | bytes accessed | tf_op | source)
XLA Modules:
  0.0 727.7 jit_solution(14930720055259401771)
XLA Ops:
  29.5 53.0 %all-gather.5.cloned.1.call-done = bf16[768,2432]{1,0:T(8,128)(2,1)} async-done(((bf16[24,2432]{1,0:T(8,128)(2,1)}), bf16[768,2432]{1,0:T(8,128)(2,1)}) %all-gather.5.cloned.1.call-update) | async-done | bytes 3735568 | tf_op jit(solution)/shard_map/all_gather | solution.py:338
  84.0 4.2 convert_reduce_fusion.1
  88.2 6.4 add_convert_fusion.2
  98.6 2.8 copy.229.q_ref
  105.8 2.8 copy.230.v_ref
  108.6 65.5 %shard_map.339 = f32[12,1024,64]{2,1,0:T(8,128)} custom-call(s32[2]{0:T(128)} %and_select_fusion.lo_ref, bf16[12,1024,64]{2,1,0:T(8,128)(2,1)} %copy.229.q_ref, bf16[12,64,1024]{2,1,0:T(8,128)(2,1)} %bitcast.81, bf16[12,1024,64]{2,1,0:T(8,128)(2,1)} %copy.230.v_ref, s32[1024,1]{1,0:T(8,128)} %copy.231.segq_ref, s32[1,1024]{1,0:T(1,128)} %bitcast.108), custom_call_target="tpu_custom_call" | custom-call | flops 1610612736 | bytes 6291456 | tf_op jit(solution)/shard_map/pallas_call | solution.py:127
  174.1 6.1 copy.232
  180.2 4.0 copy.233
  184.2 3.3 reduce_sum.276
  187.5 3.8 multiply_reduce_fusion.4
  193.6 4.2 fusion.44
  198.2 39.0 %fusion.40 = (f32[1024]{0:T(1024)S(1)}, f32[1024,3072]{1,0:T(8,128)S(1)}, f32[1024,3072]{1,0:T(8,128)}, f32[1024,3072]{1,0:T(8,128)}) fusion(f32[3072]{0:T(1024)S(1)} %reshape.540, bf16[768,3840]{1,0:T(8,128)(2,1)} %all-gather.7.cloned.1.call-done, f32[1024,768]{0,1:T(8,128)S(1)} %get-tuple-element.186, f32[768]{0:T(1024)S(1)} %get-tuple-element.141, ...), kind=kOutput, calls=%fused_computation.163 | convolution fusion | flops 5043387392 | bytes 45643776 | tf_op jit(solution)/shard_map/dot_general | solution.py:404
  238.7 3.3 copy-done
  242.0 15.4 %multiply_reduce_fusion = (bf16[3072]{0:T(1024)(128)(2,1)S(1)}, f32[1024]{0:T(1024)S(1)}, f32[1024]{0:T(1024)S(1)}, bf16[3072]{0:T(1024)(128)(2,1)S(1)}, bf16[1024,3072]{1,0:T(8,128)(2,1)}, /*index=5*/f32[1024,3072]{1,0:T(8,128)}) fusion(f32[1024,3072]{1,0:T(8,128)} %copy-done, f32[1024]{0:T(1024)S(1)} %add_rsqrt_fusion, ...), kind=kOutput, calls=%fused_computation.3 | convolution fusion | flops 4869578752 | bytes 37801984 | tf_op jit(solution)/shard_map/td,fd->tf/dot_general | solution.py:423
  257.4 18.3 %fusion.39 = (bf16[3072]{0:T(1024)(128)(2,1)S(1)}, bf16[1024,3072]{1,0:T(8,128)(2,1)S(1)}) fusion(f32[1024,3072]{1,0:T(8,128)} %get-tuple-element.170, f32[1024]{0:T(1024)S(1)} %get-tuple-element.194, f32[1024,3072]{1,0:T(8,128)} %copy-done, f32[1024]{0:T(1024)S(1)} %broadcast_multiply_fusion.2, f32[1024]{0:T(1024)S(1)} %get-tuple-element.195, ...), kind=kLoop, calls=%fused_computation.162 | loop fusion | flops 72348672 | bytes 56670208 | tf_op jit(solution)/shard_map/reduce_sum | solution.py:430
  275.8 7.2 convolution_convert_fusion.1
  283.0 6.8 fusion.45
  289.8 3.5 copy.236
  293.3 3.0 multiply_reduce_fusion.7
  296.3 9.7 %convolution_convert_fusion = bf16[3072,768]{1,0:T(8,128)(2,1)} fusion(bf16[1024,3072]{1,0:T(8,128)(2,1)} %get-tuple-element.171, bf16[1024,768]{1,0:T(8,128)(2,1)S(1)} %copy-done.16), kind=kOutput, calls=%fused_computation.26 | convolution fusion | flops 4834197504 | bytes 12582912 | tf_op jit(solution)/shard_map/tf,td->fd/dot_general | solution.py:419
  306.0 8.5 %reshape.501 = bf16[768,3072]{1,0:T(8,128)(2,1)} reshape(bf16[3072,768]{1,0:T(8,128)(2,1)} %convolution_convert_fusion) | data formatting | bytes 9437184 | tf_op jit(solution)/shard_map/reshape | solution.py:464
  314.5 3.8 convert_reduce_fusion.9
  318.3 3.0 convolution_convert_fusion.2
  325.7 4.9 multiply_reduce_fusion.5
  335.1 18.0 %concatenate.51 = bf16[768,7040]{1,0:T(8,128)(2,1)} concatenate(bf16[768,3072]{1,0:T(8,128)(2,1)} %convolution_convert_fusion.1, bf16[768,3072]{1,0:T(8,128)(2,1)} %reshape.501, bf16[768,768]{1,0:T(8,128)(2,1)} %convolution_convert_fusion.2, bf16[768,1]{1,0:T(8,128)(2,1)S(1)} %reshape.554, bf16[768,1]{1,0:T(8,128)(2,1)} %reshape.555, bf16[768,1]{1,0:T(8,128)(2,1)S(1)} %copy-done.22, ...), dimensions={1} | concatenate | bytes 21626880 | tf_op jit(solution)/shard_map/concatenate | solution.py:461
  353.1 10.1 %copy.252 = bf16[16,2,24,7040]{3,2,1,0:T(8,128)(2,1)} copy(bf16[16,2,24,7040]{3,2,0,1:T(8,128)(2,1)} %bitcast.78) | data formatting | bytes 21626880 | tf_op jit(solution)/shard_map/transpose | solution.py:245
  368.0 2.8 copy.248.do_ref
  370.9 100.6 %shard_map.340 = (f32[12,1024,64]{2,1,0:T(8,128)}, f32[12,64,1024]{2,1,0:T(8,128)}, f32[12,64,1024]{2,1,0:T(8,128)}) custom-call(s32[2]{0:T(128)} %and_select_fusion.lo_ref, bf16[12,1024,64]{2,1,0:T(8,128)(2,1)} %copy.229.q_ref, bf16[12,64,1024]{2,1,0:T(8,128)(2,1)} %bitcast.89, bf16[12,1024,64]{2,1,0:T(8,128)(2,1)} %copy.247.k_ref, ...), custom_call_target="tpu_custom_call" | custom-call | flops 4026531840 | bytes 12582912 | tf_op jit(solution)/shard_map/pallas_call | solution.py:155
  471.5 3.7 convert.89
  480.6 9.6 %fusion.46 = (f32[768]{0:T(1024)}, f32[1024,768]{1,0:T(8,128)}) fusion(bf16[768,2432]{1,0:T(8,128)(2,1)} %all-gather.5.cloned.1.call-done, bf16[1024,768]{0,1:T(8,128)(2,1)} %bitcast.96, bf16[1024,768]{0,1:T(8,128)(2,1)} %bitcast.99, bf16[1024,768]{0,1:T(8,128)(2,1)} %bitcast.102), kind=kOutput, calls=%fused_computation.168 | convolution fusion | flops 3638820096 | bytes 11406336 | tf_op jit(solution)/shard_map/te,de->td/dot_general | solution.py:489
  490.2 3.8 copy.251
  494.1 6.0 fusion.35
  500.1 3.6 copy.254
  513.9 8.5 %concatenate.58 = f32[2,16,24,2432]{3,2,0,1:T(8,128)} concatenate(f32[2,16,24,2304]{3,2,0,1:T(8,128)} %copy.254, f32[2,16,24,1]{3,2,0,1:T(8,128)S(1)} %copy.255, f32[2,16,24,1]{3,2,0,1:T(8,128)S(1)} %copy-done.21, f32[2,16,24,1]{3,2,0,1:T(8,128)S(1)} %copy.257, f32[2,16,24,1]{3,2,0,1:T(8,128)S(1)} %copy.258, f32[2,16,24,124]{3,2,0,1:T(8,128)S(1)} %broadcast_in_dim.14), dimensions={3} | concatenate | bytes 14942208 | tf_op jit(solution)/shard_map/concatenate | solution.py:500
  528.4 14.4 %collective-permute-start = (bf16[384,1152]{1,0:T(8,128)(2,1)S(1)}, bf16[384,1152]{1,0:T(8,128)(2,1)S(1)}, u32[]{:S(2)}, u32[]{:S(2)}) collective-permute-start(bf16[384,1152]{1,0:T(8,128)(2,1)S(1)} %bitcast.106), channel_id=1, source_target_pairs={{0,2},{2,0},{4,6},{6,4},{8,10},{10,8},{12,14},{14,12},{16,18},{18,... | collective-permute-start | bytes 2654216 | tf_op jit(solution)/shard_map/ppermute | solution.py:286
  546.9 32.0 %collective-permute-start.6 = (bf16[192,1280]{1,0:T(8,128)(2,1)S(1)}, bf16[192,1280]{1,0:T(8,128)(2,1)S(1)}, u32[]{:S(2)}, u32[]{:S(2)}) collective-permute-start(bf16[192,1280]{1,0:T(8,128)(2,1)S(1)} %select_convert_fusion.2), channel_id=1, source_target_pairs={{0,8},{2,10},{4,12},{6,14},{8,0},{10,2},{12,4},{14,6},{16,24},{18,... | collective-permute-start | bytes 1474568 | tf_op jit(solution)/shard_map/ppermute | solution.py:286
  579.0 10.4 %collective-permute-start.2 = (bf16[96,1152]{1,0:T(8,128)(2,1)S(1)}, bf16[96,1152]{1,0:T(8,128)(2,1)S(1)}, u32[]{:S(2)}, u32[]{:S(2)}) collective-permute-start(bf16[96,1152]{1,0:T(8,128)(2,1)S(1)} %select_convert_fusion.5), channel_id=1, source_target_pairs={{0,8},{2,10},{4,12},{6,14},{8,0},{10,2},{12,4},{14,6},{16,24},{18,... | collective-permute-start | bytes 663560 | tf_op jit(solution)/shard_map/ppermute | solution.py:286
  590.7 4.4 collective-permute-done.2
  595.2 16.4 %collective-permute-start.3 = (bf16[48,1152]{1,0:T(8,128)(2,1)S(1)}, bf16[48,1152]{1,0:T(8,128)(2,1)S(1)}, u32[]{:S(2)}, u32[]{:S(2)}) collective-permute-start(bf16[48,1152]{1,0:T(8,128)(2,1)S(1)} %select_convert_fusion.7), channel_id=1, source_target_pairs={{0,1},{1,0},{2,3},{3,2},{4,5},{5,4},{6,7},{7,6},{8,9},{9,8},{10,11... | collective-permute-start | bytes 331784 | tf_op jit(solution)/shard_map/ppermute | solution.py:286
  614.4 4.1 collective-permute-done.7
  620.4 3.1 collective-permute-done.8
  625.5 3.9 collective-permute-done.9
  630.3 9.3 %add_convert_fusion.3 = bf16[1024,768]{0,1:T(8,128)(2,1)S(1)} fusion(f32[1024,768]{0,1:T(8,128)} %copy-done.3, bf16[1024,3072]{1,0:T(8,128)(2,1)} %get-tuple-element.171, bf16[3072,768]{1,0:T(8,128)(2,1)} %all-gather.9.cloned.1.call-done, f32[768]{0:T(1024)S(1)} %copy-done.38), kind=kOutput, calls=%fused_computation.61 | convolution fusion | flops 4834197504 | bytes 15731712 | tf_op jit(solution)/shard_map/dot_general | solution.py:414
  641.2 3.9 fusion.22
  646.7 49.4 %all-gather.11.cloned.1.call-done = bf16[384,9472]{1,0:T(8,128)(2,1)} async-done(((bf16[24,9472]{1,0:T(8,128)(2,1)}), bf16[384,9472]{1,0:T(8,128)(2,1)}) %all-gather.11.cloned.1.call-update) | async-done | bytes 7274512 | tf_op jit(solution)/shard_map/all_gather | solution.py:516
  701.8 7.4 %slice_convert_fusion = (f32[384,3072]{1,0:T(8,128)}, f32[384,3072]{1,0:T(8,128)}) fusion(bf16[384,9472]{1,0:T(8,128)(2,1)} %all-gather.11.cloned.1.call-done), kind=kLoop, calls=%fused_computation.73 | loop fusion | flops 2359296 | bytes 14155776 | tf_op jit(solution)/shard_map/convert_element_type | solution.py:537
  709.1 6.1 reshape.544
  715.2 3.5 slice_convert_fusion.2
  (244 shorter events, 95.4 us)
Async XLA Ops:
  7.2 16.8 %copy-start.14 = (bf16[1024,768]{1,0:T(8,128)(2,1)S(1)}, bf16[1024,768]{1,0:T(8,128)(2,1)}, u32[]{:S(2)}) copy-start(bf16[1024,768]{1,0:T(8,128)(2,1)} %param.39) | copy-start | bytes 4718596
  7.2 17.1 %copy-start.43 = (s32[1,5]{1,0:T(1,128)S(1)}, s32[1,5]{1,0:T(1,128)}, u32[]{:S(2)}) copy-start(s32[1,5]{1,0:T(1,128)} %param.21) | copy-start | bytes 64
  7.2 75.3 %all-gather.5.cloned.1.call-start = ((), (), s32[]{:S(2)}) async-start(), calls=%async_computation.1 | async-start | bytes 3852288 | tf_op jit(solution)/shard_map/all_gather | solution.py:338
  17.1 9.0 %copy-start.20 = (bf16[1024,768]{1,0:T(8,128)(2,1)S(1)}, bf16[1024,768]{1,0:T(8,128)(2,1)}, u32[]{:S(2)}) copy-start(bf16[1024,768]{1,0:T(8,128)(2,1)} %param.20) | copy-start | bytes 4718596
  18.9 174.7 %all-gather.7.cloned.1.call-start = ((), (), s32[]{:S(2)}) async-start(), calls=%async_computation.2 | async-start | bytes 6082560 | tf_op jit(solution)/shard_map/all_gather | solution.py:356
  20.6 221.4 %all-gather.9.cloned.1.call-start = ((), (), s32[]{:S(2)}) async-start(), calls=%async_computation.3 | async-start | bytes 4866048 | tf_op jit(solution)/shard_map/all_gather | solution.py:359
  21.4 501.9 %reduce-scatter.4.cloned.1.call-start = ((), (), s32[]{:S(2)}) async-start(), calls=%async_computation.5 | async-start | bytes 11151360
  26.9 166.8 %copy-start.1 = (bf16[1024,768]{0,1:T(8,128)(2,1)}, bf16[1024,768]{0,1:T(8,128)(2,1)S(1)}, u32[]{:S(2)}) copy-start(bf16[1024,768]{0,1:T(8,128)(2,1)S(1)} %copy.215) | copy-start | bytes 4718596
  27.1 67.5 %copy-start.24 = (f32[1024]{0:T(1024)}, f32[1024]{0:T(1024)S(1)}, u32[]{:S(2)}) copy-start(f32[1024]{0:T(1024)S(1)} %broadcast_multiply_fusion.11) | copy-start | bytes 12292
  27.6 67.0 %copy-start.31 = (f32[1024]{0:T(1024)}, f32[1024]{0:T(1024)S(1)}, u32[]{:S(2)}) copy-start(f32[1024]{0:T(1024)S(1)} %add_rsqrt_fusion.3) | copy-start | bytes 12292
  88.2 6.4 copy-start.29
  88.2 6.4 copy-start.39
  88.2 105.4 %copy-start.33 = (f32[768]{0:T(1024)}, f32[768]{0:T(1024)S(1)}, u32[]{:S(2)}) copy-start(f32[768]{0:T(1024)S(1)} %get-tuple-element.145) | copy-start | bytes 9220
  88.2 105.4 %copy-start.41 = (f32[768]{0:T(1024)}, f32[768]{0:T(1024)S(1)}, u32[]{:S(2)}) copy-start(f32[768]{0:T(1024)S(1)} %get-tuple-element.144) | copy-start | bytes 9220
  98.6 5.5 copy-start.7
  105.8 68.3 %copy-start.8 = (bf16[1024,768]{0,1:T(8,128)(2,1)}, bf16[1024,768]{0,1:T(8,128)(2,1)S(1)}, u32[]{:S(2)}) copy-start(bf16[1024,768]{0,1:T(8,128)(2,1)S(1)} %copy.228) | copy-start | bytes 4718596
  187.5 6.1 copy-start.27
  191.3 6.5 copy-start.35
  197.8 39.4 %copy-start.3 = (f32[1024,768]{0,1:T(8,128)}, f32[1024,768]{0,1:T(8,128)S(1)}, u32[]{:S(2)}) copy-start(f32[1024,768]{0,1:T(8,128)S(1)} %get-tuple-element.186) | copy-start | bytes 9437188
  237.3 4.7 copy-start
  237.3 4.7 copy-start.15
  242.0 40.9 %slice-start = ((s8[5898240]{0:T(1024)(128)(4,1)}), s8[1703936]{0:T(1024)(128)(4,1)S(1)}, s32[]{:S(2)}) async-start(s8[5898240]{0:T(1024)(128)(4,1)} %bitcast.121), calls=%async_computation.6 | async-start | bytes 3407872
  257.4 18.4 %copy-start.4 = (f32[1024,768]{0,1:T(8,128)S(1)}, f32[1024,768]{0,1:T(8,128)}, u32[]{:S(2)}) copy-start(f32[1024,768]{0,1:T(8,128)} %copy-done.3) | copy-start | bytes 9437188
  257.4 25.6 %slice-start.1 = ((s8[5898240]{0:T(1024)(128)(4,1)}), s8[4194304]{0:T(1024)(128)(4,1)S(1)}, s32[]{:S(2)}) async-start(s8[5898240]{0:T(1024)(128)(4,1)} %bitcast.121), calls=%async_computation.7 | async-start | bytes 8388608
  314.4 3.9 copy-start.36
  314.4 3.9 copy-start.42
  318.3 7.4 %copy-start.11 = (f32[1024,768]{1,0:T(8,128)S(1)}, f32[1024,768]{1,0:T(8,128)}, u32[]{:S(2)}) copy-start(f32[1024,768]{1,0:T(8,128)} %copy.233) | copy-start | bytes 9437188
  363.2 4.1 copy-start.17
  363.2 332.9 %all-gather.11.cloned.1.call-start = ((), (), s32[]{:S(2)}) async-start(), calls=%async_computation.4 | async-start | bytes 7729152 | tf_op jit(solution)/shard_map/all_gather | solution.py:516
  471.5 6.1 copy-start.13
  490.1 3.9 copy-start.2
  490.1 3.9 copy-start.18
  490.1 3.9 copy-start.25
  490.2 3.9 copy-start.30
  490.2 3.9 copy-start.32
  490.2 3.9 copy-start.40
  528.4 16.5 %collective-permute-start = (bf16[384,1152]{1,0:T(8,128)(2,1)S(1)}, bf16[384,1152]{1,0:T(8,128)(2,1)S(1)}, u32[]{:S(2)}, u32[]{:S(2)}) collective-permute-start(bf16[384,1152]{1,0:T(8,128)(2,1)S(1)} %bitcast.106), channel_id=1, source_target_pairs={{0,2},{2,0},{4,6},{6,4},{8,10},{10,8},{12,14},{14,12},{16,18},{18,... | collective-permute-start | bytes 2654216 | tf_op jit(solution)/shard_map/ppermute | solution.py:286
  543.2 3.4 collective-permute-start.5
  545.1 33.8 %collective-permute-start.1 = (bf16[192,1152]{1,0:T(8,128)(2,1)S(1)}, bf16[192,1152]{1,0:T(8,128)(2,1)S(1)}, u32[]{:S(2)}, u32[]{:S(2)}) collective-permute-start(bf16[192,1152]{1,0:T(8,128)(2,1)S(1)} %select_convert_fusion.3), channel_id=1, source_target_pairs={{0,4},{2,6},{4,0},{6,2},{8,12},{10,14},{12,8},{14,10},{16,20},{18,... | collective-permute-start | bytes 1327112 | tf_op jit(solution)/shard_map/ppermute | solution.py:286
  546.9 43.7 %collective-permute-start.6 = (bf16[192,1280]{1,0:T(8,128)(2,1)S(1)}, bf16[192,1280]{1,0:T(8,128)(2,1)S(1)}, u32[]{:S(2)}, u32[]{:S(2)}) collective-permute-start(bf16[192,1280]{1,0:T(8,128)(2,1)S(1)} %select_convert_fusion.2), channel_id=1, source_target_pairs={{0,8},{2,10},{4,12},{6,14},{8,0},{10,2},{12,4},{14,6},{16,24},{18,... | collective-permute-start | bytes 1474568 | tf_op jit(solution)/shard_map/ppermute | solution.py:286
  579.0 16.1 %collective-permute-start.2 = (bf16[96,1152]{1,0:T(8,128)(2,1)S(1)}, bf16[96,1152]{1,0:T(8,128)(2,1)S(1)}, u32[]{:S(2)}, u32[]{:S(2)}) collective-permute-start(bf16[96,1152]{1,0:T(8,128)(2,1)S(1)} %select_convert_fusion.5), channel_id=1, source_target_pairs={{0,8},{2,10},{4,12},{6,14},{8,0},{10,2},{12,4},{14,6},{16,24},{18,... | collective-permute-start | bytes 663560 | tf_op jit(solution)/shard_map/ppermute | solution.py:286
  595.2 34.3 %copy-start.23 = (bf16[24,7040]{1,0:T(8,128)(2,1)S(1)}, bf16[24,7040]{1,0:T(8,128)(2,1)}, u32[]{:S(2)}) copy-start(bf16[24,7040]{1,0:T(8,128)(2,1)} %reduce-scatter.4.cloned.1.call-done) | copy-start | bytes 1013764
  595.2 19.1 %collective-permute-start.3 = (bf16[48,1152]{1,0:T(8,128)(2,1)S(1)}, bf16[48,1152]{1,0:T(8,128)(2,1)S(1)}, u32[]{:S(2)}, u32[]{:S(2)}) collective-permute-start(bf16[48,1152]{1,0:T(8,128)(2,1)S(1)} %select_convert_fusion.7), channel_id=1, source_target_pairs={{0,1},{1,0},{2,3},{3,2},{4,5},{5,4},{6,7},{7,6},{8,9},{9,8},{10,11... | collective-permute-start | bytes 331784 | tf_op jit(solution)/shard_map/ppermute | solution.py:286
  611.6 18.6 %copy-start.38 = (f32[768]{0:T(1024)S(1)}, f32[768]{0:T(1024)}, u32[]{:S(2)}) copy-start(f32[768]{0:T(1024)} %get-tuple-element.140) | copy-start | bytes 9220
  611.6 6.8 collective-permute-start.7
  618.6 4.9 collective-permute-start.8
  618.9 6.6 collective-permute-start.4
  623.6 5.8 collective-permute-start.9
  (13 other events, 36.8 us)
Sparse Core Ops, SparseCore 0:
  19.1 63.4 all-gather.4
  86.0 66.5 all-gather.6
  155.5 62.2 all-gather.8
  363.3 159.9 reduce-scatter.3
  630.4 65.6 all-gather.10

commit v9 on v8

--- a/solution.py
+++ b/solution.py
@@ -490,7 +490,6 @@
     grad_in_part, first_gain_grad, first_shift_grad = norm_back(
         unit_one, inv_one, gain_one.astype(jnp.float32), grad_normed
     )
-    input_grad = (grad_middle + grad_in_part).astype(jnp.bfloat16)
     attn_small = (
         first_gain_grad,
         first_shift_grad,
@@ -513,15 +512,20 @@
     attn_right = hypercube_reduce_scatter(
         attn_pack[:, split:], order_b, group_size, shard_size
     )
+    gather_in = jnp.concatenate(
+        [
+            ffn_part,
+            attn_left.astype(jnp.bfloat16),
+            attn_right.astype(jnp.bfloat16),
+        ],
+        axis=1,
+    )
+    gather_in, grad_middle, grad_in_part = lax.optimization_barrier(
+        (gather_in, grad_middle, grad_in_part)
+    )
+    input_grad = (grad_middle + grad_in_part).astype(jnp.bfloat16)
     both = lax.all_gather(
-        jnp.concatenate(
-            [
-                ffn_part,
-                attn_left.astype(jnp.bfloat16),
-                attn_right.astype(jnp.bfloat16),
-            ],
-            axis=1,
-        ),
+        gather_in,
         "group",
         axis=0,
         tiled=True,

time: 737 us -> 744 us (level)
  local copies, waits for them, and re-layouts: 146 us -> 154 us
    unnamed x96 -> x104, local copies, waits for them, and re-layouts: 12.4 us -> 17.1 us
  transfers between devices with their start and end apart: 15 -> 15, of which waited for: 11 -> 10; matrix products, arithmetic and copies ran while one was open for 24% -> 25% of each run, Pallas kernels for 23% -> 23%
where the time goes in v9:
time: 744 us; the launch traced here: 735 us
  Pallas kernels  166 us (22%)
  local copies, waits for them, and re-layouts  154 us (21%)
  waiting for transfers between devices  121 us (16%)
  matrix products  118 us (16%)
  other arithmetic  81.1 us (11%)
  starting transfers between devices  80.4 us (11%)
  between operations  14.9 us (2%)
    pallas_call x1, Pallas kernels, attention_backward(): pl.pallas_call(_bwd_kernel, out_shape=(jax.ShapeDtypeStruct((heads, lengt...  101 us
    ppermute x10, starting transfers between devices, hypercube_reduce_scatter(): got = lax.ppermute(send, axis, [(j, j ^ 1 << b) for j in range(size)])  80.2 us
    pallas_call x1, Pallas kernels, attention_forward(): pl.pallas_call(_fwd_kernel, out_shape=jax.ShapeDtypeStruct((heads, length...  65.5 us
    all_gather x1, waiting for transfers between devices, per_device(): lax.all_gather(first_pack, ('group', 'shard'), axis=0, tiled=True)  53 us
    all_gather x1, waiting for transfers between devices, per_device(): both = lax.all_gather(gather_in, 'group', axis=0, tiled=True)  47.2 us
    dot_general x1, matrix products, per_device(): jnp.dot(second_low, expand_full, preferred_element_type=jnp.float32)  39 us
    ppermute x10, waiting for transfers between devices, hypercube_reduce_scatter(): got = lax.ppermute(send, axis, [(j, j ^ 1 << b) for j in range(size)])  19.6 us
    concatenate x10, local copies, waits for them, and re-layouts, per_device(): jnp.concatenate([qkv_weight_grad, pack_columns(attn_small, model_width)],...  18.5 us
  transfers between devices with their start and end apart: 15, of which 10 were waited for; matrix products, arithmetic and copies ran while one was open for 25% of the time, Pallas kernels for 23%

profile of v9, /device:TPU:0, one launch (start us, length us, event | category | flops | bytes accessed | tf_op | source)
XLA Modules:
  0.0 734.7 jit_solution(16939901923655799067)
XLA Ops:
  29.5 53.0 %all-gather.5.cloned.1.call-done = bf16[768,2432]{1,0:T(8,128)(2,1)} async-done(((bf16[24,2432]{1,0:T(8,128)(2,1)}), bf16[768,2432]{1,0:T(8,128)(2,1)}) %all-gather.5.cloned.1.call-update) | async-done | bytes 3735568 | tf_op jit(solution)/shard_map/all_gather | solution.py:338
  84.0 4.2 convert_reduce_fusion.1
  88.2 6.4 add_convert_fusion.2
  108.6 65.5 %shard_map.339 = f32[12,1024,64]{2,1,0:T(8,128)} custom-call(s32[2]{0:T(128)} %and_select_fusion.lo_ref, bf16[12,1024,64]{2,1,0:T(8,128)(2,1)} %copy.229.q_ref, bf16[12,64,1024]{2,1,0:T(8,128)(2,1)} %bitcast.81, bf16[12,1024,64]{2,1,0:T(8,128)(2,1)} %copy.230.v_ref, s32[1024,1]{1,0:T(8,128)} %copy.231.segq_ref, s32[1,1024]{1,0:T(1,128)} %bitcast.108), custom_call_target="tpu_custom_call" | custom-call | flops 1610612736 | bytes 6291456 | tf_op jit(solution)/shard_map/pallas_call | solution.py:127
  174.1 6.1 copy.232
  180.2 4.0 copy.233
  184.2 3.3 reduce_sum.276
  187.5 3.8 multiply_reduce_fusion.4
  193.6 4.2 fusion.42
  198.2 39.0 %fusion.38 = (f32[1024]{0:T(1024)S(1)}, f32[1024,3072]{1,0:T(8,128)S(1)}, f32[1024,3072]{1,0:T(8,128)}, f32[1024,3072]{1,0:T(8,128)}) fusion(f32[3072]{0:T(1024)S(1)} %reshape.540, bf16[768,3840]{1,0:T(8,128)(2,1)} %all-gather.7.cloned.1.call-done, f32[1024,768]{0,1:T(8,128)S(1)} %get-tuple-element.192, f32[768]{0:T(1024)S(1)} %get-tuple-element.147, ...), kind=kOutput, calls=%fused_computation.162 | convolution fusion | flops 5043387392 | bytes 45643776 | tf_op jit(solution)/shard_map/dot_general | solution.py:404
  238.7 3.3 copy-done
  242.0 15.3 %multiply_reduce_fusion = (bf16[3072]{0:T(1024)(128)(2,1)S(1)}, f32[1024]{0:T(1024)S(1)}, f32[1024]{0:T(1024)S(1)}, bf16[3072]{0:T(1024)(128)(2,1)S(1)}, bf16[1024,3072]{1,0:T(8,128)(2,1)}, /*index=5*/f32[1024,3072]{1,0:T(8,128)}) fusion(f32[1024,3072]{1,0:T(8,128)} %copy-done, f32[1024]{0:T(1024)S(1)} %add_rsqrt_fusion, ...), kind=kOutput, calls=%fused_computation.3 | convolution fusion | flops 4869578752 | bytes 37801984 | tf_op jit(solution)/shard_map/td,fd->tf/dot_general | solution.py:423
  257.3 18.3 %fusion.37 = (bf16[3072]{0:T(1024)(128)(2,1)S(1)}, bf16[1024,3072]{1,0:T(8,128)(2,1)S(1)}) fusion(f32[1024,3072]{1,0:T(8,128)} %get-tuple-element.176, f32[1024]{0:T(1024)S(1)} %get-tuple-element.200, f32[1024,3072]{1,0:T(8,128)} %copy-done, f32[1024]{0:T(1024)S(1)} %broadcast_multiply_fusion.2, f32[1024]{0:T(1024)S(1)} %get-tuple-element.201, ...), kind=kLoop, calls=%fused_computation.161 | loop fusion | flops 72348672 | bytes 56670208 | tf_op jit(solution)/shard_map/reduce_sum | solution.py:430
  275.7 7.0 convolution_convert_fusion.1
  282.7 7.2 convolution_convert_fusion
  289.9 8.5 %reshape.501 = bf16[768,3072]{1,0:T(8,128)(2,1)} reshape(bf16[3072,768]{1,0:T(8,128)(2,1)} %convolution_convert_fusion) | data formatting | bytes 9437184 | tf_op jit(solution)/shard_map/reshape | solution.py:464
  298.4 9.7 %fusion.43 = (bf16[768]{0:T(1024)(128)(2,1)S(1)}, f32[1024,768]{1,0:T(8,128)}) fusion(bf16[1024,3072]{1,0:T(8,128)(2,1)} %copy-done.23, bf16[768,3840]{1,0:T(8,128)(2,1)} %all-gather.7.cloned.1.call-done), kind=kOutput, calls=%fused_computation.166 | convolution fusion | flops 4832623616 | bytes 14157312 | tf_op jit(solution)/shard_map/tf,df->td/dot_general | solution.py:434
  308.2 3.5 copy.236
  311.7 3.0 multiply_reduce_fusion.7
  316.9 3.0 convolution_convert_fusion.2
  324.3 4.5 multiply_reduce_fusion.5
  333.3 18.0 %concatenate.51 = bf16[768,7040]{1,0:T(8,128)(2,1)} concatenate(bf16[768,3072]{1,0:T(8,128)(2,1)} %convolution_convert_fusion.1, bf16[768,3072]{1,0:T(8,128)(2,1)} %reshape.501, bf16[768,768]{1,0:T(8,128)(2,1)} %convolution_convert_fusion.2, bf16[768,1]{1,0:T(8,128)(2,1)S(1)} %reshape.554, bf16[768,1]{1,0:T(8,128)(2,1)} %reshape.555, bf16[768,1]{1,0:T(8,128)(2,1)S(1)} %copy-done.28, ...), dimensions={1} | concatenate | bytes 21626880 | tf_op jit(solution)/shard_map/concatenate | solution.py:461
  351.3 10.1 %copy.245 = bf16[16,2,24,7040]{3,2,1,0:T(8,128)(2,1)} copy(bf16[16,2,24,7040]{3,2,0,1:T(8,128)(2,1)} %bitcast.78) | data formatting | bytes 21626880 | tf_op jit(solution)/shard_map/transpose | solution.py:245
  362.7 3.1 copy.248.k_ref
  366.6 2.8 copy.249.do_ref
  369.5 100.6 %shard_map.340 = (f32[12,1024,64]{2,1,0:T(8,128)}, f32[12,64,1024]{2,1,0:T(8,128)}, f32[12,64,1024]{2,1,0:T(8,128)}) custom-call(s32[2]{0:T(128)} %and_select_fusion.lo_ref, bf16[12,1024,64]{2,1,0:T(8,128)(2,1)} %copy.229.q_ref, bf16[12,64,1024]{2,1,0:T(8,128)(2,1)} %bitcast.89, bf16[12,1024,64]{2,1,0:T(8,128)(2,1)} %copy.248.k_ref, ...), custom_call_target="tpu_custom_call" | custom-call | flops 4026531840 | bytes 12582912 | tf_op jit(solution)/shard_map/pallas_call | solution.py:155
  477.9 4.4 copy.251
  482.3 6.0 fusion.33
  488.3 4.5 copy.253
  493.9 6.1 fusion.44
  500.0 3.7 copy.252
  503.7 3.5 fusion.19
  515.8 8.5 %concatenate.58 = f32[2,16,24,2432]{3,2,0,1:T(8,128)} concatenate(f32[2,16,24,2304]{3,2,0,1:T(8,128)} %copy.253, f32[2,16,24,1]{3,2,0,1:T(8,128)S(1)} %copy.254, f32[2,16,24,1]{3,2,0,1:T(8,128)S(1)} %copy-done.27, f32[2,16,24,1]{3,2,0,1:T(8,128)S(1)} %copy.256, f32[2,16,24,1]{3,2,0,1:T(8,128)S(1)} %copy.257, f32[2,16,24,124]{3,2,0,1:T(8,128)S(1)} %broadcast_in_dim.14), dimensions={3} | concatenate | bytes 14942208 | tf_op jit(solution)/shard_map/concatenate | solution.py:499
  525.0 4.4 fusion.21
  534.5 15.3 %collective-permute-start = (bf16[384,1152]{1,0:T(8,128)(2,1)S(1)}, bf16[384,1152]{1,0:T(8,128)(2,1)S(1)}, u32[]{:S(2)}, u32[]{:S(2)}) collective-permute-start(bf16[384,1152]{1,0:T(8,128)(2,1)S(1)} %bitcast.106), channel_id=1, source_target_pairs={{0,2},{2,0},{4,6},{6,4},{8,10},{10,8},{12,14},{14,12},{16,18},{18,... | collective-permute-start | bytes 2654216 | tf_op jit(solution)/shard_map/ppermute | solution.py:286
  554.0 31.9 %collective-permute-start.6 = (bf16[192,1280]{1,0:T(8,128)(2,1)S(1)}, bf16[192,1280]{1,0:T(8,128)(2,1)S(1)}, u32[]{:S(2)}, u32[]{:S(2)}) collective-permute-start(bf16[192,1280]{1,0:T(8,128)(2,1)S(1)} %select_convert_fusion.2), channel_id=1, source_target_pairs={{0,8},{2,10},{4,12},{6,14},{8,0},{10,2},{12,4},{14,6},{16,24},{18,... | collective-permute-start | bytes 1474568 | tf_op jit(solution)/shard_map/ppermute | solution.py:286
  586.1 10.4 %collective-permute-start.2 = (bf16[96,1152]{1,0:T(8,128)(2,1)S(1)}, bf16[96,1152]{1,0:T(8,128)(2,1)S(1)}, u32[]{:S(2)}, u32[]{:S(2)}) collective-permute-start(bf16[96,1152]{1,0:T(8,128)(2,1)S(1)} %select_convert_fusion.5), channel_id=1, source_target_pairs={{0,8},{2,10},{4,12},{6,14},{8,0},{10,2},{12,4},{14,6},{16,24},{18,... | collective-permute-start | bytes 663560 | tf_op jit(solution)/shard_map/ppermute | solution.py:286
  597.8 4.4 collective-permute-done.2
  602.2 16.4 %collective-permute-start.3 = (bf16[48,1152]{1,0:T(8,128)(2,1)S(1)}, bf16[48,1152]{1,0:T(8,128)(2,1)S(1)}, u32[]{:S(2)}, u32[]{:S(2)}) collective-permute-start(bf16[48,1152]{1,0:T(8,128)(2,1)S(1)} %select_convert_fusion.7), channel_id=1, source_target_pairs={{0,1},{1,0},{2,3},{3,2},{4,5},{5,4},{6,7},{7,6},{8,9},{9,8},{10,11... | collective-permute-start | bytes 331784 | tf_op jit(solution)/shard_map/ppermute | solution.py:286
  621.4 4.1 collective-permute-done.7
  627.4 3.2 collective-permute-done.8
  632.5 4.0 collective-permute-done.9
  637.3 9.5 %add_convert_fusion.4 = bf16[1024,768]{0,1:T(8,128)(2,1)} fusion(f32[1024,768]{0,1:T(8,128)S(1)} %copy-done.5, bf16[1024,3072]{1,0:T(8,128)(2,1)} %get-tuple-element.177, bf16[3072,768]{1,0:T(8,128)(2,1)} %all-gather.9.cloned.1.call-done, f32[768]{0:T(1024)S(1)} %copy-done.43), kind=kOutput, calls=%fused_computation.60 | convolution fusion | flops 4834197504 | bytes 15731712 | tf_op jit(solution)/shard_map/dot_general | solution.py:414
  649.5 3.5 add_convert_fusion.3
  655.8 47.2 %all-gather.11.cloned.1.call-done = bf16[384,9472]{1,0:T(8,128)(2,1)} async-done(((bf16[24,9472]{1,0:T(8,128)(2,1)}), bf16[384,9472]{1,0:T(8,128)(2,1)}) %all-gather.11.cloned.1.call-update) | async-done | bytes 7274512 | tf_op jit(solution)/shard_map/all_gather | solution.py:527
  708.8 7.4 %slice_convert_fusion = (f32[384,3072]{1,0:T(8,128)}, f32[384,3072]{1,0:T(8,128)}) fusion(bf16[384,9472]{1,0:T(8,128)(2,1)} %all-gather.11.cloned.1.call-done), kind=kLoop, calls=%fused_computation.72 | loop fusion | flops 2359296 | bytes 14155776 | tf_op jit(solution)/shard_map/convert_element_type | solution.py:541
  716.2 6.1 reshape.544
  722.3 3.5 slice_convert_fusion.2
  (252 shorter events, 104.3 us)
Async XLA Ops:
  7.2 16.8 %copy-start.16 = (bf16[1024,768]{1,0:T(8,128)(2,1)S(1)}, bf16[1024,768]{1,0:T(8,128)(2,1)}, u32[]{:S(2)}) copy-start(bf16[1024,768]{1,0:T(8,128)(2,1)} %param.39) | copy-start | bytes 4718596
  7.2 17.1 %copy-start.48 = (s32[1,5]{1,0:T(1,128)S(1)}, s32[1,5]{1,0:T(1,128)}, u32[]{:S(2)}) copy-start(s32[1,5]{1,0:T(1,128)} %param.21) | copy-start | bytes 64
  7.2 75.3 %all-gather.5.cloned.1.call-start = ((), (), s32[]{:S(2)}) async-start(), calls=%async_computation.1 | async-start | bytes 3852288 | tf_op jit(solution)/shard_map/all_gather | solution.py:338
  17.1 9.0 %copy-start.26 = (bf16[1024,768]{1,0:T(8,128)(2,1)S(1)}, bf16[1024,768]{1,0:T(8,128)(2,1)}, u32[]{:S(2)}) copy-start(bf16[1024,768]{1,0:T(8,128)(2,1)} %param.20) | copy-start | bytes 4718596
  18.9 174.6 %all-gather.7.cloned.1.call-start = ((), (), s32[]{:S(2)}) async-start(), calls=%async_computation.2 | async-start | bytes 6082560 | tf_op jit(solution)/shard_map/all_gather | solution.py:356
  20.6 221.4 %all-gather.9.cloned.1.call-start = ((), (), s32[]{:S(2)}) async-start(), calls=%async_computation.3 | async-start | bytes 4866048 | tf_op jit(solution)/shard_map/all_gather | solution.py:359
  21.4 508.1 %reduce-scatter.4.cloned.1.call-start = ((), (), s32[]{:S(2)}) async-start(), calls=%async_computation.5 | async-start | bytes 11151360
  26.9 166.7 %copy-start.1 = (bf16[1024,768]{0,1:T(8,128)(2,1)}, bf16[1024,768]{0,1:T(8,128)(2,1)S(1)}, u32[]{:S(2)}) copy-start(bf16[1024,768]{0,1:T(8,128)(2,1)S(1)} %copy.215) | copy-start | bytes 4718596
  27.1 67.4 %copy-start.30 = (f32[1024]{0:T(1024)}, f32[1024]{0:T(1024)S(1)}, u32[]{:S(2)}) copy-start(f32[1024]{0:T(1024)S(1)} %broadcast_multiply_fusion.11) | copy-start | bytes 12292
  27.6 67.0 %copy-start.35 = (f32[1024]{0:T(1024)}, f32[1024]{0:T(1024)S(1)}, u32[]{:S(2)}) copy-start(f32[1024]{0:T(1024)S(1)} %add_rsqrt_fusion.3) | copy-start | bytes 12292
  88.2 6.4 copy-start.33
  88.2 6.4 copy-start.44
  88.2 105.4 %copy-start.39 = (f32[768]{0:T(1024)}, f32[768]{0:T(1024)S(1)}, u32[]{:S(2)}) copy-start(f32[768]{0:T(1024)S(1)} %get-tuple-element.151) | copy-start | bytes 9220
  88.2 105.4 %copy-start.46 = (f32[768]{0:T(1024)}, f32[768]{0:T(1024)S(1)}, u32[]{:S(2)}) copy-start(f32[768]{0:T(1024)S(1)} %get-tuple-element.150) | copy-start | bytes 9220
  98.6 5.5 copy-start.8
  105.8 68.3 %copy-start.9 = (bf16[1024,768]{0,1:T(8,128)(2,1)}, bf16[1024,768]{0,1:T(8,128)(2,1)S(1)}, u32[]{:S(2)}) copy-start(bf16[1024,768]{0,1:T(8,128)(2,1)S(1)} %copy.228) | copy-start | bytes 4718596
  187.5 6.1 copy-start.37
  191.3 6.5 copy-start.41
  197.8 39.5 %copy-start.3 = (f32[1024,768]{0,1:T(8,128)}, f32[1024,768]{0,1:T(8,128)S(1)}, u32[]{:S(2)}) copy-start(f32[1024,768]{0,1:T(8,128)S(1)} %get-tuple-element.192) | copy-start | bytes 9437188
  237.3 4.7 copy-start
  237.3 4.7 copy-start.17
  257.3 18.4 %copy-start.4 = (f32[1024,768]{0,1:T(8,128)S(1)}, f32[1024,768]{0,1:T(8,128)}, u32[]{:S(2)}) copy-start(f32[1024,768]{0,1:T(8,128)} %copy-done.3) | copy-start | bytes 9437188
  275.7 7.0 copy-start.23
  275.7 7.0 copy-start.18
  275.7 7.0 copy-start.49
  316.9 7.4 %copy-start.12 = (f32[1024,768]{1,0:T(8,128)S(1)}, f32[1024,768]{1,0:T(8,128)}, u32[]{:S(2)}) copy-start(f32[1024,768]{1,0:T(8,128)} %copy.233) | copy-start | bytes 9437188
  361.4 4.5 copy-start.19
  361.4 341.7 %all-gather.11.cloned.1.call-start = ((), (), s32[]{:S(2)}) async-start(), calls=%async_computation.4 | async-start | bytes 7729152 | tf_op jit(solution)/shard_map/all_gather | solution.py:527
  470.1 5.5 copy-start.15
  477.8 4.4 copy-start.34
  477.8 4.5 copy-start.36
  477.8 4.5 copy-start.45
  488.3 4.5 copy-start.20
  488.3 4.5 copy-start.21
  488.3 5.6 copy-start.25
  534.5 17.3 %collective-permute-start = (bf16[384,1152]{1,0:T(8,128)(2,1)S(1)}, bf16[384,1152]{1,0:T(8,128)(2,1)S(1)}, u32[]{:S(2)}, u32[]{:S(2)}) collective-permute-start(bf16[384,1152]{1,0:T(8,128)(2,1)S(1)} %bitcast.106), channel_id=1, source_target_pairs={{0,2},{2,0},{4,6},{6,4},{8,10},{10,8},{12,14},{14,12},{16,18},{18,... | collective-permute-start | bytes 2654216 | tf_op jit(solution)/shard_map/ppermute | solution.py:286
  550.2 3.5 collective-permute-start.5
  552.1 33.8 %collective-permute-start.1 = (bf16[192,1152]{1,0:T(8,128)(2,1)S(1)}, bf16[192,1152]{1,0:T(8,128)(2,1)S(1)}, u32[]{:S(2)}, u32[]{:S(2)}) collective-permute-start(bf16[192,1152]{1,0:T(8,128)(2,1)S(1)} %select_convert_fusion.3), channel_id=1, source_target_pairs={{0,4},{2,6},{4,0},{6,2},{8,12},{10,14},{12,8},{14,10},{16,20},{18,... | collective-permute-start | bytes 1327112 | tf_op jit(solution)/shard_map/ppermute | solution.py:286
  554.0 43.6 %collective-permute-start.6 = (bf16[192,1280]{1,0:T(8,128)(2,1)S(1)}, bf16[192,1280]{1,0:T(8,128)(2,1)S(1)}, u32[]{:S(2)}, u32[]{:S(2)}) collective-permute-start(bf16[192,1280]{1,0:T(8,128)(2,1)S(1)} %select_convert_fusion.2), channel_id=1, source_target_pairs={{0,8},{2,10},{4,12},{6,14},{8,0},{10,2},{12,4},{14,6},{16,24},{18,... | collective-permute-start | bytes 1474568 | tf_op jit(solution)/shard_map/ppermute | solution.py:286
  586.1 16.1 %collective-permute-start.2 = (bf16[96,1152]{1,0:T(8,128)(2,1)S(1)}, bf16[96,1152]{1,0:T(8,128)(2,1)S(1)}, u32[]{:S(2)}, u32[]{:S(2)}) collective-permute-start(bf16[96,1152]{1,0:T(8,128)(2,1)S(1)} %select_convert_fusion.5), channel_id=1, source_target_pairs={{0,8},{2,10},{4,12},{6,14},{8,0},{10,2},{12,4},{14,6},{16,24},{18,... | collective-permute-start | bytes 663560 | tf_op jit(solution)/shard_map/ppermute | solution.py:286
  602.2 34.3 %copy-start.29 = (bf16[24,7040]{1,0:T(8,128)(2,1)S(1)}, bf16[24,7040]{1,0:T(8,128)(2,1)}, u32[]{:S(2)}) copy-start(bf16[24,7040]{1,0:T(8,128)(2,1)} %reduce-scatter.4.cloned.1.call-done) | copy-start | bytes 1013764
  602.2 19.1 %collective-permute-start.3 = (bf16[48,1152]{1,0:T(8,128)(2,1)S(1)}, bf16[48,1152]{1,0:T(8,128)(2,1)S(1)}, u32[]{:S(2)}, u32[]{:S(2)}) collective-permute-start(bf16[48,1152]{1,0:T(8,128)(2,1)S(1)} %select_convert_fusion.7), channel_id=1, source_target_pairs={{0,1},{1,0},{2,3},{3,2},{4,5},{5,4},{6,7},{7,6},{8,9},{9,8},{10,11... | collective-permute-start | bytes 331784 | tf_op jit(solution)/shard_map/ppermute | solution.py:286
  618.6 18.6 %copy-start.5 = (f32[1024,768]{0,1:T(8,128)S(1)}, f32[1024,768]{0,1:T(8,128)}, u32[]{:S(2)}) copy-start(f32[1024,768]{0,1:T(8,128)} %copy-done.3) | copy-start | bytes 9437188
  618.7 18.6 %copy-start.43 = (f32[768]{0:T(1024)S(1)}, f32[768]{0:T(1024)}, u32[]{:S(2)}) copy-start(f32[768]{0:T(1024)} %get-tuple-element.146) | copy-start | bytes 9220
  618.7 6.8 collective-permute-start.7
  625.6 4.9 collective-permute-start.8
  626.0 6.5 collective-permute-start.4
  630.6 5.8 collective-permute-start.9
  (17 other events, 44.2 us)
Sparse Core Ops, SparseCore 0:
  19.1 63.4 all-gather.4
  86.0 66.4 all-gather.6
  155.5 62.3 all-gather.8
  361.5 159.8 reduce-scatter.3
  637.4 65.6 all-gather.10

commit v10 on v8

--- a/solution.py
+++ b/solution.py
@@ -237,6 +237,14 @@
     return out
 
 
+def destination_order(x, group_size, shard_size, axis):
+    shape = x.shape
+    lead, size, rest = shape[:axis], shape[axis], shape[axis + 1 :]
+    blocks = x.reshape(lead + (shard_size, group_size, size // (group_size * shard_size)) + rest)
+    moved = jnp.swapaxes(blocks, len(lead), len(lead) + 1)
+    return moved.reshape(shape)
+
+
 def grad_rows_reduce(packed, group_size, shard_size):
     rows, cols = packed.shape
     n = rows // (group_size * shard_size)
@@ -483,8 +491,9 @@
     grad_qkv_wide = grad_qkv.astype(jnp.float32)
     query_bias_grad = jnp.sum(grad_qkv_wide[:, :model_width], axis=0)
     value_bias_grad = jnp.sum(grad_qkv_wide[:, 2 * model_width :], axis=0)
-    qkv_weight_grad = jnp.einsum(
-        "td,te->de", normed_low, grad_qkv, preferred_element_type=jnp.float32
+    split = ((qkv_width + 128) // 256) * 128
+    left_grad = jnp.einsum(
+        "td,te->de", normed_low, grad_qkv[:, :split], preferred_element_type=jnp.float32
     )
     grad_normed = jnp.einsum("te,de->td", grad_qkv, qkv_full, preferred_element_type=jnp.float32)
     grad_in_part, first_gain_grad, first_shift_grad = norm_back(
@@ -497,22 +506,20 @@
         query_bias_grad,
         value_bias_grad,
     )
-    attn_pack = jnp.concatenate(
-        [qkv_weight_grad, pack_columns(attn_small, model_width)], axis=1
-    )
-    attn_pack = (
-        attn_pack.reshape(shard_size, group_size, n, -1)
-        .transpose(1, 0, 2, 3)
-        .reshape(model_width, -1)
-    )
-    ffn_part, attn_pack = lax.optimization_barrier((ffn_part, attn_pack))
-    split = (attn_pack.shape[1] // 256) * 128
-    attn_left = hypercube_reduce_scatter(
-        attn_pack[:, :split], order_a, group_size, shard_size
-    )
-    attn_right = hypercube_reduce_scatter(
-        attn_pack[:, split:], order_b, group_size, shard_size
-    )
+    right_grad = jnp.concatenate(
+        [
+            jnp.einsum(
+                "td,te->de", normed_low, grad_qkv[:, split:], preferred_element_type=jnp.float32
+            ),
+            pack_columns(attn_small, model_width),
+        ],
+        axis=1,
+    )
+    left_grad = destination_order(left_grad, group_size, shard_size, 0)
+    right_grad = destination_order(right_grad, group_size, shard_size, 0)
+    ffn_part, left_grad = lax.optimization_barrier((ffn_part, left_grad))
+    attn_left = hypercube_reduce_scatter(left_grad, order_a, group_size, shard_size)
+    attn_right = hypercube_reduce_scatter(right_grad, order_b, group_size, shard_size)
     both = lax.all_gather(
         jnp.concatenate(
             [

time: 737 us -> 746 us (1.012)
  other arithmetic: 76.3 us -> 85.8 us
    concatenate x10 -> x5, local copies, waits for them, and re-layouts: 17.6 us -> 10.7 us  [per_device(): jnp.concatenate([jnp.einsum('td,te->de', normed_low, grad_qkv[:, split:],...]
  transfers between devices with their start and end apart: 15 -> 15, of which waited for: 11 -> 10; matrix products, arithmetic and copies ran while one was open for 24% -> 25% of each run, Pallas kernels for 23% -> 23%
where the time goes in v10:
time: 746 us; the launch traced here: 737 us
  Pallas kernels  166 us (22%)
  local copies, waits for them, and re-layouts  141 us (19%)
  waiting for transfers between devices  125 us (17%)
  matrix products  123 us (16%)
  other arithmetic  85.8 us (12%)
  starting transfers between devices  80.2 us (11%)
  between operations  15 us (2%)
    pallas_call x1, Pallas kernels, attention_backward(): pl.pallas_call(_bwd_kernel, out_shape=(jax.ShapeDtypeStruct((heads, lengt...  101 us
    ppermute x10, starting transfers between devices, hypercube_reduce_scatter(): got = lax.ppermute(send, axis, [(j, j ^ 1 << b) for j in range(size)])  80 us
    pallas_call x1, Pallas kernels, attention_forward(): pl.pallas_call(_fwd_kernel, out_shape=jax.ShapeDtypeStruct((heads, length...  65.5 us
    all_gather x1, waiting for transfers between devices, per_device(): lax.all_gather(first_pack, ('group', 'shard'), axis=0, tiled=True)  53 us
    all_gather x1, waiting for transfers between devices, per_device(): lax.all_gather(jnp.concatenate([ffn_part, attn_left.astype(jnp.bfloat16),...  50.5 us
    dot_general x1, matrix products, per_device(): jnp.dot(second_low, expand_full, preferred_element_type=jnp.float32)  39 us
    ppermute x10, waiting for transfers between devices, hypercube_reduce_scatter(): got = lax.ppermute(send, axis, [(j, j ^ 1 << b) for j in range(size)])  21.2 us
    reduce_sum x1, other arithmetic, per_device(): expand_bias_grad = jnp.sum(grad_pre.astype(jnp.float32), axis=0)  18.3 us
  transfers between devices with their start and end apart: 15, of which 10 were waited for; matrix products, arithmetic and copies ran while one was open for 25% of the time, Pallas kernels for 23%

profile of v10, /device:TPU:0, one launch (start us, length us, event | category | flops | bytes accessed | tf_op | source)
XLA Modules:
  0.0 737.0 jit_solution(5671235772510976169)
XLA Ops:
  29.5 53.0 %all-gather.5.cloned.1.call-done = bf16[768,2432]{1,0:T(8,128)(2,1)} async-done(((bf16[24,2432]{1,0:T(8,128)(2,1)}), bf16[768,2432]{1,0:T(8,128)(2,1)}) %all-gather.5.cloned.1.call-update) | async-done | bytes 3735568 | tf_op jit(solution)/shard_map/all_gather | solution.py:346
  84.0 4.2 convert_reduce_fusion.1
  88.2 6.4 add_convert_fusion.2
  98.6 2.8 copy.229.q_ref
  108.6 65.5 %shard_map.339 = f32[12,1024,64]{2,1,0:T(8,128)} custom-call(s32[2]{0:T(128)} %and_select_fusion.lo_ref, bf16[12,1024,64]{2,1,0:T(8,128)(2,1)} %copy.229.q_ref, bf16[12,64,1024]{2,1,0:T(8,128)(2,1)} %bitcast.83, bf16[12,1024,64]{2,1,0:T(8,128)(2,1)} %copy.230.v_ref, s32[1024,1]{1,0:T(8,128)} %copy.231.segq_ref, s32[1,1024]{1,0:T(1,128)} %bitcast.112), custom_call_target="tpu_custom_call" | custom-call | flops 1610612736 | bytes 6291456 | tf_op jit(solution)/shard_map/pallas_call | solution.py:127
  174.1 6.1 copy.232
  180.2 4.0 copy.233
  184.2 3.3 reduce_sum.276
  187.5 3.8 multiply_reduce_fusion.4
  193.6 4.2 fusion.51
  198.2 39.0 %fusion.47 = (f32[1024]{0:T(1024)S(1)}, f32[1024,3072]{1,0:T(8,128)S(1)}, f32[1024,3072]{1,0:T(8,128)}, f32[1024,3072]{1,0:T(8,128)}) fusion(f32[3072]{0:T(1024)S(1)} %reshape.540, bf16[768,3840]{1,0:T(8,128)(2,1)} %all-gather.7.cloned.1.call-done, f32[1024,768]{0,1:T(8,128)S(1)} %get-tuple-element.186, f32[768]{0:T(1024)S(1)} %get-tuple-element.141, ...), kind=kOutput, calls=%fused_computation.172 | convolution fusion | flops 5043387392 | bytes 45643776 | tf_op jit(solution)/shard_map/dot_general | solution.py:412
  238.7 3.3 copy-done
  242.0 15.4 %multiply_reduce_fusion = (bf16[3072]{0:T(1024)(128)(2,1)S(1)}, f32[1024]{0:T(1024)S(1)}, f32[1024]{0:T(1024)S(1)}, bf16[3072]{0:T(1024)(128)(2,1)S(1)}, bf16[1024,3072]{1,0:T(8,128)(2,1)}, /*index=5*/f32[1024,3072]{1,0:T(8,128)}) fusion(f32[1024,3072]{1,0:T(8,128)} %copy-done, f32[1024]{0:T(1024)S(1)} %add_rsqrt_fusion, ...), kind=kOutput, calls=%fused_computation.3 | convolution fusion | flops 4869578752 | bytes 37801984 | tf_op jit(solution)/shard_map/td,fd->tf/dot_general | solution.py:431
  257.4 18.3 %fusion.46 = (bf16[3072]{0:T(1024)(128)(2,1)S(1)}, bf16[1024,3072]{1,0:T(8,128)(2,1)S(1)}) fusion(f32[1024,3072]{1,0:T(8,128)} %get-tuple-element.170, f32[1024]{0:T(1024)S(1)} %get-tuple-element.194, f32[1024,3072]{1,0:T(8,128)} %copy-done, f32[1024]{0:T(1024)S(1)} %broadcast_multiply_fusion.2, f32[1024]{0:T(1024)S(1)} %get-tuple-element.195, ...), kind=kLoop, calls=%fused_computation.171 | loop fusion | flops 72348672 | bytes 56670208 | tf_op jit(solution)/shard_map/reduce_sum | solution.py:438
  275.8 7.2 convolution_convert_fusion.1
  283.0 6.8 fusion.52
  289.8 3.5 copy.236
  293.3 3.0 multiply_reduce_fusion.7
  296.3 9.7 %convolution_convert_fusion = bf16[3072,768]{1,0:T(8,128)(2,1)} fusion(bf16[1024,3072]{1,0:T(8,128)(2,1)} %get-tuple-element.171, bf16[1024,768]{1,0:T(8,128)(2,1)S(1)} %copy-done.17), kind=kOutput, calls=%fused_computation.26 | convolution fusion | flops 4834197504 | bytes 12582912 | tf_op jit(solution)/shard_map/tf,td->fd/dot_general | solution.py:427
  306.0 8.5 %reshape.501 = bf16[768,3072]{1,0:T(8,128)(2,1)} reshape(bf16[3072,768]{1,0:T(8,128)(2,1)} %convolution_convert_fusion) | data formatting | bytes 9437184 | tf_op jit(solution)/shard_map/reshape | solution.py:472
  314.5 3.8 convert_reduce_fusion.9
  318.3 3.0 convolution_convert_fusion.2
  325.7 4.9 multiply_reduce_fusion.5
  335.1 18.0 %concatenate.57 = bf16[768,7040]{1,0:T(8,128)(2,1)} concatenate(bf16[768,3072]{1,0:T(8,128)(2,1)} %convolution_convert_fusion.1, bf16[768,3072]{1,0:T(8,128)(2,1)} %reshape.501, bf16[768,768]{1,0:T(8,128)(2,1)} %convolution_convert_fusion.2, bf16[768,1]{1,0:T(8,128)(2,1)S(1)} %reshape.554, bf16[768,1]{1,0:T(8,128)(2,1)} %reshape.555, bf16[768,1]{1,0:T(8,128)(2,1)S(1)} %copy-done.23, ...), dimensions={1} | concatenate | bytes 21626880 | tf_op jit(solution)/shard_map/concatenate | solution.py:469
  353.1 10.1 %copy.252 = bf16[16,2,24,7040]{3,2,1,0:T(8,128)(2,1)} copy(bf16[16,2,24,7040]{3,2,0,1:T(8,128)(2,1)} %bitcast.82) | data formatting | bytes 21626880 | tf_op jit(solution)/shard_map/transpose | solution.py:253
  368.0 2.8 copy.248.do_ref
  370.9 100.6 %shard_map.340 = (f32[12,1024,64]{2,1,0:T(8,128)}, f32[12,64,1024]{2,1,0:T(8,128)}, f32[12,64,1024]{2,1,0:T(8,128)}) custom-call(s32[2]{0:T(128)} %and_select_fusion.lo_ref, bf16[12,1024,64]{2,1,0:T(8,128)(2,1)} %copy.229.q_ref, bf16[12,64,1024]{2,1,0:T(8,128)(2,1)} %bitcast.92, bf16[12,1024,64]{2,1,0:T(8,128)(2,1)} %copy.247.k_ref, ...), custom_call_target="tpu_custom_call" | custom-call | flops 4026531840 | bytes 12582912 | tf_op jit(solution)/shard_map/pallas_call | solution.py:155
  471.5 3.7 convert.89
  480.6 9.6 %fusion.53 = (f32[768]{0:T(1024)}, f32[1024,768]{1,0:T(8,128)}) fusion(bf16[768,2432]{1,0:T(8,128)(2,1)} %all-gather.5.cloned.1.call-done, bf16[1024,768]{0,1:T(8,128)(2,1)} %bitcast.105, bf16[1024,768]{0,1:T(8,128)(2,1)} %bitcast.98, bf16[1024,768]{0,1:T(8,128)(2,1)} %bitcast.102), kind=kOutput, calls=%fused_computation.177 | convolution fusion | flops 3638820096 | bytes 11406336 | tf_op jit(solution)/shard_map/te,de->td/dot_general | solution.py:498
  490.2 3.7 copy.251
  493.9 3.6 fusion.23
  499.5 2.9 fusion.33
  506.1 5.6 fusion.29
  512.5 6.0 concatenate.66
  524.1 15.2 %collective-permute-start.5 = (bf16[384,1280]{1,0:T(8,128)(2,1)}, bf16[384,1280]{1,0:T(8,128)(2,1)}, u32[]{:S(2)}, u32[]{:S(2)}) collective-permute-start(bf16[384,1280]{1,0:T(8,128)(2,1)} %bitcast.55), channel_id=1, source_target_pairs={{0,2},{2,0},{4,6},{6,4},{8,10},{10,8},{12,14},{14,12},{16,18},{18,... | collective-permute-start | bytes 2949128 | tf_op jit(solution)/shard_map/ppermute | solution.py:294
  543.6 16.3 %collective-permute-start.6 = (bf16[192,1280]{1,0:T(8,128)(2,1)S(1)}, bf16[192,1280]{1,0:T(8,128)(2,1)S(1)}, u32[]{:S(2)}, u32[]{:S(2)}) collective-permute-start(bf16[192,1280]{1,0:T(8,128)(2,1)S(1)} %select_convert_fusion.2), channel_id=1, source_target_pairs={{0,8},{2,10},{4,12},{6,14},{8,0},{10,2},{12,4},{14,6},{16,24},{18,... | collective-permute-start | bytes 1474568 | tf_op jit(solution)/shard_map/ppermute | solution.py:294
  564.4 7.2 collective-permute-done.6
  571.7 17.1 %collective-permute-start.7 = (bf16[96,1280]{1,0:T(8,128)(2,1)S(1)}, bf16[96,1280]{1,0:T(8,128)(2,1)S(1)}, u32[]{:S(2)}, u32[]{:S(2)}) collective-permute-start(bf16[96,1280]{1,0:T(8,128)(2,1)S(1)} %select_convert_fusion.4), channel_id=1, source_target_pairs={{0,4},{2,6},{4,0},{6,2},{8,12},{10,14},{12,8},{14,10},{16,20},{18,... | collective-permute-start | bytes 737288 | tf_op jit(solution)/shard_map/ppermute | solution.py:294
  591.3 3.3 collective-permute-done.7
  597.1 16.3 %collective-permute-start.8 = (bf16[48,1280]{1,0:T(8,128)(2,1)S(1)}, bf16[48,1280]{1,0:T(8,128)(2,1)S(1)}, u32[]{:S(2)}, u32[]{:S(2)}) collective-permute-start(bf16[48,1280]{1,0:T(8,128)(2,1)S(1)} %select_convert_fusion.6), channel_id=1, source_target_pairs={{0,1},{1,0},{2,3},{3,2},{4,5},{5,4},{6,7},{7,6},{8,9},{9,8},{10,11... | collective-permute-start | bytes 368648 | tf_op jit(solution)/shard_map/ppermute | solution.py:294
  616.3 3.3 collective-permute-done.2
  619.7 9.4 %collective-permute-start.3 = (bf16[48,1152]{1,0:T(8,128)(2,1)S(1)}, bf16[48,1152]{1,0:T(8,128)(2,1)S(1)}, u32[]{:S(2)}, u32[]{:S(2)}) collective-permute-start(bf16[48,1152]{1,0:T(8,128)(2,1)S(1)} %select_convert_fusion.7), channel_id=1, source_target_pairs={{0,1},{1,0},{2,3},{3,2},{4,5},{5,4},{6,7},{7,6},{8,9},{9,8},{10,11... | collective-permute-start | bytes 331784 | tf_op jit(solution)/shard_map/ppermute | solution.py:294
  638.5 9.1 %add_convert_fusion.3 = bf16[1024,768]{0,1:T(8,128)(2,1)S(1)} fusion(f32[1024,768]{0,1:T(8,128)} %copy-done.3, bf16[1024,3072]{1,0:T(8,128)(2,1)} %get-tuple-element.171, bf16[3072,768]{1,0:T(8,128)(2,1)} %all-gather.9.cloned.1.call-done, f32[768]{0:T(1024)S(1)} %copy-done.40), kind=kOutput, calls=%fused_computation.62 | convolution fusion | flops 4834197504 | bytes 15731712 | tf_op jit(solution)/shard_map/dot_general | solution.py:422
  649.5 3.9 fusion.22
  654.9 50.5 %all-gather.11.cloned.1.call-done = bf16[384,9472]{1,0:T(8,128)(2,1)} async-done(((bf16[24,9472]{1,0:T(8,128)(2,1)}), bf16[384,9472]{1,0:T(8,128)(2,1)}) %all-gather.11.cloned.1.call-update) | async-done | bytes 7274512 | tf_op jit(solution)/shard_map/all_gather | solution.py:523
  711.1 7.4 %slice_convert_fusion = (f32[384,3072]{1,0:T(8,128)}, f32[384,3072]{1,0:T(8,128)}) fusion(bf16[384,9472]{1,0:T(8,128)(2,1)} %all-gather.11.cloned.1.call-done), kind=kLoop, calls=%fused_computation.74 | loop fusion | flops 2359296 | bytes 14155776 | tf_op jit(solution)/shard_map/convert_element_type | solution.py:544
  718.5 6.1 reshape.544
  724.6 3.5 slice_convert_fusion.2
  (242 shorter events, 107.3 us)
Async XLA Ops:
  7.2 16.8 %copy-start.15 = (bf16[1024,768]{1,0:T(8,128)(2,1)S(1)}, bf16[1024,768]{1,0:T(8,128)(2,1)}, u32[]{:S(2)}) copy-start(bf16[1024,768]{1,0:T(8,128)(2,1)} %param.39) | copy-start | bytes 4718596
  7.2 17.1 %copy-start.45 = (s32[1,5]{1,0:T(1,128)S(1)}, s32[1,5]{1,0:T(1,128)}, u32[]{:S(2)}) copy-start(s32[1,5]{1,0:T(1,128)} %param.21) | copy-start | bytes 64
  7.2 75.3 %all-gather.5.cloned.1.call-start = ((), (), s32[]{:S(2)}) async-start(), calls=%async_computation.1 | async-start | bytes 3852288 | tf_op jit(solution)/shard_map/all_gather | solution.py:346
  17.1 9.0 %copy-start.22 = (bf16[1024,768]{1,0:T(8,128)(2,1)S(1)}, bf16[1024,768]{1,0:T(8,128)(2,1)}, u32[]{:S(2)}) copy-start(bf16[1024,768]{1,0:T(8,128)(2,1)} %param.20) | copy-start | bytes 4718596
  18.9 174.7 %all-gather.7.cloned.1.call-start = ((), (), s32[]{:S(2)}) async-start(), calls=%async_computation.2 | async-start | bytes 6082560 | tf_op jit(solution)/shard_map/all_gather | solution.py:364
  20.6 221.4 %all-gather.9.cloned.1.call-start = ((), (), s32[]{:S(2)}) async-start(), calls=%async_computation.3 | async-start | bytes 4866048 | tf_op jit(solution)/shard_map/all_gather | solution.py:367
  21.4 567.5 %reduce-scatter.4.cloned.1.call-start = ((), (), s32[]{:S(2)}) async-start(), calls=%async_computation.5 | async-start | bytes 11151360
  26.9 166.8 %copy-start.1 = (bf16[1024,768]{0,1:T(8,128)(2,1)}, bf16[1024,768]{0,1:T(8,128)(2,1)S(1)}, u32[]{:S(2)}) copy-start(bf16[1024,768]{0,1:T(8,128)(2,1)S(1)} %copy.215) | copy-start | bytes 4718596
  27.1 67.5 %copy-start.25 = (f32[1024]{0:T(1024)}, f32[1024]{0:T(1024)S(1)}, u32[]{:S(2)}) copy-start(f32[1024]{0:T(1024)S(1)} %broadcast_multiply_fusion.11) | copy-start | bytes 12292
  27.6 67.0 %copy-start.32 = (f32[1024]{0:T(1024)}, f32[1024]{0:T(1024)S(1)}, u32[]{:S(2)}) copy-start(f32[1024]{0:T(1024)S(1)} %add_rsqrt_fusion.3) | copy-start | bytes 12292
  88.2 6.4 copy-start.30
  88.2 6.4 copy-start.41
  88.2 105.4 %copy-start.34 = (f32[768]{0:T(1024)}, f32[768]{0:T(1024)S(1)}, u32[]{:S(2)}) copy-start(f32[768]{0:T(1024)S(1)} %get-tuple-element.145) | copy-start | bytes 9220
  88.2 105.4 %copy-start.43 = (f32[768]{0:T(1024)}, f32[768]{0:T(1024)S(1)}, u32[]{:S(2)}) copy-start(f32[768]{0:T(1024)S(1)} %get-tuple-element.144) | copy-start | bytes 9220
  98.6 5.5 copy-start.8
  105.8 68.3 %copy-start.9 = (bf16[1024,768]{0,1:T(8,128)(2,1)}, bf16[1024,768]{0,1:T(8,128)(2,1)S(1)}, u32[]{:S(2)}) copy-start(bf16[1024,768]{0,1:T(8,128)(2,1)S(1)} %copy.228) | copy-start | bytes 4718596
  187.5 6.1 copy-start.28
  191.3 6.5 copy-start.36
  197.8 39.4 %copy-start.3 = (f32[1024,768]{0,1:T(8,128)}, f32[1024,768]{0,1:T(8,128)S(1)}, u32[]{:S(2)}) copy-start(f32[1024,768]{0,1:T(8,128)S(1)} %get-tuple-element.186) | copy-start | bytes 9437188
  237.3 4.7 copy-start
  237.3 4.7 copy-start.16
  242.0 40.9 %slice-start = ((s8[5898240]{0:T(1024)(128)(4,1)}), s8[1703936]{0:T(1024)(128)(4,1)S(1)}, s32[]{:S(2)}) async-start(s8[5898240]{0:T(1024)(128)(4,1)} %bitcast.125), calls=%async_computation.6 | async-start | bytes 3407872
  257.4 18.4 %copy-start.4 = (f32[1024,768]{0,1:T(8,128)S(1)}, f32[1024,768]{0,1:T(8,128)}, u32[]{:S(2)}) copy-start(f32[1024,768]{0,1:T(8,128)} %copy-done.3) | copy-start | bytes 9437188
  257.4 25.6 %slice-start.1 = ((s8[5898240]{0:T(1024)(128)(4,1)}), s8[4194304]{0:T(1024)(128)(4,1)S(1)}, s32[]{:S(2)}) async-start(s8[5898240]{0:T(1024)(128)(4,1)} %bitcast.125), calls=%async_computation.7 | async-start | bytes 8388608
  314.4 3.9 copy-start.29
  314.4 3.9 copy-start.35
  314.4 3.9 copy-start.37
  314.4 3.9 copy-start.44
  318.3 7.4 %copy-start.12 = (f32[1024,768]{1,0:T(8,128)S(1)}, f32[1024,768]{1,0:T(8,128)}, u32[]{:S(2)}) copy-start(f32[1024,768]{1,0:T(8,128)} %copy.233) | copy-start | bytes 9437188
  363.2 4.1 copy-start.20
  363.2 342.2 %all-gather.11.cloned.1.call-start = ((), (), s32[]{:S(2)}) async-start(), calls=%async_computation.4 | async-start | bytes 7729152 | tf_op jit(solution)/shard_map/all_gather | solution.py:523
  471.5 6.1 copy-start.14
  493.9 5.6 copy-start.18
  524.1 17.7 %collective-permute-start.5 = (bf16[384,1280]{1,0:T(8,128)(2,1)}, bf16[384,1280]{1,0:T(8,128)(2,1)}, u32[]{:S(2)}, u32[]{:S(2)}) collective-permute-start(bf16[384,1280]{1,0:T(8,128)(2,1)} %bitcast.55), channel_id=1, source_target_pairs={{0,2},{2,0},{4,6},{6,4},{8,10},{10,8},{12,14},{14,12},{16,18},{18,... | collective-permute-start | bytes 2949128 | tf_op jit(solution)/shard_map/ppermute | solution.py:294
  541.7 18.2 %copy-start.19 = (bf16[1024,12,64]{0,2,1:T(8,128)(2,1)S(1)}, bf16[1024,12,64]{0,2,1:T(8,128)(2,1)}, u32[]{:S(2)}) copy-start(bf16[1024,12,64]{0,2,1:T(8,128)(2,1)} %copy.250) | copy-start | bytes 4718596
  541.7 18.2 %copy-start.42 = (f32[768]{0:T(1024)S(1)}, f32[768]{0:T(1024)}, u32[]{:S(2)}) copy-start(f32[768]{0:T(1024)} %copy-done.41) | copy-start | bytes 9220
  543.6 28.0 %collective-permute-start.6 = (bf16[192,1280]{1,0:T(8,128)(2,1)S(1)}, bf16[192,1280]{1,0:T(8,128)(2,1)S(1)}, u32[]{:S(2)}, u32[]{:S(2)}) collective-permute-start(bf16[192,1280]{1,0:T(8,128)(2,1)S(1)} %select_convert_fusion.2), channel_id=1, source_target_pairs={{0,8},{2,10},{4,12},{6,14},{8,0},{10,2},{12,4},{14,6},{16,24},{18,... | collective-permute-start | bytes 1474568 | tf_op jit(solution)/shard_map/ppermute | solution.py:294
  571.7 22.9 %collective-permute-start.7 = (bf16[96,1280]{1,0:T(8,128)(2,1)S(1)}, bf16[96,1280]{1,0:T(8,128)(2,1)S(1)}, u32[]{:S(2)}, u32[]{:S(2)}) collective-permute-start(bf16[96,1280]{1,0:T(8,128)(2,1)S(1)} %select_convert_fusion.4), channel_id=1, source_target_pairs={{0,4},{2,6},{4,0},{6,2},{8,12},{10,14},{12,8},{14,10},{16,20},{18,... | collective-permute-start | bytes 737288 | tf_op jit(solution)/shard_map/ppermute | solution.py:294
  588.8 5.8 copy-start.7
  591.2 3.7 collective-permute-start
  595.3 18.1 %collective-permute-start.1 = (bf16[192,1152]{1,0:T(8,128)(2,1)S(1)}, bf16[192,1152]{1,0:T(8,128)(2,1)S(1)}, u32[]{:S(2)}, u32[]{:S(2)}) collective-permute-start(bf16[192,1152]{1,0:T(8,128)(2,1)S(1)} %select_convert_fusion.3), channel_id=1, source_target_pairs={{0,4},{2,6},{4,0},{6,2},{8,12},{10,14},{12,8},{14,10},{16,20},{18,... | collective-permute-start | bytes 1327112 | tf_op jit(solution)/shard_map/ppermute | solution.py:294
  597.1 19.1 %collective-permute-start.8 = (bf16[48,1280]{1,0:T(8,128)(2,1)S(1)}, bf16[48,1280]{1,0:T(8,128)(2,1)S(1)}, u32[]{:S(2)}, u32[]{:S(2)}) collective-permute-start(bf16[48,1280]{1,0:T(8,128)(2,1)S(1)} %select_convert_fusion.6), channel_id=1, source_target_pairs={{0,1},{1,0},{2,3},{3,2},{4,5},{5,4},{6,7},{7,6},{8,9},{9,8},{10,11... | collective-permute-start | bytes 368648 | tf_op jit(solution)/shard_map/ppermute | solution.py:294
  613.6 24.1 %copy-start.24 = (bf16[24,7040]{1,0:T(8,128)(2,1)S(1)}, bf16[24,7040]{1,0:T(8,128)(2,1)}, u32[]{:S(2)}) copy-start(bf16[24,7040]{1,0:T(8,128)(2,1)} %reduce-scatter.4.cloned.1.call-done) | copy-start | bytes 1013764
  613.6 24.9 %copy-start.40 = (f32[768]{0:T(1024)S(1)}, f32[768]{0:T(1024)}, u32[]{:S(2)}) copy-start(f32[768]{0:T(1024)} %get-tuple-element.140) | copy-start | bytes 9220
  613.6 6.0 collective-permute-start.2
  619.7 12.1 %collective-permute-start.3 = (bf16[48,1152]{1,0:T(8,128)(2,1)S(1)}, bf16[48,1152]{1,0:T(8,128)(2,1)S(1)}, u32[]{:S(2)}, u32[]{:S(2)}) collective-permute-start(bf16[48,1152]{1,0:T(8,128)(2,1)S(1)} %select_convert_fusion.7), channel_id=1, source_target_pairs={{0,1},{1,0},{2,3},{3,2},{4,5},{5,4},{6,7},{7,6},{8,9},{9,8},{10,11... | collective-permute-start | bytes 331784 | tf_op jit(solution)/shard_map/ppermute | solution.py:294
  629.2 5.8 collective-permute-start.9
  631.9 5.7 collective-permute-start.4
  (15 other events, 43.0 us)
Sparse Core Ops, SparseCore 0:
  19.1 63.4 all-gather.4
  86.0 66.5 all-gather.6
  155.5 62.2 all-gather.8
  363.3 159.8 reduce-scatter.3
  638.6 66.7 all-gather.10

commit v11 on v8

--- a/solution.py
+++ b/solution.py
@@ -288,6 +288,28 @@
     return cur
 
 
+def hypercube_all_gather(x, order, group_size, shard_size):
+    total = group_size * shard_size
+    levels = total.bit_length() - 1
+    n, cols = x.shape
+    sbits = shard_size.bit_length() - 1
+    cur = x
+    for axis, b in order:
+        size = group_size if axis == "group" else shard_size
+        got = lax.ppermute(cur, axis, [(j, j ^ (1 << b)) for j in range(size)])
+        mine = (lax.axis_index(axis) >> b) & 1
+        low = jnp.where(mine == 1, got, cur)
+        high = jnp.where(mine == 1, cur, got)
+        cur = jnp.concatenate([low, high], axis=0)
+    kbits = [b if axis == "shard" else sbits + b for axis, b in order]
+    perm = [levels - 1 - kbits.index(levels - 1 - a) for a in range(levels)]
+    return (
+        cur.reshape([2] * levels + [n, cols])
+        .transpose(perm + [levels, levels + 1])
+        .reshape(total * n, cols)
+    )
+
+
 def per_device(
     tokens,
     doc_lengths,
@@ -335,7 +357,19 @@
     )
     small_widths = [p.shape[0] // n for p in small_parts]
     first_pack = jnp.concatenate([qkv_weight, pack_columns(small_parts, n)], axis=1)
-    first_full = lax.all_gather(first_pack, ("group", "shard"), axis=0, tiled=True)
+    gather_a, gather_b = hypercube_orders(group_size, shard_size)
+    cut = (first_pack.shape[1] // 256) * 128
+    first_full = jnp.concatenate(
+        [
+            hypercube_all_gather(
+                first_pack[:, :cut], gather_a[::-1], group_size, shard_size
+            ),
+            hypercube_all_gather(
+                first_pack[:, cut:], gather_b[::-1], group_size, shard_size
+            ),
+        ],
+        axis=1,
+    )
     qkv_full = first_full[:, :qkv_width]
     (
         gain_one,

time: 737 us -> 729 us (0.989)
  waiting for transfers between devices: 124 us -> 97.2 us
  starting transfers between devices: 79.6 us -> 90.7 us
    all_gather x1 -> x0, waiting for transfers between devices: 53 us -> none  [per_device(): lax.all_gather(first_pack, ('group', 'shard'), axis=0, tiled=True)]
    ppermute x0 -> x10, waiting for transfers between devices: none -> 27 us  [hypercube_all_gather(): got = lax.ppermute(cur, axis, [(j, j ^ 1 << b) for j in range(size)])]
    ppermute x0 -> x10, starting transfers between devices: none -> 10.8 us  [hypercube_all_gather(): got = lax.ppermute(cur, axis, [(j, j ^ 1 << b) for j in range(size)])]
  transfers between devices with their start and end apart: 15 -> 24, of which waited for: 11 -> 17; matrix products, arithmetic and copies ran while one was open for 24% -> 26% of each run, Pallas kernels for 23% -> 23%
where the time goes in v11:
time: 729 us; the launch traced here: 718 us
  Pallas kernels  166 us (23%)
  local copies, waits for them, and re-layouts  147 us (20%)
  matrix products  120 us (16%)
  waiting for transfers between devices  97.2 us (13%)
  starting transfers between devices  90.7 us (12%)
  other arithmetic  82.3 us (11%)
  between operations  15.2 us (2%)
    pallas_call x1, Pallas kernels, attention_backward(): pl.pallas_call(_bwd_kernel, out_shape=(jax.ShapeDtypeStruct((heads, lengt...  101 us
    ppermute x10, starting transfers between devices, hypercube_reduce_scatter(): got = lax.ppermute(send, axis, [(j, j ^ 1 << b) for j in range(size)])  79.7 us
    pallas_call x1, Pallas kernels, attention_forward(): pl.pallas_call(_fwd_kernel, out_shape=jax.ShapeDtypeStruct((heads, length...  65.5 us
    all_gather x1, waiting for transfers between devices, per_device(): lax.all_gather(jnp.concatenate([ffn_part, attn_left.astype(jnp.bfloat16),...  49.8 us
    dot_general x1, matrix products, per_device(): jnp.dot(second_low, expand_full, preferred_element_type=jnp.float32)  38.9 us
    ppermute x10, waiting for transfers between devices, hypercube_all_gather(): got = lax.ppermute(cur, axis, [(j, j ^ 1 << b) for j in range(size)])  27 us
    reduce_sum x1, other arithmetic, per_device(): expand_bias_grad = jnp.sum(grad_pre.astype(jnp.float32), axis=0)  20.1 us
    ppermute x10, waiting for transfers between devices, hypercube_reduce_scatter(): got = lax.ppermute(send, axis, [(j, j ^ 1 << b) for j in range(size)])  18.9 us
  transfers between devices with their start and end apart: 24, of which 17 were waited for; matrix products, arithmetic and copies ran while one was open for 26% of the time, Pallas kernels for 23%

profile of v11, /device:TPU:0, one launch (start us, length us, event | category | flops | bytes accessed | tf_op | source)
XLA Modules:
  0.0 718.3 jit_solution(10944706894707036084)
XLA Ops:
  19.7 4.1 collective-permute-start
  34.6 3.8 collective-permute-done.6
  41.7 2.9 collective-permute-done.7
  46.7 4.8 collective-permute-done.2
  52.3 6.7 collective-permute-done.8
  60.3 4.9 collective-permute-done.3
  79.3 5.2 add_convert_fusion.2
  98.5 65.5 %shard_map.339 = f32[12,1024,64]{2,1,0:T(8,128)} custom-call(s32[2]{0:T(128)} %and_select_fusion.lo_ref, bf16[12,1024,64]{2,1,0:T(8,128)(2,1)} %copy.235.q_ref, bf16[12,64,1024]{2,1,0:T(8,128)(2,1)} %bitcast.89, bf16[12,1024,64]{2,1,0:T(8,128)(2,1)} %copy.236.v_ref, s32[1024,1]{1,0:T(8,128)} %copy.237.segq_ref, s32[1,1024]{1,0:T(1,128)} %bitcast.125), custom_call_target="tpu_custom_call" | custom-call | flops 1610612736 | bytes 6291456 | tf_op jit(solution)/shard_map/pallas_call | solution.py:127
  164.0 6.3 copy.238
  170.2 3.6 copy.239
  173.8 3.3 reduce_sum.276
  177.2 3.8 multiply_reduce_fusion.4
  181.8 4.2 fusion.44
  186.7 38.9 %fusion.40 = (f32[1024]{0:T(1024)S(1)}, f32[1024,3072]{1,0:T(8,128)S(1)}, f32[1024,3072]{1,0:T(8,128)}, f32[1024,3072]{1,0:T(8,128)}) fusion(f32[3072]{0:T(1024)S(1)} %reshape.556, bf16[768,3840]{1,0:T(8,128)(2,1)} %all-gather.4.cloned.1.call-done, f32[1024,768]{0,1:T(8,128)S(1)} %get-tuple-element.206, f32[768]{0:T(1024)S(1)} %copy-done.54, ...), kind=kOutput, calls=%fused_computation.194 | convolution fusion | flops 5043387392 | bytes 45643776 | tf_op jit(solution)/shard_map/dot_general | solution.py:438
  227.0 3.3 copy-done
  230.3 15.4 %multiply_reduce_fusion = (bf16[3072]{0:T(1024)(128)(2,1)S(1)}, f32[1024]{0:T(1024)S(1)}, f32[1024]{0:T(1024)S(1)}, bf16[3072]{0:T(1024)(128)(2,1)S(1)}, bf16[1024,3072]{1,0:T(8,128)(2,1)}, /*index=5*/f32[1024,3072]{1,0:T(8,128)}) fusion(f32[1024,3072]{1,0:T(8,128)} %copy-done, f32[1024]{0:T(1024)S(1)} %add_rsqrt_fusion, ...), kind=kOutput, calls=%fused_computation.3 | convolution fusion | flops 4869578752 | bytes 37801984 | tf_op jit(solution)/shard_map/td,fd->tf/dot_general | solution.py:457
  245.8 20.1 %fusion.39 = (bf16[3072]{0:T(1024)(128)(2,1)S(1)}, bf16[1024,3072]{1,0:T(8,128)(2,1)S(1)}) fusion(f32[1024,3072]{1,0:T(8,128)} %get-tuple-element.170, f32[1024]{0:T(1024)S(1)} %get-tuple-element.214, f32[1024,3072]{1,0:T(8,128)} %copy-done, f32[1024]{0:T(1024)S(1)} %broadcast_multiply_fusion.2, f32[1024]{0:T(1024)S(1)} %get-tuple-element.215, ...), kind=kLoop, calls=%fused_computation.193 | loop fusion | flops 72348672 | bytes 56670208 | tf_op jit(solution)/shard_map/reduce_sum | solution.py:464
  265.9 7.1 convolution_convert_fusion.1
  273.1 6.8 fusion.45
  279.8 3.5 copy.242
  283.4 3.0 multiply_reduce_fusion.7
  286.4 9.7 %convolution_convert_fusion = bf16[3072,768]{1,0:T(8,128)(2,1)} fusion(bf16[1024,3072]{1,0:T(8,128)(2,1)} %get-tuple-element.171, bf16[1024,768]{1,0:T(8,128)(2,1)S(1)} %copy-done.17), kind=kOutput, calls=%fused_computation.26 | convolution fusion | flops 4834197504 | bytes 12582912 | tf_op jit(solution)/shard_map/tf,td->fd/dot_general | solution.py:453
  296.0 8.5 %reshape.517 = bf16[768,3072]{1,0:T(8,128)(2,1)} reshape(bf16[3072,768]{1,0:T(8,128)(2,1)} %convolution_convert_fusion) | data formatting | bytes 9437184 | tf_op jit(solution)/shard_map/reshape | solution.py:498
  304.5 3.8 convert_reduce_fusion.9
  308.4 3.0 convolution_convert_fusion.2
  315.8 4.7 multiply_reduce_fusion.5
  325.0 18.0 %concatenate.95 = bf16[768,7040]{1,0:T(8,128)(2,1)} concatenate(bf16[768,3072]{1,0:T(8,128)(2,1)} %convolution_convert_fusion.1, bf16[768,3072]{1,0:T(8,128)(2,1)} %reshape.517, bf16[768,768]{1,0:T(8,128)(2,1)} %convolution_convert_fusion.2, bf16[768,1]{1,0:T(8,128)(2,1)S(1)} %reshape.570, bf16[768,1]{1,0:T(8,128)(2,1)} %reshape.571, bf16[768,1]{1,0:T(8,128)(2,1)S(1)} %copy-done.31, ...), dimensions={1} | concatenate | bytes 21626880 | tf_op jit(solution)/shard_map/concatenate | solution.py:495
  343.0 10.1 %copy.258 = bf16[16,2,24,7040]{3,2,1,0:T(8,128)(2,1)} copy(bf16[16,2,24,7040]{3,2,0,1:T(8,128)(2,1)} %bitcast.86) | data formatting | bytes 21626880 | tf_op jit(solution)/shard_map/transpose | solution.py:245
  360.8 100.6 %shard_map.340 = (f32[12,1024,64]{2,1,0:T(8,128)}, f32[12,64,1024]{2,1,0:T(8,128)}, f32[12,64,1024]{2,1,0:T(8,128)}) custom-call(s32[2]{0:T(128)} %and_select_fusion.lo_ref, bf16[12,1024,64]{2,1,0:T(8,128)(2,1)} %copy.235.q_ref, bf16[12,64,1024]{2,1,0:T(8,128)(2,1)} %bitcast.97, bf16[12,1024,64]{2,1,0:T(8,128)(2,1)} %copy.253.k_ref, ...), custom_call_target="tpu_custom_call" | custom-call | flops 4026531840 | bytes 12582912 | tf_op jit(solution)/shard_map/pallas_call | solution.py:155
  461.4 3.5 convert.89
  470.4 9.6 %fusion.46 = (f32[768]{0:T(1024)}, f32[1024,768]{1,0:T(8,128)}) fusion(bf16[768,1280]{1,0:T(8,128)(2,1)} %bitcast.107, bf16[768,1152]{1,0:T(8,128)(2,1)} %bitcast.121, bf16[1024,768]{0,1:T(8,128)(2,1)} %bitcast.111, bf16[1024,768]{0,1:T(8,128)(2,1)} %bitcast.114, bf16[1024,768]{0,1:T(8,128)(2,1)} %bitcast.117), kind=kOutput, calls=%fused_computation.199 | convolution fusion | flops 3645897984 | bytes 11602944 | tf_op jit(solution)/shard_map/te,de->td/dot_general | solution.py:523
  480.0 4.1 copy.257
  484.2 6.0 fusion.35
  490.2 3.6 copy.260
  504.0 8.6 %concatenate.102 = f32[2,16,24,2432]{3,2,0,1:T(8,128)} concatenate(f32[2,16,24,2304]{3,2,0,1:T(8,128)} %copy.260, f32[2,16,24,1]{3,2,0,1:T(8,128)S(1)} %copy.261, f32[2,16,24,1]{3,2,0,1:T(8,128)S(1)} %copy-done.30, f32[2,16,24,1]{3,2,0,1:T(8,128)S(1)} %copy.263, f32[2,16,24,1]{3,2,0,1:T(8,128)S(1)} %copy.264, f32[2,16,24,124]{3,2,0,1:T(8,128)S(1)} %broadcast_in_dim.14), dimensions={3} | concatenate | bytes 14942208 | tf_op jit(solution)/shard_map/concatenate | solution.py:534
  519.1 14.1 %collective-permute-start.10 = (bf16[384,1152]{1,0:T(8,128)(2,1)S(1)}, bf16[384,1152]{1,0:T(8,128)(2,1)S(1)}, u32[]{:S(2)}, u32[]{:S(2)}) collective-permute-start(bf16[384,1152]{1,0:T(8,128)(2,1)S(1)} %bitcast.123), channel_id=1, source_target_pairs={{0,2},{2,0},{4,6},{6,4},{8,10},{10,8},{12,14},{14,12},{16,18},{18,... | collective-permute-start | bytes 2654216 | tf_op jit(solution)/shard_map/ppermute | solution.py:286
  537.3 31.0 %collective-permute-start.16 = (bf16[192,1280]{1,0:T(8,128)(2,1)S(1)}, bf16[192,1280]{1,0:T(8,128)(2,1)S(1)}, u32[]{:S(2)}, u32[]{:S(2)}) collective-permute-start(bf16[192,1280]{1,0:T(8,128)(2,1)S(1)} %select_convert_fusion.2), channel_id=1, source_target_pairs={{0,8},{2,10},{4,12},{6,14},{8,0},{10,2},{12,4},{14,6},{16,24},{18,... | collective-permute-start | bytes 1474568 | tf_op jit(solution)/shard_map/ppermute | solution.py:286
  568.5 10.4 %collective-permute-start.12 = (bf16[96,1152]{1,0:T(8,128)(2,1)S(1)}, bf16[96,1152]{1,0:T(8,128)(2,1)S(1)}, u32[]{:S(2)}, u32[]{:S(2)}) collective-permute-start(bf16[96,1152]{1,0:T(8,128)(2,1)S(1)} %select_convert_fusion.5), channel_id=1, source_target_pairs={{0,8},{2,10},{4,12},{6,14},{8,0},{10,2},{12,4},{14,6},{16,24},{18,... | collective-permute-start | bytes 663560 | tf_op jit(solution)/shard_map/ppermute | solution.py:286
  580.2 4.4 collective-permute-done.12
  584.6 17.3 %collective-permute-start.13 = (bf16[48,1152]{1,0:T(8,128)(2,1)S(1)}, bf16[48,1152]{1,0:T(8,128)(2,1)S(1)}, u32[]{:S(2)}, u32[]{:S(2)}) collective-permute-start(bf16[48,1152]{1,0:T(8,128)(2,1)S(1)} %select_convert_fusion.7), channel_id=1, source_target_pairs={{0,1},{1,0},{2,3},{3,2},{4,5},{5,4},{6,7},{7,6},{8,9},{9,8},{10,11... | collective-permute-start | bytes 331784 | tf_op jit(solution)/shard_map/ppermute | solution.py:286
  604.7 4.1 collective-permute-done.17
  616.1 3.6 collective-permute-done.19
  620.6 9.3 %add_convert_fusion.3 = bf16[1024,768]{0,1:T(8,128)(2,1)S(1)} fusion(f32[1024,768]{0,1:T(8,128)} %copy-done.3, bf16[1024,3072]{1,0:T(8,128)(2,1)} %get-tuple-element.171, bf16[3072,768]{1,0:T(8,128)(2,1)} %all-gather.6.cloned.1.call-done, f32[768]{0:T(1024)S(1)} %copy-done.49), kind=kOutput, calls=%fused_computation.62 | convolution fusion | flops 4834197504 | bytes 15731712 | tf_op jit(solution)/shard_map/dot_general | solution.py:448
  631.5 3.9 fusion.22
  636.9 49.8 %all-gather.8.cloned.1.call-done = bf16[384,9472]{1,0:T(8,128)(2,1)} async-done(((bf16[24,9472]{1,0:T(8,128)(2,1)}), bf16[384,9472]{1,0:T(8,128)(2,1)}) %all-gather.8.cloned.1.call-update) | async-done | bytes 7274512 | tf_op jit(solution)/shard_map/all_gather | solution.py:550
  692.4 7.4 %slice_convert_fusion = (f32[384,3072]{1,0:T(8,128)}, f32[384,3072]{1,0:T(8,128)}) fusion(bf16[384,9472]{1,0:T(8,128)(2,1)} %all-gather.8.cloned.1.call-done), kind=kLoop, calls=%fused_computation.71 | loop fusion | flops 2359296 | bytes 14155776 | tf_op jit(solution)/shard_map/convert_element_type | solution.py:571
  699.8 6.1 reshape.560
  705.9 3.5 slice_convert_fusion.2
  (309 shorter events, 127.6 us)
Async XLA Ops:
  7.2 174.5 %all-gather.4.cloned.1.call-start = ((), (), s32[]{:S(2)}) async-start(), calls=%async_computation.1 | async-start | bytes 6082560 | tf_op jit(solution)/shard_map/all_gather | solution.py:390
  8.9 221.5 %all-gather.6.cloned.1.call-start = ((), (), s32[]{:S(2)}) async-start(), calls=%async_computation.2 | async-start | bytes 4866048 | tf_op jit(solution)/shard_map/all_gather | solution.py:393
  19.7 14.5 %collective-permute-start = (bf16[24,1280]{1,0:T(8,128)(2,1)S(1)}, bf16[24,1280]{1,0:T(8,128)(2,1)S(1)}, u32[]{:S(2)}, u32[]{:S(2)}) collective-permute-start(bf16[24,1280]{1,0:T(8,128)(2,1)S(1)} %slice.296), channel_id=1, source_target_pairs={{0,16},{2,18},{4,20},{6,22},{8,24},{10,26},{12,28},{14,30},{16,0},... | collective-permute-start | bytes 184328 | tf_op jit(solution)/shard_map/ppermute | solution.py:299
  24.7 7.7 %collective-permute-start.5 = (bf16[24,1152]{1,0:T(8,128)(2,1)S(1)}, bf16[24,1152]{1,0:T(8,128)(2,1)S(1)}, u32[]{:S(2)}, u32[]{:S(2)}) collective-permute-start(bf16[24,1152]{1,0:T(8,128)(2,1)S(1)} %slice.233), channel_id=1, source_target_pairs={{0,16},{2,18},{4,20},{6,22},{8,24},{10,26},{12,28},{14,30},{16,0},... | collective-permute-start | bytes 165896 | tf_op jit(solution)/shard_map/ppermute | solution.py:299
  24.7 489.3 %reduce-scatter.4.cloned.1.call-start = ((), (), s32[]{:S(2)}) async-start(), calls=%async_computation.4 | async-start | bytes 11151360
  26.5 43.1 %copy-start.36 = (s32[1024]{0:T(1024)}, s32[1024]{0:T(1024)S(1)}, u32[]{:S(2)}) copy-start(s32[1024]{0:T(1024)S(1)} %fusion.30) | copy-start | bytes 12292
  26.6 5.7 copy-start.32
  28.4 153.3 %copy-start.1 = (bf16[1024,768]{0,1:T(8,128)(2,1)}, bf16[1024,768]{0,1:T(8,128)(2,1)S(1)}, u32[]{:S(2)}) copy-start(bf16[1024,768]{0,1:T(8,128)(2,1)S(1)} %copy.219) | copy-start | bytes 4718596
  28.7 50.6 %copy-start.34 = (f32[1024]{0:T(1024)}, f32[1024]{0:T(1024)S(1)}, u32[]{:S(2)}) copy-start(f32[1024]{0:T(1024)S(1)} %broadcast_multiply_fusion.11) | copy-start | bytes 12292
  29.1 50.1 %copy-start.42 = (f32[1024]{0:T(1024)}, f32[1024]{0:T(1024)S(1)}, u32[]{:S(2)}) copy-start(f32[1024]{0:T(1024)S(1)} %add_rsqrt_fusion.3) | copy-start | bytes 12292
  32.4 6.0 collective-permute-start.6
  34.2 5.7 collective-permute-start.1
  38.4 6.1 collective-permute-start.7
  40.0 11.5 %collective-permute-start.2 = (bf16[96,1280]{1,0:T(8,128)(2,1)S(1)}, bf16[96,1280]{1,0:T(8,128)(2,1)S(1)}, u32[]{:S(2)}, u32[]{:S(2)}) collective-permute-start(bf16[96,1280]{1,0:T(8,128)(2,1)S(1)} %pad_maximum_fusion.11), channel_id=1, source_target_pairs={{0,4},{2,6},{4,0},{6,2},{8,12},{10,14},{12,8},{14,10},{16,20},{18,... | collective-permute-start | bytes 737288 | tf_op jit(solution)/shard_map/ppermute | solution.py:299
  44.7 14.4 %collective-permute-start.8 = (bf16[192,1152]{1,0:T(8,128)(2,1)S(1)}, bf16[192,1152]{1,0:T(8,128)(2,1)S(1)}, u32[]{:S(2)}, u32[]{:S(2)}) collective-permute-start(bf16[192,1152]{1,0:T(8,128)(2,1)S(1)} %pad_maximum_fusion.10), channel_id=1, source_target_pairs={{0,4},{2,6},{4,0},{6,2},{8,12},{10,14},{12,8},{14,10},{16,20},{18,... | collective-permute-start | bytes 1327112 | tf_op jit(solution)/shard_map/ppermute | solution.py:299
  51.7 13.6 %collective-permute-start.3 = (bf16[192,1280]{1,0:T(8,128)(2,1)S(1)}, bf16[192,1280]{1,0:T(8,128)(2,1)S(1)}, u32[]{:S(2)}, u32[]{:S(2)}) collective-permute-start(bf16[192,1280]{1,0:T(8,128)(2,1)S(1)} %pad_maximum_fusion.8), channel_id=1, source_target_pairs={{0,8},{2,10},{4,12},{6,14},{8,0},{10,2},{12,4},{14,6},{16,24},{18,... | collective-permute-start | bytes 1474568 | tf_op jit(solution)/shard_map/ppermute | solution.py:299
  59.2 6.0 copy-start.25
  59.3 8.4 %copy-start.15 = (bf16[1024,768]{1,0:T(8,128)(2,1)S(1)}, bf16[1024,768]{1,0:T(8,128)(2,1)}, u32[]{:S(2)}) copy-start(bf16[1024,768]{1,0:T(8,128)(2,1)} %param.39) | copy-start | bytes 4718596
  60.3 11.3 %collective-permute-start.9 = (bf16[384,1152]{1,0:T(8,128)(2,1)}, bf16[384,1152]{1,0:T(8,128)(2,1)}, u32[]{:S(2)}, u32[]{:S(2)}) collective-permute-start(bf16[384,1152]{1,0:T(8,128)(2,1)} %pad_maximum_fusion.7), channel_id=1, source_target_pairs={{0,2},{2,0},{4,6},{6,4},{8,10},{10,8},{12,14},{14,12},{16,18},{18,... | collective-permute-start | bytes 2654216 | tf_op jit(solution)/shard_map/ppermute | solution.py:299
  67.2 6.4 collective-permute-start.4
  73.6 5.7 copy-start.27
  76.4 8.1 %copy-start.13 = (bf16[2,2,2,2,2,24,1280]{6,5,4,3,2,1,0:T(8,128)(2,1)}, bf16[2,2,2,2,2,24,1280]{6,5,4,3,2,1,0:T(8,128)(2,1)S(1)}, u32[]{:S(2)}) copy-start(bf16[2,2,2,2,2,24,1280]{6,5,4,3,2,1,0:T(8,128)(2,1)S(1)} %copy.230) | copy-start | bytes 5898244
  77.8 6.7 copy-start.40
  77.8 6.7 copy-start.50
  88.5 5.5 copy-start.7
  95.7 68.3 %copy-start.8 = (bf16[1024,768]{0,1:T(8,128)(2,1)}, bf16[1024,768]{0,1:T(8,128)(2,1)S(1)}, u32[]{:S(2)}) copy-start(bf16[1024,768]{0,1:T(8,128)(2,1)S(1)} %copy.234) | copy-start | bytes 4718596
  181.0 4.9 copy-start.46
  181.5 48.9 %copy-start.37 = (f32[3072]{0:T(1024)}, f32[3072]{0:T(1024)S(1)}, u32[]{:S(2)}) copy-start(f32[3072]{0:T(1024)S(1)} %reshape.557) | copy-start | bytes 36868
  185.9 39.6 %copy-start.3 = (f32[1024,768]{0,1:T(8,128)}, f32[1024,768]{0,1:T(8,128)S(1)}, u32[]{:S(2)}) copy-start(f32[1024,768]{0,1:T(8,128)S(1)} %get-tuple-element.206) | copy-start | bytes 9437188
  225.6 4.7 copy-start
  230.3 42.7 %slice-start = ((s8[5898240]{0:T(1024)(128)(4,1)}), s8[1703936]{0:T(1024)(128)(4,1)S(1)}, s32[]{:S(2)}) async-start(s8[5898240]{0:T(1024)(128)(4,1)} %bitcast.138), calls=%async_computation.5 | async-start | bytes 3407872
  245.7 20.1 %copy-start.4 = (f32[1024,768]{0,1:T(8,128)S(1)}, f32[1024,768]{0,1:T(8,128)}, u32[]{:S(2)}) copy-start(f32[1024,768]{0,1:T(8,128)} %copy-done.3) | copy-start | bytes 9437188
  245.7 27.3 %slice-start.1 = ((s8[5898240]{0:T(1024)(128)(4,1)}), s8[4194304]{0:T(1024)(128)(4,1)S(1)}, s32[]{:S(2)}) async-start(s8[5898240]{0:T(1024)(128)(4,1)} %bitcast.138), calls=%async_computation.6 | async-start | bytes 8388608
  308.4 7.4 %copy-start.11 = (f32[1024,768]{1,0:T(8,128)S(1)}, f32[1024,768]{1,0:T(8,128)}, u32[]{:S(2)}) copy-start(f32[1024,768]{1,0:T(8,128)} %copy.239) | copy-start | bytes 9437188
  353.1 333.7 %all-gather.8.cloned.1.call-start = ((), (), s32[]{:S(2)}) async-start(), calls=%async_computation.3 | async-start | bytes 7729152 | tf_op jit(solution)/shard_map/all_gather | solution.py:550
  461.4 6.1 copy-start.14
  519.1 16.1 %collective-permute-start.10 = (bf16[384,1152]{1,0:T(8,128)(2,1)S(1)}, bf16[384,1152]{1,0:T(8,128)(2,1)S(1)}, u32[]{:S(2)}, u32[]{:S(2)}) collective-permute-start(bf16[384,1152]{1,0:T(8,128)(2,1)S(1)} %bitcast.123), channel_id=1, source_target_pairs={{0,2},{2,0},{4,6},{6,4},{8,10},{10,8},{12,14},{14,12},{16,18},{18,... | collective-permute-start | bytes 2654216 | tf_op jit(solution)/shard_map/ppermute | solution.py:286
  533.6 3.5 collective-permute-start.15
  535.5 32.8 %collective-permute-start.11 = (bf16[192,1152]{1,0:T(8,128)(2,1)S(1)}, bf16[192,1152]{1,0:T(8,128)(2,1)S(1)}, u32[]{:S(2)}, u32[]{:S(2)}) collective-permute-start(bf16[192,1152]{1,0:T(8,128)(2,1)S(1)} %select_convert_fusion.3), channel_id=1, source_target_pairs={{0,4},{2,6},{4,0},{6,2},{8,12},{10,14},{12,8},{14,10},{16,20},{18,... | collective-permute-start | bytes 1327112 | tf_op jit(solution)/shard_map/ppermute | solution.py:286
  537.3 42.7 %collective-permute-start.16 = (bf16[192,1280]{1,0:T(8,128)(2,1)S(1)}, bf16[192,1280]{1,0:T(8,128)(2,1)S(1)}, u32[]{:S(2)}, u32[]{:S(2)}) collective-permute-start(bf16[192,1280]{1,0:T(8,128)(2,1)S(1)} %select_convert_fusion.2), channel_id=1, source_target_pairs={{0,8},{2,10},{4,12},{6,14},{8,0},{10,2},{12,4},{14,6},{16,24},{18,... | collective-permute-start | bytes 1474568 | tf_op jit(solution)/shard_map/ppermute | solution.py:286
  568.5 16.1 %collective-permute-start.12 = (bf16[96,1152]{1,0:T(8,128)(2,1)S(1)}, bf16[96,1152]{1,0:T(8,128)(2,1)S(1)}, u32[]{:S(2)}, u32[]{:S(2)}) collective-permute-start(bf16[96,1152]{1,0:T(8,128)(2,1)S(1)} %select_convert_fusion.5), channel_id=1, source_target_pairs={{0,8},{2,10},{4,12},{6,14},{8,0},{10,2},{12,4},{14,6},{16,24},{18,... | collective-permute-start | bytes 663560 | tf_op jit(solution)/shard_map/ppermute | solution.py:286
  584.6 35.2 %copy-start.33 = (bf16[24,7040]{1,0:T(8,128)(2,1)S(1)}, bf16[24,7040]{1,0:T(8,128)(2,1)}, u32[]{:S(2)}) copy-start(bf16[24,7040]{1,0:T(8,128)(2,1)} %reduce-scatter.4.cloned.1.call-done) | copy-start | bytes 1013764
  584.6 20.0 %collective-permute-start.13 = (bf16[48,1152]{1,0:T(8,128)(2,1)S(1)}, bf16[48,1152]{1,0:T(8,128)(2,1)S(1)}, u32[]{:S(2)}, u32[]{:S(2)}) collective-permute-start(bf16[48,1152]{1,0:T(8,128)(2,1)S(1)} %select_convert_fusion.7), channel_id=1, source_target_pairs={{0,1},{1,0},{2,3},{3,2},{4,5},{5,4},{6,7},{7,6},{8,9},{9,8},{10,11... | collective-permute-start | bytes 331784 | tf_op jit(solution)/shard_map/ppermute | solution.py:286
  602.0 18.6 %copy-start.49 = (f32[768]{0:T(1024)S(1)}, f32[768]{0:T(1024)}, u32[]{:S(2)}) copy-start(f32[768]{0:T(1024)} %get-tuple-element.144) | copy-start | bytes 9220
  602.0 6.8 collective-permute-start.17
  608.9 4.9 collective-permute-start.18
  609.3 6.8 collective-permute-start.14
  613.9 5.8 collective-permute-start.19
  (34 other events, 108.0 us)
Sparse Core Ops, SparseCore 0:
  10.9 75.1 all-gather.3
  89.0 62.3 all-gather.5
  353.2 160.7 reduce-scatter.3
  620.7 65.9 all-gather.7

commit v12 on v11

--- a/solution.py
+++ b/solution.py
@@ -365,7 +365,10 @@
                 first_pack[:, :cut], gather_a[::-1], group_size, shard_size
             ),
             hypercube_all_gather(
-                first_pack[:, cut:], gather_b[::-1], group_size, shard_size
+                first_pack[:, cut:],
+                gather_b[::-1][1:2] + gather_b[::-1][:1] + gather_b[::-1][2:],
+                group_size,
+                shard_size,
             ),
         ],
         axis=1,

time: 729 us -> 728 us (level)
  transfers between devices with their start and end apart: 24 -> 24, of which waited for: 17 -> 16; matrix products, arithmetic and copies ran while one was open for 26% -> 26% of each run, Pallas kernels for 23% -> 23%
where the time goes in v12:
time: 728 us; the launch traced here: 717 us
  Pallas kernels  166 us (23%)
  local copies, waits for them, and re-layouts  147 us (20%)
  matrix products  120 us (16%)
  waiting for transfers between devices  99.5 us (14%)
  starting transfers between devices  87.2 us (12%)
  other arithmetic  82.3 us (11%)
  between operations  15.2 us (2%)
    pallas_call x1, Pallas kernels, attention_backward(): pl.pallas_call(_bwd_kernel, out_shape=(jax.ShapeDtypeStruct((heads, lengt...  101 us
    ppermute x10, starting transfers between devices, hypercube_reduce_scatter(): got = lax.ppermute(send, axis, [(j, j ^ 1 << b) for j in range(size)])  75.2 us
    pallas_call x1, Pallas kernels, attention_forward(): pl.pallas_call(_fwd_kernel, out_shape=jax.ShapeDtypeStruct((heads, length...  65.5 us
    all_gather x1, waiting for transfers between devices, per_device(): lax.all_gather(jnp.concatenate([ffn_part, attn_left.astype(jnp.bfloat16),...  49.7 us
    dot_general x1, matrix products, per_device(): jnp.dot(second_low, expand_full, preferred_element_type=jnp.float32)  38.9 us
    ppermute x10, waiting for transfers between devices, hypercube_all_gather(): got = lax.ppermute(cur, axis, [(j, j ^ 1 << b) for j in range(size)])  29.6 us
    ppermute x10, waiting for transfers between devices, hypercube_reduce_scatter(): got = lax.ppermute(send, axis, [(j, j ^ 1 << b) for j in range(size)])  20.2 us
    reduce_sum x1, other arithmetic, per_device(): expand_bias_grad = jnp.sum(grad_pre.astype(jnp.float32), axis=0)  20.1 us
  transfers between devices with their start and end apart: 24, of which 16 were waited for; matrix products, arithmetic and copies ran while one was open for 26% of the time, Pallas kernels for 23%

profile of v12, /device:TPU:0, one launch (start us, length us, event | category | flops | bytes accessed | tf_op | source)
XLA Modules:
  0.0 717.2 jit_solution(10526130844173314319)
XLA Ops:
  19.7 3.0 collective-permute-start
  32.1 4.1 collective-permute-done.6
  41.9 4.3 collective-permute-done.7
  51.6 8.0 %collective-permute-done.8 = bf16[192,1152]{1,0:T(8,128)(2,1)S(1)} collective-permute-done((bf16[192,1152]{1,0:T(8,128)(2,1)S(1)}, bf16[192,1152]{1,0:T(8,128)(2,1)S(1)}, u32[]{:S(2)}, u32[]{:S(2)}) %collective-permute-start.8) | collective-permute-done | bytes 442400 | tf_op jit(solution)/shard_map/ppermute | solution.py:299
  60.9 8.0 %collective-permute-done.3 = bf16[192,1280]{1,0:T(8,128)(2,1)S(1)} collective-permute-done((bf16[192,1280]{1,0:T(8,128)(2,1)S(1)}, bf16[192,1280]{1,0:T(8,128)(2,1)S(1)}, u32[]{:S(2)}, u32[]{:S(2)}) %collective-permute-start.3) | collective-permute-done | bytes 491552 | tf_op jit(solution)/shard_map/ppermute | solution.py:299
  83.0 5.2 add_convert_fusion.2
  102.2 65.5 %shard_map.339 = f32[12,1024,64]{2,1,0:T(8,128)} custom-call(s32[2]{0:T(128)} %and_select_fusion.lo_ref, bf16[12,1024,64]{2,1,0:T(8,128)(2,1)} %copy.235.q_ref, bf16[12,64,1024]{2,1,0:T(8,128)(2,1)} %bitcast.89, bf16[12,1024,64]{2,1,0:T(8,128)(2,1)} %copy.236.v_ref, s32[1024,1]{1,0:T(8,128)} %copy.237.segq_ref, s32[1,1024]{1,0:T(1,128)} %bitcast.125), custom_call_target="tpu_custom_call" | custom-call | flops 1610612736 | bytes 6291456 | tf_op jit(solution)/shard_map/pallas_call | solution.py:127
  167.7 6.3 copy.238
  174.0 3.6 copy.239
  177.6 3.3 reduce_sum.276
  180.9 3.8 multiply_reduce_fusion.4
  185.5 4.2 fusion.44
  190.4 38.9 %fusion.40 = (f32[1024]{0:T(1024)S(1)}, f32[1024,3072]{1,0:T(8,128)S(1)}, f32[1024,3072]{1,0:T(8,128)}, f32[1024,3072]{1,0:T(8,128)}) fusion(f32[3072]{0:T(1024)S(1)} %reshape.556, bf16[768,3840]{1,0:T(8,128)(2,1)} %all-gather.4.cloned.1.call-done, f32[1024,768]{0,1:T(8,128)S(1)} %get-tuple-element.206, f32[768]{0:T(1024)S(1)} %copy-done.54, ...), kind=kOutput, calls=%fused_computation.194 | convolution fusion | flops 5043387392 | bytes 45643776 | tf_op jit(solution)/shard_map/dot_general | solution.py:441
  230.7 3.3 copy-done
  234.1 15.4 %multiply_reduce_fusion = (bf16[3072]{0:T(1024)(128)(2,1)S(1)}, f32[1024]{0:T(1024)S(1)}, f32[1024]{0:T(1024)S(1)}, bf16[3072]{0:T(1024)(128)(2,1)S(1)}, bf16[1024,3072]{1,0:T(8,128)(2,1)}, /*index=5*/f32[1024,3072]{1,0:T(8,128)}) fusion(f32[1024,3072]{1,0:T(8,128)} %copy-done, f32[1024]{0:T(1024)S(1)} %add_rsqrt_fusion, ...), kind=kOutput, calls=%fused_computation.3 | convolution fusion | flops 4869578752 | bytes 37801984 | tf_op jit(solution)/shard_map/td,fd->tf/dot_general | solution.py:460
  249.5 20.1 %fusion.39 = (bf16[3072]{0:T(1024)(128)(2,1)S(1)}, bf16[1024,3072]{1,0:T(8,128)(2,1)S(1)}) fusion(f32[1024,3072]{1,0:T(8,128)} %get-tuple-element.170, f32[1024]{0:T(1024)S(1)} %get-tuple-element.214, f32[1024,3072]{1,0:T(8,128)} %copy-done, f32[1024]{0:T(1024)S(1)} %broadcast_multiply_fusion.2, f32[1024]{0:T(1024)S(1)} %get-tuple-element.215, ...), kind=kLoop, calls=%fused_computation.193 | loop fusion | flops 72348672 | bytes 56670208 | tf_op jit(solution)/shard_map/reduce_sum | solution.py:467
  269.6 7.1 convolution_convert_fusion.1
  276.8 6.8 fusion.45
  283.5 3.5 copy.242
  287.1 3.0 multiply_reduce_fusion.7
  290.1 9.7 %convolution_convert_fusion = bf16[3072,768]{1,0:T(8,128)(2,1)} fusion(bf16[1024,3072]{1,0:T(8,128)(2,1)} %get-tuple-element.171, bf16[1024,768]{1,0:T(8,128)(2,1)S(1)} %copy-done.17), kind=kOutput, calls=%fused_computation.26 | convolution fusion | flops 4834197504 | bytes 12582912 | tf_op jit(solution)/shard_map/tf,td->fd/dot_general | solution.py:456
  299.8 8.5 %reshape.517 = bf16[768,3072]{1,0:T(8,128)(2,1)} reshape(bf16[3072,768]{1,0:T(8,128)(2,1)} %convolution_convert_fusion) | data formatting | bytes 9437184 | tf_op jit(solution)/shard_map/reshape | solution.py:501
  308.2 3.8 convert_reduce_fusion.9
  312.2 3.0 convolution_convert_fusion.2
  319.5 4.7 multiply_reduce_fusion.5
  328.7 18.0 %concatenate.95 = bf16[768,7040]{1,0:T(8,128)(2,1)} concatenate(bf16[768,3072]{1,0:T(8,128)(2,1)} %convolution_convert_fusion.1, bf16[768,3072]{1,0:T(8,128)(2,1)} %reshape.517, bf16[768,768]{1,0:T(8,128)(2,1)} %convolution_convert_fusion.2, bf16[768,1]{1,0:T(8,128)(2,1)S(1)} %reshape.570, bf16[768,1]{1,0:T(8,128)(2,1)} %reshape.571, bf16[768,1]{1,0:T(8,128)(2,1)S(1)} %copy-done.31, ...), dimensions={1} | concatenate | bytes 21626880 | tf_op jit(solution)/shard_map/concatenate | solution.py:498
  346.7 10.1 %copy.258 = bf16[16,2,24,7040]{3,2,1,0:T(8,128)(2,1)} copy(bf16[16,2,24,7040]{3,2,0,1:T(8,128)(2,1)} %bitcast.86) | data formatting | bytes 21626880 | tf_op jit(solution)/shard_map/transpose | solution.py:245
  364.5 100.6 %shard_map.340 = (f32[12,1024,64]{2,1,0:T(8,128)}, f32[12,64,1024]{2,1,0:T(8,128)}, f32[12,64,1024]{2,1,0:T(8,128)}) custom-call(s32[2]{0:T(128)} %and_select_fusion.lo_ref, bf16[12,1024,64]{2,1,0:T(8,128)(2,1)} %copy.235.q_ref, bf16[12,64,1024]{2,1,0:T(8,128)(2,1)} %bitcast.97, bf16[12,1024,64]{2,1,0:T(8,128)(2,1)} %copy.253.k_ref, ...), custom_call_target="tpu_custom_call" | custom-call | flops 4026531840 | bytes 12582912 | tf_op jit(solution)/shard_map/pallas_call | solution.py:155
  465.1 3.4 convert.89
  474.2 9.5 %fusion.46 = (f32[768]{0:T(1024)}, f32[1024,768]{1,0:T(8,128)}) fusion(bf16[768,1280]{1,0:T(8,128)(2,1)} %bitcast.107, bf16[768,1152]{1,0:T(8,128)(2,1)} %bitcast.121, bf16[1024,768]{0,1:T(8,128)(2,1)} %bitcast.111, bf16[1024,768]{0,1:T(8,128)(2,1)} %bitcast.114, bf16[1024,768]{0,1:T(8,128)(2,1)} %bitcast.117), kind=kOutput, calls=%fused_computation.199 | convolution fusion | flops 3645897984 | bytes 11602944 | tf_op jit(solution)/shard_map/te,de->td/dot_general | solution.py:526
  483.7 4.1 copy.257
  487.9 6.0 fusion.35
  493.9 3.6 copy.260
  507.7 8.5 %concatenate.102 = f32[2,16,24,2432]{3,2,0,1:T(8,128)} concatenate(f32[2,16,24,2304]{3,2,0,1:T(8,128)} %copy.260, f32[2,16,24,1]{3,2,0,1:T(8,128)S(1)} %copy.261, f32[2,16,24,1]{3,2,0,1:T(8,128)S(1)} %copy-done.30, f32[2,16,24,1]{3,2,0,1:T(8,128)S(1)} %copy.263, f32[2,16,24,1]{3,2,0,1:T(8,128)S(1)} %copy.264, f32[2,16,24,124]{3,2,0,1:T(8,128)S(1)} %broadcast_in_dim.14), dimensions={3} | concatenate | bytes 14942208 | tf_op jit(solution)/shard_map/concatenate | solution.py:537
  521.3 15.7 %collective-permute-start.10 = (bf16[384,1152]{1,0:T(8,128)(2,1)S(1)}, bf16[384,1152]{1,0:T(8,128)(2,1)S(1)}, u32[]{:S(2)}, u32[]{:S(2)}) collective-permute-start(bf16[384,1152]{1,0:T(8,128)(2,1)S(1)} %bitcast.123), channel_id=1, source_target_pairs={{0,2},{2,0},{4,6},{6,4},{8,10},{10,8},{12,14},{14,12},{16,18},{18,... | collective-permute-start | bytes 2654216 | tf_op jit(solution)/shard_map/ppermute | solution.py:286
  540.8 26.5 %collective-permute-start.16 = (bf16[192,1280]{1,0:T(8,128)(2,1)S(1)}, bf16[192,1280]{1,0:T(8,128)(2,1)S(1)}, u32[]{:S(2)}, u32[]{:S(2)}) collective-permute-start(bf16[192,1280]{1,0:T(8,128)(2,1)S(1)} %select_convert_fusion.2), channel_id=1, source_target_pairs={{0,8},{2,10},{4,12},{6,14},{8,0},{10,2},{12,4},{14,6},{16,24},{18,... | collective-permute-start | bytes 1474568 | tf_op jit(solution)/shard_map/ppermute | solution.py:286
  567.5 10.4 %collective-permute-start.12 = (bf16[96,1152]{1,0:T(8,128)(2,1)S(1)}, bf16[96,1152]{1,0:T(8,128)(2,1)S(1)}, u32[]{:S(2)}, u32[]{:S(2)}) collective-permute-start(bf16[96,1152]{1,0:T(8,128)(2,1)S(1)} %select_convert_fusion.5), channel_id=1, source_target_pairs={{0,8},{2,10},{4,12},{6,14},{8,0},{10,2},{12,4},{14,6},{16,24},{18,... | collective-permute-start | bytes 663560 | tf_op jit(solution)/shard_map/ppermute | solution.py:286
  579.2 4.4 collective-permute-done.12
  583.7 17.3 %collective-permute-start.13 = (bf16[48,1152]{1,0:T(8,128)(2,1)S(1)}, bf16[48,1152]{1,0:T(8,128)(2,1)S(1)}, u32[]{:S(2)}, u32[]{:S(2)}) collective-permute-start(bf16[48,1152]{1,0:T(8,128)(2,1)S(1)} %select_convert_fusion.7), channel_id=1, source_target_pairs={{0,1},{1,0},{2,3},{3,2},{4,5},{5,4},{6,7},{7,6},{8,9},{9,8},{10,11... | collective-permute-start | bytes 331784 | tf_op jit(solution)/shard_map/ppermute | solution.py:286
  603.7 4.1 collective-permute-done.17
  609.9 2.9 collective-permute-done.18
  615.2 3.5 collective-permute-done.19
  619.6 9.3 %add_convert_fusion.3 = bf16[1024,768]{0,1:T(8,128)(2,1)S(1)} fusion(f32[1024,768]{0,1:T(8,128)} %copy-done.3, bf16[1024,3072]{1,0:T(8,128)(2,1)} %get-tuple-element.171, bf16[3072,768]{1,0:T(8,128)(2,1)} %all-gather.6.cloned.1.call-done, f32[768]{0:T(1024)S(1)} %copy-done.49), kind=kOutput, calls=%fused_computation.62 | convolution fusion | flops 4834197504 | bytes 15731712 | tf_op jit(solution)/shard_map/dot_general | solution.py:451
  630.5 3.9 fusion.22
  636.0 49.7 %all-gather.8.cloned.1.call-done = bf16[384,9472]{1,0:T(8,128)(2,1)} async-done(((bf16[24,9472]{1,0:T(8,128)(2,1)}), bf16[384,9472]{1,0:T(8,128)(2,1)}) %all-gather.8.cloned.1.call-update) | async-done | bytes 7274512 | tf_op jit(solution)/shard_map/all_gather | solution.py:553
  691.3 7.4 %slice_convert_fusion = (f32[384,3072]{1,0:T(8,128)}, f32[384,3072]{1,0:T(8,128)}) fusion(bf16[384,9472]{1,0:T(8,128)(2,1)} %all-gather.8.cloned.1.call-done), kind=kLoop, calls=%fused_computation.71 | loop fusion | flops 2359296 | bytes 14155776 | tf_op jit(solution)/shard_map/convert_element_type | solution.py:574
  698.7 6.1 reshape.560
  704.8 3.5 slice_convert_fusion.2
  (309 shorter events, 126.4 us)
Async XLA Ops:
  7.2 178.2 %all-gather.4.cloned.1.call-start = ((), (), s32[]{:S(2)}) async-start(), calls=%async_computation.1 | async-start | bytes 6082560 | tf_op jit(solution)/shard_map/all_gather | solution.py:393
  8.9 225.2 %all-gather.6.cloned.1.call-start = ((), (), s32[]{:S(2)}) async-start(), calls=%async_computation.2 | async-start | bytes 4866048 | tf_op jit(solution)/shard_map/all_gather | solution.py:396
  19.7 12.3 %collective-permute-start = (bf16[24,1280]{1,0:T(8,128)(2,1)S(1)}, bf16[24,1280]{1,0:T(8,128)(2,1)S(1)}, u32[]{:S(2)}, u32[]{:S(2)}) collective-permute-start(bf16[24,1280]{1,0:T(8,128)(2,1)S(1)} %slice.296), channel_id=1, source_target_pairs={{0,1},{1,0},{2,3},{3,2},{4,5},{5,4},{6,7},{7,6},{8,9},{9,8},{10,11... | collective-permute-start | bytes 184328 | tf_op jit(solution)/shard_map/ppermute | solution.py:299
  23.6 7.8 %collective-permute-start.5 = (bf16[24,1152]{1,0:T(8,128)(2,1)S(1)}, bf16[24,1152]{1,0:T(8,128)(2,1)S(1)}, u32[]{:S(2)}, u32[]{:S(2)}) collective-permute-start(bf16[24,1152]{1,0:T(8,128)(2,1)S(1)} %slice.233), channel_id=1, source_target_pairs={{0,16},{2,18},{4,20},{6,22},{8,24},{10,26},{12,28},{14,30},{16,0},... | collective-permute-start | bytes 165896 | tf_op jit(solution)/shard_map/ppermute | solution.py:299
  26.2 490.1 %reduce-scatter.4.cloned.1.call-start = ((), (), s32[]{:S(2)}) async-start(), calls=%async_computation.4 | async-start | bytes 11151360
  28.0 45.3 %copy-start.36 = (s32[1024]{0:T(1024)}, s32[1024]{0:T(1024)S(1)}, u32[]{:S(2)}) copy-start(s32[1024]{0:T(1024)S(1)} %fusion.30) | copy-start | bytes 12292
  29.9 155.6 %copy-start.1 = (bf16[1024,768]{0,1:T(8,128)(2,1)}, bf16[1024,768]{0,1:T(8,128)(2,1)S(1)}, u32[]{:S(2)}) copy-start(bf16[1024,768]{0,1:T(8,128)(2,1)S(1)} %copy.219) | copy-start | bytes 4718596
  30.1 52.8 %copy-start.34 = (f32[1024]{0:T(1024)}, f32[1024]{0:T(1024)S(1)}, u32[]{:S(2)}) copy-start(f32[1024]{0:T(1024)S(1)} %broadcast_multiply_fusion.11) | copy-start | bytes 12292
  30.6 52.3 %copy-start.42 = (f32[1024]{0:T(1024)}, f32[1024]{0:T(1024)S(1)}, u32[]{:S(2)}) copy-start(f32[1024]{0:T(1024)S(1)} %add_rsqrt_fusion.3) | copy-start | bytes 12292
  31.4 4.8 collective-permute-start.6
  32.0 8.2 %collective-permute-start.1 = (bf16[48,1280]{1,0:T(8,128)(2,1)S(1)}, bf16[48,1280]{1,0:T(8,128)(2,1)S(1)}, u32[]{:S(2)}, u32[]{:S(2)}) collective-permute-start(bf16[48,1280]{1,0:T(8,128)(2,1)S(1)} %pad_maximum_fusion.14), channel_id=1, source_target_pairs={{0,16},{2,18},{4,20},{6,22},{8,24},{10,26},{12,28},{14,30},{16,0},... | collective-permute-start | bytes 368648 | tf_op jit(solution)/shard_map/ppermute | solution.py:299
  36.3 10.0 %collective-permute-start.7 = (bf16[96,1152]{1,0:T(8,128)(2,1)S(1)}, bf16[96,1152]{1,0:T(8,128)(2,1)S(1)}, u32[]{:S(2)}, u32[]{:S(2)}) collective-permute-start(bf16[96,1152]{1,0:T(8,128)(2,1)S(1)} %pad_maximum_fusion.12), channel_id=1, source_target_pairs={{0,8},{2,10},{4,12},{6,14},{8,0},{10,2},{12,4},{14,6},{16,24},{18,... | collective-permute-start | bytes 663560 | tf_op jit(solution)/shard_map/ppermute | solution.py:299
  40.4 10.5 %collective-permute-start.2 = (bf16[96,1280]{1,0:T(8,128)(2,1)S(1)}, bf16[96,1280]{1,0:T(8,128)(2,1)S(1)}, u32[]{:S(2)}, u32[]{:S(2)}) collective-permute-start(bf16[96,1280]{1,0:T(8,128)(2,1)S(1)} %pad_maximum_fusion.11), channel_id=1, source_target_pairs={{0,4},{2,6},{4,0},{6,2},{8,12},{10,14},{12,8},{14,10},{16,20},{18,... | collective-permute-start | bytes 737288 | tf_op jit(solution)/shard_map/ppermute | solution.py:299
  46.4 13.3 %collective-permute-start.8 = (bf16[192,1152]{1,0:T(8,128)(2,1)S(1)}, bf16[192,1152]{1,0:T(8,128)(2,1)S(1)}, u32[]{:S(2)}, u32[]{:S(2)}) collective-permute-start(bf16[192,1152]{1,0:T(8,128)(2,1)S(1)} %pad_maximum_fusion.10), channel_id=1, source_target_pairs={{0,4},{2,6},{4,0},{6,2},{8,12},{10,14},{12,8},{14,10},{16,20},{18,... | collective-permute-start | bytes 1327112 | tf_op jit(solution)/shard_map/ppermute | solution.py:299
  51.0 17.9 %collective-permute-start.3 = (bf16[192,1280]{1,0:T(8,128)(2,1)S(1)}, bf16[192,1280]{1,0:T(8,128)(2,1)S(1)}, u32[]{:S(2)}, u32[]{:S(2)}) collective-permute-start(bf16[192,1280]{1,0:T(8,128)(2,1)S(1)} %pad_maximum_fusion.8), channel_id=1, source_target_pairs={{0,8},{2,10},{4,12},{6,14},{8,0},{10,2},{12,4},{14,6},{16,24},{18,... | collective-permute-start | bytes 1474568 | tf_op jit(solution)/shard_map/ppermute | solution.py:299
  59.8 9.1 %copy-start.25 = (bf16[192,1152]{1,0:T(8,128)(2,1)}, bf16[192,1152]{1,0:T(8,128)(2,1)S(1)}, u32[]{:S(2)}) copy-start(bf16[192,1152]{1,0:T(8,128)(2,1)S(1)} %get-tuple-element.189) | copy-start | bytes 1327108
  59.8 11.5 %copy-start.15 = (bf16[1024,768]{1,0:T(8,128)(2,1)S(1)}, bf16[1024,768]{1,0:T(8,128)(2,1)}, u32[]{:S(2)}) copy-start(bf16[1024,768]{1,0:T(8,128)(2,1)} %param.39) | copy-start | bytes 4718596
  60.8 14.4 %collective-permute-start.9 = (bf16[384,1152]{1,0:T(8,128)(2,1)}, bf16[384,1152]{1,0:T(8,128)(2,1)}, u32[]{:S(2)}, u32[]{:S(2)}) collective-permute-start(bf16[384,1152]{1,0:T(8,128)(2,1)} %pad_maximum_fusion.7), channel_id=1, source_target_pairs={{0,2},{2,0},{4,6},{6,4},{8,10},{10,8},{12,14},{14,12},{16,18},{18,... | collective-permute-start | bytes 2654216 | tf_op jit(solution)/shard_map/ppermute | solution.py:299
  70.9 6.5 collective-permute-start.4
  77.3 5.7 copy-start.27
  80.1 8.1 %copy-start.13 = (bf16[2,2,2,2,2,24,1280]{6,5,4,3,2,1,0:T(8,128)(2,1)}, bf16[2,2,2,2,2,24,1280]{6,5,4,3,2,1,0:T(8,128)(2,1)S(1)}, u32[]{:S(2)}) copy-start(bf16[2,2,2,2,2,24,1280]{6,5,4,3,2,1,0:T(8,128)(2,1)S(1)} %copy.230) | copy-start | bytes 5898244
  81.5 6.7 copy-start.40
  81.5 6.7 copy-start.50
  92.2 5.5 copy-start.7
  99.4 68.3 %copy-start.8 = (bf16[1024,768]{0,1:T(8,128)(2,1)}, bf16[1024,768]{0,1:T(8,128)(2,1)S(1)}, u32[]{:S(2)}) copy-start(bf16[1024,768]{0,1:T(8,128)(2,1)S(1)} %copy.234) | copy-start | bytes 4718596
  184.7 4.9 copy-start.46
  185.2 48.9 %copy-start.37 = (f32[3072]{0:T(1024)}, f32[3072]{0:T(1024)S(1)}, u32[]{:S(2)}) copy-start(f32[3072]{0:T(1024)S(1)} %reshape.557) | copy-start | bytes 36868
  189.7 39.6 %copy-start.3 = (f32[1024,768]{0,1:T(8,128)}, f32[1024,768]{0,1:T(8,128)S(1)}, u32[]{:S(2)}) copy-start(f32[1024,768]{0,1:T(8,128)S(1)} %get-tuple-element.206) | copy-start | bytes 9437188
  229.3 4.7 copy-start
  229.3 4.7 copy-start.16
  234.1 42.7 %slice-start = ((s8[5898240]{0:T(1024)(128)(4,1)}), s8[1703936]{0:T(1024)(128)(4,1)S(1)}, s32[]{:S(2)}) async-start(s8[5898240]{0:T(1024)(128)(4,1)} %bitcast.138), calls=%async_computation.5 | async-start | bytes 3407872
  249.5 20.1 %copy-start.4 = (f32[1024,768]{0,1:T(8,128)S(1)}, f32[1024,768]{0,1:T(8,128)}, u32[]{:S(2)}) copy-start(f32[1024,768]{0,1:T(8,128)} %copy-done.3) | copy-start | bytes 9437188
  249.5 27.3 %slice-start.1 = ((s8[5898240]{0:T(1024)(128)(4,1)}), s8[4194304]{0:T(1024)(128)(4,1)S(1)}, s32[]{:S(2)}) async-start(s8[5898240]{0:T(1024)(128)(4,1)} %bitcast.138), calls=%async_computation.6 | async-start | bytes 8388608
  312.1 7.4 %copy-start.11 = (f32[1024,768]{1,0:T(8,128)S(1)}, f32[1024,768]{1,0:T(8,128)}, u32[]{:S(2)}) copy-start(f32[1024,768]{1,0:T(8,128)} %copy.239) | copy-start | bytes 9437188
  356.8 328.8 %all-gather.8.cloned.1.call-start = ((), (), s32[]{:S(2)}) async-start(), calls=%async_computation.3 | async-start | bytes 7729152 | tf_op jit(solution)/shard_map/all_gather | solution.py:553
  465.1 6.2 copy-start.14
  521.3 17.8 %collective-permute-start.10 = (bf16[384,1152]{1,0:T(8,128)(2,1)S(1)}, bf16[384,1152]{1,0:T(8,128)(2,1)S(1)}, u32[]{:S(2)}, u32[]{:S(2)}) collective-permute-start(bf16[384,1152]{1,0:T(8,128)(2,1)S(1)} %bitcast.123), channel_id=1, source_target_pairs={{0,2},{2,0},{4,6},{6,4},{8,10},{10,8},{12,14},{14,12},{16,18},{18,... | collective-permute-start | bytes 2654216 | tf_op jit(solution)/shard_map/ppermute | solution.py:286
  537.5 3.0 collective-permute-start.15
  539.4 27.9 %collective-permute-start.11 = (bf16[192,1152]{1,0:T(8,128)(2,1)S(1)}, bf16[192,1152]{1,0:T(8,128)(2,1)S(1)}, u32[]{:S(2)}, u32[]{:S(2)}) collective-permute-start(bf16[192,1152]{1,0:T(8,128)(2,1)S(1)} %select_convert_fusion.3), channel_id=1, source_target_pairs={{0,4},{2,6},{4,0},{6,2},{8,12},{10,14},{12,8},{14,10},{16,20},{18,... | collective-permute-start | bytes 1327112 | tf_op jit(solution)/shard_map/ppermute | solution.py:286
  540.8 38.2 %collective-permute-start.16 = (bf16[192,1280]{1,0:T(8,128)(2,1)S(1)}, bf16[192,1280]{1,0:T(8,128)(2,1)S(1)}, u32[]{:S(2)}, u32[]{:S(2)}) collective-permute-start(bf16[192,1280]{1,0:T(8,128)(2,1)S(1)} %select_convert_fusion.2), channel_id=1, source_target_pairs={{0,8},{2,10},{4,12},{6,14},{8,0},{10,2},{12,4},{14,6},{16,24},{18,... | collective-permute-start | bytes 1474568 | tf_op jit(solution)/shard_map/ppermute | solution.py:286
  567.5 16.1 %collective-permute-start.12 = (bf16[96,1152]{1,0:T(8,128)(2,1)S(1)}, bf16[96,1152]{1,0:T(8,128)(2,1)S(1)}, u32[]{:S(2)}, u32[]{:S(2)}) collective-permute-start(bf16[96,1152]{1,0:T(8,128)(2,1)S(1)} %select_convert_fusion.5), channel_id=1, source_target_pairs={{0,8},{2,10},{4,12},{6,14},{8,0},{10,2},{12,4},{14,6},{16,24},{18,... | collective-permute-start | bytes 663560 | tf_op jit(solution)/shard_map/ppermute | solution.py:286
  583.6 35.2 %copy-start.33 = (bf16[24,7040]{1,0:T(8,128)(2,1)S(1)}, bf16[24,7040]{1,0:T(8,128)(2,1)}, u32[]{:S(2)}) copy-start(bf16[24,7040]{1,0:T(8,128)(2,1)} %reduce-scatter.4.cloned.1.call-done) | copy-start | bytes 1013764
  583.7 20.0 %collective-permute-start.13 = (bf16[48,1152]{1,0:T(8,128)(2,1)S(1)}, bf16[48,1152]{1,0:T(8,128)(2,1)S(1)}, u32[]{:S(2)}, u32[]{:S(2)}) collective-permute-start(bf16[48,1152]{1,0:T(8,128)(2,1)S(1)} %select_convert_fusion.7), channel_id=1, source_target_pairs={{0,1},{1,0},{2,3},{3,2},{4,5},{5,4},{6,7},{7,6},{8,9},{9,8},{10,11... | collective-permute-start | bytes 331784 | tf_op jit(solution)/shard_map/ppermute | solution.py:286
  601.0 18.6 %copy-start.49 = (f32[768]{0:T(1024)S(1)}, f32[768]{0:T(1024)}, u32[]{:S(2)}) copy-start(f32[768]{0:T(1024)} %get-tuple-element.144) | copy-start | bytes 9220
  601.0 6.8 collective-permute-start.17
  607.9 4.9 collective-permute-start.18
  608.3 6.9 collective-permute-start.14
  612.9 5.8 collective-permute-start.19
  (34 other events, 106.5 us)
Sparse Core Ops, SparseCore 0:
  10.9 73.4 all-gather.3
  87.4 62.3 all-gather.5
  356.9 155.6 reduce-scatter.3
  619.7 65.8 all-gather.7
